TPU v7x, 32 devices: a whole 2x2x4 slice. The times are simulated.
32 devices in a mesh: seq: 8 (over z, x), tp: 4 (over y, core).
Axes of the slice: x: 2, y: 2, z: 4, core: 2. Of those that a mesh axis runs over, the one named last changes fastest.
Arguments:
- query_in: bfloat16 [4096, 4096], P('seq', 'tp'), may hold values from -6 to 6
- key_in: bfloat16 [4096, 4096], P('seq', 'tp'), may hold values from -6 to 6
- value_in: bfloat16 [4096, 4096], P('seq', 'tp'), may hold values from -6 to 6
- feature_taps: float32 [7, 3, 4096], P(None, None, 'tp'), may hold values from -2 to 2
- filter_taps: bfloat16 [256, 128], P('tp'), may hold values from -0.5 to 0.5
- out_weight: bfloat16 [4096, 4096], P('tp'), may hold values from -0.09375 to 0.09375
- cotangent: bfloat16 [4096, 4096], P(('seq', 'tp')), may hold values from -6 to 6
Outputs:
- block_out: bfloat16 [4096, 4096], P(('seq', 'tp'))
- query_grad: bfloat16 [4096, 4096], P('seq', 'tp')
- key_grad: bfloat16 [4096, 4096], P('seq', 'tp')
- value_grad: bfloat16 [4096, 4096], P('seq', 'tp')
- weight_grad: bfloat16 [4096, 4096], P('tp', 'seq')
All inputs are finite; a program needn't handle non-finite values.
Results may differ from a plain program's by a relative error of at most 0.012.
Values may be sent and summed in bfloat16 or wider, within the bound.
No kernel may reach another device: no remote copies, remote signals or barrier semaphores. Data moves between devices by JAX's collectives and lax.ppermute only.
A program may use at most 128 MiB of HBM per device.

v0:
```python
import functools

import jax
import jax.numpy as jnp
from jax import lax
from jax.sharding import PartitionSpec as P


def passed_along(value, axis, steps):
    count = lax.axis_size(axis)
    leading, last = (max(0, -steps), min(count, count - steps))
    return lax.ppermute(value, axis, [(source, source + steps) for source in range(leading, last)])


def featurize(extended, feature_taps, out_rows):
    tap_span = feature_taps.shape[0]
    summed = jnp.zeros((out_rows,) + extended.shape[1:], jnp.float32)
    for offset in range(tap_span):
        first_row = tap_span - 1 - offset
        summed = summed + feature_taps[offset] * extended[first_row : first_row + out_rows].astype(
            jnp.float32
        )
    return summed


def spread_back(extended, feature_taps, out_rows):
    tap_span = feature_taps.shape[0]
    summed = jnp.zeros((out_rows,) + extended.shape[1:], jnp.float32)
    for offset in range(tap_span):
        summed = summed + feature_taps[offset] * extended[offset : offset + out_rows]
    return summed


def band_table(filter_taps, reverse=False):
    tap_count = filter_taps.shape[1]
    window_rows = 2 * tap_count
    lag_index = jnp.arange(tap_count)[:, None, None]
    row_index = jnp.arange(window_rows)[None, :, None]
    col_index = jnp.arange(tap_count)[None, None, :]
    if reverse:
        select = (row_index - col_index == lag_index).astype(jnp.bfloat16)
    else:
        select = (col_index + tap_count - row_index == lag_index).astype(jnp.bfloat16)
    select = select.reshape(tap_count, window_rows * tap_count)
    toeplitz_table = jnp.dot(filter_taps, select, preferred_element_type=jnp.float32)
    return toeplitz_table.astype(jnp.bfloat16).reshape(filter_taps.shape[0], window_rows, tap_count)


def band_mix(padded_rows, toeplitz_table):
    group_count, window_rows, tap_count = toeplitz_table.shape
    row_count = padded_rows.shape[0] - tap_count
    block_count = row_count // tap_count
    channels = padded_rows.shape[1]
    members = channels // group_count
    by_channel = padded_rows.T
    lower_half = by_channel[:, :row_count].reshape(group_count, members * block_count, tap_count)
    upper_half = by_channel[:, tap_count:].reshape(group_count, members * block_count, tap_count)
    mixed = jnp.einsum(
        "gmw,gwt->gmt", lower_half, toeplitz_table[:, :tap_count], preferred_element_type=jnp.float32
    ) + jnp.einsum(
        "gmw,gwt->gmt", upper_half, toeplitz_table[:, tap_count:], preferred_element_type=jnp.float32
    )
    mixed = mixed.reshape(group_count, members, block_count, tap_count)
    return mixed.transpose(2, 3, 0, 1).reshape(row_count, channels)


def per_device(query_in, key_in, value_in, feature_taps, filter_taps, out_weight, cotangent, ring):
    row_count, channels = query_in.shape
    tap_count = filter_taps.shape[1]
    tap_span = feature_taps.shape[0]
    inputs = (query_in, key_in, value_in)
    before = passed_along(
        jnp.stack([rows[row_count - tap_span + 1 :] for rows in inputs], axis=0), "seq", 1
    )
    query_feat, key_feat, value_feat = (
        featurize(jnp.concatenate([before[i], inputs[i]], axis=0), feature_taps[:, i], row_count)
        for i in range(3)
    )
    mix_rows = (key_feat * value_feat).astype(jnp.bfloat16)
    mix_before = passed_along(mix_rows[row_count - tap_count :], "seq", 1)
    padded_mix = jnp.concatenate([mix_before, mix_rows], axis=0)
    toeplitz_rows = band_table(filter_taps)
    long_conv = band_mix(padded_mix, toeplitz_rows)
    gated_rows = (query_feat * long_conv).astype(jnp.bfloat16)
    block_out = lax.psum_scatter(
        jnp.dot(gated_rows, out_weight, preferred_element_type=jnp.float32).astype(jnp.bfloat16),
        "tp",
        scatter_dimension=0,
        tiled=True,
    )
    full_cotangent = lax.all_gather(cotangent, "tp", axis=0, tiled=True)
    seq_count = lax.axis_size("seq")
    grad_scale = (row_count * seq_count) ** (-0.5)
    summed_grad = ring_reduce_scatter(gated_rows, full_cotangent, grad_scale, ring)
    grad_gated = lax.dot_general(
        full_cotangent, out_weight, (((1,), (1,)), ((), ())), preferred_element_type=jnp.float32
    )
    grad_conv = (grad_gated * query_feat).astype(jnp.bfloat16)
    grad_query = grad_gated * long_conv
    conv_after = passed_along(grad_conv[:tap_count], "seq", -1)
    grad_mix = band_mix(
        jnp.concatenate([grad_conv, conv_after], axis=0), band_table(filter_taps, reverse=True)
    )
    grad_features = (grad_query, grad_mix * value_feat, grad_mix * key_feat)
    features_after = passed_along(
        jnp.stack([rows[: tap_span - 1] for rows in grad_features], axis=0).astype(jnp.bfloat16),
        "seq",
        -1,
    ).astype(jnp.float32)
    query_grad, key_grad, value_grad = (
        spread_back(
            jnp.concatenate([grad_features[i], features_after[i]], axis=0),
            feature_taps[:, i],
            row_count,
        ).astype(jnp.bfloat16)
        for i in range(3)
    )
    return (block_out, query_grad, key_grad, value_grad, summed_grad)


def ring_reduce_scatter(gated_rows, full_cotangent, grad_scale, ring):
    count = len(ring)
    width = full_cotangent.shape[1] // count
    half = width // 2
    place_of = [0] * count
    for place, member in enumerate(ring):
        place_of[member] = place
    place = jnp.asarray(place_of, jnp.int32)[lax.axis_index("seq")]
    members = jnp.asarray(ring, jnp.int32)
    forward = [(ring[i], ring[(i + 1) % count]) for i in range(count)]
    backward = [(ring[(i + 1) % count], ring[i]) for i in range(count)]

    local_grad = (
        lax.dot_general(
            gated_rows, full_cotangent, (((0,), (0,)), ((), ())), preferred_element_type=jnp.float32
        )
        * grad_scale
    )

    def contribution(step, direction):
        owner = members[(place - direction * (1 + step)) % count]
        first = owner * width + (0 if direction == 1 else half)
        return lax.dynamic_slice_in_dim(local_grad, first, half, 1)

    ahead = contribution(0, 1)
    behind = contribution(0, -1)
    for step in range(1, count):
        ahead = lax.ppermute(ahead.astype(jnp.bfloat16), "seq", forward).astype(jnp.float32)
        behind = lax.ppermute(behind.astype(jnp.bfloat16), "seq", backward).astype(jnp.float32)
        ahead = ahead + contribution(step, 1)
        behind = behind + contribution(step, -1)
    return jnp.concatenate([ahead, behind], axis=1).astype(jnp.bfloat16)


def ring_order(mesh):
    axis = mesh.axis_names.index("seq")
    members = jnp.moveaxis(jnp.arange(mesh.devices.size).reshape(mesh.devices.shape), axis, 0)
    devices = mesh.devices.reshape(-1)
    column = [devices[int(i)] for i in members[:, 0].reshape(-1)]
    count = len(column)
    try:
        coords = [tuple(d.coords) + (d.core_on_chip,) for d in column]
    except AttributeError:
        return list(range(count))
    varying = [k for k in range(len(coords[0])) if len({c[k] for c in coords}) > 1]
    if len(varying) != 2:
        return list(range(count))
    sizes = [len({c[k] for c in coords}) for k in varying]
    if 2 not in sizes or sizes[0] * sizes[1] != count:
        return list(range(count))
    short, long = (varying[0], varying[1]) if sizes[0] == 2 else (varying[1], varying[0])
    low_short = min(c[short] for c in coords)
    lanes = [[], []]
    for index, c in enumerate(coords):
        lanes[0 if c[short] == low_short else 1].append((c[long], index))
    return [i for _, i in sorted(lanes[0])] + [i for _, i in sorted(lanes[1], reverse=True)]


def solution(mesh):
    placed = (
        P("seq", "tp"),
        P("seq", "tp"),
        P("seq", "tp"),
        P(None, None, "tp"),
        P("tp", None),
        P("tp", None),
        P(("seq", "tp"), None),
    )
    ring = ring_order(mesh)
    return jax.shard_map(
        functools.partial(per_device, ring=ring),
        mesh=mesh,
        in_specs=placed,
        out_specs=(
            P(("seq", "tp"), None),
            P("seq", "tp"),
            P("seq", "tp"),
            P("seq", "tp"),
            P("tp", "seq"),
        ),
        check_vma=False,
    )
```

profile of v0, /device:TPU:0, one launch (start us, length us, event | category | flops | bytes accessed | tf_op | source)
XLA Modules:
  0.0 257.0 jit_solution(16649966832498616983)
XLA Ops:
  9.5 4.9 %collective-permute-start = (bf16[3,6,1024]{2,1,0:T(8,128)(2,1)S(1)}, bf16[3,6,1024]{2,1,0:T(8,128)(2,1)S(1)}, u32[]{:S(2)}, u32[]{:S(2)}) collective-permute-start(bf16[3,6,1024]{2,1,0:T(8,128)(2,1)S(1)} %pad_maximum_fusion.7), channel_id=1, source_target_pairs={{0,4},{4,8},{8,12},{12,16},{16,20},{20,24},{24,28},{1,5},{5,9},{9,... | collective-permute-start | bytes 110600 | tf_op jit(solution)/shard_map/ppermute | solution.py:12
  14.3 1.3 fusion.95
  15.7 6.1 %fusion.3 = bf16[8,8,256,128]{3,1,2,0:T(8,128)(2,1)} fusion(bf16[64,128]{1,0:T(8,128)(2,1)S(1)} %copy-done, s32[32768]{0:T(1024)S(1)} %subtract_bitcast_fusion), kind=kOutput, calls=%fused_computation.39 | convolution fusion | flops 543162368 | bytes 4341760 | tf_op jit(solution)/shard_map/dot_general | solution.py:45
  21.7 25.0 %all-gather.2.cloned.1.call-done = bf16[512,4096]{1,0:T(8,128)(2,1)} async-done(((bf16[128,4096]{1,0:T(8,128)(2,1)}), bf16[512,4096]{1,0:T(8,128)(2,1)}) %all-gather.2.cloned.1.call-update) | async-done | bytes 4194320 | tf_op jit(solution)/shard_map/all_gather | solution.py:91
  46.8 11.2 %multiply_convert_fusion = (bf16[512,1024]{1,0:T(8,128)(2,1)S(1)}, f32[512,1024]{1,0:T(8,128)}, f32[512,1024]{1,0:T(8,128)}) fusion(bf16[512,1024]{1,0:T(8,128)(2,1)S(1)} %copy-done.11, bf16[6,1024]{1,0:T(8,128)(2,1)S(1)} %get-tuple-element.59, f32[1024]{0:T(1024)S(1)} %bitcast.169, f32[1024]{0:T(1024)S(1)} %bitcast.171, f32[1024]{0:T(1024)S(1)} %bitcast.173, ...), kind=kOutput, calls=%fused_computation.116 | convolution fusion | flops 4315938816 | bytes 18915328 | tf_op jit(solution)/shard_map/dot_general | solution.py:95
  58.0 1.5 collective-permute-start.2
  59.5 3.2 %copy.28 = bf16[8,8,256,128]{3,2,1,0:T(8,128)(2,1)} copy(bf16[8,8,256,128]{3,1,2,0:T(8,128)(2,1)S(1)} %copy-done.7) | data formatting | bytes 8388608
  63.5 4.8 %collective-permute-done.2 = bf16[128,1024]{1,0:T(8,128)(2,1)S(1)} collective-permute-done((bf16[128,1024]{1,0:T(8,128)(2,1)S(1)}, bf16[128,1024]{1,0:T(8,128)(2,1)S(1)}, u32[]{:S(2)}, u32[]{:S(2)}) %collective-permute-start.2) | collective-permute-done | bytes 262176 | tf_op jit(solution)/shard_map/ppermute | solution.py:12
  70.9 1.5 copy.22
  73.1 2.4 fusion.58
  76.6 1.5 copy.32
  78.1 2.0 copy.24
  80.2 3.0 %fusion.91 = (f32[512,1024]{1,0:T(8,128)}, f32[512,1024]{1,0:T(8,128)S(1)}) fusion(f32[512,1024]{1,0:T(8,128)S(1)} %copy.24, bf16[512,1024]{1,0:T(8,128)(2,1)S(1)} %copy-done.8, bf16[6,1024]{1,0:T(8,128)(2,1)S(1)} %get-tuple-element.58, f32[1024]{0:T(1024)S(1)} %bitcast.151, f32[1024]{0:T(1024)S(1)} %bitcast.153, f32[1024]{0:T(1024)S(1)} %bitcast.155, ...), kind=kLoop, calls=%fused_computation.191 | loop fusion | flops 20447232 | bytes 7380992 | tf_op jit(solution)/shard_map/mul | solution.py:104
  83.2 3.0 %fusion.90 = (f32[512,1024]{1,0:T(8,128)}, f32[512,1024]{1,0:T(8,128)S(1)}) fusion(f32[512,1024]{1,0:T(8,128)S(1)} %copy.24, bf16[512,1024]{1,0:T(8,128)(2,1)S(1)} %copy-done.9, bf16[6,1024]{1,0:T(8,128)(2,1)S(1)} %get-tuple-element.57, f32[1024]{0:T(1024)S(1)} %bitcast.167, f32[1024]{0:T(1024)S(1)} %bitcast.165, f32[1024]{0:T(1024)S(1)} %bitcast.143, ...), kind=kLoop, calls=%fused_computation.190 | loop fusion | flops 20447232 | bytes 7380992 | tf_op jit(solution)/shard_map/mul | solution.py:104
  86.7 4.3 %collective-permute-start.1 = (bf16[128,1024]{1,0:T(8,128)(2,1)S(1)}, bf16[128,1024]{1,0:T(8,128)(2,1)S(1)}, u32[]{:S(2)}, u32[]{:S(2)}) collective-permute-start(bf16[128,1024]{1,0:T(8,128)(2,1)S(1)} %slice.421), channel_id=1, source_target_pairs={{0,4},{4,8},{8,12},{12,16},{16,20},{20,24},{24,28},{1,5},{5,9},{9,... | collective-permute-start | bytes 786440 | tf_op jit(solution)/shard_map/ppermute | solution.py:12
  91.1 3.9 %fusion.2 = bf16[8,8,256,128]{3,1,2,0:T(8,128)(2,1)S(1)} fusion(bf16[64,128]{1,0:T(8,128)(2,1)S(1)} %copy-done, s32[32768]{0:T(1024)S(1)} %subtract_bitcast_fusion.1), kind=kOutput, calls=%fused_computation.38 | convolution fusion | flops 543162368 | bytes 4341760 | tf_op jit(solution)/shard_map/dot_general | solution.py:45
  95.0 3.2 %copy.26 = bf16[8,8,256,128]{3,2,1,0:T(8,128)(2,1)} copy(bf16[8,8,256,128]{3,1,2,0:T(8,128)(2,1)S(1)} %fusion.2) | data formatting | bytes 8388608
  100.7 1.5 copy.18
  102.9 2.4 fusion.62
  106.6 1.9 copy.20
  108.4 3.5 %fusion.92 = (f32[512,1024]{1,0:T(8,128)S(1)}, bf16[512,1024]{1,0:T(8,128)(2,1)S(1)}) fusion(f32[512,1024]{1,0:T(8,128)} %get-tuple-element.76, f32[512,1024]{1,0:T(8,128)} %copy.20, f32[512,1024]{1,0:T(8,128)} %get-tuple-element.10), kind=kLoop, calls=%fused_computation.192 | loop fusion | flops 1572864 | bytes 9437184 | tf_op jit(solution)/shard_map/mul | solution.py:99
  111.9 9.5 %convolution_convert_fusion.2 = bf16[512,4096]{1,0:T(8,128)(2,1)} fusion(bf16[512,1024]{1,0:T(8,128)(2,1)S(1)} %get-tuple-element.28, bf16[1024,4096]{1,0:T(8,128)(2,1)} %param.14), kind=kOutput, calls=%fused_computation.7 | convolution fusion | flops 4297064448 | bytes 13631488 | tf_op jit(solution)/shard_map/dot_general | solution.py:86
  135.5 6.5 %convolution_multiply_fusion = f32[1024,4096]{1,0:T(8,128)S(1)} fusion(bf16[512,1024]{1,0:T(8,128)(2,1)S(1)} %get-tuple-element.28, bf16[512,4096]{1,0:T(8,128)(2,1)} %all-gather.2.cloned.1.call-done), kind=kOutput, calls=%fused_computation.4 | convolution fusion | flops 4299161600 | bytes 22020096 | tf_op jit(solution)/shard_map/dot_general | solution.py:134
  142.0 5.8 %copy-done.2 = f32[1024,4096]{1,0:T(8,128)} copy-done((f32[1024,4096]{1,0:T(8,128)}, f32[1024,4096]{1,0:T(8,128)S(1)}, u32[]{:S(2)}) %copy-start.2) | copy-done | bytes 16777240
  148.7 1.5 collective-permute-start.4
  151.9 10.0 %collective-permute-done.4 = bf16[1024,256]{1,0:T(8,128)(2,1)S(1)} collective-permute-done((bf16[1024,256]{1,0:T(8,128)(2,1)}, bf16[1024,256]{1,0:T(8,128)(2,1)S(1)}, u32[]{:S(2)}, u32[]{:S(2)}) %collective-permute-start.4) | collective-permute-done | bytes 524320 | tf_op jit(solution)/shard_map/ppermute | solution.py:148
  162.9 2.8 %add_convert_fusion.13 = (bf16[1024,256]{1,0:T(8,128)(2,1)}, bf16[1024,256]{1,0:T(8,128)(2,1)S(1)}) fusion(f32[1024,4096]{1,0:T(8,128)} %copy-done.2, s32[]{:T(128)S(6)} %select_n.172, bf16[1024,256]{1,0:T(8,128)(2,1)S(1)} %collective-permute-done.4, s32[]{:T(128)S(6)} %select_n.196, bf16[1024,256]{1,0:T(8,128)(2,1)} %collective-permute-done.11), kind=kLoop, calls=%fused_computation.168 | loop fusion | flops 1572864 | bytes 4194312 | tf_op jit(solution)/shard_map/convert_element_type | solution.py:148
  165.7 1.4 collective-permute-start.5
  169.0 8.7 %collective-permute-done.5 = bf16[1024,256]{1,0:T(8,128)(2,1)S(1)} collective-permute-done((bf16[1024,256]{1,0:T(8,128)(2,1)}, bf16[1024,256]{1,0:T(8,128)(2,1)S(1)}, u32[]{:S(2)}, u32[]{:S(2)}) %collective-permute-start.5) | collective-permute-done | bytes 524320 | tf_op jit(solution)/shard_map/ppermute | solution.py:148
  178.7 2.7 %add_convert_fusion.12 = (bf16[1024,256]{1,0:T(8,128)(2,1)}, bf16[1024,256]{1,0:T(8,128)(2,1)S(1)}) fusion(f32[1024,4096]{1,0:T(8,128)} %copy-done.2, s32[]{:T(128)S(6)} %select_n.175, bf16[1024,256]{1,0:T(8,128)(2,1)S(1)} %collective-permute-done.5, s32[]{:T(128)S(6)} %select_n.199, bf16[1024,256]{1,0:T(8,128)(2,1)} %collective-permute-done.12), kind=kLoop, calls=%fused_computation.167 | loop fusion | flops 1572864 | bytes 4194312 | tf_op jit(solution)/shard_map/convert_element_type | solution.py:148
  186.2 6.1 %collective-permute-done.6 = bf16[1024,256]{1,0:T(8,128)(2,1)S(1)} collective-permute-done((bf16[1024,256]{1,0:T(8,128)(2,1)}, bf16[1024,256]{1,0:T(8,128)(2,1)S(1)}, u32[]{:S(2)}, u32[]{:S(2)}) %collective-permute-start.6) | collective-permute-done | bytes 524320 | tf_op jit(solution)/shard_map/ppermute | solution.py:148
  193.1 2.7 %add_convert_fusion.11 = (bf16[1024,256]{1,0:T(8,128)(2,1)}, bf16[1024,256]{1,0:T(8,128)(2,1)S(1)}) fusion(f32[1024,4096]{1,0:T(8,128)} %copy-done.2, s32[]{:T(128)S(6)} %select_n.178, bf16[1024,256]{1,0:T(8,128)(2,1)S(1)} %collective-permute-done.6, s32[]{:T(128)S(6)} %select_n.202, bf16[1024,256]{1,0:T(8,128)(2,1)} %collective-permute-done.13), kind=kLoop, calls=%fused_computation.166 | loop fusion | flops 1572864 | bytes 4194312 | tf_op jit(solution)/shard_map/convert_element_type | solution.py:148
  197.9 1.3 collective-permute-start.3
  204.3 2.7 %collective-permute-done.3 = bf16[3,6,1024]{2,1,0:T(8,128)(2,1)S(1)} collective-permute-done((bf16[3,6,1024]{2,1,0:T(8,128)(2,1)S(1)}, bf16[3,6,1024]{2,1,0:T(8,128)(2,1)S(1)}, u32[]{:S(2)}, u32[]{:S(2)}) %collective-permute-start.3) | collective-permute-done | bytes 36896 | tf_op jit(solution)/shard_map/ppermute | solution.py:12
  207.2 1.9 add_convert_fusion.10
  210.0 1.7 collective-permute-start.15
  211.7 3.0 %fusion.42 = bf16[512,1024]{1,0:T(8,128)(2,1)} fusion(f32[6,1024]{1,0:T(8,128)S(1)} %get-tuple-element.35, f32[512,1024]{1,0:T(8,128)S(1)} %get-tuple-element.27, f32[1024]{0:T(1024)S(1)} %bitcast.170, f32[1024]{0:T(1024)S(1)} %bitcast.172, f32[1024]{0:T(1024)S(1)} %bitcast.174, f32[1024]{0:T(1024)S(1)} %bitcast.176, f32[1024]{0:T(1024)S(1)} %bitcast.178, ...), kind=kLoop, calls=%fused_computation.78 | loop fusion | flops 10485760 | bytes 3198976 | tf_op jit(solution)/shard_map/convert_element_type | solution.py:115
  214.6 5.1 %collective-permute-done.8 = bf16[1024,256]{1,0:T(8,128)(2,1)S(1)} collective-permute-done((bf16[1024,256]{1,0:T(8,128)(2,1)S(1)}, bf16[1024,256]{1,0:T(8,128)(2,1)S(1)}, u32[]{:S(2)}, u32[]{:S(2)}) %collective-permute-start.8) | collective-permute-done | bytes 524320 | tf_op jit(solution)/shard_map/ppermute | solution.py:148
  220.0 1.8 add_convert_fusion.9
  222.0 2.4 collective-permute-start.16
  224.4 3.0 %fusion.25 = bf16[512,1024]{1,0:T(8,128)(2,1)} fusion(f32[6,1024]{1,0:T(8,128)S(1)} %get-tuple-element.34, f32[512,1024]{1,0:T(8,128)S(1)} %copy-done.6, f32[1024]{0:T(1024)S(1)} %bitcast.152, f32[1024]{0:T(1024)S(1)} %bitcast.154, f32[1024]{0:T(1024)S(1)} %bitcast.156, f32[1024]{0:T(1024)S(1)} %bitcast.158, f32[1024]{0:T(1024)S(1)} %bitcast.160, ...), kind=kLoop, calls=%fused_computation.61 | loop fusion | flops 10485760 | bytes 3198976 | tf_op jit(solution)/shard_map/convert_element_type | solution.py:115
  227.3 6.6 %collective-permute-done.9 = bf16[1024,256]{1,0:T(8,128)(2,1)S(1)} collective-permute-done((bf16[1024,256]{1,0:T(8,128)(2,1)S(1)}, bf16[1024,256]{1,0:T(8,128)(2,1)S(1)}, u32[]{:S(2)}, u32[]{:S(2)}) %collective-permute-start.9) | collective-permute-done | bytes 524320 | tf_op jit(solution)/shard_map/ppermute | solution.py:148
  233.9 1.8 add_convert_fusion.8
  235.7 2.5 collective-permute-start.10
  238.5 3.0 %fusion.8 = bf16[512,1024]{1,0:T(8,128)(2,1)} fusion(f32[6,1024]{1,0:T(8,128)S(1)} %get-tuple-element.33, f32[512,1024]{1,0:T(8,128)S(1)} %copy-done.5, f32[1024]{0:T(1024)S(1)} %bitcast.168, f32[1024]{0:T(1024)S(1)} %bitcast.166, f32[1024]{0:T(1024)S(1)} %bitcast.144, f32[1024]{0:T(1024)S(1)} %bitcast.146, f32[1024]{0:T(1024)S(1)} %bitcast.148, ...), kind=kLoop, calls=%fused_computation.44 | loop fusion | flops 10485760 | bytes 3198976 | tf_op jit(solution)/shard_map/convert_element_type | solution.py:115
  241.5 4.1 %collective-permute-done.10 = bf16[1024,256]{1,0:T(8,128)(2,1)S(1)} collective-permute-done((bf16[1024,256]{1,0:T(8,128)(2,1)S(1)}, bf16[1024,256]{1,0:T(8,128)(2,1)S(1)}, u32[]{:S(2)}, u32[]{:S(2)}) %collective-permute-start.10) | collective-permute-done | bytes 524320 | tf_op jit(solution)/shard_map/ppermute | solution.py:148
  245.6 1.7 collective-permute-done.17
  247.3 1.8 add_convert_fusion.7
  (82 shorter events, 28.1 us)
Async XLA Ops:
  7.2 8.5 %copy-start = (bf16[64,128]{1,0:T(8,128)(2,1)S(1)}, bf16[64,128]{1,0:T(8,128)(2,1)}, u32[]{:S(2)}) copy-start(bf16[64,128]{1,0:T(8,128)(2,1)} %param.13) | copy-start | bytes 49156
  7.2 39.6 %all-gather.2.cloned.1.call-start = ((), (), s32[]{:S(2)}) async-start(), calls=%async_computation.2 | async-start | bytes 5242880 | tf_op jit(solution)/shard_map/all_gather | solution.py:91
  7.9 242.3 %reduce-scatter.2.cloned.1.call-start = ((), (), s32[]{:S(2)}) async-start(), calls=%async_computation.1 | async-start | bytes 5242880 | tf_op jit(solution)/shard_map/reduce_scatter | solution.py:85
  9.5 12.3 %collective-permute-start = (bf16[3,6,1024]{2,1,0:T(8,128)(2,1)S(1)}, bf16[3,6,1024]{2,1,0:T(8,128)(2,1)S(1)}, u32[]{:S(2)}, u32[]{:S(2)}) collective-permute-start(bf16[3,6,1024]{2,1,0:T(8,128)(2,1)S(1)} %pad_maximum_fusion.7), channel_id=1, source_target_pairs={{0,4},{4,8},{8,12},{12,16},{16,20},{20,24},{24,28},{1,5},{5,9},{9,... | collective-permute-start | bytes 110600 | tf_op jit(solution)/shard_map/ppermute | solution.py:12
  15.6 31.1 %copy-start.11 = (bf16[512,1024]{1,0:T(8,128)(2,1)S(1)}, bf16[512,1024]{1,0:T(8,128)(2,1)}, u32[]{:S(2)}) copy-start(bf16[512,1024]{1,0:T(8,128)(2,1)} %param.9) | copy-start | bytes 3145732
  46.8 12.7 %copy-start.7 = (bf16[8,8,256,128]{3,1,2,0:T(8,128)(2,1)S(1)}, bf16[8,8,256,128]{3,1,2,0:T(8,128)(2,1)}, u32[]{:S(2)}) copy-start(bf16[8,8,256,128]{3,1,2,0:T(8,128)(2,1)} %fusion.3) | copy-start | bytes 12582916
  58.0 10.3 %collective-permute-start.2 = (bf16[128,1024]{1,0:T(8,128)(2,1)S(1)}, bf16[128,1024]{1,0:T(8,128)(2,1)S(1)}, u32[]{:S(2)}, u32[]{:S(2)}) collective-permute-start(bf16[128,1024]{1,0:T(8,128)(2,1)S(1)} %slice.427), channel_id=1, source_target_pairs={{4,0},{8,4},{12,8},{16,12},{20,16},{24,20},{28,24},{5,1},{9,5},{13... | collective-permute-start | bytes 786440 | tf_op jit(solution)/shard_map/ppermute | solution.py:12
  73.1 2.8 %copy-start.3 = (bf16[8,8,256,128]{3,2,1,0:T(8,128)(2,1)S(1)}, bf16[8,8,256,128]{3,2,1,0:T(8,128)(2,1)}, u32[]{:S(2)}) copy-start(bf16[8,8,256,128]{3,2,1,0:T(8,128)(2,1)} %copy.28) | copy-start | bytes 12582916
  78.1 2.0 copy-start.8
  80.2 3.0 %copy-start.9 = (bf16[512,1024]{1,0:T(8,128)(2,1)S(1)}, bf16[512,1024]{1,0:T(8,128)(2,1)}, u32[]{:S(2)}) copy-start(bf16[512,1024]{1,0:T(8,128)(2,1)} %param.11) | copy-start | bytes 3145732
  86.7 11.4 %collective-permute-start.1 = (bf16[128,1024]{1,0:T(8,128)(2,1)S(1)}, bf16[128,1024]{1,0:T(8,128)(2,1)S(1)}, u32[]{:S(2)}, u32[]{:S(2)}) collective-permute-start(bf16[128,1024]{1,0:T(8,128)(2,1)S(1)} %slice.421), channel_id=1, source_target_pairs={{0,4},{4,8},{8,12},{12,16},{16,20},{20,24},{24,28},{1,5},{5,9},{9,... | collective-permute-start | bytes 786440 | tf_op jit(solution)/shard_map/ppermute | solution.py:12
  102.9 2.8 %copy-start.4 = (bf16[8,8,256,128]{3,2,1,0:T(8,128)(2,1)S(1)}, bf16[8,8,256,128]{3,2,1,0:T(8,128)(2,1)}, u32[]{:S(2)}) copy-start(bf16[8,8,256,128]{3,2,1,0:T(8,128)(2,1)} %copy.26) | copy-start | bytes 12582916
  121.4 0.7 copy-start.12
  121.4 12.0 %copy-start.10 = (s32[8]{0:T(128)S(1)}, s32[8]{0:T(128)}, u32[]{:S(2)}) copy-start(s32[8]{0:T(128)} %constant.199.clone) | copy-start | bytes 100
  142.0 5.8 %copy-start.2 = (f32[1024,4096]{1,0:T(8,128)}, f32[1024,4096]{1,0:T(8,128)S(1)}, u32[]{:S(2)}) copy-start(f32[1024,4096]{1,0:T(8,128)S(1)} %convolution_multiply_fusion) | copy-start | bytes 50331652
  148.7 13.1 %collective-permute-start.4 = (bf16[1024,256]{1,0:T(8,128)(2,1)}, bf16[1024,256]{1,0:T(8,128)(2,1)S(1)}, u32[]{:S(2)}, u32[]{:S(2)}) collective-permute-start(bf16[1024,256]{1,0:T(8,128)(2,1)} %get-tuple-element.25), channel_id=1, source_target_pairs={{0,8},{8,16},{16,24},{24,28},{28,20},{20,12},{12,4},{4,0},{1,9},{9... | collective-permute-start | bytes 1572872 | tf_op jit(solution)/shard_map/ppermute | solution.py:148
  150.2 12.8 %collective-permute-start.11 = (bf16[1024,256]{1,0:T(8,128)(2,1)S(1)}, bf16[1024,256]{1,0:T(8,128)(2,1)}, u32[]{:S(2)}, u32[]{:S(2)}) collective-permute-start(bf16[1024,256]{1,0:T(8,128)(2,1)S(1)} %get-tuple-element.26), channel_id=1, source_target_pairs={{8,0},{16,8},{24,16},{28,24},{20,28},{12,20},{4,12},{0,4},{9,1},{1... | collective-permute-start | bytes 1572872 | tf_op jit(solution)/shard_map/ppermute | solution.py:149
  165.7 12.0 %collective-permute-start.5 = (bf16[1024,256]{1,0:T(8,128)(2,1)}, bf16[1024,256]{1,0:T(8,128)(2,1)S(1)}, u32[]{:S(2)}, u32[]{:S(2)}) collective-permute-start(bf16[1024,256]{1,0:T(8,128)(2,1)} %get-tuple-element.23), channel_id=1, source_target_pairs={{0,8},{8,16},{16,24},{24,28},{28,20},{20,12},{12,4},{4,0},{1,9},{9... | collective-permute-start | bytes 1572872 | tf_op jit(solution)/shard_map/ppermute | solution.py:148
  167.1 11.6 %collective-permute-start.12 = (bf16[1024,256]{1,0:T(8,128)(2,1)S(1)}, bf16[1024,256]{1,0:T(8,128)(2,1)}, u32[]{:S(2)}, u32[]{:S(2)}) collective-permute-start(bf16[1024,256]{1,0:T(8,128)(2,1)S(1)} %get-tuple-element.24), channel_id=1, source_target_pairs={{8,0},{16,8},{24,16},{28,24},{20,28},{12,20},{4,12},{0,4},{9,1},{1... | collective-permute-start | bytes 1572872 | tf_op jit(solution)/shard_map/ppermute | solution.py:149
  181.4 10.8 %collective-permute-start.6 = (bf16[1024,256]{1,0:T(8,128)(2,1)}, bf16[1024,256]{1,0:T(8,128)(2,1)S(1)}, u32[]{:S(2)}, u32[]{:S(2)}) collective-permute-start(bf16[1024,256]{1,0:T(8,128)(2,1)} %get-tuple-element.21), channel_id=1, source_target_pairs={{0,8},{8,16},{16,24},{24,28},{28,20},{20,12},{12,4},{4,0},{1,9},{9... | collective-permute-start | bytes 1572872 | tf_op jit(solution)/shard_map/ppermute | solution.py:148
  182.2 10.9 %collective-permute-start.13 = (bf16[1024,256]{1,0:T(8,128)(2,1)S(1)}, bf16[1024,256]{1,0:T(8,128)(2,1)}, u32[]{:S(2)}, u32[]{:S(2)}) collective-permute-start(bf16[1024,256]{1,0:T(8,128)(2,1)S(1)} %get-tuple-element.22), channel_id=1, source_target_pairs={{8,0},{16,8},{24,16},{28,24},{20,28},{12,20},{4,12},{0,4},{9,1},{1... | collective-permute-start | bytes 1572872 | tf_op jit(solution)/shard_map/ppermute | solution.py:149
  195.8 11.2 %collective-permute-start.7 = (bf16[1024,256]{1,0:T(8,128)(2,1)}, bf16[1024,256]{1,0:T(8,128)(2,1)S(1)}, u32[]{:S(2)}, u32[]{:S(2)}) collective-permute-start(bf16[1024,256]{1,0:T(8,128)(2,1)} %get-tuple-element.19), channel_id=1, source_target_pairs={{0,8},{8,16},{16,24},{24,28},{28,20},{20,12},{12,4},{4,0},{1,9},{9... | collective-permute-start | bytes 1572872 | tf_op jit(solution)/shard_map/ppermute | solution.py:148
  196.6 10.6 %collective-permute-start.14 = (bf16[1024,256]{1,0:T(8,128)(2,1)S(1)}, bf16[1024,256]{1,0:T(8,128)(2,1)}, u32[]{:S(2)}, u32[]{:S(2)}) collective-permute-start(bf16[1024,256]{1,0:T(8,128)(2,1)S(1)} %get-tuple-element.20), channel_id=1, source_target_pairs={{8,0},{16,8},{24,16},{28,24},{20,28},{12,20},{4,12},{0,4},{9,1},{1... | collective-permute-start | bytes 1572872 | tf_op jit(solution)/shard_map/ppermute | solution.py:149
  197.9 9.1 %collective-permute-start.3 = (bf16[3,6,1024]{2,1,0:T(8,128)(2,1)S(1)}, bf16[3,6,1024]{2,1,0:T(8,128)(2,1)S(1)}, u32[]{:S(2)}, u32[]{:S(2)}) collective-permute-start(bf16[3,6,1024]{2,1,0:T(8,128)(2,1)S(1)} %pad_maximum_fusion.8), channel_id=1, source_target_pairs={{4,0},{8,4},{12,8},{16,12},{20,16},{24,20},{28,24},{5,1},{9,5},{13... | collective-permute-start | bytes 110600 | tf_op jit(solution)/shard_map/ppermute | solution.py:12
  209.2 10.5 %collective-permute-start.8 = (bf16[1024,256]{1,0:T(8,128)(2,1)S(1)}, bf16[1024,256]{1,0:T(8,128)(2,1)S(1)}, u32[]{:S(2)}, u32[]{:S(2)}) collective-permute-start(bf16[1024,256]{1,0:T(8,128)(2,1)S(1)} %get-tuple-element.17), channel_id=1, source_target_pairs={{0,8},{8,16},{16,24},{24,28},{28,20},{20,12},{12,4},{4,0},{1,9},{9... | collective-permute-start | bytes 1572872 | tf_op jit(solution)/shard_map/ppermute | solution.py:148
  210.0 10.0 %collective-permute-start.15 = (bf16[1024,256]{1,0:T(8,128)(2,1)S(1)}, bf16[1024,256]{1,0:T(8,128)(2,1)S(1)}, u32[]{:S(2)}, u32[]{:S(2)}) collective-permute-start(bf16[1024,256]{1,0:T(8,128)(2,1)S(1)} %get-tuple-element.18), channel_id=1, source_target_pairs={{8,0},{16,8},{24,16},{28,24},{20,28},{12,20},{4,12},{0,4},{9,1},{1... | collective-permute-start | bytes 1572872 | tf_op jit(solution)/shard_map/ppermute | solution.py:149
  214.6 9.8 %copy-start.6 = (f32[512,1024]{1,0:T(8,128)S(1)}, f32[512,1024]{1,0:T(8,128)}, u32[]{:S(2)}) copy-start(f32[512,1024]{1,0:T(8,128)} %get-tuple-element.5) | copy-start | bytes 6291460
  221.8 12.1 %collective-permute-start.9 = (bf16[1024,256]{1,0:T(8,128)(2,1)S(1)}, bf16[1024,256]{1,0:T(8,128)(2,1)S(1)}, u32[]{:S(2)}, u32[]{:S(2)}) collective-permute-start(bf16[1024,256]{1,0:T(8,128)(2,1)S(1)} %get-tuple-element.15), channel_id=1, source_target_pairs={{0,8},{8,16},{16,24},{24,28},{28,20},{20,12},{12,4},{4,0},{1,9},{9... | collective-permute-start | bytes 1572872 | tf_op jit(solution)/shard_map/ppermute | solution.py:148
  222.0 12.0 %collective-permute-start.16 = (bf16[1024,256]{1,0:T(8,128)(2,1)S(1)}, bf16[1024,256]{1,0:T(8,128)(2,1)S(1)}, u32[]{:S(2)}, u32[]{:S(2)}) collective-permute-start(bf16[1024,256]{1,0:T(8,128)(2,1)S(1)} %get-tuple-element.16), channel_id=1, source_target_pairs={{8,0},{16,8},{24,16},{28,24},{20,28},{12,20},{4,12},{0,4},{9,1},{1... | collective-permute-start | bytes 1572872 | tf_op jit(solution)/shard_map/ppermute | solution.py:149
  227.3 11.2 %copy-start.5 = (f32[512,1024]{1,0:T(8,128)S(1)}, f32[512,1024]{1,0:T(8,128)}, u32[]{:S(2)}) copy-start(f32[512,1024]{1,0:T(8,128)} %get-tuple-element.7) | copy-start | bytes 6291460
  235.7 9.9 %collective-permute-start.10 = (bf16[1024,256]{1,0:T(8,128)(2,1)S(1)}, bf16[1024,256]{1,0:T(8,128)(2,1)S(1)}, u32[]{:S(2)}, u32[]{:S(2)}) collective-permute-start(bf16[1024,256]{1,0:T(8,128)(2,1)S(1)} %get-tuple-element.13), channel_id=1, source_target_pairs={{0,8},{8,16},{16,24},{24,28},{28,20},{20,12},{12,4},{4,0},{1,9},{9... | collective-permute-start | bytes 1572872 | tf_op jit(solution)/shard_map/ppermute | solution.py:148
  238.2 9.2 %collective-permute-start.17 = (bf16[1024,256]{1,0:T(8,128)(2,1)S(1)}, bf16[1024,256]{1,0:T(8,128)(2,1)S(1)}, u32[]{:S(2)}, u32[]{:S(2)}) collective-permute-start(bf16[1024,256]{1,0:T(8,128)(2,1)S(1)} %get-tuple-element.14), channel_id=1, source_target_pairs={{8,0},{16,8},{24,16},{28,24},{20,28},{12,20},{4,12},{0,4},{9,1},{1... | collective-permute-start | bytes 1572872 | tf_op jit(solution)/shard_map/ppermute | solution.py:149
  247.3 2.9 %copy-start.1 = (bf16[64,128]{1,0:T(8,128)(2,1)S(1)}, bf16[64,128]{1,0:T(8,128)(2,1)}, u32[]{:S(2)}) copy-start(bf16[64,128]{1,0:T(8,128)(2,1)} %param.13) | copy-start | bytes 49156
Sparse Core Ops, SparseCore 0:
  9.5 37.1 all-gather.1
  121.5 42.7 reduce-scatter.1
where the time goes:
time: 258 us; the launch traced here: 257 us
  waiting for transfers between devices  78.9 us (31%)
  matrix products  43.3 us (17%)
  local copies, waits for them, and re-layouts  35.8 us (14%)
  other arithmetic  35.7 us (14%)
  between operations  35.3 us (14%)
  starting transfers between devices  28 us (11%)
    ppermute x7, waiting for transfers between devices, ring_reduce_scatter(): lax.ppermute(ahead.astype(jnp.bfloat16), 'seq', forward).astype(jnp.float32)  40.5 us
    all_gather x1, waiting for transfers between devices, per_device(): full_cotangent = lax.all_gather(cotangent, 'tp', axis=0, tiled=True)  25 us
    unnamed x30, local copies, waits for them, and re-layouts  15.3 us
    convert_element_type x6, other arithmetic, ring_reduce_scatter(): ahead.astype(jnp.bfloat16)  13.7 us
    ppermute x4, starting transfers between devices, passed_along(): lax.ppermute(value, axis, [(source, source + steps) for source in range(l...  11.9 us
    dot_general x1, matrix products, per_device(): lax.dot_general(full_cotangent, out_weight, (((1,), (1,)), ((), ())), pre...  11.2 us
    dot_general x2, matrix products, band_table(): jnp.dot(filter_taps, select, preferred_element_type=jnp.float32)  9.94 us
    dot_general x1, matrix products, per_device(): jnp.dot(gated_rows, out_weight, preferred_element_type=jnp.float32)  9.45 us
  transfers between devices with their start and end apart: 20, of which 15 were waited for; matrix products, arithmetic and copies ran while one was open for 22% of the time, Pallas kernels for 0%

commit v1 on v0

--- a/solution.py
+++ b/solution.py
@@ -68,6 +68,7 @@
     row_count, channels = query_in.shape
     tap_count = filter_taps.shape[1]
     tap_span = feature_taps.shape[0]
+    full_cotangent = lax.all_gather(cotangent, "tp", axis=0, tiled=True)
     inputs = (query_in, key_in, value_in)
     before = passed_along(
         jnp.stack([rows[row_count - tap_span + 1 :] for rows in inputs], axis=0), "seq", 1
@@ -79,46 +80,64 @@
     mix_rows = (key_feat * value_feat).astype(jnp.bfloat16)
     mix_before = passed_along(mix_rows[row_count - tap_count :], "seq", 1)
     padded_mix = jnp.concatenate([mix_before, mix_rows], axis=0)
-    toeplitz_rows = band_table(filter_taps)
-    long_conv = band_mix(padded_mix, toeplitz_rows)
+    long_conv = band_mix(padded_mix, band_table(filter_taps))
     gated_rows = (query_feat * long_conv).astype(jnp.bfloat16)
-    block_out = lax.psum_scatter(
-        jnp.dot(gated_rows, out_weight, preferred_element_type=jnp.float32).astype(jnp.bfloat16),
-        "tp",
-        scatter_dimension=0,
-        tiled=True,
-    )
-    full_cotangent = lax.all_gather(cotangent, "tp", axis=0, tiled=True)
     seq_count = lax.axis_size("seq")
     grad_scale = (row_count * seq_count) ** (-0.5)
-    summed_grad = ring_reduce_scatter(gated_rows, full_cotangent, grad_scale, ring)
-    grad_gated = lax.dot_general(
-        full_cotangent, out_weight, (((1,), (1,)), ((), ())), preferred_element_type=jnp.float32
-    )
-    grad_conv = (grad_gated * query_feat).astype(jnp.bfloat16)
-    grad_query = grad_gated * long_conv
-    conv_after = passed_along(grad_conv[:tap_count], "seq", -1)
-    grad_mix = band_mix(
-        jnp.concatenate([grad_conv, conv_after], axis=0), band_table(filter_taps, reverse=True)
-    )
-    grad_features = (grad_query, grad_mix * value_feat, grad_mix * key_feat)
-    features_after = passed_along(
-        jnp.stack([rows[: tap_span - 1] for rows in grad_features], axis=0).astype(jnp.bfloat16),
-        "seq",
-        -1,
-    ).astype(jnp.float32)
-    query_grad, key_grad, value_grad = (
-        spread_back(
-            jnp.concatenate([grad_features[i], features_after[i]], axis=0),
-            feature_taps[:, i],
-            row_count,
-        ).astype(jnp.bfloat16)
-        for i in range(3)
-    )
-    return (block_out, query_grad, key_grad, value_grad, summed_grad)
-
-
-def ring_reduce_scatter(gated_rows, full_cotangent, grad_scale, ring):
+
+    def project(state):
+        gated_rows, out_weight = state
+        block_out = lax.psum_scatter(
+            jnp.dot(gated_rows, out_weight, preferred_element_type=jnp.float32).astype(jnp.bfloat16),
+            "tp",
+            scatter_dimension=0,
+            tiled=True,
+        )
+        return (block_out, out_weight)
+
+    def gate_back(state):
+        block_out, out_weight = state
+        grad_gated = lax.dot_general(
+            full_cotangent, out_weight, (((1,), (1,)), ((), ())), preferred_element_type=jnp.float32
+        )
+        grad_conv = (grad_gated * query_feat).astype(jnp.bfloat16)
+        grad_query = grad_gated * long_conv
+        conv_after = passed_along(grad_conv[:tap_count], "seq", -1)
+        return (block_out, grad_conv, conv_after, grad_query)
+
+    def filter_back(state):
+        block_out, grad_conv, conv_after, grad_query = state
+        grad_mix = band_mix(
+            jnp.concatenate([grad_conv, conv_after], axis=0), band_table(filter_taps, reverse=True)
+        )
+        grad_features = (grad_query, grad_mix * value_feat, grad_mix * key_feat)
+        features_after = passed_along(
+            jnp.stack([rows[: tap_span - 1] for rows in grad_features], axis=0).astype(jnp.bfloat16),
+            "seq",
+            -1,
+        )
+        return (block_out, grad_features, features_after)
+
+    def feature_back(state):
+        block_out, grad_features, features_after = state
+        grads = tuple(
+            spread_back(
+                jnp.concatenate([grad_features[i], features_after[i].astype(jnp.float32)], axis=0),
+                feature_taps[:, i],
+                row_count,
+            ).astype(jnp.bfloat16)
+            for i in range(3)
+        )
+        return (block_out,) + grads
+
+    stages = [project, gate_back, filter_back, feature_back]
+    state, summed_grad = ring_reduce_scatter(
+        gated_rows, full_cotangent, grad_scale, ring, stages, (gated_rows, out_weight)
+    )
+    return state + (summed_grad,)
+
+
+def ring_reduce_scatter(gated_rows, full_cotangent, grad_scale, ring, stages, state):
     count = len(ring)
     width = full_cotangent.shape[1] // count
     half = width // 2
@@ -129,27 +148,36 @@
     members = jnp.asarray(ring, jnp.int32)
     forward = [(ring[i], ring[(i + 1) % count]) for i in range(count)]
     backward = [(ring[(i + 1) % count], ring[i]) for i in range(count)]
-
+    blocks = full_cotangent.reshape(full_cotangent.shape[0], count, 2, half).transpose(1, 2, 0, 3)
     local_grad = (
-        lax.dot_general(
-            gated_rows, full_cotangent, (((0,), (0,)), ((), ())), preferred_element_type=jnp.float32
-        )
+        jnp.einsum("tc,bhtd->bhcd", gated_rows, blocks, preferred_element_type=jnp.float32)
         * grad_scale
     )
 
     def contribution(step, direction):
         owner = members[(place - direction * (1 + step)) % count]
-        first = owner * width + (0 if direction == 1 else half)
-        return lax.dynamic_slice_in_dim(local_grad, first, half, 1)
+        block = lax.dynamic_index_in_dim(local_grad, owner, 0, keepdims=False)
+        return block[0 if direction == 1 else 1]
 
     ahead = contribution(0, 1)
     behind = contribution(0, -1)
+    stages = list(stages)
     for step in range(1, count):
-        ahead = lax.ppermute(ahead.astype(jnp.bfloat16), "seq", forward).astype(jnp.float32)
-        behind = lax.ppermute(behind.astype(jnp.bfloat16), "seq", backward).astype(jnp.float32)
+        sent_ahead = ahead.astype(jnp.bfloat16)
+        sent_behind = behind.astype(jnp.bfloat16)
+        if stages:
+            sent_ahead, sent_behind, state = lax.optimization_barrier(
+                (sent_ahead, sent_behind, state)
+            )
+        ahead = lax.ppermute(sent_ahead, "seq", forward).astype(jnp.float32)
+        behind = lax.ppermute(sent_behind, "seq", backward).astype(jnp.float32)
+        if stages:
+            state = stages.pop(0)(state)
         ahead = ahead + contribution(step, 1)
         behind = behind + contribution(step, -1)
-    return jnp.concatenate([ahead, behind], axis=1).astype(jnp.bfloat16)
+    while stages:
+        state = stages.pop(0)(state)
+    return state, jnp.concatenate([ahead, behind], axis=1).astype(jnp.bfloat16)
 
 
 def ring_order(mesh):

time: 258 us -> 274 us (1.062); the launches traced: 257 us -> 270 us
  waiting for transfers between devices: 78.9 us -> 20.3 us
  local copies, waits for them, and re-layouts: 35.8 us -> 65.1 us
  other arithmetic: 35.7 us -> 61.1 us
  between operations: 35.3 us -> 55 us
    ppermute x14, waiting for transfers between devices: 45.7 us -> 14.5 us  [the longest x7 8.99 us: ring_reduce_scatter(): ahead = lax.ppermute(sent_ahead, 'seq', forward).astype(jnp.float32)]
    all_gather x1, waiting for transfers between devices: 25 us -> 0.01 us  [per_device(): full_cotangent = lax.all_gather(cotangent, 'tp', axis=0, tiled=True)]
    convert_element_type x10 -> x19, other arithmetic: 22.6 us -> 46.3 us  [the longest x3 21.2 us: feature_back(): grads = tuple((spread_back(jnp.concatenate([grad_features[i], features_af...]
    dynamic_slice x0 -> x2, local copies, waits for them, and re-layouts: none -> 19.2 us  [contribution(): block = lax.dynamic_index_in_dim(local_grad, owner, 0, keepdims=False)]
    unnamed x30 -> x66, local copies, waits for them, and re-layouts: 15.3 us -> 26.3 us
    convert_element_type x1, other arithmetic: 0.5 us -> 9.59 us  [per_device(): mix_rows = (key_feat * value_feat).astype(jnp.bfloat16)]
    mul x3 -> x1, other arithmetic: 9.52 us -> 2.09 us  [filter_back(): grad_features = (grad_query, grad_mix * value_feat, grad_mix * key_feat)]
    all_gather x0 -> x1, local copies, waits for them, and re-layouts: none -> 6.46 us  [per_device(): full_cotangent = lax.all_gather(cotangent, 'tp', axis=0, tiled=True)]
  transfers between devices with their start and end apart: 20 -> 20, of which waited for: 15 -> 4; matrix products, arithmetic and copies ran while one was open for 22% -> 46% of each run, Pallas kernels for 0% -> 0%
where the time goes in v1:
time: 274 us; the launch traced here: 270 us
  local copies, waits for them, and re-layouts  65.1 us (24%)
  other arithmetic  61.1 us (22%)
  between operations  55 us (20%)
  matrix products  41.4 us (15%)
  starting transfers between devices  26.9 us (10%)
  waiting for transfers between devices  20.3 us (7%)
    unnamed x66, local copies, waits for them, and re-layouts  26.3 us
    convert_element_type x3, other arithmetic, feature_back(): grads = tuple((spread_back(jnp.concatenate([grad_features[i], features_af...  21.2 us
    dynamic_slice x2, local copies, waits for them, and re-layouts, contribution(): block = lax.dynamic_index_in_dim(local_grad, owner, 0, keepdims=False)  19.2 us
    ppermute x7, starting transfers between devices, ring_reduce_scatter(): behind = lax.ppermute(sent_behind, 'seq', backward).astype(jnp.float32)  13.1 us
    ppermute x4, starting transfers between devices, passed_along(): lax.ppermute(value, axis, [(source, source + steps) for source in range(l...  11.7 us
    convert_element_type x6, other arithmetic, ring_reduce_scatter(): sent_ahead = ahead.astype(jnp.bfloat16)  11.4 us
    dot_general x1, matrix products, gate_back(): lax.dot_general(full_cotangent, out_weight, (((1,), (1,)), ((), ())), pre...  11.2 us
    dot_general x1, matrix products, project(): jnp.dot(gated_rows, out_weight, preferred_element_type=jnp.float32)  9.76 us
  transfers between devices with their start and end apart: 20, of which 4 were waited for; matrix products, arithmetic and copies ran while one was open for 46% of the time, Pallas kernels for 0%

profile of v1, /device:TPU:0, one launch (start us, length us, event | category | flops | bytes accessed | tf_op | source)
XLA Modules:
  0.0 269.8 jit_solution(978707976243989898)
XLA Ops:
  9.5 4.9 %collective-permute-start = (bf16[3,6,1024]{2,1,0:T(8,128)(2,1)S(1)}, bf16[3,6,1024]{2,1,0:T(8,128)(2,1)S(1)}, u32[]{:S(2)}, u32[]{:S(2)}) collective-permute-start(bf16[3,6,1024]{2,1,0:T(8,128)(2,1)S(1)} %pad_maximum_fusion.7), channel_id=1, source_target_pairs={{0,4},{4,8},{8,12},{12,16},{16,20},{20,24},{24,28},{1,5},{5,9},{9,... | collective-permute-start | bytes 110600 | tf_op jit(solution)/shard_map/ppermute | solution.py:12
  15.2 1.4 fusion.125
  17.2 1.5 copy.47
  19.9 9.6 %multiply_convert_fusion = (bf16[512,1024]{0,1:T(8,128)(2,1)S(1)}, f32[512,1024]{0,1:T(8,128)}, f32[512,1024]{0,1:T(8,128)}) fusion(bf16[512,1024]{0,1:T(8,128)(2,1)S(1)} %copy.47, bf16[6,1024]{0,1:T(8,128)(2,1)} %bitcast.267, f32[1024]{0:T(1024)S(1)} %bitcast.294, f32[1024]{0:T(1024)S(1)} %bitcast.292, f32[1024]{0:T(1024)S(1)} %bitcast.282, ...), kind=kLoop, calls=%fused_computation.143 | loop fusion | flops 40894464 | bytes 7421952 | tf_op jit(solution)/shard_map/convert_element_type | solution.py:80
  29.5 3.9 %collective-permute-start.1 = (bf16[128,1024]{0,1:T(8,128)(2,1)S(1)}, bf16[128,1024]{0,1:T(8,128)(2,1)S(1)}, u32[]{:S(2)}, u32[]{:S(2)}) collective-permute-start(bf16[128,1024]{0,1:T(8,128)(2,1)S(1)} %slice.503), channel_id=1, source_target_pairs={{0,4},{4,8},{8,12},{12,16},{16,20},{20,24},{24,28},{1,5},{5,9},{9,... | collective-permute-start | bytes 786440 | tf_op jit(solution)/shard_map/ppermute | solution.py:12
  33.5 2.3 copy.41
  50.4 3.9 %fusion.2 = bf16[8,8,256,128]{3,1,2,0:T(8,128)(2,1)S(1)} fusion(bf16[64,128]{1,0:T(8,128)(2,1)S(1)} %copy-done, s32[32768]{0:T(1024)S(1)} %subtract_bitcast_fusion.1), kind=kOutput, calls=%fused_computation.53 | convolution fusion | flops 543162368 | bytes 4341760 | tf_op jit(solution)/shard_map/dot_general | solution.py:45
  54.3 3.2 %copy.67 = bf16[8,8,256,128]{3,2,1,0:T(8,128)(2,1)} copy(bf16[8,8,256,128]{3,1,2,0:T(8,128)(2,1)S(1)} %fusion.2) | data formatting | bytes 8388608
  60.7 2.4 fusion.63
  64.7 4.6 %fusion.55 = (bf16[512,1024]{0,1:T(8,128)(2,1)S(1)}, f32[512,1024]{0,1:T(8,128)}) fusion(f32[128,8,4,128]{3,2,1,0:T(4,128)S(1)} %bitcast.262, bf16[512,1024]{0,1:T(8,128)(2,1)S(1)} %copy-done.18, bf16[6,1024]{0,1:T(8,128)(2,1)S(1)} %bitcast.265, f32[1024]{0:T(1024)S(1)} %bitcast.298, f32[1024]{0:T(1024)S(1)} %bitcast.300, f32[1024]{0:T(1024)S(1)} %bitcast.302, ...), kind=kLoop, calls=%fused_computation.110 | loop fusion | flops 20971520 | bytes 6332416 | tf_op jit(solution)/shard_map/convert_element_type | solution.py:84
  69.3 6.5 %copy.50 = bf16[512,4096]{0,1:T(8,128)(2,1)} copy(bf16[512,4096]{1,0:T(8,128)(2,1)} %all-gather.2.cloned.1.call-done) | data formatting | bytes 8388608 | tf_op jit(solution)/shard_map/all_gather | solution.py:71
  75.8 6.4 %convolution_multiply_fusion = f32[1024,8,2,256]{0,3,2,1:T(8,128)S(1)} fusion(bf16[8,2,512,256]{2,3,1,0:T(8,128)(2,1)} %bitcast.264, bf16[512,1024]{0,1:T(8,128)(2,1)S(1)} %get-tuple-element.28), kind=kOutput, calls=%fused_computation.4 | convolution fusion | flops 4299161600 | bytes 22020096 | tf_op jit(solution)/shard_map/tc,bhtd->bhcd/dot_general | solution.py:153
  82.2 5.8 %copy-done.2 = f32[1024,8,2,256]{0,3,2,1:T(8,128)} copy-done((f32[1024,8,2,256]{0,3,2,1:T(8,128)}, f32[1024,8,2,256]{0,3,2,1:T(8,128)S(1)}, u32[]{:S(2)}) %copy-start.2) | copy-done | bytes 16777240
  90.0 9.8 %convolution_convert_fusion.2 = bf16[512,4096]{1,0:T(8,128)(2,1)} fusion(bf16[512,1024]{0,1:T(8,128)(2,1)S(1)} %get-tuple-element.28, bf16[1024,4096]{1,0:T(8,128)(2,1)} %param.14), kind=kOutput, calls=%fused_computation.22 | convolution fusion | flops 4297064448 | bytes 13631488 | tf_op jit(solution)/shard_map/dot_general | solution.py:91
  116.9 3.9 %fusion.3 = bf16[8,8,256,128]{3,1,2,0:T(8,128)(2,1)S(1)} fusion(bf16[64,128]{1,0:T(8,128)(2,1)S(1)} %copy-done, s32[32768]{0:T(1024)S(1)} %subtract_bitcast_fusion), kind=kOutput, calls=%fused_computation.54 | convolution fusion | flops 543162368 | bytes 4341760 | tf_op jit(solution)/shard_map/dot_general | solution.py:45
  120.8 3.2 %copy.69 = bf16[8,8,256,128]{3,2,1,0:T(8,128)(2,1)} copy(bf16[8,8,256,128]{3,1,2,0:T(8,128)(2,1)S(1)} %fusion.3) | data formatting | bytes 8388608
  132.5 1.5 collective-permute-start.3
  134.6 18.9 %dynamic-slice_bitcast_fusion.7 = (f32[1,2,1024,256]{2,3,1,0:T(8,128)}, f32[1,2,1024,256]{2,3,1,0:T(8,128)}, f32[1,2,1024,256]{2,3,1,0:T(8,128)}, f32[1,2,1024,2...) fusion(f32[1024,8,2,256]{0,3,2,1:T(8,128)} %copy-done.2, ...), kind=kLoop, calls=%fused_computation.134 | loop fusion | bytes 58720312 | tf_op jit(solution)/shard_map/jit(dynamic_index_in_dim)/dynamic_slice | solution.py:159
  153.5 1.6 fusion.116
  156.7 1.6 collective-permute-start.5
  159.0 11.2 %bitcast_multiply_fusion.2 = (f32[512,1024]{0,1:T(8,128)}, bf16[512,1024]{0,1:T(8,128)(2,1)S(1)}) fusion(f32[128,8,4,128]{3,2,1,0:T(4,128)S(1)} %bitcast.263, f32[512,1024]{0,1:T(8,128)} %get-tuple-element.63, bf16[1024,4096]{1,0:T(8,128)(2,1)} %param.14, bf16[512,4096]{1,0:T(8,128)(2,1)} %all-gather.2.cloned.1.call-done), kind=kOutput, calls=%fused_computation.108 | convolution fusion | flops 4296540160 | bytes 19922944 | tf_op jit(solution)/shard_map/dot_general | solution.py:100
  170.3 1.4 collective-permute-start.6
  173.6 5.1 %collective-permute-done.6 = bf16[128,1024]{0,1:T(8,128)(2,1)S(1)} collective-permute-done((bf16[128,1024]{0,1:T(8,128)(2,1)S(1)}, bf16[128,1024]{0,1:T(8,128)(2,1)S(1)}, u32[]{:S(2)}, u32[]{:S(2)}) %collective-permute-start.6) | collective-permute-done | bytes 262176 | tf_op jit(solution)/shard_map/ppermute | solution.py:12
  180.4 2.4 fusion.59
  185.4 2.1 bitcast_multiply_fusion
  187.7 2.5 collective-permute-start.8
  192.7 1.4 collective-permute-start.9
  194.1 5.5 %collective-permute-done.8 = bf16[1024,256]{0,1:T(8,128)(2,1)} collective-permute-done((bf16[1024,256]{0,1:T(8,128)(2,1)S(1)}, bf16[1024,256]{0,1:T(8,128)(2,1)}, u32[]{:S(2)}, u32[]{:S(2)}) %collective-permute-start.8) | collective-permute-done | bytes 524320 | tf_op jit(solution)/shard_map/ppermute | solution.py:173
  199.6 1.5 fusion.108
  201.1 1.5 collective-permute-done.7
  202.6 2.0 fusion.110
  204.6 2.0 collective-permute-start.14
  206.9 7.5 %collective-permute-done.10 = bf16[1024,256]{0,1:T(8,128)(2,1)} collective-permute-done((bf16[1024,256]{0,1:T(8,128)(2,1)}, bf16[1024,256]{0,1:T(8,128)(2,1)}, u32[]{:S(2)}, u32[]{:S(2)}) %collective-permute-start.10) | collective-permute-done | bytes 524320 | tf_op jit(solution)/shard_map/ppermute | solution.py:172
  214.4 2.4 fusion.106
  218.0 1.8 collective-permute-start.15
  219.8 6.6 %fusion.8 = bf16[512,1024]{0,1:T(8,128)(2,1)S(1)} fusion(f32[512,1024]{0,1:T(8,128)S(1)} %copy-done.5, f32[6,1024]{0,1:T(8,128)S(1)} %bitcast_convert_fusion, f32[1024]{0:T(1024)S(1)} %bitcast.295, f32[1024]{0:T(1024)S(1)} %bitcast.293, f32[1024]{0:T(1024)S(1)} %bitcast.283, f32[1024]{0:T(1024)S(1)} %bitcast.285, f32[1024]{0:T(1024)S(1)} %bitcast.287, ...), kind=kLoop, calls=%fused_computation.59 | loop fusion | flops 10485760 | bytes 3198976 | tf_op jit(solution)/shard_map/convert_element_type | solution.py:128
  226.6 2.4 fusion.104
  229.4 2.0 fusion.96
  231.3 2.0 collective-permute-start.16
  233.3 7.3 %fusion.25 = bf16[512,1024]{0,1:T(8,128)(2,1)} fusion(f32[512,1024]{0,1:T(8,128)S(1)} %get-tuple-element.43, f32[6,1024]{0,1:T(8,128)S(1)} %bitcast_convert_fusion.1, f32[1024]{0:T(1024)S(1)} %bitcast.269, f32[1024]{0:T(1024)S(1)} %bitcast.271, f32[1024]{0:T(1024)S(1)} %bitcast.273, f32[1024]{0:T(1024)S(1)} %bitcast.275, f32[1024]{0:T(1024)S(1)} %bitcast.277, ...), kind=kLoop, calls=%fused_computation.76 | loop fusion | flops 10485760 | bytes 3198976 | tf_op jit(solution)/shard_map/convert_element_type | solution.py:128
  240.9 2.5 fusion.102
  243.6 2.0 fusion.94
  245.6 1.8 collective-permute-start.17
  247.4 7.3 %fusion.42 = bf16[512,1024]{0,1:T(8,128)(2,1)} fusion(f32[512,1024]{0,1:T(8,128)S(1)} %copy-done.19, f32[6,1024]{0,1:T(8,128)S(1)} %bitcast_convert_fusion.2, f32[1024]{0:T(1024)S(1)} %bitcast.299, f32[1024]{0:T(1024)S(1)} %bitcast.301, f32[1024]{0:T(1024)S(1)} %bitcast.303, f32[1024]{0:T(1024)S(1)} %bitcast.305, f32[1024]{0:T(1024)S(1)} %bitcast.307, ...), kind=kLoop, calls=%fused_computation.93 | loop fusion | flops 10485760 | bytes 3198976 | tf_op jit(solution)/shard_map/convert_element_type | solution.py:128
  256.0 1.3 copy.59
  257.3 1.3 copy.58
  258.6 1.5 fusion.100
  261.4 1.3 copy.61
  (130 shorter events, 28.5 us)
Async XLA Ops:
  7.2 43.2 %copy-start = (bf16[64,128]{1,0:T(8,128)(2,1)S(1)}, bf16[64,128]{1,0:T(8,128)(2,1)}, u32[]{:S(2)}) copy-start(bf16[64,128]{1,0:T(8,128)(2,1)} %param.13) | copy-start | bytes 49156
  7.2 9.5 %copy-start.20 = (bf16[512,1024]{1,0:T(8,128)(2,1)S(1)}, bf16[512,1024]{1,0:T(8,128)(2,1)}, u32[]{:S(2)}) copy-start(bf16[512,1024]{1,0:T(8,128)(2,1)} %param.10) | copy-start | bytes 3145732
  7.2 62.2 %all-gather.2.cloned.1.call-start = ((), (), s32[]{:S(2)}) async-start(), calls=%async_computation.1 | async-start | bytes 5242880 | tf_op jit(solution)/shard_map/all_gather | solution.py:71
  7.9 148.8 %reduce-scatter.2.cloned.1.call-start = ((), (), s32[]{:S(2)}) async-start(), calls=%async_computation.2 | async-start | bytes 5242880 | tf_op jit(solution)/shard_map/reduce_scatter | solution.py:90
  9.5 9.3 %collective-permute-start = (bf16[3,6,1024]{2,1,0:T(8,128)(2,1)S(1)}, bf16[3,6,1024]{2,1,0:T(8,128)(2,1)S(1)}, u32[]{:S(2)}, u32[]{:S(2)}) collective-permute-start(bf16[3,6,1024]{2,1,0:T(8,128)(2,1)S(1)} %pad_maximum_fusion.7), channel_id=1, source_target_pairs={{0,4},{4,8},{8,12},{12,16},{16,20},{20,24},{24,28},{1,5},{5,9},{9,... | collective-permute-start | bytes 110600 | tf_op jit(solution)/shard_map/ppermute | solution.py:12
  29.5 6.3 %copy-start.26 = (s32[8]{0:T(128)S(1)}, s32[8]{0:T(128)}, u32[]{:S(2)}) copy-start(s32[8]{0:T(128)} %constant.185.clone) | copy-start | bytes 100
  29.5 17.6 %copy-start.25 = (s32[8]{0:T(128)S(1)}, s32[8]{0:T(128)}, u32[]{:S(2)}) copy-start(s32[8]{0:T(128)} %constant.186.clone) | copy-start | bytes 100
  29.5 29.4 %collective-permute-start.1 = (bf16[128,1024]{0,1:T(8,128)(2,1)S(1)}, bf16[128,1024]{0,1:T(8,128)(2,1)S(1)}, u32[]{:S(2)}, u32[]{:S(2)}) collective-permute-start(bf16[128,1024]{0,1:T(8,128)(2,1)S(1)} %slice.503), channel_id=1, source_target_pairs={{0,4},{4,8},{8,12},{12,16},{16,20},{20,24},{24,28},{1,5},{5,9},{9,... | collective-permute-start | bytes 786440 | tf_op jit(solution)/shard_map/ppermute | solution.py:12
  60.7 2.8 %copy-start.4 = (bf16[8,8,256,128]{3,2,1,0:T(8,128)(2,1)S(1)}, bf16[8,8,256,128]{3,2,1,0:T(8,128)(2,1)}, u32[]{:S(2)}) copy-start(bf16[8,8,256,128]{3,2,1,0:T(8,128)(2,1)} %copy.67) | copy-start | bytes 12582916
  63.5 1.2 copy-start.18
  82.2 5.8 %copy-start.2 = (f32[1024,8,2,256]{0,3,2,1:T(8,128)}, f32[1024,8,2,256]{0,3,2,1:T(8,128)S(1)}, u32[]{:S(2)}) copy-start(f32[1024,8,2,256]{0,3,2,1:T(8,128)S(1)} %convolution_multiply_fusion) | copy-start | bytes 50331652
  120.8 11.7 %copy-start.22 = (bf16[1024,256]{0,1:T(8,128)(2,1)S(1)}, bf16[1024,256]{0,1:T(8,128)(2,1)}, u32[]{:S(2)}) copy-start(bf16[1024,256]{0,1:T(8,128)(2,1)} %slice_bitcast_fusion.14) | copy-start | bytes 1572868
  120.8 13.2 %copy-start.21 = (bf16[1024,256]{0,1:T(8,128)(2,1)S(1)}, bf16[1024,256]{0,1:T(8,128)(2,1)}, u32[]{:S(2)}) copy-start(bf16[1024,256]{0,1:T(8,128)(2,1)} %slice_bitcast_fusion.15) | copy-start | bytes 1572868
  132.5 21.0 %collective-permute-start.3 = (bf16[1024,256]{0,1:T(8,128)(2,1)S(1)}, bf16[1024,256]{0,1:T(8,128)(2,1)}, u32[]{:S(2)}, u32[]{:S(2)}) collective-permute-start(bf16[1024,256]{0,1:T(8,128)(2,1)S(1)} %copy-done.22), channel_id=1, source_target_pairs={{8,0},{16,8},{24,16},{28,24},{20,28},{12,20},{4,12},{0,4},{9,1},{1... | collective-permute-start | bytes 1572872 | tf_op jit(solution)/shard_map/ppermute | solution.py:173
  134.0 21.1 %collective-permute-start.2 = (bf16[1024,256]{0,1:T(8,128)(2,1)S(1)}, bf16[1024,256]{0,1:T(8,128)(2,1)}, u32[]{:S(2)}, u32[]{:S(2)}) collective-permute-start(bf16[1024,256]{0,1:T(8,128)(2,1)S(1)} %copy-done.21), channel_id=1, source_target_pairs={{0,8},{8,16},{16,24},{24,28},{28,20},{20,12},{12,4},{4,0},{1,9},{9... | collective-permute-start | bytes 1572872 | tf_op jit(solution)/shard_map/ppermute | solution.py:172
  153.5 2.1 copy-start.15
  156.7 15.0 %collective-permute-start.5 = (bf16[1024,256]{0,1:T(8,128)(2,1)S(1)}, bf16[1024,256]{0,1:T(8,128)(2,1)S(1)}, u32[]{:S(2)}, u32[]{:S(2)}) collective-permute-start(bf16[1024,256]{0,1:T(8,128)(2,1)S(1)} %fusion.116), channel_id=1, source_target_pairs={{8,0},{16,8},{24,16},{28,24},{20,28},{12,20},{4,12},{0,4},{9,1},{1... | collective-permute-start | bytes 1572872 | tf_op jit(solution)/shard_map/ppermute | solution.py:173
  158.3 14.4 %collective-permute-start.4 = (bf16[1024,256]{0,1:T(8,128)(2,1)S(1)}, bf16[1024,256]{0,1:T(8,128)(2,1)S(1)}, u32[]{:S(2)}, u32[]{:S(2)}) collective-permute-start(bf16[1024,256]{0,1:T(8,128)(2,1)S(1)} %fusion.118), channel_id=1, source_target_pairs={{0,8},{8,16},{16,24},{24,28},{28,20},{20,12},{12,4},{4,0},{1,9},{9... | collective-permute-start | bytes 1572872 | tf_op jit(solution)/shard_map/ppermute | solution.py:172
  159.0 12.7 %copy-start.14 = (f32[1,2,1024,256]{2,3,1,0:T(8,128)S(1)}, f32[1,2,1024,256]{2,3,1,0:T(8,128)}, u32[]{:S(2)}) copy-start(f32[1,2,1024,256]{2,3,1,0:T(8,128)} %get-tuple-element.77) | copy-start | bytes 6291460
  170.2 2.4 copy-start.13
  170.3 8.4 %collective-permute-start.6 = (bf16[128,1024]{0,1:T(8,128)(2,1)S(1)}, bf16[128,1024]{0,1:T(8,128)(2,1)S(1)}, u32[]{:S(2)}, u32[]{:S(2)}) collective-permute-start(bf16[128,1024]{0,1:T(8,128)(2,1)S(1)} %slice.514), channel_id=1, source_target_pairs={{4,0},{8,4},{12,8},{16,12},{20,16},{24,20},{28,24},{5,1},{9,5},{13... | collective-permute-start | bytes 786440 | tf_op jit(solution)/shard_map/ppermute | solution.py:12
  180.3 2.8 %copy-start.3 = (bf16[8,8,256,128]{3,2,1,0:T(8,128)(2,1)S(1)}, bf16[8,8,256,128]{3,2,1,0:T(8,128)(2,1)}, u32[]{:S(2)}) copy-start(bf16[8,8,256,128]{3,2,1,0:T(8,128)(2,1)} %copy.69) | copy-start | bytes 12582916
  183.2 1.6 copy-start.6
  183.2 2.2 copy-start.7
  185.4 2.3 copy-start.23
  185.4 6.0 %copy-start.24 = (bf16[1024,256]{0,1:T(8,128)(2,1)S(1)}, bf16[1024,256]{0,1:T(8,128)(2,1)}, u32[]{:S(2)}) copy-start(bf16[1024,256]{0,1:T(8,128)(2,1)} %fusion.114) | copy-start | bytes 1572868
  187.7 11.9 %collective-permute-start.8 = (bf16[1024,256]{0,1:T(8,128)(2,1)S(1)}, bf16[1024,256]{0,1:T(8,128)(2,1)}, u32[]{:S(2)}, u32[]{:S(2)}) collective-permute-start(bf16[1024,256]{0,1:T(8,128)(2,1)S(1)} %copy-done.23), channel_id=1, source_target_pairs={{8,0},{16,8},{24,16},{28,24},{20,28},{12,20},{4,12},{0,4},{9,1},{1... | collective-permute-start | bytes 1572872 | tf_op jit(solution)/shard_map/ppermute | solution.py:173
  191.4 11.2 %collective-permute-start.7 = (bf16[1024,256]{0,1:T(8,128)(2,1)S(1)}, bf16[1024,256]{0,1:T(8,128)(2,1)}, u32[]{:S(2)}, u32[]{:S(2)}) collective-permute-start(bf16[1024,256]{0,1:T(8,128)(2,1)S(1)} %copy-done.24), channel_id=1, source_target_pairs={{0,8},{8,16},{16,24},{24,28},{28,20},{20,12},{12,4},{4,0},{1,9},{9... | collective-permute-start | bytes 1572872 | tf_op jit(solution)/shard_map/ppermute | solution.py:172
  192.6 10.0 %copy-start.12 = (f32[1,2,1024,256]{2,3,1,0:T(8,128)S(1)}, f32[1,2,1024,256]{2,3,1,0:T(8,128)}, u32[]{:S(2)}) copy-start(f32[1,2,1024,256]{2,3,1,0:T(8,128)} %get-tuple-element.76) | copy-start | bytes 6291460
  192.7 11.9 %collective-permute-start.9 = (bf16[3,6,1024]{2,1,0:T(8,128)(2,1)S(1)}, bf16[3,6,1024]{2,1,0:T(8,128)(2,1)S(1)}, u32[]{:S(2)}, u32[]{:S(2)}) collective-permute-start(bf16[3,6,1024]{2,1,0:T(8,128)(2,1)S(1)} %pad_maximum_fusion.8), channel_id=1, source_target_pairs={{4,0},{8,4},{12,8},{16,12},{20,16},{24,20},{28,24},{5,1},{9,5},{13... | collective-permute-start | bytes 110600 | tf_op jit(solution)/shard_map/ppermute | solution.py:12
  204.6 9.8 %collective-permute-start.10 = (bf16[1024,256]{0,1:T(8,128)(2,1)}, bf16[1024,256]{0,1:T(8,128)(2,1)}, u32[]{:S(2)}, u32[]{:S(2)}) collective-permute-start(bf16[1024,256]{0,1:T(8,128)(2,1)} %fusion.110), channel_id=1, source_target_pairs={{0,8},{8,16},{16,24},{24,28},{28,20},{20,12},{12,4},{4,0},{1,9},{9... | collective-permute-start | bytes 1572872 | tf_op jit(solution)/shard_map/ppermute | solution.py:172
  204.6 12.5 %collective-permute-start.14 = (bf16[1024,256]{0,1:T(8,128)(2,1)S(1)}, bf16[1024,256]{0,1:T(8,128)(2,1)S(1)}, u32[]{:S(2)}, u32[]{:S(2)}) collective-permute-start(bf16[1024,256]{0,1:T(8,128)(2,1)S(1)} %fusion.108), channel_id=1, source_target_pairs={{8,0},{16,8},{24,16},{28,24},{20,28},{12,20},{4,12},{0,4},{9,1},{1... | collective-permute-start | bytes 1572872 | tf_op jit(solution)/shard_map/ppermute | solution.py:173
  206.8 10.3 %copy-start.11 = (f32[1,2,1024,256]{2,3,1,0:T(8,128)S(1)}, f32[1,2,1024,256]{2,3,1,0:T(8,128)}, u32[]{:S(2)}) copy-start(f32[1,2,1024,256]{2,3,1,0:T(8,128)} %get-tuple-element.71) | copy-start | bytes 6291460
  214.4 5.4 %copy-start.5 = (f32[512,1024]{0,1:T(8,128)S(1)}, f32[512,1024]{0,1:T(8,128)}, u32[]{:S(2)}) copy-start(f32[512,1024]{0,1:T(8,128)} %get-tuple-element.44) | copy-start | bytes 6291460
  216.8 9.8 %collective-permute-start.11 = (bf16[1024,256]{0,1:T(8,128)(2,1)}, bf16[1024,256]{0,1:T(8,128)(2,1)}, u32[]{:S(2)}, u32[]{:S(2)}) collective-permute-start(bf16[1024,256]{0,1:T(8,128)(2,1)} %fusion.106), channel_id=1, source_target_pairs={{0,8},{8,16},{16,24},{24,28},{28,20},{20,12},{12,4},{4,0},{1,9},{9... | collective-permute-start | bytes 1572872 | tf_op jit(solution)/shard_map/ppermute | solution.py:172
  218.0 11.3 %collective-permute-start.15 = (bf16[1024,256]{0,1:T(8,128)(2,1)}, bf16[1024,256]{0,1:T(8,128)(2,1)}, u32[]{:S(2)}, u32[]{:S(2)}) collective-permute-start(bf16[1024,256]{0,1:T(8,128)(2,1)} %fusion.98), channel_id=1, source_target_pairs={{8,0},{16,8},{24,16},{28,24},{20,28},{12,20},{4,12},{0,4},{9,1},{1... | collective-permute-start | bytes 1572872 | tf_op jit(solution)/shard_map/ppermute | solution.py:173
  226.6 2.8 %copy-start.10 = (f32[1,2,1024,256]{2,3,1,0:T(8,128)S(1)}, f32[1,2,1024,256]{2,3,1,0:T(8,128)}, u32[]{:S(2)}) copy-start(f32[1,2,1024,256]{2,3,1,0:T(8,128)} %get-tuple-element.70) | copy-start | bytes 6291460
  229.1 11.8 %collective-permute-start.12 = (bf16[1024,256]{0,1:T(8,128)(2,1)}, bf16[1024,256]{0,1:T(8,128)(2,1)}, u32[]{:S(2)}, u32[]{:S(2)}) collective-permute-start(bf16[1024,256]{0,1:T(8,128)(2,1)} %fusion.104), channel_id=1, source_target_pairs={{0,8},{8,16},{16,24},{24,28},{28,20},{20,12},{12,4},{4,0},{1,9},{9... | collective-permute-start | bytes 1572872 | tf_op jit(solution)/shard_map/ppermute | solution.py:172
  231.3 12.3 %collective-permute-start.16 = (bf16[1024,256]{0,1:T(8,128)(2,1)}, bf16[1024,256]{0,1:T(8,128)(2,1)}, u32[]{:S(2)}, u32[]{:S(2)}) collective-permute-start(bf16[1024,256]{0,1:T(8,128)(2,1)} %fusion.96), channel_id=1, source_target_pairs={{8,0},{16,8},{24,16},{28,24},{20,28},{12,20},{4,12},{0,4},{9,1},{1... | collective-permute-start | bytes 1572872 | tf_op jit(solution)/shard_map/ppermute | solution.py:173
  240.6 3.0 %copy-start.9 = (f32[1,2,1024,256]{2,3,1,0:T(8,128)S(1)}, f32[1,2,1024,256]{2,3,1,0:T(8,128)}, u32[]{:S(2)}) copy-start(f32[1,2,1024,256]{2,3,1,0:T(8,128)} %get-tuple-element.69) | copy-start | bytes 6291460
  240.9 6.5 %copy-start.19 = (f32[512,1024]{0,1:T(8,128)S(1)}, f32[512,1024]{0,1:T(8,128)}, u32[]{:S(2)}) copy-start(f32[512,1024]{0,1:T(8,128)} %get-tuple-element.41) | copy-start | bytes 6291460
  243.3 15.2 %collective-permute-start.13 = (bf16[1024,256]{0,1:T(8,128)(2,1)}, bf16[1024,256]{0,1:T(8,128)(2,1)}, u32[]{:S(2)}, u32[]{:S(2)}) collective-permute-start(bf16[1024,256]{0,1:T(8,128)(2,1)} %fusion.102), channel_id=1, source_target_pairs={{0,8},{8,16},{16,24},{24,28},{28,20},{20,12},{12,4},{4,0},{1,9},{9... | collective-permute-start | bytes 1572872 | tf_op jit(solution)/shard_map/ppermute | solution.py:172
  245.6 10.4 %copy-start.16 = (bf16[512,1024]{0,1:T(8,128)(2,1)S(1)}, bf16[512,1024]{0,1:T(8,128)(2,1)}, u32[]{:S(2)}) copy-start(bf16[512,1024]{0,1:T(8,128)(2,1)} %fusion.25) | copy-start | bytes 3145732
  245.6 14.5 %collective-permute-start.17 = (bf16[1024,256]{0,1:T(8,128)(2,1)}, bf16[1024,256]{0,1:T(8,128)(2,1)}, u32[]{:S(2)}, u32[]{:S(2)}) collective-permute-start(bf16[1024,256]{0,1:T(8,128)(2,1)} %fusion.94), channel_id=1, source_target_pairs={{8,0},{16,8},{24,16},{28,24},{20,28},{12,20},{4,12},{0,4},{9,1},{1... | collective-permute-start | bytes 1572872 | tf_op jit(solution)/shard_map/ppermute | solution.py:173
  256.0 1.3 copy-start.17
  257.3 2.8 %copy-start.8 = (f32[1,2,1024,256]{2,3,1,0:T(8,128)S(1)}, f32[1,2,1024,256]{2,3,1,0:T(8,128)}, u32[]{:S(2)}) copy-start(f32[1,2,1024,256]{2,3,1,0:T(8,128)} %get-tuple-element.68) | copy-start | bytes 6291460
  260.1 2.6 copy-start.1
Sparse Core Ops, SparseCore 0:
  9.6 37.1 all-gather.1
  99.9 44.8 reduce-scatter.1

commit v2 on v1

--- a/solution.py
+++ b/solution.py
@@ -148,16 +148,17 @@
     members = jnp.asarray(ring, jnp.int32)
     forward = [(ring[i], ring[(i + 1) % count]) for i in range(count)]
     backward = [(ring[(i + 1) % count], ring[i]) for i in range(count)]
-    blocks = full_cotangent.reshape(full_cotangent.shape[0], count, 2, half).transpose(1, 2, 0, 3)
     local_grad = (
-        jnp.einsum("tc,bhtd->bhcd", gated_rows, blocks, preferred_element_type=jnp.float32)
+        lax.dot_general(
+            gated_rows, full_cotangent, (((0,), (0,)), ((), ())), preferred_element_type=jnp.float32
+        )
         * grad_scale
     )
 
     def contribution(step, direction):
         owner = members[(place - direction * (1 + step)) % count]
-        block = lax.dynamic_index_in_dim(local_grad, owner, 0, keepdims=False)
-        return block[0 if direction == 1 else 1]
+        first = owner * width + (0 if direction == 1 else half)
+        return lax.dynamic_slice_in_dim(local_grad, first, half, 1)
 
     ahead = contribution(0, 1)
     behind = contribution(0, -1)
@@ -169,12 +170,13 @@
             sent_ahead, sent_behind, state = lax.optimization_barrier(
                 (sent_ahead, sent_behind, state)
             )
-        ahead = lax.ppermute(sent_ahead, "seq", forward).astype(jnp.float32)
-        behind = lax.ppermute(sent_behind, "seq", backward).astype(jnp.float32)
+        ahead = lax.ppermute(sent_ahead, "seq", forward)
+        behind = lax.ppermute(sent_behind, "seq", backward)
         if stages:
             state = stages.pop(0)(state)
-        ahead = ahead + contribution(step, 1)
-        behind = behind + contribution(step, -1)
+            ahead, behind, state = lax.optimization_barrier((ahead, behind, state))
+        ahead = ahead.astype(jnp.float32) + contribution(step, 1)
+        behind = behind.astype(jnp.float32) + contribution(step, -1)
     while stages:
         state = stages.pop(0)(state)
     return state, jnp.concatenate([ahead, behind], axis=1).astype(jnp.bfloat16)

time: 274 us -> 274 us (level)
  waiting for transfers between devices: 20.3 us -> 65 us
  local copies, waits for them, and re-layouts: 65.1 us -> 37.1 us
  between operations: 55 us -> 35.6 us
  other arithmetic: 61.1 us -> 65 us
    reduce_scatter x1, waiting for transfers between devices: 0.02 us -> 30.3 us  [project(): lax.psum_scatter(jnp.dot(gated_rows, out_weight, preferred_element_type=j...]
    dynamic_slice x2 -> x0, local copies, waits for them, and re-layouts: 19.2 us -> none  [contribution(): block = lax.dynamic_index_in_dim(local_grad, owner, 0, keepdims=False)]
    ppermute x14, waiting for transfers between devices: 14.5 us -> 31.9 us  [the longest x7 25.8 us: ring_reduce_scatter(): ahead = lax.ppermute(sent_ahead, 'seq', forward)]
    convert_element_type x3, other arithmetic: 21.2 us -> 28 us  [feature_back(): grads = tuple((spread_back(jnp.concatenate([grad_features[i], features_af...]
    all_gather x1 -> x0, local copies, waits for them, and re-layouts: 6.46 us -> none  [per_device(): full_cotangent = lax.all_gather(cotangent, 'tp', axis=0, tiled=True)]
    convert_element_type x6 -> x3, other arithmetic: 11.4 us -> 6.63 us  [ring_reduce_scatter(): sent_ahead = ahead.astype(jnp.bfloat16)]
    ppermute x4, waiting for transfers between devices: 5.06 us -> 2.07 us  [passed_along(): lax.ppermute(value, axis, [(source, source + steps) for source in range(l...]
    unnamed x66 -> x41, local copies, waits for them, and re-layouts: 26.3 us -> 24.5 us
  transfers between devices with their start and end apart: 20 -> 20, of which waited for: 4 -> 10; matrix products, arithmetic and copies ran while one was open for 46% -> 36% of each run, Pallas kernels for 0% -> 0%
where the time goes in v2:
time: 274 us; the launch traced here: 270 us
  waiting for transfers between devices  65 us (24%)
  other arithmetic  65 us (24%)
  matrix products  40.6 us (15%)
  local copies, waits for them, and re-layouts  37.1 us (14%)
  between operations  35.6 us (13%)
  starting transfers between devices  27.1 us (10%)
    reduce_scatter x1, waiting for transfers between devices, project(): lax.psum_scatter(jnp.dot(gated_rows, out_weight, preferred_element_type=j...  30.3 us
    convert_element_type x3, other arithmetic, feature_back(): grads = tuple((spread_back(jnp.concatenate([grad_features[i], features_af...  28 us
    ppermute x7, waiting for transfers between devices, ring_reduce_scatter(): ahead = lax.ppermute(sent_ahead, 'seq', forward)  25.8 us
    unnamed x41, local copies, waits for them, and re-layouts  24.5 us
    ppermute x7, starting transfers between devices, ring_reduce_scatter(): ahead = lax.ppermute(sent_ahead, 'seq', forward)  14.1 us
    ppermute x4, starting transfers between devices, passed_along(): lax.ppermute(value, axis, [(source, source + steps) for source in range(l...  11.1 us
    dot_general x1, matrix products, gate_back(): lax.dot_general(full_cotangent, out_weight, (((1,), (1,)), ((), ())), pre...  10.5 us
    dot_general x1, matrix products, project(): jnp.dot(gated_rows, out_weight, preferred_element_type=jnp.float32)  9.75 us
  transfers between devices with their start and end apart: 20, of which 10 were waited for; matrix products, arithmetic and copies ran while one was open for 36% of the time, Pallas kernels for 0%

profile of v2, /device:TPU:0, one launch (start us, length us, event | category | flops | bytes accessed | tf_op | source)
XLA Modules:
  0.0 270.2 jit_solution(3306764727992153134)
XLA Ops:
  9.5 4.9 %collective-permute-start = (bf16[3,6,1024]{2,1,0:T(8,128)(2,1)S(1)}, bf16[3,6,1024]{2,1,0:T(8,128)(2,1)S(1)}, u32[]{:S(2)}, u32[]{:S(2)}) collective-permute-start(bf16[3,6,1024]{2,1,0:T(8,128)(2,1)S(1)} %pad_maximum_fusion.7), channel_id=1, source_target_pairs={{0,4},{4,8},{8,12},{12,16},{16,20},{20,24},{24,28},{1,5},{5,9},{9,... | collective-permute-start | bytes 110600 | tf_op jit(solution)/shard_map/ppermute | solution.py:12
  17.0 1.5 copy.38
  19.7 9.5 %multiply_convert_fusion = (bf16[512,1024]{0,1:T(8,128)(2,1)S(1)}, f32[512,1024]{0,1:T(8,128)}, f32[512,1024]{0,1:T(8,128)}) fusion(bf16[512,1024]{0,1:T(8,128)(2,1)S(1)} %copy.41, bf16[6,1024]{0,1:T(8,128)(2,1)S(1)} %bitcast.148, f32[1024]{0:T(1024)S(1)} %bitcast.176, f32[1024]{0:T(1024)S(1)} %bitcast.174, f32[1024]{0:T(1024)S(1)} %bitcast.150, ...), kind=kLoop, calls=%fused_computation.127 | loop fusion | flops 40894464 | bytes 7421952 | tf_op jit(solution)/shard_map/convert_element_type | solution.py:80
  29.3 3.6 %collective-permute-start.1 = (bf16[128,1024]{0,1:T(8,128)(2,1)S(1)}, bf16[128,1024]{0,1:T(8,128)(2,1)S(1)}, u32[]{:S(2)}, u32[]{:S(2)}) collective-permute-start(bf16[128,1024]{0,1:T(8,128)(2,1)S(1)} %slice.421), channel_id=1, source_target_pairs={{0,4},{4,8},{8,12},{12,16},{16,20},{20,24},{24,28},{1,5},{5,9},{9,... | collective-permute-start | bytes 786440 | tf_op jit(solution)/shard_map/ppermute | solution.py:12
  32.9 2.3 copy.35
  46.4 3.9 %fusion.2 = bf16[8,8,256,128]{3,1,2,0:T(8,128)(2,1)S(1)} fusion(bf16[64,128]{1,0:T(8,128)(2,1)S(1)} %copy-done, s32[32768]{0:T(1024)S(1)} %subtract_bitcast_fusion.1), kind=kOutput, calls=%fused_computation.53 | convolution fusion | flops 543162368 | bytes 4341760 | tf_op jit(solution)/shard_map/dot_general | solution.py:45
  50.3 3.1 %copy.56 = bf16[8,8,256,128]{3,2,1,0:T(8,128)(2,1)} copy(bf16[8,8,256,128]{3,1,2,0:T(8,128)(2,1)S(1)} %fusion.2) | data formatting | bytes 8388608
  57.4 2.4 fusion.63
  61.5 4.6 %fusion.55 = (bf16[512,1024]{0,1:T(8,128)(2,1)S(1)}, f32[512,1024]{0,1:T(8,128)}) fusion(f32[128,8,4,128]{3,2,1,0:T(4,128)S(1)} %bitcast.145, bf16[512,1024]{0,1:T(8,128)(2,1)S(1)} %copy-done.9, bf16[6,1024]{0,1:T(8,128)(2,1)S(1)} %bitcast.147, f32[1024]{0:T(1024)S(1)} %bitcast.180, f32[1024]{0:T(1024)S(1)} %bitcast.182, f32[1024]{0:T(1024)S(1)} %bitcast.184, ...), kind=kLoop, calls=%fused_computation.110 | loop fusion | flops 20971520 | bytes 6332416 | tf_op jit(solution)/shard_map/convert_element_type | solution.py:84
  66.1 6.3 %convolution_multiply_fusion = f32[1024,4096]{1,0:T(8,128)S(1)} fusion(bf16[512,1024]{0,1:T(8,128)(2,1)S(1)} %get-tuple-element.51, bf16[512,4096]{1,0:T(8,128)(2,1)} %all-gather.2.cloned.1.call-done), kind=kOutput, calls=%fused_computation.4 | convolution fusion | flops 4299161600 | bytes 22020096 | tf_op jit(solution)/shard_map/dot_general | solution.py:152
  72.4 5.8 %copy-done.3 = f32[1024,4096]{1,0:T(8,128)} copy-done((f32[1024,4096]{1,0:T(8,128)}, f32[1024,4096]{1,0:T(8,128)S(1)}, u32[]{:S(2)}) %copy-start.3) | copy-done | bytes 16777240
  79.3 9.8 %convolution_convert_fusion.2 = bf16[512,4096]{1,0:T(8,128)(2,1)} fusion(bf16[512,1024]{0,1:T(8,128)(2,1)S(1)} %get-tuple-element.51, bf16[1024,4096]{1,0:T(8,128)(2,1)} %param.14), kind=kOutput, calls=%fused_computation.22 | convolution fusion | flops 4297064448 | bytes 13631488 | tf_op jit(solution)/shard_map/dot_general | solution.py:91
  89.1 1.6 collective-permute-start.2
  92.3 10.1 %collective-permute-done.2 = bf16[1024,256]{1,0:T(8,128)(2,1)S(1)} collective-permute-done((bf16[1024,256]{1,0:T(8,128)(2,1)}, bf16[1024,256]{1,0:T(8,128)(2,1)S(1)}, u32[]{:S(2)}, u32[]{:S(2)}) %collective-permute-start.2) | collective-permute-done | bytes 524320 | tf_op jit(solution)/shard_map/ppermute | solution.py:173
  103.7 30.3 %reduce-scatter.2.cloned.1.call-done = bf16[128,4096]{1,0:T(8,128)(2,1)} async-done(((bf16[512,4096]{1,0:T(8,128)(2,1)}), bf16[128,4096]{1,0:T(8,128)(2,1)}) %reduce-scatter.2.cloned.1.call-update) | async-done | bytes 1048592 | tf_op jit(solution)/shard_map/reduce_scatter | solution.py:90
  134.0 2.9 %add_convert_fusion.12 = (bf16[1024,256]{1,0:T(8,128)(2,1)}, bf16[1024,256]{1,0:T(8,128)(2,1)}) fusion(f32[1024,4096]{1,0:T(8,128)} %copy-done.3, s32[]{:T(128)S(6)} %select_n.178, bf16[1024,256]{1,0:T(8,128)(2,1)S(1)} %collective-permute-done.3, s32[]{:T(128)S(6)} %select_n.175, bf16[1024,256]{1,0:T(8,128)(2,1)S(1)} %collective-permute-done.2), kind=kLoop, calls=%fused_computation.181 | loop fusion | flops 1572864 | bytes 4194312 | tf_op jit(solution)/shard_map/convert_element_type | solution.py:168
  136.9 1.5 collective-permute-start.4
  139.0 10.5 %bitcast_multiply_fusion.2 = (f32[512,1024]{0,1:T(8,128)}, bf16[512,1024]{0,1:T(8,128)(2,1)S(1)}) fusion(f32[128,8,4,128]{3,2,1,0:T(4,128)S(1)} %bitcast.146, f32[512,1024]{0,1:T(8,128)S(1)} %copy-done.10, bf16[1024,4096]{1,0:T(8,128)(2,1)} %param.14, bf16[512,4096]{1,0:T(8,128)(2,1)} %all-gather.2.cloned.1.call-done), kind=kOutput, calls=%fused_computation.108 | convolution fusion | flops 4296540160 | bytes 19922944 | tf_op jit(solution)/shard_map/dot_general | solution.py:100
  149.5 1.3 collective-permute-start.6
  152.0 3.9 %fusion.3 = bf16[8,8,256,128]{3,1,2,0:T(8,128)(2,1)S(1)} fusion(bf16[64,128]{1,0:T(8,128)(2,1)S(1)} %copy-done, s32[32768]{0:T(1024)S(1)} %subtract_bitcast_fusion), kind=kOutput, calls=%fused_computation.54 | convolution fusion | flops 543162368 | bytes 4341760 | tf_op jit(solution)/shard_map/dot_general | solution.py:45
  155.9 3.1 %copy.58 = bf16[8,8,256,128]{3,2,1,0:T(8,128)(2,1)} copy(bf16[8,8,256,128]{3,1,2,0:T(8,128)(2,1)S(1)} %fusion.3) | data formatting | bytes 8388608
  159.1 3.1 %add_convert_fusion.10 = (bf16[1024,256]{1,0:T(8,128)(2,1)}, bf16[1024,256]{1,0:T(8,128)(2,1)}) fusion(f32[1024,4096]{1,0:T(8,128)} %copy-done.3, s32[]{:T(128)S(6)} %select_n.184, bf16[1024,256]{1,0:T(8,128)(2,1)} %collective-permute-done.5, s32[]{:T(128)S(6)} %select_n.181, bf16[1024,256]{1,0:T(8,128)(2,1)} %collective-permute-done.4), kind=kLoop, calls=%fused_computation.179 | loop fusion | flops 1572864 | bytes 4194312 | tf_op jit(solution)/shard_map/convert_element_type | solution.py:168
  162.1 3.5 %collective-permute-start.7 = (bf16[1024,256]{1,0:T(8,128)(2,1)}, bf16[1024,256]{1,0:T(8,128)(2,1)}, u32[]{:S(2)}, u32[]{:S(2)}) collective-permute-start(bf16[1024,256]{1,0:T(8,128)(2,1)} %get-tuple-element.67), channel_id=1, source_target_pairs={{0,8},{8,16},{16,24},{24,28},{28,20},{20,12},{12,4},{4,0},{1,9},{9... | collective-permute-start | bytes 1572872 | tf_op jit(solution)/shard_map/ppermute | solution.py:173
  167.6 2.4 fusion.59
  172.6 2.1 bitcast_multiply_fusion
  177.4 1.3 collective-permute-start.9
  181.3 2.1 collective-permute-done.9
  183.4 3.0 %add_convert_fusion.8 = (bf16[1024,256]{1,0:T(8,128)(2,1)}, bf16[1024,256]{1,0:T(8,128)(2,1)}) fusion(f32[1024,4096]{1,0:T(8,128)} %copy-done.3, s32[]{:T(128)S(6)} %select_n.190, bf16[1024,256]{1,0:T(8,128)(2,1)} %collective-permute-done.8, s32[]{:T(128)S(6)} %select_n.187, bf16[1024,256]{1,0:T(8,128)(2,1)} %collective-permute-done.7), kind=kLoop, calls=%fused_computation.177 | loop fusion | flops 1572864 | bytes 4194312 | tf_op jit(solution)/shard_map/convert_element_type | solution.py:168
  186.5 2.0 collective-permute-start.10
  190.9 13.4 %fusion.42 = bf16[512,1024]{0,1:T(8,128)(2,1)S(1)} fusion(f32[512,1024]{0,1:T(8,128)} %get-tuple-element.83, f32[6,1024]{0,1:T(8,128)} %bitcast_convert_fusion.2, f32[1024]{0:T(1024)S(1)} %bitcast.181, f32[1024]{0:T(1024)S(1)} %bitcast.183, f32[1024]{0:T(1024)S(1)} %bitcast.185, f32[1024]{0:T(1024)S(1)} %bitcast.187, f32[1024]{0:T(1024)S(1)} %bitcast.189, ...), kind=kLoop, calls=%fused_computation.93 | loop fusion | flops 10485760 | bytes 3198976 | tf_op jit(solution)/shard_map/convert_element_type | solution.py:128
  204.3 7.3 %fusion.25 = bf16[512,1024]{0,1:T(8,128)(2,1)} fusion(f32[512,1024]{0,1:T(8,128)S(1)} %copy-done.4, f32[6,1024]{0,1:T(8,128)S(1)} %copy-done.11, f32[1024]{0:T(1024)S(1)} %bitcast.161, f32[1024]{0:T(1024)S(1)} %bitcast.163, f32[1024]{0:T(1024)S(1)} %bitcast.165, f32[1024]{0:T(1024)S(1)} %bitcast.167, f32[1024]{0:T(1024)S(1)} %bitcast.169, ...), kind=kLoop, calls=%fused_computation.76 | loop fusion | flops 10485760 | bytes 3198976 | tf_op jit(solution)/shard_map/convert_element_type | solution.py:128
  211.6 7.3 %fusion.8 = bf16[512,1024]{0,1:T(8,128)(2,1)} fusion(f32[512,1024]{0,1:T(8,128)S(1)} %get-tuple-element.86, f32[6,1024]{0,1:T(8,128)S(1)} %bitcast_convert_fusion, f32[1024]{0:T(1024)S(1)} %bitcast.177, f32[1024]{0:T(1024)S(1)} %bitcast.175, f32[1024]{0:T(1024)S(1)} %bitcast.151, f32[1024]{0:T(1024)S(1)} %bitcast.153, f32[1024]{0:T(1024)S(1)} %bitcast.155, ...), kind=kLoop, calls=%fused_computation.59 | loop fusion | flops 10485760 | bytes 3198976 | tf_op jit(solution)/shard_map/convert_element_type | solution.py:128
  218.9 2.1 add_convert_fusion.7
  221.0 2.1 collective-permute-start.12
  224.3 7.4 %collective-permute-done.12 = bf16[1024,256]{1,0:T(8,128)(2,1)S(1)} collective-permute-done((bf16[1024,256]{1,0:T(8,128)(2,1)S(1)}, bf16[1024,256]{1,0:T(8,128)(2,1)S(1)}, u32[]{:S(2)}, u32[]{:S(2)}) %collective-permute-start.12) | collective-permute-done | bytes 524320 | tf_op jit(solution)/shard_map/ppermute | solution.py:173
  231.7 1.5 collective-permute-done.15
  233.2 1.8 add_convert_fusion.6
  234.9 1.5 collective-permute-start.13
  238.3 6.0 %collective-permute-done.13 = bf16[1024,256]{1,0:T(8,128)(2,1)S(1)} collective-permute-done((bf16[1024,256]{1,0:T(8,128)(2,1)S(1)}, bf16[1024,256]{1,0:T(8,128)(2,1)S(1)}, u32[]{:S(2)}, u32[]{:S(2)}) %collective-permute-start.13) | collective-permute-done | bytes 524320 | tf_op jit(solution)/shard_map/ppermute | solution.py:173
  244.3 1.4 collective-permute-done.16
  245.7 2.8 %add_convert_fusion.5 = (bf16[1024,256]{1,0:T(8,128)(2,1)}, bf16[1024,256]{1,0:T(8,128)(2,1)}) fusion(f32[1024,4096]{1,0:T(8,128)} %copy-done.3, s32[]{:T(128)S(6)} %select_n.199, bf16[1024,256]{1,0:T(8,128)(2,1)S(1)} %collective-permute-done.13, s32[]{:T(128)S(6)} %select_n.211, bf16[1024,256]{1,0:T(8,128)(2,1)S(1)} %collective-permute-done.16), kind=kLoop, calls=%fused_computation.174 | loop fusion | flops 1572864 | bytes 4194312 | tf_op jit(solution)/shard_map/convert_element_type | solution.py:167
  248.4 1.9 collective-permute-start.14
  251.7 1.3 copy.50
  253.0 1.3 copy.51
  254.3 1.3 copy.52
  255.6 2.3 collective-permute-done.14
  257.9 1.9 collective-permute-done.17
  259.8 2.1 add_convert_fusion.4
  (94 shorter events, 25.6 us)
Async XLA Ops:
  7.2 39.3 %copy-start = (bf16[64,128]{1,0:T(8,128)(2,1)S(1)}, bf16[64,128]{1,0:T(8,128)(2,1)}, u32[]{:S(2)}) copy-start(bf16[64,128]{1,0:T(8,128)(2,1)} %param.13) | copy-start | bytes 49156
  7.2 9.3 %copy-start.12 = (bf16[512,1024]{1,0:T(8,128)(2,1)S(1)}, bf16[512,1024]{1,0:T(8,128)(2,1)}, u32[]{:S(2)}) copy-start(bf16[512,1024]{1,0:T(8,128)(2,1)} %param.11) | copy-start | bytes 3145732
  7.2 58.9 %all-gather.2.cloned.1.call-start = ((), (), s32[]{:S(2)}) async-start(), calls=%async_computation.1 | async-start | bytes 5242880 | tf_op jit(solution)/shard_map/all_gather | solution.py:71
  7.9 126.1 %reduce-scatter.2.cloned.1.call-start = ((), (), s32[]{:S(2)}) async-start(), calls=%async_computation.2 | async-start | bytes 5242880 | tf_op jit(solution)/shard_map/reduce_scatter | solution.py:90
  9.5 9.1 %collective-permute-start = (bf16[3,6,1024]{2,1,0:T(8,128)(2,1)S(1)}, bf16[3,6,1024]{2,1,0:T(8,128)(2,1)S(1)}, u32[]{:S(2)}, u32[]{:S(2)}) collective-permute-start(bf16[3,6,1024]{2,1,0:T(8,128)(2,1)S(1)} %pad_maximum_fusion.7), channel_id=1, source_target_pairs={{0,4},{4,8},{8,12},{12,16},{16,20},{20,24},{24,28},{1,5},{5,9},{9,... | collective-permute-start | bytes 110600 | tf_op jit(solution)/shard_map/ppermute | solution.py:12
  29.2 6.0 %copy-start.14 = (s32[8]{0:T(128)S(1)}, s32[8]{0:T(128)}, u32[]{:S(2)}) copy-start(s32[8]{0:T(128)} %constant.198.clone) | copy-start | bytes 100
  29.3 26.4 %collective-permute-start.1 = (bf16[128,1024]{0,1:T(8,128)(2,1)S(1)}, bf16[128,1024]{0,1:T(8,128)(2,1)S(1)}, u32[]{:S(2)}, u32[]{:S(2)}) collective-permute-start(bf16[128,1024]{0,1:T(8,128)(2,1)S(1)} %slice.421), channel_id=1, source_target_pairs={{0,4},{4,8},{8,12},{12,16},{16,20},{20,24},{24,28},{1,5},{5,9},{9,... | collective-permute-start | bytes 786440 | tf_op jit(solution)/shard_map/ppermute | solution.py:12
  50.3 3.2 %copy-start.13 = (s32[8]{0:T(128)S(1)}, s32[8]{0:T(128)}, u32[]{:S(2)}) copy-start(s32[8]{0:T(128)} %constant.199.clone) | copy-start | bytes 100
  57.4 2.8 %copy-start.1 = (bf16[8,8,256,128]{3,2,1,0:T(8,128)(2,1)S(1)}, bf16[8,8,256,128]{3,2,1,0:T(8,128)(2,1)}, u32[]{:S(2)}) copy-start(bf16[8,8,256,128]{3,2,1,0:T(8,128)(2,1)} %copy.56) | copy-start | bytes 12582916
  60.2 1.2 copy-start.9
  72.4 5.8 %copy-start.3 = (f32[1024,4096]{1,0:T(8,128)}, f32[1024,4096]{1,0:T(8,128)S(1)}, u32[]{:S(2)}) copy-start(f32[1024,4096]{1,0:T(8,128)S(1)} %convolution_multiply_fusion) | copy-start | bytes 50331652
  89.1 13.4 %collective-permute-start.2 = (bf16[1024,256]{1,0:T(8,128)(2,1)}, bf16[1024,256]{1,0:T(8,128)(2,1)S(1)}, u32[]{:S(2)}, u32[]{:S(2)}) collective-permute-start(bf16[1024,256]{1,0:T(8,128)(2,1)} %get-tuple-element.49), channel_id=1, source_target_pairs={{0,8},{8,16},{16,24},{24,28},{28,20},{20,12},{12,4},{4,0},{1,9},{9... | collective-permute-start | bytes 1572872 | tf_op jit(solution)/shard_map/ppermute | solution.py:173
  90.7 13.0 %collective-permute-start.3 = (bf16[1024,256]{1,0:T(8,128)(2,1)}, bf16[1024,256]{1,0:T(8,128)(2,1)S(1)}, u32[]{:S(2)}, u32[]{:S(2)}) collective-permute-start(bf16[1024,256]{1,0:T(8,128)(2,1)} %get-tuple-element.50), channel_id=1, source_target_pairs={{8,0},{16,8},{24,16},{28,24},{20,28},{12,20},{4,12},{0,4},{9,1},{1... | collective-permute-start | bytes 1572872 | tf_op jit(solution)/shard_map/ppermute | solution.py:174
  134.0 4.9 %copy-start.10 = (f32[512,1024]{0,1:T(8,128)S(1)}, f32[512,1024]{0,1:T(8,128)}, u32[]{:S(2)}) copy-start(f32[512,1024]{0,1:T(8,128)} %get-tuple-element.109) | copy-start | bytes 6291460
  136.9 22.1 %collective-permute-start.4 = (bf16[1024,256]{1,0:T(8,128)(2,1)}, bf16[1024,256]{1,0:T(8,128)(2,1)}, u32[]{:S(2)}, u32[]{:S(2)}) collective-permute-start(bf16[1024,256]{1,0:T(8,128)(2,1)} %get-tuple-element.57), channel_id=1, source_target_pairs={{0,8},{8,16},{16,24},{24,28},{28,20},{20,12},{12,4},{4,0},{1,9},{9... | collective-permute-start | bytes 1572872 | tf_op jit(solution)/shard_map/ppermute | solution.py:173
  138.4 20.7 %collective-permute-start.5 = (bf16[1024,256]{1,0:T(8,128)(2,1)}, bf16[1024,256]{1,0:T(8,128)(2,1)}, u32[]{:S(2)}, u32[]{:S(2)}) collective-permute-start(bf16[1024,256]{1,0:T(8,128)(2,1)} %get-tuple-element.58), channel_id=1, source_target_pairs={{8,0},{16,8},{24,16},{28,24},{20,28},{12,20},{4,12},{0,4},{9,1},{1... | collective-permute-start | bytes 1572872 | tf_op jit(solution)/shard_map/ppermute | solution.py:174
  149.5 9.6 %collective-permute-start.6 = (bf16[128,1024]{0,1:T(8,128)(2,1)S(1)}, bf16[128,1024]{0,1:T(8,128)(2,1)S(1)}, u32[]{:S(2)}, u32[]{:S(2)}) collective-permute-start(bf16[128,1024]{0,1:T(8,128)(2,1)S(1)} %slice.426), channel_id=1, source_target_pairs={{4,0},{8,4},{12,8},{16,12},{20,16},{24,20},{28,24},{5,1},{9,5},{13... | collective-permute-start | bytes 786440 | tf_op jit(solution)/shard_map/ppermute | solution.py:12
  162.1 21.3 %collective-permute-start.7 = (bf16[1024,256]{1,0:T(8,128)(2,1)}, bf16[1024,256]{1,0:T(8,128)(2,1)}, u32[]{:S(2)}, u32[]{:S(2)}) collective-permute-start(bf16[1024,256]{1,0:T(8,128)(2,1)} %get-tuple-element.67), channel_id=1, source_target_pairs={{0,8},{8,16},{16,24},{24,28},{28,20},{20,12},{12,4},{4,0},{1,9},{9... | collective-permute-start | bytes 1572872 | tf_op jit(solution)/shard_map/ppermute | solution.py:173
  165.7 17.7 %collective-permute-start.8 = (bf16[1024,256]{1,0:T(8,128)(2,1)}, bf16[1024,256]{1,0:T(8,128)(2,1)}, u32[]{:S(2)}, u32[]{:S(2)}) collective-permute-start(bf16[1024,256]{1,0:T(8,128)(2,1)} %get-tuple-element.68), channel_id=1, source_target_pairs={{8,0},{16,8},{24,16},{28,24},{20,28},{12,20},{4,12},{0,4},{9,1},{1... | collective-permute-start | bytes 1572872 | tf_op jit(solution)/shard_map/ppermute | solution.py:174
  167.6 2.8 %copy-start.2 = (bf16[8,8,256,128]{3,2,1,0:T(8,128)(2,1)S(1)}, bf16[8,8,256,128]{3,2,1,0:T(8,128)(2,1)}, u32[]{:S(2)}) copy-start(bf16[8,8,256,128]{3,2,1,0:T(8,128)(2,1)} %copy.58) | copy-start | bytes 12582916
  170.4 1.6 copy-start.5
  170.4 2.2 copy-start.6
  177.4 6.0 %collective-permute-start.9 = (bf16[3,6,1024]{2,1,0:T(8,128)(2,1)S(1)}, bf16[3,6,1024]{2,1,0:T(8,128)(2,1)S(1)}, u32[]{:S(2)}, u32[]{:S(2)}) collective-permute-start(bf16[3,6,1024]{2,1,0:T(8,128)(2,1)S(1)} %pad_maximum_fusion.8), channel_id=1, source_target_pairs={{4,0},{8,4},{12,8},{16,12},{20,16},{24,20},{28,24},{5,1},{9,5},{13... | collective-permute-start | bytes 110600 | tf_op jit(solution)/shard_map/ppermute | solution.py:12
  186.5 32.4 %collective-permute-start.10 = (bf16[1024,256]{1,0:T(8,128)(2,1)}, bf16[1024,256]{1,0:T(8,128)(2,1)}, u32[]{:S(2)}, u32[]{:S(2)}) collective-permute-start(bf16[1024,256]{1,0:T(8,128)(2,1)} %get-tuple-element.80), channel_id=1, source_target_pairs={{0,8},{8,16},{16,24},{24,28},{28,20},{20,12},{12,4},{4,0},{1,9},{9... | collective-permute-start | bytes 1572872 | tf_op jit(solution)/shard_map/ppermute | solution.py:173
  188.5 30.4 %collective-permute-start.11 = (bf16[1024,256]{1,0:T(8,128)(2,1)}, bf16[1024,256]{1,0:T(8,128)(2,1)}, u32[]{:S(2)}, u32[]{:S(2)}) collective-permute-start(bf16[1024,256]{1,0:T(8,128)(2,1)} %get-tuple-element.81), channel_id=1, source_target_pairs={{8,0},{16,8},{24,16},{28,24},{20,28},{12,20},{4,12},{0,4},{9,1},{1... | collective-permute-start | bytes 1572872 | tf_op jit(solution)/shard_map/ppermute | solution.py:174
  190.8 13.5 %copy-start.4 = (f32[512,1024]{0,1:T(8,128)S(1)}, f32[512,1024]{0,1:T(8,128)}, u32[]{:S(2)}) copy-start(f32[512,1024]{0,1:T(8,128)} %get-tuple-element.85) | copy-start | bytes 6291460
  190.8 13.5 %copy-start.11 = (f32[6,1024]{0,1:T(8,128)S(1)}, f32[6,1024]{0,1:T(8,128)}, u32[]{:S(2)}) copy-start(f32[6,1024]{0,1:T(8,128)} %bitcast_convert_fusion.1) | copy-start | bytes 73732
  221.0 10.7 %collective-permute-start.12 = (bf16[1024,256]{1,0:T(8,128)(2,1)S(1)}, bf16[1024,256]{1,0:T(8,128)(2,1)S(1)}, u32[]{:S(2)}, u32[]{:S(2)}) collective-permute-start(bf16[1024,256]{1,0:T(8,128)(2,1)S(1)} %get-tuple-element.119), channel_id=1, source_target_pairs={{0,8},{8,16},{16,24},{24,28},{28,20},{20,12},{12,4},{4,0},{1,9},{9... | collective-permute-start | bytes 1572872 | tf_op jit(solution)/shard_map/ppermute | solution.py:173
  223.0 10.1 %collective-permute-start.15 = (bf16[1024,256]{1,0:T(8,128)(2,1)S(1)}, bf16[1024,256]{1,0:T(8,128)(2,1)S(1)}, u32[]{:S(2)}, u32[]{:S(2)}) collective-permute-start(bf16[1024,256]{1,0:T(8,128)(2,1)S(1)} %get-tuple-element.120), channel_id=1, source_target_pairs={{8,0},{16,8},{24,16},{28,24},{20,28},{12,20},{4,12},{0,4},{9,1},{1... | collective-permute-start | bytes 1572872 | tf_op jit(solution)/shard_map/ppermute | solution.py:174
  234.9 9.3 %collective-permute-start.13 = (bf16[1024,256]{1,0:T(8,128)(2,1)S(1)}, bf16[1024,256]{1,0:T(8,128)(2,1)S(1)}, u32[]{:S(2)}, u32[]{:S(2)}) collective-permute-start(bf16[1024,256]{1,0:T(8,128)(2,1)S(1)} %get-tuple-element.117), channel_id=1, source_target_pairs={{0,8},{8,16},{16,24},{24,28},{28,20},{20,12},{12,4},{4,0},{1,9},{9... | collective-permute-start | bytes 1572872 | tf_op jit(solution)/shard_map/ppermute | solution.py:173
  236.5 9.2 %collective-permute-start.16 = (bf16[1024,256]{1,0:T(8,128)(2,1)S(1)}, bf16[1024,256]{1,0:T(8,128)(2,1)S(1)}, u32[]{:S(2)}, u32[]{:S(2)}) collective-permute-start(bf16[1024,256]{1,0:T(8,128)(2,1)S(1)} %get-tuple-element.118), channel_id=1, source_target_pairs={{8,0},{16,8},{24,16},{28,24},{20,28},{12,20},{4,12},{0,4},{9,1},{1... | collective-permute-start | bytes 1572872 | tf_op jit(solution)/shard_map/ppermute | solution.py:174
  248.4 4.6 %copy-start.7 = (bf16[512,1024]{0,1:T(8,128)(2,1)S(1)}, bf16[512,1024]{0,1:T(8,128)(2,1)}, u32[]{:S(2)}) copy-start(bf16[512,1024]{0,1:T(8,128)(2,1)} %fusion.25) | copy-start | bytes 3145732
  248.4 9.5 %collective-permute-start.14 = (bf16[1024,256]{1,0:T(8,128)(2,1)}, bf16[1024,256]{1,0:T(8,128)(2,1)}, u32[]{:S(2)}, u32[]{:S(2)}) collective-permute-start(bf16[1024,256]{1,0:T(8,128)(2,1)} %get-tuple-element.115), channel_id=1, source_target_pairs={{0,8},{8,16},{16,24},{24,28},{28,20},{20,12},{12,4},{4,0},{1,9},{9... | collective-permute-start | bytes 1572872 | tf_op jit(solution)/shard_map/ppermute | solution.py:173
  250.3 9.5 %collective-permute-start.17 = (bf16[1024,256]{1,0:T(8,128)(2,1)}, bf16[1024,256]{1,0:T(8,128)(2,1)}, u32[]{:S(2)}, u32[]{:S(2)}) collective-permute-start(bf16[1024,256]{1,0:T(8,128)(2,1)} %get-tuple-element.116), channel_id=1, source_target_pairs={{8,0},{16,8},{24,16},{28,24},{20,28},{12,20},{4,12},{0,4},{9,1},{1... | collective-permute-start | bytes 1572872 | tf_op jit(solution)/shard_map/ppermute | solution.py:174
  251.7 2.6 copy-start.8
Sparse Core Ops, SparseCore 0:
  9.6 37.1 all-gather.1
  89.2 44.8 reduce-scatter.1

commit v3 on v2

--- a/solution.py
+++ b/solution.py
@@ -85,28 +85,33 @@
     seq_count = lax.axis_size("seq")
     grad_scale = (row_count * seq_count) ** (-0.5)
 
+    projected = []
+
     def project(state):
         gated_rows, out_weight = state
-        block_out = lax.psum_scatter(
-            jnp.dot(gated_rows, out_weight, preferred_element_type=jnp.float32).astype(jnp.bfloat16),
-            "tp",
-            scatter_dimension=0,
-            tiled=True,
-        )
-        return (block_out, out_weight)
-
-    def gate_back(state):
-        block_out, out_weight = state
+        projected.append(
+            lax.psum_scatter(
+                jnp.dot(gated_rows, out_weight, preferred_element_type=jnp.float32).astype(
+                    jnp.bfloat16
+                ),
+                "tp",
+                scatter_dimension=0,
+                tiled=True,
+            )
+        )
+        return out_weight
+
+    def gate_back(out_weight):
         grad_gated = lax.dot_general(
             full_cotangent, out_weight, (((1,), (1,)), ((), ())), preferred_element_type=jnp.float32
         )
         grad_conv = (grad_gated * query_feat).astype(jnp.bfloat16)
         grad_query = grad_gated * long_conv
         conv_after = passed_along(grad_conv[:tap_count], "seq", -1)
-        return (block_out, grad_conv, conv_after, grad_query)
+        return (grad_conv, conv_after, grad_query)
 
     def filter_back(state):
-        block_out, grad_conv, conv_after, grad_query = state
+        grad_conv, conv_after, grad_query = state
         grad_mix = band_mix(
             jnp.concatenate([grad_conv, conv_after], axis=0), band_table(filter_taps, reverse=True)
         )
@@ -116,10 +121,10 @@
             "seq",
             -1,
         )
-        return (block_out, grad_features, features_after)
+        return (grad_features, features_after)
 
     def feature_back(state):
-        block_out, grad_features, features_after = state
+        grad_features, features_after = state
         grads = tuple(
             spread_back(
                 jnp.concatenate([grad_features[i], features_after[i].astype(jnp.float32)], axis=0),
@@ -128,13 +133,13 @@
             ).astype(jnp.bfloat16)
             for i in range(3)
         )
-        return (block_out,) + grads
+        return grads
 
     stages = [project, gate_back, filter_back, feature_back]
     state, summed_grad = ring_reduce_scatter(
         gated_rows, full_cotangent, grad_scale, ring, stages, (gated_rows, out_weight)
     )
-    return state + (summed_grad,)
+    return (projected[0],) + state + (summed_grad,)
 
 
 def ring_reduce_scatter(gated_rows, full_cotangent, grad_scale, ring, stages, state):

time: 274 us -> 236 us (0.86); the launches traced: 270 us -> 235 us
  waiting for transfers between devices: 65 us -> 41.2 us
  other arithmetic: 65 us -> 57.7 us
  matrix products: 40.6 us -> 37.5 us
    reduce_scatter x1, waiting for transfers between devices: 30.3 us -> 0.01 us  [project(): lax.psum_scatter(jnp.dot(gated_rows, out_weight, preferred_element_type=j...]
    convert_element_type x3, other arithmetic: 28 us -> 20.5 us  [feature_back(): grads = tuple((spread_back(jnp.concatenate([grad_features[i], features_af...]
    ppermute x7, waiting for transfers between devices: 25.8 us -> 32.8 us  [ring_reduce_scatter(): ahead = lax.ppermute(sent_ahead, 'seq', forward)]
    ppermute x7, starting transfers between devices: 14.1 us -> 7.28 us  [ring_reduce_scatter(): ahead = lax.ppermute(sent_ahead, 'seq', forward)]
    ppermute x7, starting transfers between devices: 1.77 us -> 7.99 us  [ring_reduce_scatter(): behind = lax.ppermute(sent_behind, 'seq', backward)]
    ppermute x7, waiting for transfers between devices: 6.04 us -> 1.36 us  [ring_reduce_scatter(): behind = lax.ppermute(sent_behind, 'seq', backward)]
    ppermute x4, waiting for transfers between devices: 2.07 us -> 6.35 us  [passed_along(): lax.ppermute(value, axis, [(source, source + steps) for source in range(l...]
    dot_general x1, matrix products: 9.75 us -> 6.19 us  [project(): jnp.dot(gated_rows, out_weight, preferred_element_type=jnp.float32)]
  transfers between devices with their start and end apart: 20 -> 20, of which waited for: 10 -> 9; matrix products, arithmetic and copies ran while one was open for 36% -> 43% of each run, Pallas kernels for 0% -> 0%
where the time goes in v3:
time: 236 us; the launch traced here: 235 us
  other arithmetic  57.7 us (24%)
  waiting for transfers between devices  41.2 us (17%)
  matrix products  37.5 us (16%)
  local copies, waits for them, and re-layouts  37 us (16%)
  between operations  35.3 us (15%)
  starting transfers between devices  26.4 us (11%)
    ppermute x7, waiting for transfers between devices, ring_reduce_scatter(): ahead = lax.ppermute(sent_ahead, 'seq', forward)  32.8 us
    unnamed x53, local copies, waits for them, and re-layouts  24.6 us
    convert_element_type x3, other arithmetic, feature_back(): grads = tuple((spread_back(jnp.concatenate([grad_features[i], features_af...  20.5 us
    ppermute x4, starting transfers between devices, passed_along(): lax.ppermute(value, axis, [(source, source + steps) for source in range(l...  11.1 us
    dot_general x1, matrix products, gate_back(): lax.dot_general(full_cotangent, out_weight, (((1,), (1,)), ((), ())), pre...  10.6 us
    convert_element_type x1, other arithmetic, per_device(): mix_rows = (key_feat * value_feat).astype(jnp.bfloat16)  9.58 us
    convert_element_type x3, other arithmetic, ring_reduce_scatter(): sent_behind = behind.astype(jnp.bfloat16)  9.06 us
    convert_element_type x3, other arithmetic, ring_reduce_scatter(): sent_ahead = ahead.astype(jnp.bfloat16)  8.25 us
  transfers between devices with their start and end apart: 20, of which 9 were waited for; matrix products, arithmetic and copies ran while one was open for 43% of the time, Pallas kernels for 0%

profile of v3, /device:TPU:0, one launch (start us, length us, event | category | flops | bytes accessed | tf_op | source)
XLA Modules:
  0.0 235.2 jit_solution(11174327738825914619)
XLA Ops:
  9.5 4.9 %collective-permute-start = (bf16[3,6,1024]{2,1,0:T(8,128)(2,1)S(1)}, bf16[3,6,1024]{2,1,0:T(8,128)(2,1)S(1)}, u32[]{:S(2)}, u32[]{:S(2)}) collective-permute-start(bf16[3,6,1024]{2,1,0:T(8,128)(2,1)S(1)} %pad_maximum_fusion.7), channel_id=1, source_target_pairs={{0,4},{4,8},{8,12},{12,16},{16,20},{20,24},{24,28},{1,5},{5,9},{9,... | collective-permute-start | bytes 110600 | tf_op jit(solution)/shard_map/ppermute | solution.py:12
  15.2 1.3 fusion.94
  17.0 1.5 copy.41
  19.7 9.6 %multiply_convert_fusion = (bf16[512,1024]{0,1:T(8,128)(2,1)S(1)}, f32[512,1024]{0,1:T(8,128)}, f32[512,1024]{0,1:T(8,128)}) fusion(bf16[512,1024]{0,1:T(8,128)(2,1)S(1)} %copy.41, bf16[6,1024]{0,1:T(8,128)(2,1)} %bitcast.149, f32[1024]{0:T(1024)S(1)} %bitcast.176, f32[1024]{0:T(1024)S(1)} %bitcast.174, f32[1024]{0:T(1024)S(1)} %bitcast.164, ...), kind=kLoop, calls=%fused_computation.127 | loop fusion | flops 40894464 | bytes 7421952 | tf_op jit(solution)/shard_map/convert_element_type | solution.py:80
  29.3 3.6 %collective-permute-start.1 = (bf16[128,1024]{0,1:T(8,128)(2,1)S(1)}, bf16[128,1024]{0,1:T(8,128)(2,1)S(1)}, u32[]{:S(2)}, u32[]{:S(2)}) collective-permute-start(bf16[128,1024]{0,1:T(8,128)(2,1)S(1)} %slice.421), channel_id=1, source_target_pairs={{0,4},{4,8},{8,12},{12,16},{16,20},{20,24},{24,28},{1,5},{5,9},{9,... | collective-permute-start | bytes 786440 | tf_op jit(solution)/shard_map/ppermute | solution.py:12
  33.0 2.3 copy.35
  51.1 3.9 %fusion.2 = bf16[8,8,256,128]{3,1,2,0:T(8,128)(2,1)S(1)} fusion(bf16[64,128]{1,0:T(8,128)(2,1)S(1)} %copy-done, s32[32768]{0:T(1024)S(1)} %subtract_bitcast_fusion.1), kind=kOutput, calls=%fused_computation.53 | convolution fusion | flops 543162368 | bytes 4341760 | tf_op jit(solution)/shard_map/dot_general | solution.py:45
  55.0 3.2 %copy.56 = bf16[8,8,256,128]{3,2,1,0:T(8,128)(2,1)} copy(bf16[8,8,256,128]{3,1,2,0:T(8,128)(2,1)S(1)} %fusion.2) | data formatting | bytes 8388608
  60.0 2.4 %fusion.63 = f32[64,64,128]{2,1,0:T(8,128)S(1)} fusion(bf16[64,64,128]{2,1,0:T(8,128)(2,1)S(1)} %reshape.235, bf16[64,256,128]{2,1,0:T(8,128)(2,1)} %bitcast.142), kind=kOutput, calls=%fused_computation.121 | convolution fusion | flops 134217728 | bytes 5242880 | tf_op jit(solution)/shard_map/gmw,gwt->gmt/dot_general | solution.py:60
  64.1 4.6 %fusion.55 = (bf16[512,1024]{0,1:T(8,128)(2,1)S(1)}, f32[512,1024]{0,1:T(8,128)}) fusion(f32[128,8,4,128]{3,2,1,0:T(4,128)S(1)} %bitcast.145, bf16[512,1024]{0,1:T(8,128)(2,1)S(1)} %copy-done.9, bf16[6,1024]{0,1:T(8,128)(2,1)S(1)} %bitcast.147, f32[1024]{0:T(1024)S(1)} %bitcast.180, f32[1024]{0:T(1024)S(1)} %bitcast.182, f32[1024]{0:T(1024)S(1)} %bitcast.184, ...), kind=kLoop, calls=%fused_computation.110 | loop fusion | flops 20971520 | bytes 6332416 | tf_op jit(solution)/shard_map/convert_element_type | solution.py:84
  68.7 6.7 %convolution_multiply_fusion = f32[1024,4096]{1,0:T(8,128)S(1)} fusion(bf16[512,1024]{0,1:T(8,128)(2,1)S(1)} %get-tuple-element.42, bf16[512,4096]{1,0:T(8,128)(2,1)} %all-gather.2.cloned.1.call-done), kind=kOutput, calls=%fused_computation.4 | convolution fusion | flops 4299161600 | bytes 22020096 | tf_op jit(solution)/shard_map/dot_general | solution.py:157
  75.4 5.8 %copy-done.4 = f32[1024,4096]{1,0:T(8,128)} copy-done((f32[1024,4096]{1,0:T(8,128)}, f32[1024,4096]{1,0:T(8,128)S(1)}, u32[]{:S(2)}) %copy-start.4) | copy-done | bytes 16777240
  81.2 1.1 dynamic-slice_convert_fusion
  82.3 1.6 collective-permute-start.2
  84.4 3.9 %fusion.3 = bf16[8,8,256,128]{3,1,2,0:T(8,128)(2,1)S(1)} fusion(bf16[64,128]{1,0:T(8,128)(2,1)S(1)} %copy-done, s32[32768]{0:T(1024)S(1)} %subtract_bitcast_fusion), kind=kOutput, calls=%fused_computation.54 | convolution fusion | flops 543162368 | bytes 4341760 | tf_op jit(solution)/shard_map/dot_general | solution.py:45
  88.3 3.2 %copy.58 = bf16[8,8,256,128]{3,2,1,0:T(8,128)(2,1)} copy(bf16[8,8,256,128]{3,1,2,0:T(8,128)(2,1)S(1)} %fusion.3) | data formatting | bytes 8388608
  91.5 4.2 %collective-permute-done.2 = bf16[1024,256]{1,0:T(8,128)(2,1)S(1)} collective-permute-done((bf16[1024,256]{1,0:T(8,128)(2,1)}, bf16[1024,256]{1,0:T(8,128)(2,1)S(1)}, u32[]{:S(2)}, u32[]{:S(2)}) %collective-permute-start.2) | collective-permute-done | bytes 524320 | tf_op jit(solution)/shard_map/ppermute | solution.py:178
  95.7 1.3 collective-permute-done.3
  96.9 2.9 %add_convert_fusion.12 = (bf16[1024,256]{1,0:T(8,128)(2,1)}, bf16[1024,256]{1,0:T(8,128)(2,1)}) fusion(f32[1024,4096]{1,0:T(8,128)} %copy-done.4, s32[]{:T(128)S(6)} %select_n.178, bf16[1024,256]{1,0:T(8,128)(2,1)S(1)} %collective-permute-done.3, s32[]{:T(128)S(6)} %select_n.175, bf16[1024,256]{1,0:T(8,128)(2,1)S(1)} %collective-permute-done.2), kind=kLoop, calls=%fused_computation.181 | loop fusion | flops 1572864 | bytes 4194312 | tf_op jit(solution)/shard_map/convert_element_type | solution.py:173
  99.9 10.6 %bitcast_multiply_fusion.2 = (f32[512,1024]{0,1:T(8,128)}, bf16[512,1024]{0,1:T(8,128)(2,1)S(1)}) fusion(f32[128,8,4,128]{3,2,1,0:T(4,128)S(1)} %bitcast.146, f32[512,1024]{0,1:T(8,128)S(1)} %copy-done.11, bf16[1024,4096]{1,0:T(8,128)(2,1)} %param.14, bf16[512,4096]{1,0:T(8,128)(2,1)} %all-gather.2.cloned.1.call-done), kind=kOutput, calls=%fused_computation.108 | convolution fusion | flops 4296540160 | bytes 19922944 | tf_op jit(solution)/shard_map/dot_general | solution.py:105
  110.5 1.3 collective-permute-start.6
  111.8 2.6 %collective-permute-start.4 = (bf16[1024,256]{1,0:T(8,128)(2,1)}, bf16[1024,256]{1,0:T(8,128)(2,1)S(1)}, u32[]{:S(2)}, u32[]{:S(2)}) collective-permute-start(bf16[1024,256]{1,0:T(8,128)(2,1)} %get-tuple-element.49), channel_id=1, source_target_pairs={{0,8},{8,16},{16,24},{24,28},{28,20},{20,12},{12,4},{4,0},{1,9},{9... | collective-permute-start | bytes 1572872 | tf_op jit(solution)/shard_map/ppermute | solution.py:178
  114.8 6.2 %convolution_convert_fusion.2 = bf16[512,4096]{1,0:T(8,128)(2,1)} fusion(bf16[512,1024]{0,1:T(8,128)(2,1)S(1)} %copy-done.14, bf16[1024,4096]{1,0:T(8,128)(2,1)S(1)} %bitcast.193), kind=kOutput, calls=%fused_computation.22 | convolution fusion | flops 4297064448 | bytes 13631488 | tf_op jit(solution)/shard_map/dot_general | solution.py:94
  121.5 8.4 %collective-permute-done.4 = bf16[1024,256]{1,0:T(8,128)(2,1)S(1)} collective-permute-done((bf16[1024,256]{1,0:T(8,128)(2,1)}, bf16[1024,256]{1,0:T(8,128)(2,1)S(1)}, u32[]{:S(2)}, u32[]{:S(2)}) %collective-permute-start.4) | collective-permute-done | bytes 524320 | tf_op jit(solution)/shard_map/ppermute | solution.py:178
  129.9 3.1 %add_convert_fusion.10 = (bf16[1024,256]{1,0:T(8,128)(2,1)}, bf16[1024,256]{1,0:T(8,128)(2,1)}) fusion(f32[1024,4096]{1,0:T(8,128)} %copy-done.4, s32[]{:T(128)S(6)} %select_n.184, bf16[1024,256]{1,0:T(8,128)(2,1)S(1)} %collective-permute-done.5, s32[]{:T(128)S(6)} %select_n.181, bf16[1024,256]{1,0:T(8,128)(2,1)S(1)} %collective-permute-done.4), kind=kLoop, calls=%fused_computation.179 | loop fusion | flops 1572864 | bytes 4194312 | tf_op jit(solution)/shard_map/convert_element_type | solution.py:173
  134.7 2.4 %fusion.59 = f32[64,64,128]{2,1,0:T(8,128)S(1)} fusion(bf16[64,64,128]{2,1,0:T(8,128)(2,1)S(1)} %reshape.240, bf16[64,256,128]{2,1,0:T(8,128)(2,1)} %bitcast.140), kind=kOutput, calls=%fused_computation.117 | convolution fusion | flops 134217728 | bytes 5242880 | tf_op jit(solution)/shard_map/gmw,gwt->gmt/dot_general | solution.py:60
  139.8 2.1 bitcast_multiply_fusion
  142.1 1.7 collective-permute-start.7
  146.6 1.3 collective-permute-start.9
  150.5 5.8 %collective-permute-done.9 = bf16[3,6,1024]{2,1,0:T(8,128)(2,1)S(1)} collective-permute-done((bf16[3,6,1024]{2,1,0:T(8,128)(2,1)S(1)}, bf16[3,6,1024]{2,1,0:T(8,128)(2,1)S(1)}, u32[]{:S(2)}, u32[]{:S(2)}) %collective-permute-start.9) | collective-permute-done | bytes 36896 | tf_op jit(solution)/shard_map/ppermute | solution.py:12
  156.4 3.0 %add_convert_fusion.8 = (bf16[1024,256]{1,0:T(8,128)(2,1)}, bf16[1024,256]{1,0:T(8,128)(2,1)}) fusion(f32[1024,4096]{1,0:T(8,128)} %copy-done.4, s32[]{:T(128)S(6)} %select_n.190, bf16[1024,256]{1,0:T(8,128)(2,1)} %collective-permute-done.8, s32[]{:T(128)S(6)} %select_n.187, bf16[1024,256]{1,0:T(8,128)(2,1)} %collective-permute-done.7), kind=kLoop, calls=%fused_computation.177 | loop fusion | flops 1572864 | bytes 4194312 | tf_op jit(solution)/shard_map/convert_element_type | solution.py:173
  160.4 1.7 collective-permute-start.11
  162.3 6.6 %fusion.8 = bf16[512,1024]{0,1:T(8,128)(2,1)S(1)} fusion(f32[512,1024]{0,1:T(8,128)S(1)} %copy-done.5, f32[6,1024]{0,1:T(8,128)S(1)} %bitcast_convert_fusion, f32[1024]{0:T(1024)S(1)} %bitcast.177, f32[1024]{0:T(1024)S(1)} %bitcast.175, f32[1024]{0:T(1024)S(1)} %bitcast.165, f32[1024]{0:T(1024)S(1)} %bitcast.167, f32[1024]{0:T(1024)S(1)} %bitcast.169, ...), kind=kLoop, calls=%fused_computation.59 | loop fusion | flops 10485760 | bytes 3198976 | tf_op jit(solution)/shard_map/convert_element_type | solution.py:133
  168.9 7.3 %fusion.25 = bf16[512,1024]{0,1:T(8,128)(2,1)} fusion(f32[512,1024]{0,1:T(8,128)S(1)} %get-tuple-element.72, f32[6,1024]{0,1:T(8,128)S(1)} %bitcast_convert_fusion.1, f32[1024]{0:T(1024)S(1)} %bitcast.151, f32[1024]{0:T(1024)S(1)} %bitcast.153, f32[1024]{0:T(1024)S(1)} %bitcast.155, f32[1024]{0:T(1024)S(1)} %bitcast.157, f32[1024]{0:T(1024)S(1)} %bitcast.159, ...), kind=kLoop, calls=%fused_computation.76 | loop fusion | flops 10485760 | bytes 3198976 | tf_op jit(solution)/shard_map/convert_element_type | solution.py:133
  176.2 6.6 %fusion.42 = bf16[512,1024]{0,1:T(8,128)(2,1)S(1)} fusion(f32[512,1024]{0,1:T(8,128)S(1)} %copy-done.10, f32[6,1024]{0,1:T(8,128)S(1)} %bitcast_convert_fusion.2, f32[1024]{0:T(1024)S(1)} %bitcast.181, f32[1024]{0:T(1024)S(1)} %bitcast.183, f32[1024]{0:T(1024)S(1)} %bitcast.185, f32[1024]{0:T(1024)S(1)} %bitcast.187, f32[1024]{0:T(1024)S(1)} %bitcast.189, ...), kind=kLoop, calls=%fused_computation.93 | loop fusion | flops 10485760 | bytes 3198976 | tf_op jit(solution)/shard_map/convert_element_type | solution.py:133
  182.8 2.6 %add_convert_fusion.7 = (bf16[1024,256]{1,0:T(8,128)(2,1)}, bf16[1024,256]{1,0:T(8,128)(2,1)S(1)}) fusion(f32[1024,4096]{1,0:T(8,128)} %copy-done.4, s32[]{:T(128)S(6)} %select_n.193, bf16[1024,256]{1,0:T(8,128)(2,1)S(1)} %collective-permute-done.10, s32[]{:T(128)S(6)} %select_n.205, bf16[1024,256]{1,0:T(8,128)(2,1)S(1)} %collective-permute-done.11), kind=kLoop, calls=%fused_computation.176 | loop fusion | flops 1572864 | bytes 4194312 | tf_op jit(solution)/shard_map/convert_element_type | solution.py:172
  185.8 1.7 collective-permute-start.15
  188.8 8.7 %collective-permute-done.12 = bf16[1024,256]{1,0:T(8,128)(2,1)S(1)} collective-permute-done((bf16[1024,256]{1,0:T(8,128)(2,1)}, bf16[1024,256]{1,0:T(8,128)(2,1)S(1)}, u32[]{:S(2)}, u32[]{:S(2)}) %collective-permute-start.12) | collective-permute-done | bytes 524320 | tf_op jit(solution)/shard_map/ppermute | solution.py:178
  197.5 2.7 %add_convert_fusion.6 = (bf16[1024,256]{1,0:T(8,128)(2,1)}, bf16[1024,256]{1,0:T(8,128)(2,1)S(1)}) fusion(f32[1024,4096]{1,0:T(8,128)} %copy-done.4, s32[]{:T(128)S(6)} %select_n.196, bf16[1024,256]{1,0:T(8,128)(2,1)S(1)} %collective-permute-done.12, s32[]{:T(128)S(6)} %select_n.208, bf16[1024,256]{1,0:T(8,128)(2,1)} %collective-permute-done.15), kind=kLoop, calls=%fused_computation.175 | loop fusion | flops 1572864 | bytes 4194312 | tf_op jit(solution)/shard_map/convert_element_type | solution.py:172
  200.6 1.7 collective-permute-start.16
  203.4 8.1 %collective-permute-done.13 = bf16[1024,256]{1,0:T(8,128)(2,1)S(1)} collective-permute-done((bf16[1024,256]{1,0:T(8,128)(2,1)}, bf16[1024,256]{1,0:T(8,128)(2,1)S(1)}, u32[]{:S(2)}, u32[]{:S(2)}) %collective-permute-start.13) | collective-permute-done | bytes 524320 | tf_op jit(solution)/shard_map/ppermute | solution.py:178
  211.5 2.9 %add_convert_fusion.5 = (bf16[1024,256]{1,0:T(8,128)(2,1)}, bf16[1024,256]{1,0:T(8,128)(2,1)}) fusion(f32[1024,4096]{1,0:T(8,128)} %copy-done.4, s32[]{:T(128)S(6)} %select_n.199, bf16[1024,256]{1,0:T(8,128)(2,1)S(1)} %collective-permute-done.13, s32[]{:T(128)S(6)} %select_n.211, bf16[1024,256]{1,0:T(8,128)(2,1)} %collective-permute-done.16), kind=kLoop, calls=%fused_computation.174 | loop fusion | flops 1572864 | bytes 4194312 | tf_op jit(solution)/shard_map/convert_element_type | solution.py:172
  214.8 1.7 collective-permute-start.17
  217.7 1.3 copy.50
  219.0 1.3 copy.51
  220.4 1.3 copy.52
  221.7 3.4 %collective-permute-done.14 = bf16[1024,256]{1,0:T(8,128)(2,1)} collective-permute-done((bf16[1024,256]{1,0:T(8,128)(2,1)}, bf16[1024,256]{1,0:T(8,128)(2,1)}, u32[]{:S(2)}, u32[]{:S(2)}) %collective-permute-start.14) | collective-permute-done | bytes 524320 | tf_op jit(solution)/shard_map/ppermute | solution.py:178
  225.2 2.1 add_convert_fusion.4
  (107 shorter events, 21.7 us)
Async XLA Ops:
  7.2 43.9 %copy-start = (bf16[64,128]{1,0:T(8,128)(2,1)S(1)}, bf16[64,128]{1,0:T(8,128)(2,1)}, u32[]{:S(2)}) copy-start(bf16[64,128]{1,0:T(8,128)(2,1)} %param.13) | copy-start | bytes 49156
  7.2 9.3 %copy-start.12 = (bf16[512,1024]{1,0:T(8,128)(2,1)S(1)}, bf16[512,1024]{1,0:T(8,128)(2,1)}, u32[]{:S(2)}) copy-start(bf16[512,1024]{1,0:T(8,128)(2,1)} %param.10) | copy-start | bytes 3145732
  7.2 61.5 %all-gather.2.cloned.1.call-start = ((), (), s32[]{:S(2)}) async-start(), calls=%async_computation.1 | async-start | bytes 5242880 | tf_op jit(solution)/shard_map/all_gather | solution.py:71
  7.9 220.4 %reduce-scatter.2.cloned.1.call-start = ((), (), s32[]{:S(2)}) async-start(), calls=%async_computation.2 | async-start | bytes 5242880 | tf_op jit(solution)/shard_map/reduce_scatter | solution.py:93
  9.5 9.1 %collective-permute-start = (bf16[3,6,1024]{2,1,0:T(8,128)(2,1)S(1)}, bf16[3,6,1024]{2,1,0:T(8,128)(2,1)S(1)}, u32[]{:S(2)}, u32[]{:S(2)}) collective-permute-start(bf16[3,6,1024]{2,1,0:T(8,128)(2,1)S(1)} %pad_maximum_fusion.7), channel_id=1, source_target_pairs={{0,4},{4,8},{8,12},{12,16},{16,20},{20,24},{24,28},{1,5},{5,9},{9,... | collective-permute-start | bytes 110600 | tf_op jit(solution)/shard_map/ppermute | solution.py:12
  29.3 6.0 %copy-start.18 = (s32[8]{0:T(128)S(1)}, s32[8]{0:T(128)}, u32[]{:S(2)}) copy-start(s32[8]{0:T(128)} %constant.198.clone) | copy-start | bytes 100
  29.3 17.2 %copy-start.17 = (s32[8]{0:T(128)S(1)}, s32[8]{0:T(128)}, u32[]{:S(2)}) copy-start(s32[8]{0:T(128)} %constant.199.clone) | copy-start | bytes 100
  29.3 29.0 %collective-permute-start.1 = (bf16[128,1024]{0,1:T(8,128)(2,1)S(1)}, bf16[128,1024]{0,1:T(8,128)(2,1)S(1)}, u32[]{:S(2)}, u32[]{:S(2)}) collective-permute-start(bf16[128,1024]{0,1:T(8,128)(2,1)S(1)} %slice.421), channel_id=1, source_target_pairs={{0,4},{4,8},{8,12},{12,16},{16,20},{20,24},{24,28},{1,5},{5,9},{9,... | collective-permute-start | bytes 786440 | tf_op jit(solution)/shard_map/ppermute | solution.py:12
  60.0 2.8 %copy-start.3 = (bf16[8,8,256,128]{3,2,1,0:T(8,128)(2,1)S(1)}, bf16[8,8,256,128]{3,2,1,0:T(8,128)(2,1)}, u32[]{:S(2)}) copy-start(bf16[8,8,256,128]{3,2,1,0:T(8,128)(2,1)} %copy.56) | copy-start | bytes 12582916
  62.9 1.2 copy-start.9
  68.7 6.7 %copy-start.13 = (bf16[512,1024]{0,1:T(8,128)(2,1)}, bf16[512,1024]{0,1:T(8,128)(2,1)S(1)}, u32[]{:S(2)}) copy-start(bf16[512,1024]{0,1:T(8,128)(2,1)S(1)} %get-tuple-element.42) | copy-start | bytes 3145732
  75.4 5.8 %copy-start.4 = (f32[1024,4096]{1,0:T(8,128)}, f32[1024,4096]{1,0:T(8,128)S(1)}, u32[]{:S(2)}) copy-start(f32[1024,4096]{1,0:T(8,128)S(1)} %convolution_multiply_fusion) | copy-start | bytes 50331652
  82.3 13.3 %collective-permute-start.2 = (bf16[1024,256]{1,0:T(8,128)(2,1)}, bf16[1024,256]{1,0:T(8,128)(2,1)S(1)}, u32[]{:S(2)}, u32[]{:S(2)}) collective-permute-start(bf16[1024,256]{1,0:T(8,128)(2,1)} %get-tuple-element.44), channel_id=1, source_target_pairs={{0,8},{8,16},{16,24},{24,28},{28,20},{20,12},{12,4},{4,0},{1,9},{9... | collective-permute-start | bytes 1572872 | tf_op jit(solution)/shard_map/ppermute | solution.py:178
  83.9 13.0 %collective-permute-start.3 = (bf16[1024,256]{1,0:T(8,128)(2,1)}, bf16[1024,256]{1,0:T(8,128)(2,1)S(1)}, u32[]{:S(2)}, u32[]{:S(2)}) collective-permute-start(bf16[1024,256]{1,0:T(8,128)(2,1)} %get-tuple-element.45), channel_id=1, source_target_pairs={{8,0},{16,8},{24,16},{28,24},{20,28},{12,20},{4,12},{0,4},{9,1},{1... | collective-permute-start | bytes 1572872 | tf_op jit(solution)/shard_map/ppermute | solution.py:179
  91.5 8.4 %copy-start.11 = (f32[512,1024]{0,1:T(8,128)S(1)}, f32[512,1024]{0,1:T(8,128)}, u32[]{:S(2)}) copy-start(f32[512,1024]{0,1:T(8,128)} %get-tuple-element.95) | copy-start | bytes 6291460
  96.9 17.8 %slice-start = ((s8[8388608]{0:T(1024)(128)(4,1)}), s8[4194304]{0:T(1024)(128)(4,1)S(1)}, s32[]{:S(2)}) async-start(s8[8388608]{0:T(1024)(128)(4,1)} %bitcast.192), calls=%async_computation.3 | async-start | bytes 8388608
  99.9 14.9 %copy-start.14 = (bf16[512,1024]{0,1:T(8,128)(2,1)S(1)}, bf16[512,1024]{0,1:T(8,128)(2,1)}, u32[]{:S(2)}) copy-start(bf16[512,1024]{0,1:T(8,128)(2,1)} %copy-done.13) | copy-start | bytes 3145732
  99.9 14.9 %slice-start.1 = ((s8[8388608]{0:T(1024)(128)(4,1)}), s8[4194304]{0:T(1024)(128)(4,1)S(1)}, s32[]{:S(2)}) async-start(s8[8388608]{0:T(1024)(128)(4,1)} %bitcast.192), calls=%async_computation.4 | async-start | bytes 8388608
  110.5 11.1 %collective-permute-start.6 = (bf16[128,1024]{0,1:T(8,128)(2,1)S(1)}, bf16[128,1024]{0,1:T(8,128)(2,1)S(1)}, u32[]{:S(2)}, u32[]{:S(2)}) collective-permute-start(bf16[128,1024]{0,1:T(8,128)(2,1)S(1)} %slice.426), channel_id=1, source_target_pairs={{4,0},{8,4},{12,8},{16,12},{20,16},{24,20},{28,24},{5,1},{9,5},{13... | collective-permute-start | bytes 786440 | tf_op jit(solution)/shard_map/ppermute | solution.py:12
  111.8 18.2 %collective-permute-start.4 = (bf16[1024,256]{1,0:T(8,128)(2,1)}, bf16[1024,256]{1,0:T(8,128)(2,1)S(1)}, u32[]{:S(2)}, u32[]{:S(2)}) collective-permute-start(bf16[1024,256]{1,0:T(8,128)(2,1)} %get-tuple-element.49), channel_id=1, source_target_pairs={{0,8},{8,16},{16,24},{24,28},{28,20},{20,12},{12,4},{4,0},{1,9},{9... | collective-permute-start | bytes 1572872 | tf_op jit(solution)/shard_map/ppermute | solution.py:178
  114.4 15.6 %collective-permute-start.5 = (bf16[1024,256]{1,0:T(8,128)(2,1)}, bf16[1024,256]{1,0:T(8,128)(2,1)S(1)}, u32[]{:S(2)}, u32[]{:S(2)}) collective-permute-start(bf16[1024,256]{1,0:T(8,128)(2,1)} %get-tuple-element.50), channel_id=1, source_target_pairs={{8,0},{16,8},{24,16},{28,24},{20,28},{12,20},{4,12},{0,4},{9,1},{1... | collective-permute-start | bytes 1572872 | tf_op jit(solution)/shard_map/ppermute | solution.py:179
  134.7 2.8 %copy-start.2 = (bf16[8,8,256,128]{3,2,1,0:T(8,128)(2,1)S(1)}, bf16[8,8,256,128]{3,2,1,0:T(8,128)(2,1)}, u32[]{:S(2)}) copy-start(bf16[8,8,256,128]{3,2,1,0:T(8,128)(2,1)} %copy.58) | copy-start | bytes 12582916
  137.5 1.6 copy-start.6
  137.5 2.2 copy-start.7
  139.8 2.3 copy-start.16
  139.8 4.0 %copy-start.15 = (bf16[1024,256]{1,0:T(8,128)(2,1)S(1)}, bf16[1024,256]{1,0:T(8,128)(2,1)}, u32[]{:S(2)}) copy-start(bf16[1024,256]{1,0:T(8,128)(2,1)} %get-tuple-element.58) | copy-start | bytes 1572868
  142.1 14.3 %collective-permute-start.7 = (bf16[1024,256]{1,0:T(8,128)(2,1)S(1)}, bf16[1024,256]{1,0:T(8,128)(2,1)}, u32[]{:S(2)}, u32[]{:S(2)}) collective-permute-start(bf16[1024,256]{1,0:T(8,128)(2,1)S(1)} %copy-done.16), channel_id=1, source_target_pairs={{0,8},{8,16},{16,24},{24,28},{28,20},{20,12},{12,4},{4,0},{1,9},{9... | collective-permute-start | bytes 1572872 | tf_op jit(solution)/shard_map/ppermute | solution.py:178
  143.8 12.6 %collective-permute-start.8 = (bf16[1024,256]{1,0:T(8,128)(2,1)S(1)}, bf16[1024,256]{1,0:T(8,128)(2,1)}, u32[]{:S(2)}, u32[]{:S(2)}) collective-permute-start(bf16[1024,256]{1,0:T(8,128)(2,1)S(1)} %copy-done.15), channel_id=1, source_target_pairs={{8,0},{16,8},{24,16},{28,24},{20,28},{12,20},{4,12},{0,4},{9,1},{1... | collective-permute-start | bytes 1572872 | tf_op jit(solution)/shard_map/ppermute | solution.py:179
  146.6 9.7 %collective-permute-start.9 = (bf16[3,6,1024]{2,1,0:T(8,128)(2,1)S(1)}, bf16[3,6,1024]{2,1,0:T(8,128)(2,1)S(1)}, u32[]{:S(2)}, u32[]{:S(2)}) collective-permute-start(bf16[3,6,1024]{2,1,0:T(8,128)(2,1)S(1)} %pad_maximum_fusion.8), channel_id=1, source_target_pairs={{4,0},{8,4},{12,8},{16,12},{20,16},{24,20},{28,24},{5,1},{9,5},{13... | collective-permute-start | bytes 110600 | tf_op jit(solution)/shard_map/ppermute | solution.py:12
  160.0 2.2 copy-start.5
  160.1 22.8 %collective-permute-start.10 = (bf16[1024,256]{1,0:T(8,128)(2,1)}, bf16[1024,256]{1,0:T(8,128)(2,1)S(1)}, u32[]{:S(2)}, u32[]{:S(2)}) collective-permute-start(bf16[1024,256]{1,0:T(8,128)(2,1)} %get-tuple-element.68), channel_id=1, source_target_pairs={{0,8},{8,16},{16,24},{24,28},{28,20},{20,12},{12,4},{4,0},{1,9},{9... | collective-permute-start | bytes 1572872 | tf_op jit(solution)/shard_map/ppermute | solution.py:178
  160.4 22.4 %collective-permute-start.11 = (bf16[1024,256]{1,0:T(8,128)(2,1)}, bf16[1024,256]{1,0:T(8,128)(2,1)S(1)}, u32[]{:S(2)}, u32[]{:S(2)}) collective-permute-start(bf16[1024,256]{1,0:T(8,128)(2,1)} %get-tuple-element.69), channel_id=1, source_target_pairs={{8,0},{16,8},{24,16},{28,24},{20,28},{12,20},{4,12},{0,4},{9,1},{1... | collective-permute-start | bytes 1572872 | tf_op jit(solution)/shard_map/ppermute | solution.py:179
  168.9 7.3 %copy-start.10 = (f32[512,1024]{0,1:T(8,128)S(1)}, f32[512,1024]{0,1:T(8,128)}, u32[]{:S(2)}) copy-start(f32[512,1024]{0,1:T(8,128)} %get-tuple-element.70) | copy-start | bytes 6291460
  185.5 12.0 %collective-permute-start.12 = (bf16[1024,256]{1,0:T(8,128)(2,1)}, bf16[1024,256]{1,0:T(8,128)(2,1)S(1)}, u32[]{:S(2)}, u32[]{:S(2)}) collective-permute-start(bf16[1024,256]{1,0:T(8,128)(2,1)} %get-tuple-element.105), channel_id=1, source_target_pairs={{0,8},{8,16},{16,24},{24,28},{28,20},{20,12},{12,4},{4,0},{1,9},{9... | collective-permute-start | bytes 1572872 | tf_op jit(solution)/shard_map/ppermute | solution.py:178
  185.8 11.7 %collective-permute-start.15 = (bf16[1024,256]{1,0:T(8,128)(2,1)S(1)}, bf16[1024,256]{1,0:T(8,128)(2,1)}, u32[]{:S(2)}, u32[]{:S(2)}) collective-permute-start(bf16[1024,256]{1,0:T(8,128)(2,1)S(1)} %get-tuple-element.106), channel_id=1, source_target_pairs={{8,0},{16,8},{24,16},{28,24},{20,28},{12,20},{4,12},{0,4},{9,1},{1... | collective-permute-start | bytes 1572872 | tf_op jit(solution)/shard_map/ppermute | solution.py:179
  200.2 11.3 %collective-permute-start.13 = (bf16[1024,256]{1,0:T(8,128)(2,1)}, bf16[1024,256]{1,0:T(8,128)(2,1)S(1)}, u32[]{:S(2)}, u32[]{:S(2)}) collective-permute-start(bf16[1024,256]{1,0:T(8,128)(2,1)} %get-tuple-element.103), channel_id=1, source_target_pairs={{0,8},{8,16},{16,24},{24,28},{28,20},{20,12},{12,4},{4,0},{1,9},{9... | collective-permute-start | bytes 1572872 | tf_op jit(solution)/shard_map/ppermute | solution.py:178
  200.6 11.0 %collective-permute-start.16 = (bf16[1024,256]{1,0:T(8,128)(2,1)S(1)}, bf16[1024,256]{1,0:T(8,128)(2,1)}, u32[]{:S(2)}, u32[]{:S(2)}) collective-permute-start(bf16[1024,256]{1,0:T(8,128)(2,1)S(1)} %get-tuple-element.104), channel_id=1, source_target_pairs={{8,0},{16,8},{24,16},{28,24},{20,28},{12,20},{4,12},{0,4},{9,1},{1... | collective-permute-start | bytes 1572872 | tf_op jit(solution)/shard_map/ppermute | solution.py:179
  214.4 4.6 %copy-start.8 = (bf16[512,1024]{0,1:T(8,128)(2,1)S(1)}, bf16[512,1024]{0,1:T(8,128)(2,1)}, u32[]{:S(2)}) copy-start(bf16[512,1024]{0,1:T(8,128)(2,1)} %fusion.25) | copy-start | bytes 3145732
  214.4 10.7 %collective-permute-start.14 = (bf16[1024,256]{1,0:T(8,128)(2,1)}, bf16[1024,256]{1,0:T(8,128)(2,1)}, u32[]{:S(2)}, u32[]{:S(2)}) collective-permute-start(bf16[1024,256]{1,0:T(8,128)(2,1)} %get-tuple-element.101), channel_id=1, source_target_pairs={{0,8},{8,16},{16,24},{24,28},{28,20},{20,12},{12,4},{4,0},{1,9},{9... | collective-permute-start | bytes 1572872 | tf_op jit(solution)/shard_map/ppermute | solution.py:178
  214.8 10.4 %collective-permute-start.17 = (bf16[1024,256]{1,0:T(8,128)(2,1)}, bf16[1024,256]{1,0:T(8,128)(2,1)}, u32[]{:S(2)}, u32[]{:S(2)}) collective-permute-start(bf16[1024,256]{1,0:T(8,128)(2,1)} %get-tuple-element.102), channel_id=1, source_target_pairs={{8,0},{16,8},{24,16},{28,24},{20,28},{12,20},{4,12},{0,4},{9,1},{1... | collective-permute-start | bytes 1572872 | tf_op jit(solution)/shard_map/ppermute | solution.py:179
  225.2 3.2 %copy-start.1 = (bf16[64,128]{1,0:T(8,128)(2,1)S(1)}, bf16[64,128]{1,0:T(8,128)(2,1)}, u32[]{:S(2)}) copy-start(bf16[64,128]{1,0:T(8,128)(2,1)} %param.13) | copy-start | bytes 49156
Sparse Core Ops, SparseCore 0:
  9.6 37.1 all-gather.1
  121.1 44.8 reduce-scatter.1

commit v4 on v3

--- a/solution.py
+++ b/solution.py
@@ -3,6 +3,7 @@
 import jax
 import jax.numpy as jnp
 from jax import lax
+from jax.experimental import pallas as pl
 from jax.sharding import PartitionSpec as P
 
 
@@ -35,33 +36,47 @@
     tap_count = filter_taps.shape[1]
     window_rows = 2 * tap_count
     lag_index = jnp.arange(tap_count)[:, None, None]
-    row_index = jnp.arange(window_rows)[None, :, None]
-    col_index = jnp.arange(tap_count)[None, None, :]
+    out_index = jnp.arange(tap_count)[None, :, None]
+    row_index = jnp.arange(window_rows)[None, None, :]
     if reverse:
-        select = (row_index - col_index == lag_index).astype(jnp.bfloat16)
+        select = (row_index - out_index == lag_index).astype(jnp.bfloat16)
     else:
-        select = (col_index + tap_count - row_index == lag_index).astype(jnp.bfloat16)
-    select = select.reshape(tap_count, window_rows * tap_count)
-    toeplitz_table = jnp.dot(filter_taps, select, preferred_element_type=jnp.float32)
-    return toeplitz_table.astype(jnp.bfloat16).reshape(filter_taps.shape[0], window_rows, tap_count)
-
-
-def band_mix(padded_rows, toeplitz_table):
-    group_count, window_rows, tap_count = toeplitz_table.shape
+        select = (out_index + tap_count - row_index == lag_index).astype(jnp.bfloat16)
+    select = select.reshape(tap_count, tap_count * window_rows)
+    table = jnp.dot(filter_taps, select, preferred_element_type=jnp.float32)
+    return table.astype(jnp.bfloat16).reshape(filter_taps.shape[0], tap_count, window_rows)
+
+
+def band_mix(padded_rows, table, lane_tile=128):
+    group_count, tap_count, window_rows = table.shape
     row_count = padded_rows.shape[0] - tap_count
-    block_count = row_count // tap_count
     channels = padded_rows.shape[1]
     members = channels // group_count
-    by_channel = padded_rows.T
-    lower_half = by_channel[:, :row_count].reshape(group_count, members * block_count, tap_count)
-    upper_half = by_channel[:, tap_count:].reshape(group_count, members * block_count, tap_count)
-    mixed = jnp.einsum(
-        "gmw,gwt->gmt", lower_half, toeplitz_table[:, :tap_count], preferred_element_type=jnp.float32
-    ) + jnp.einsum(
-        "gmw,gwt->gmt", upper_half, toeplitz_table[:, tap_count:], preferred_element_type=jnp.float32
-    )
-    mixed = mixed.reshape(group_count, members, block_count, tap_count)
-    return mixed.transpose(2, 3, 0, 1).reshape(row_count, channels)
+    per_tile = lane_tile // members
+
+    def body(table_ref, lower_ref, upper_ref, out_ref):
+        lane_group = lax.broadcasted_iota(jnp.int32, (1, lane_tile), 1) // members
+        lower = lower_ref[...]
+        upper = upper_ref[...]
+        mixed = jnp.zeros((tap_count, lane_tile), jnp.float32)
+        for member in range(per_tile):
+            part = jnp.dot(table_ref[member, :, :tap_count], lower, preferred_element_type=jnp.float32)
+            part = part + jnp.dot(table_ref[member, :, tap_count:], upper, preferred_element_type=jnp.float32)
+            mixed = jnp.where(lane_group == member, part, mixed)
+        out_ref[...] = mixed
+
+    grid = (channels // lane_tile, row_count // tap_count)
+    return pl.pallas_call(
+        body,
+        grid=grid,
+        in_specs=[
+            pl.BlockSpec((per_tile, tap_count, window_rows), lambda j, n: (j, 0, 0)),
+            pl.BlockSpec((tap_count, lane_tile), lambda j, n: (n, j)),
+            pl.BlockSpec((tap_count, lane_tile), lambda j, n: (n + 1, j)),
+        ],
+        out_specs=pl.BlockSpec((tap_count, lane_tile), lambda j, n: (n, j)),
+        out_shape=jax.ShapeDtypeStruct((row_count, channels), jnp.float32),
+    )(table, padded_rows, padded_rows)
 
 
 def per_device(query_in, key_in, value_in, feature_taps, filter_taps, out_weight, cotangent, ring):
@@ -149,8 +164,8 @@
     place_of = [0] * count
     for place, member in enumerate(ring):
         place_of[member] = place
-    place = jnp.asarray(place_of, jnp.int32)[lax.axis_index("seq")]
-    members = jnp.asarray(ring, jnp.int32)
+    seq_index = lax.axis_index("seq")
+    place = sum(jnp.where(seq_index == member, place_of[member], 0) for member in range(count))
     forward = [(ring[i], ring[(i + 1) % count]) for i in range(count)]
     backward = [(ring[(i + 1) % count], ring[i]) for i in range(count)]
     local_grad = (
@@ -161,7 +176,8 @@
     )
 
     def contribution(step, direction):
-        owner = members[(place - direction * (1 + step)) % count]
+        position = (place - direction * (1 + step)) % count
+        owner = sum(jnp.where(position == i, ring[i], 0) for i in range(count))
         first = owner * width + (0 if direction == 1 else half)
         return lax.dynamic_slice_in_dim(local_grad, first, half, 1)
 

time: 236 us -> 222 us (0.941); the launches traced: 235 us -> 218 us
  Pallas kernels: 0 us -> 42.7 us
  between operations: 35.3 us -> 14.8 us
  local copies, waits for them, and re-layouts: 37 us -> 19.3 us
  other arithmetic: 57.7 us -> 44.1 us
  matrix products: 37.5 us -> 31.4 us
  waiting for transfers between devices: 41.2 us -> 36.9 us
    pallas_call x0 -> x2, Pallas kernels: none -> 42.7 us  [band_mix(): pl.pallas_call(body, grid=grid, in_specs=[pl.BlockSpec((per_tile, tap_cou...]
    convert_element_type x3, other arithmetic: 20.5 us -> 8.9 us  [feature_back(): grads = tuple((spread_back(jnp.concatenate([grad_features[i], features_af...]
    unnamed x53 -> x24, local copies, waits for them, and re-layouts: 24.6 us -> 13.5 us
    dot_general x6 -> x2, matrix products: 14.1 us -> 7.78 us  [band_table(): table = jnp.dot(filter_taps, select, preferred_element_type=jnp.float32)]
    convert_element_type x1, other arithmetic: 9.58 us -> 5 us  [per_device(): mix_rows = (key_feat * value_feat).astype(jnp.bfloat16)]
    ppermute x7, waiting for transfers between devices: 32.8 us -> 28.4 us  [ring_reduce_scatter(): ahead = lax.ppermute(sent_ahead, 'seq', forward)]
    ppermute x7, starting transfers between devices: 7.28 us -> 11.5 us  [ring_reduce_scatter(): ahead = lax.ppermute(sent_ahead, 'seq', forward)]
    dot_general x1, matrix products: 6.19 us -> 9.4 us  [project(): jnp.dot(gated_rows, out_weight, preferred_element_type=jnp.float32)]
  transfers between devices with their start and end apart: 20 -> 20, of which waited for: 9 -> 7; matrix products, arithmetic and copies ran while one was open for 43% -> 37% of each run, Pallas kernels for 0% -> 20%
where the time goes in v4:
time: 222 us; the launch traced here: 218 us
  other arithmetic  44.1 us (20%)
  Pallas kernels  42.7 us (19%)
  waiting for transfers between devices  36.9 us (17%)
  matrix products  31.4 us (14%)
  starting transfers between devices  28.7 us (13%)
  local copies, waits for them, and re-layouts  19.3 us (9%)
  between operations  14.8 us (7%)
    pallas_call x2, Pallas kernels, band_mix(): pl.pallas_call(body, grid=grid, in_specs=[pl.BlockSpec((per_tile, tap_cou...  42.7 us
    ppermute x7, waiting for transfers between devices, ring_reduce_scatter(): ahead = lax.ppermute(sent_ahead, 'seq', forward)  28.4 us
    unnamed x24, local copies, waits for them, and re-layouts  13.5 us
    ppermute x7, starting transfers between devices, ring_reduce_scatter(): ahead = lax.ppermute(sent_ahead, 'seq', forward)  11.5 us
    ppermute x4, starting transfers between devices, passed_along(): lax.ppermute(value, axis, [(source, source + steps) for source in range(l...  10.9 us
    dot_general x1, matrix products, project(): jnp.dot(gated_rows, out_weight, preferred_element_type=jnp.float32)  9.4 us
    convert_element_type x3, other arithmetic, feature_back(): grads = tuple((spread_back(jnp.concatenate([grad_features[i], features_af...  8.9 us
    convert_element_type x3, other arithmetic, ring_reduce_scatter(): sent_behind = behind.astype(jnp.bfloat16)  8.18 us
  transfers between devices with their start and end apart: 20, of which 7 were waited for; matrix products, arithmetic and copies ran while one was open for 37% of the time, Pallas kernels for 20%

profile of v4, /device:TPU:0, one launch (start us, length us, event | category | flops | bytes accessed | tf_op | source)
XLA Modules:
  0.0 218.0 jit_solution(11339845772222660920)
XLA Ops:
  9.5 4.9 %collective-permute-start = (bf16[3,6,1024]{2,1,0:T(8,128)(2,1)S(1)}, bf16[3,6,1024]{2,1,0:T(8,128)(2,1)S(1)}, u32[]{:S(2)}, u32[]{:S(2)}) collective-permute-start(bf16[3,6,1024]{2,1,0:T(8,128)(2,1)S(1)} %pad_maximum_fusion.9), channel_id=1, source_target_pairs={{0,4},{4,8},{8,12},{12,16},{16,20},{20,24},{24,28},{1,5},{5,9},{9,... | collective-permute-start | bytes 110600 | tf_op jit(solution)/shard_map/ppermute | solution.py:13
  14.6 1.4 fusion.77
  17.4 5.0 %multiply_convert_fusion.1 = (bf16[512,1024]{1,0:T(8,128)(2,1)S(1)}, f32[512,1024]{1,0:T(8,128)}, f32[512,1024]{1,0:T(8,128)}) fusion(bf16[512,1024]{1,0:T(8,128)(2,1)S(1)} %copy-done.7, bf16[6,1024]{1,0:T(8,128)(2,1)S(1)} %get-tuple-element.131, f32[1024]{0:T(1024)S(1)} %bitcast.107, f32[1024]{0:T(1024)S(1)} %bitcast.105, f32[1024]{0:T(1024)S(1)} %bitcast.95, ...), kind=kLoop, calls=%fused_computation.108 | loop fusion | flops 40894464 | bytes 7421952 | tf_op jit(solution)/shard_map/convert_element_type | solution.py:95
  22.4 3.5 %collective-permute-start.1 = (bf16[128,1024]{1,0:T(8,128)(2,1)S(1)}, bf16[128,1024]{1,0:T(8,128)(2,1)S(1)}, u32[]{:S(2)}, u32[]{:S(2)}) collective-permute-start(bf16[128,1024]{1,0:T(8,128)(2,1)S(1)} %slice.389), channel_id=1, source_target_pairs={{0,4},{4,8},{8,12},{12,16},{16,20},{20,24},{24,28},{1,5},{5,9},{9,... | collective-permute-start | bytes 786440 | tf_op jit(solution)/shard_map/ppermute | solution.py:13
  25.9 3.9 %convolution_convert_fusion.1 = bf16[32768,64]{0,1:T(8,128)(2,1)S(1)} fusion(bf16[64,128]{1,0:T(8,128)(2,1)S(1)} %copy-done, s32[32768]{0:T(1024)S(1)} %get-tuple-element.105), kind=kOutput, calls=%fused_computation.1 | convolution fusion | flops 543162368 | bytes 4341760 | tf_op jit(solution)/shard_map/dot_general | solution.py:46
  29.8 3.1 %copy.15 = bf16[8,8,128,256]{3,2,1,0:T(8,128)(2,1)} copy(bf16[8,8,128,256]{3,1,2,0:T(8,128)(2,1)S(1)} %bitcast.76) | data formatting | bytes 8388608
  32.9 1.2 pad_maximum_fusion.3.lower_ref.upper_ref
  34.1 21.4 %shard_map.110 = f32[512,1024]{1,0:T(8,128)} custom-call(bf16[64,128,256]{2,1,0:T(8,128)(2,1)} %bitcast.75, bf16[640,1024]{1,0:T(8,128)(2,1)} %pad_maximum_fusion.3.lower_ref.upper_ref, bf16[640,1024]{1,0:T(8,128)(2,1)} %pad_maximum_fusion.3.lower_ref.upper_ref), custom_call_target="tpu_custom_call" | custom-call | tf_op jit(solution)/shard_map/pallas_call | solution.py:69
  55.4 5.8 %multiply_convert_fusion = (bf16[512,1024]{1,0:T(8,128)(2,1)S(1)}, f32[512,1024]{1,0:T(8,128)S(1)}) fusion(f32[512,1024]{1,0:T(8,128)} %shard_map.110, bf16[512,1024]{1,0:T(8,128)(2,1)} %param.7, bf16[6,1024]{1,0:T(8,128)(2,1)S(1)} %get-tuple-element.130, f32[1024]{0:T(1024)S(1)} %bitcast.111, f32[1024]{0:T(1024)S(1)} %bitcast.113, f32[1024]{0:T(1024)S(1)} %bitcast.115, ...), kind=kLoop, calls=%fused_computation.107 | loop fusion | flops 20971520 | bytes 6332416 | tf_op jit(solution)/shard_map/convert_element_type | solution.py:99
  61.3 6.5 %convolution_multiply_fusion = f32[1024,4096]{1,0:T(8,128)S(1)} fusion(bf16[512,1024]{1,0:T(8,128)(2,1)S(1)} %get-tuple-element.42, bf16[512,4096]{1,0:T(8,128)(2,1)} %all-gather.2.cloned.1.call-done), kind=kOutput, calls=%fused_computation.4 | convolution fusion | flops 4299161600 | bytes 22020096 | tf_op jit(solution)/shard_map/dot_general | solution.py:172
  67.7 5.7 %copy-done.1 = f32[1024,4096]{1,0:T(8,128)} copy-done((f32[1024,4096]{1,0:T(8,128)}, f32[1024,4096]{1,0:T(8,128)S(1)}, u32[]{:S(2)}) %copy-start.1) | copy-done | bytes 16777240
  74.6 1.7 collective-permute-start.2
  76.6 9.4 %convolution_convert_fusion.2 = bf16[512,4096]{1,0:T(8,128)(2,1)} fusion(bf16[512,1024]{1,0:T(8,128)(2,1)S(1)} %get-tuple-element.42, bf16[1024,4096]{1,0:T(8,128)(2,1)} %param.12), kind=kOutput, calls=%fused_computation.7 | convolution fusion | flops 4297064448 | bytes 13631488 | tf_op jit(solution)/shard_map/dot_general | solution.py:109
  86.1 2.0 collective-permute-done.2
  88.0 1.3 collective-permute-done.3
  89.3 3.0 %add_convert_fusion.12 = (bf16[1024,256]{1,0:T(8,128)(2,1)}, bf16[1024,256]{1,0:T(8,128)(2,1)}) fusion(f32[1024,4096]{1,0:T(8,128)} %copy-done.1, s32[]{:T(128)S(6)} %select_n.533, bf16[1024,256]{1,0:T(8,128)(2,1)} %collective-permute-done.3, s32[]{:T(128)S(6)} %select_n.524, bf16[1024,256]{1,0:T(8,128)(2,1)} %collective-permute-done.2), kind=kLoop, calls=%fused_computation.154 | loop fusion | flops 1572864 | bytes 4194312 | tf_op jit(solution)/shard_map/convert_element_type | solution.py:189
  92.3 1.6 collective-permute-start.4
  94.4 7.8 %fusion.79 = f32[1024,512]{0,1:T(8,128)S(1)} fusion(bf16[1024,4096]{1,0:T(8,128)(2,1)} %param.12, bf16[512,4096]{1,0:T(8,128)(2,1)S(1)} %copy-done.6), kind=kOutput, calls=%fused_computation.182 | convolution fusion | flops 4294967296 | bytes 14680064 | tf_op jit(solution)/shard_map/dot_general | solution.py:120
  102.2 2.0 bitcast_multiply_fusion
  104.3 1.3 collective-permute-start.6
  105.6 3.9 %convolution_convert_fusion = bf16[32768,64]{0,1:T(8,128)(2,1)S(1)} fusion(bf16[64,128]{1,0:T(8,128)(2,1)S(1)} %copy-done, s32[32768]{0:T(1024)S(1)} %get-tuple-element.104), kind=kOutput, calls=%fused_computation | convolution fusion | flops 543162368 | bytes 4341760 | tf_op jit(solution)/shard_map/dot_general | solution.py:46
  109.5 3.1 %copy.17 = bf16[8,8,128,256]{3,2,1,0:T(8,128)(2,1)} copy(bf16[8,8,128,256]{3,1,2,0:T(8,128)(2,1)S(1)} %bitcast.77) | data formatting | bytes 8388608
  112.6 3.1 %add_convert_fusion.10 = (bf16[1024,256]{1,0:T(8,128)(2,1)}, bf16[1024,256]{1,0:T(8,128)(2,1)}) fusion(f32[1024,4096]{1,0:T(8,128)} %copy-done.1, s32[]{:T(128)S(6)} %select_n.551, bf16[1024,256]{1,0:T(8,128)(2,1)} %collective-permute-done.5, s32[]{:T(128)S(6)} %select_n.542, bf16[1024,256]{1,0:T(8,128)(2,1)} %collective-permute-done.4), kind=kLoop, calls=%fused_computation.152 | loop fusion | flops 1572864 | bytes 4194312 | tf_op jit(solution)/shard_map/convert_element_type | solution.py:189
  115.7 2.3 %collective-permute-start.7 = (bf16[1024,256]{1,0:T(8,128)(2,1)}, bf16[1024,256]{1,0:T(8,128)(2,1)}, u32[]{:S(2)}, u32[]{:S(2)}) collective-permute-start(bf16[1024,256]{1,0:T(8,128)(2,1)} %get-tuple-element.57), channel_id=1, source_target_pairs={{0,8},{8,16},{16,24},{24,28},{28,20},{20,12},{12,4},{4,0},{1,9},{9... | collective-permute-start | bytes 1572872 | tf_op jit(solution)/shard_map/ppermute | solution.py:194
  118.4 1.2 pad_maximum_fusion.4.lower_ref.upper_ref
  119.6 21.4 %shard_map.111 = f32[512,1024]{1,0:T(8,128)} custom-call(bf16[64,128,256]{2,1,0:T(8,128)(2,1)} %bitcast.74, bf16[640,1024]{1,0:T(8,128)(2,1)} %pad_maximum_fusion.4.lower_ref.upper_ref, bf16[640,1024]{1,0:T(8,128)(2,1)} %pad_maximum_fusion.4.lower_ref.upper_ref), custom_call_target="tpu_custom_call" | custom-call | tf_op jit(solution)/shard_map/pallas_call | solution.py:69
  140.9 3.5 %fusion.75 = (f32[512,1024]{1,0:T(8,128)S(1)}, f32[512,1024]{1,0:T(8,128)S(1)}) fusion(f32[512,1024]{1,0:T(8,128)} %shard_map.111, f32[512,1024]{1,0:T(8,128)} %get-tuple-element.83, f32[512,1024]{1,0:T(8,128)} %get-tuple-element.82), kind=kLoop, calls=%fused_computation.178 | loop fusion | flops 1048576 | bytes 10485760 | tf_op jit(solution)/shard_map/mul | solution.py:133
  144.5 1.3 copy-done.3
  146.6 1.3 collective-permute-start.9
  148.1 4.5 %collective-permute-done.9 = bf16[3,6,1024]{2,1,0:T(8,128)(2,1)S(1)} collective-permute-done((bf16[3,6,1024]{2,1,0:T(8,128)(2,1)S(1)}, bf16[3,6,1024]{2,1,0:T(8,128)(2,1)S(1)}, u32[]{:S(2)}, u32[]{:S(2)}) %collective-permute-start.9) | collective-permute-done | bytes 36896 | tf_op jit(solution)/shard_map/ppermute | solution.py:13
  152.6 2.1 add_convert_fusion.8
  154.7 1.7 collective-permute-start.10
  156.4 1.6 collective-permute-start.11
  158.0 3.0 %fusion.6 = bf16[512,1024]{1,0:T(8,128)(2,1)} fusion(f32[6,1024]{1,0:T(8,128)S(1)} %get-tuple-element.127, f32[512,1024]{1,0:T(8,128)S(1)} %copy-done.4, f32[1024]{0:T(1024)S(1)} %bitcast.108, f32[1024]{0:T(1024)S(1)} %bitcast.106, f32[1024]{0:T(1024)S(1)} %bitcast.96, f32[1024]{0:T(1024)S(1)} %bitcast.98, f32[1024]{0:T(1024)S(1)} %bitcast.100, ...), kind=kLoop, calls=%fused_computation.42 | loop fusion | flops 10485760 | bytes 3198976 | tf_op jit(solution)/shard_map/convert_element_type | solution.py:148
  161.0 3.0 %fusion.23 = bf16[512,1024]{1,0:T(8,128)(2,1)} fusion(f32[6,1024]{1,0:T(8,128)S(1)} %get-tuple-element.128, f32[512,1024]{1,0:T(8,128)S(1)} %get-tuple-element.72, f32[1024]{0:T(1024)S(1)} %bitcast.82, f32[1024]{0:T(1024)S(1)} %bitcast.84, f32[1024]{0:T(1024)S(1)} %bitcast.86, f32[1024]{0:T(1024)S(1)} %bitcast.88, f32[1024]{0:T(1024)S(1)} %bitcast.90, ...), kind=kLoop, calls=%fused_computation.59 | loop fusion | flops 10485760 | bytes 3198976 | tf_op jit(solution)/shard_map/convert_element_type | solution.py:148
  164.0 3.0 %fusion.40 = bf16[512,1024]{1,0:T(8,128)(2,1)} fusion(f32[6,1024]{1,0:T(8,128)S(1)} %get-tuple-element.129, f32[512,1024]{1,0:T(8,128)S(1)} %copy-done.5, f32[1024]{0:T(1024)S(1)} %bitcast.112, f32[1024]{0:T(1024)S(1)} %bitcast.114, f32[1024]{0:T(1024)S(1)} %bitcast.116, f32[1024]{0:T(1024)S(1)} %bitcast.118, f32[1024]{0:T(1024)S(1)} %bitcast.120, ...), kind=kLoop, calls=%fused_computation.76 | loop fusion | flops 10485760 | bytes 3198976 | tf_op jit(solution)/shard_map/convert_element_type | solution.py:148
  166.9 1.8 add_convert_fusion.7
  169.2 1.8 collective-permute-start.15
  171.0 9.0 %collective-permute-done.12 = bf16[1024,256]{1,0:T(8,128)(2,1)S(1)} collective-permute-done((bf16[1024,256]{1,0:T(8,128)(2,1)S(1)}, bf16[1024,256]{1,0:T(8,128)(2,1)S(1)}, u32[]{:S(2)}, u32[]{:S(2)}) %collective-permute-start.12) | collective-permute-done | bytes 524320 | tf_op jit(solution)/shard_map/ppermute | solution.py:194
  180.0 1.8 add_convert_fusion.6
  181.8 1.2 collective-permute-start.13
  183.0 1.5 collective-permute-start.16
  184.4 10.3 %collective-permute-done.13 = bf16[1024,256]{1,0:T(8,128)(2,1)S(1)} collective-permute-done((bf16[1024,256]{1,0:T(8,128)(2,1)S(1)}, bf16[1024,256]{1,0:T(8,128)(2,1)S(1)}, u32[]{:S(2)}, u32[]{:S(2)}) %collective-permute-start.13) | collective-permute-done | bytes 524320 | tf_op jit(solution)/shard_map/ppermute | solution.py:194
  194.8 1.8 add_convert_fusion.5
  196.6 2.5 %collective-permute-start.14 = (bf16[1024,256]{1,0:T(8,128)(2,1)S(1)}, bf16[1024,256]{1,0:T(8,128)(2,1)S(1)}, u32[]{:S(2)}, u32[]{:S(2)}) collective-permute-start(bf16[1024,256]{1,0:T(8,128)(2,1)S(1)} %get-tuple-element.86), channel_id=1, source_target_pairs={{0,8},{8,16},{16,24},{24,28},{28,20},{20,12},{12,4},{4,0},{1,9},{9... | collective-permute-start | bytes 1572872 | tf_op jit(solution)/shard_map/ppermute | solution.py:194
  199.3 7.1 %collective-permute-done.14 = bf16[1024,256]{1,0:T(8,128)(2,1)S(1)} collective-permute-done((bf16[1024,256]{1,0:T(8,128)(2,1)S(1)}, bf16[1024,256]{1,0:T(8,128)(2,1)S(1)}, u32[]{:S(2)}, u32[]{:S(2)}) %collective-permute-start.14) | collective-permute-done | bytes 524320 | tf_op jit(solution)/shard_map/ppermute | solution.py:194
  206.4 1.9 collective-permute-done.17
  208.3 1.8 add_convert_fusion.4
  (59 shorter events, 8.5 us)
Async XLA Ops:
  7.2 18.8 %copy-start = (bf16[64,128]{1,0:T(8,128)(2,1)S(1)}, bf16[64,128]{1,0:T(8,128)(2,1)}, u32[]{:S(2)}) copy-start(bf16[64,128]{1,0:T(8,128)(2,1)} %param.11) | copy-start | bytes 49156
  7.2 10.2 %copy-start.8 = (bf16[512,1024]{1,0:T(8,128)(2,1)S(1)}, bf16[512,1024]{1,0:T(8,128)(2,1)}, u32[]{:S(2)}) copy-start(bf16[512,1024]{1,0:T(8,128)(2,1)} %param.8) | copy-start | bytes 3145732
  7.2 10.2 %copy-start.7 = (bf16[512,1024]{1,0:T(8,128)(2,1)S(1)}, bf16[512,1024]{1,0:T(8,128)(2,1)}, u32[]{:S(2)}) copy-start(bf16[512,1024]{1,0:T(8,128)(2,1)} %param.9) | copy-start | bytes 3145732
  7.2 54.0 %all-gather.2.cloned.1.call-start = ((), (), s32[]{:S(2)}) async-start(), calls=%async_computation.1 | async-start | bytes 5242880 | tf_op jit(solution)/shard_map/all_gather | solution.py:86
  7.9 203.2 %reduce-scatter.2.cloned.1.call-start = ((), (), s32[]{:S(2)}) async-start(), calls=%async_computation.2 | async-start | bytes 5242880 | tf_op jit(solution)/shard_map/reduce_scatter | solution.py:108
  9.5 7.9 %collective-permute-start = (bf16[3,6,1024]{2,1,0:T(8,128)(2,1)S(1)}, bf16[3,6,1024]{2,1,0:T(8,128)(2,1)S(1)}, u32[]{:S(2)}, u32[]{:S(2)}) collective-permute-start(bf16[3,6,1024]{2,1,0:T(8,128)(2,1)S(1)} %pad_maximum_fusion.9), channel_id=1, source_target_pairs={{0,4},{4,8},{8,12},{12,16},{16,20},{20,24},{24,28},{1,5},{5,9},{9,... | collective-permute-start | bytes 110600 | tf_op jit(solution)/shard_map/ppermute | solution.py:13
  22.4 10.4 %collective-permute-start.1 = (bf16[128,1024]{1,0:T(8,128)(2,1)S(1)}, bf16[128,1024]{1,0:T(8,128)(2,1)S(1)}, u32[]{:S(2)}, u32[]{:S(2)}) collective-permute-start(bf16[128,1024]{1,0:T(8,128)(2,1)S(1)} %slice.389), channel_id=1, source_target_pairs={{0,4},{4,8},{8,12},{12,16},{16,20},{20,24},{24,28},{1,5},{5,9},{9,... | collective-permute-start | bytes 786440 | tf_op jit(solution)/shard_map/ppermute | solution.py:13
  67.7 5.8 %copy-start.1 = (f32[1024,4096]{1,0:T(8,128)}, f32[1024,4096]{1,0:T(8,128)S(1)}, u32[]{:S(2)}) copy-start(f32[1024,4096]{1,0:T(8,128)S(1)} %convolution_multiply_fusion) | copy-start | bytes 50331652
  74.6 13.4 %collective-permute-start.2 = (bf16[1024,256]{1,0:T(8,128)(2,1)}, bf16[1024,256]{1,0:T(8,128)(2,1)}, u32[]{:S(2)}, u32[]{:S(2)}) collective-permute-start(bf16[1024,256]{1,0:T(8,128)(2,1)} %get-tuple-element.44), channel_id=1, source_target_pairs={{0,8},{8,16},{16,24},{24,28},{28,20},{20,12},{12,4},{4,0},{1,9},{9... | collective-permute-start | bytes 1572872 | tf_op jit(solution)/shard_map/ppermute | solution.py:194
  76.3 13.0 %collective-permute-start.3 = (bf16[1024,256]{1,0:T(8,128)(2,1)}, bf16[1024,256]{1,0:T(8,128)(2,1)}, u32[]{:S(2)}, u32[]{:S(2)}) collective-permute-start(bf16[1024,256]{1,0:T(8,128)(2,1)} %get-tuple-element.45), channel_id=1, source_target_pairs={{8,0},{16,8},{24,16},{28,24},{20,28},{12,20},{4,12},{0,4},{9,1},{1... | collective-permute-start | bytes 1572872 | tf_op jit(solution)/shard_map/ppermute | solution.py:195
  86.0 8.3 %copy-start.6 = (bf16[512,4096]{1,0:T(8,128)(2,1)S(1)}, bf16[512,4096]{1,0:T(8,128)(2,1)}, u32[]{:S(2)}) copy-start(bf16[512,4096]{1,0:T(8,128)(2,1)} %all-gather.2.cloned.1.call-done) | copy-start | bytes 12582916
  92.3 9.9 %copy-start.2 = (f32[512,1024]{1,0:T(8,128)S(1)}, f32[512,1024]{1,0:T(8,128)}, u32[]{:S(2)}) copy-start(f32[512,1024]{1,0:T(8,128)} %shard_map.110) | copy-start | bytes 6291460
  92.3 20.2 %collective-permute-start.4 = (bf16[1024,256]{1,0:T(8,128)(2,1)}, bf16[1024,256]{1,0:T(8,128)(2,1)}, u32[]{:S(2)}, u32[]{:S(2)}) collective-permute-start(bf16[1024,256]{1,0:T(8,128)(2,1)} %get-tuple-element.49), channel_id=1, source_target_pairs={{0,8},{8,16},{16,24},{24,28},{28,20},{20,12},{12,4},{4,0},{1,9},{9... | collective-permute-start | bytes 1572872 | tf_op jit(solution)/shard_map/ppermute | solution.py:194
  93.9 18.7 %collective-permute-start.5 = (bf16[1024,256]{1,0:T(8,128)(2,1)}, bf16[1024,256]{1,0:T(8,128)(2,1)}, u32[]{:S(2)}, u32[]{:S(2)}) collective-permute-start(bf16[1024,256]{1,0:T(8,128)(2,1)} %get-tuple-element.50), channel_id=1, source_target_pairs={{8,0},{16,8},{24,16},{28,24},{20,28},{12,20},{4,12},{0,4},{9,1},{1... | collective-permute-start | bytes 1572872 | tf_op jit(solution)/shard_map/ppermute | solution.py:195
  104.3 8.3 %collective-permute-start.6 = (bf16[128,1024]{1,0:T(8,128)(2,1)S(1)}, bf16[128,1024]{1,0:T(8,128)(2,1)S(1)}, u32[]{:S(2)}, u32[]{:S(2)}) collective-permute-start(bf16[128,1024]{1,0:T(8,128)(2,1)S(1)} %slice.390), channel_id=1, source_target_pairs={{4,0},{8,4},{12,8},{16,12},{20,16},{24,20},{28,24},{5,1},{9,5},{13... | collective-permute-start | bytes 786440 | tf_op jit(solution)/shard_map/ppermute | solution.py:13
  115.7 37.0 %collective-permute-start.7 = (bf16[1024,256]{1,0:T(8,128)(2,1)}, bf16[1024,256]{1,0:T(8,128)(2,1)}, u32[]{:S(2)}, u32[]{:S(2)}) collective-permute-start(bf16[1024,256]{1,0:T(8,128)(2,1)} %get-tuple-element.57), channel_id=1, source_target_pairs={{0,8},{8,16},{16,24},{24,28},{28,20},{20,12},{12,4},{4,0},{1,9},{9... | collective-permute-start | bytes 1572872 | tf_op jit(solution)/shard_map/ppermute | solution.py:194
  118.0 34.7 %collective-permute-start.8 = (bf16[1024,256]{1,0:T(8,128)(2,1)}, bf16[1024,256]{1,0:T(8,128)(2,1)}, u32[]{:S(2)}, u32[]{:S(2)}) collective-permute-start(bf16[1024,256]{1,0:T(8,128)(2,1)} %get-tuple-element.58), channel_id=1, source_target_pairs={{8,0},{16,8},{24,16},{28,24},{20,28},{12,20},{4,12},{0,4},{9,1},{1... | collective-permute-start | bytes 1572872 | tf_op jit(solution)/shard_map/ppermute | solution.py:195
  144.5 1.4 copy-start.3
  146.6 6.0 %collective-permute-start.9 = (bf16[3,6,1024]{2,1,0:T(8,128)(2,1)S(1)}, bf16[3,6,1024]{2,1,0:T(8,128)(2,1)S(1)}, u32[]{:S(2)}, u32[]{:S(2)}) collective-permute-start(bf16[3,6,1024]{2,1,0:T(8,128)(2,1)S(1)} %pad_maximum_fusion.10), channel_id=1, source_target_pairs={{4,0},{8,4},{12,8},{16,12},{20,16},{24,20},{28,24},{5,1},{9,5},{13... | collective-permute-start | bytes 110600 | tf_op jit(solution)/shard_map/ppermute | solution.py:13
  148.1 9.9 %copy-start.4 = (f32[512,1024]{1,0:T(8,128)S(1)}, f32[512,1024]{1,0:T(8,128)}, u32[]{:S(2)}) copy-start(f32[512,1024]{1,0:T(8,128)} %copy-done.3) | copy-start | bytes 6291460
  154.7 12.2 %collective-permute-start.10 = (bf16[1024,256]{1,0:T(8,128)(2,1)S(1)}, bf16[1024,256]{1,0:T(8,128)(2,1)S(1)}, u32[]{:S(2)}, u32[]{:S(2)}) collective-permute-start(bf16[1024,256]{1,0:T(8,128)(2,1)S(1)} %get-tuple-element.68), channel_id=1, source_target_pairs={{0,8},{8,16},{16,24},{24,28},{28,20},{20,12},{12,4},{4,0},{1,9},{9... | collective-permute-start | bytes 1572872 | tf_op jit(solution)/shard_map/ppermute | solution.py:194
  156.4 10.5 %collective-permute-start.11 = (bf16[1024,256]{1,0:T(8,128)(2,1)S(1)}, bf16[1024,256]{1,0:T(8,128)(2,1)S(1)}, u32[]{:S(2)}, u32[]{:S(2)}) collective-permute-start(bf16[1024,256]{1,0:T(8,128)(2,1)S(1)} %get-tuple-element.69), channel_id=1, source_target_pairs={{8,0},{16,8},{24,16},{28,24},{20,28},{12,20},{4,12},{0,4},{9,1},{1... | collective-permute-start | bytes 1572872 | tf_op jit(solution)/shard_map/ppermute | solution.py:195
  161.0 3.0 %copy-start.5 = (f32[512,1024]{1,0:T(8,128)S(1)}, f32[512,1024]{1,0:T(8,128)}, u32[]{:S(2)}) copy-start(f32[512,1024]{1,0:T(8,128)} %get-tuple-element.70) | copy-start | bytes 6291460
  168.7 11.3 %collective-permute-start.12 = (bf16[1024,256]{1,0:T(8,128)(2,1)S(1)}, bf16[1024,256]{1,0:T(8,128)(2,1)S(1)}, u32[]{:S(2)}, u32[]{:S(2)}) collective-permute-start(bf16[1024,256]{1,0:T(8,128)(2,1)S(1)} %get-tuple-element.90), channel_id=1, source_target_pairs={{0,8},{8,16},{16,24},{24,28},{28,20},{20,12},{12,4},{4,0},{1,9},{9... | collective-permute-start | bytes 1572872 | tf_op jit(solution)/shard_map/ppermute | solution.py:194
  169.2 10.8 %collective-permute-start.15 = (bf16[1024,256]{1,0:T(8,128)(2,1)S(1)}, bf16[1024,256]{1,0:T(8,128)(2,1)S(1)}, u32[]{:S(2)}, u32[]{:S(2)}) collective-permute-start(bf16[1024,256]{1,0:T(8,128)(2,1)S(1)} %get-tuple-element.91), channel_id=1, source_target_pairs={{8,0},{16,8},{24,16},{28,24},{20,28},{12,20},{4,12},{0,4},{9,1},{1... | collective-permute-start | bytes 1572872 | tf_op jit(solution)/shard_map/ppermute | solution.py:195
  181.8 13.0 %collective-permute-start.13 = (bf16[1024,256]{1,0:T(8,128)(2,1)S(1)}, bf16[1024,256]{1,0:T(8,128)(2,1)S(1)}, u32[]{:S(2)}, u32[]{:S(2)}) collective-permute-start(bf16[1024,256]{1,0:T(8,128)(2,1)S(1)} %get-tuple-element.88), channel_id=1, source_target_pairs={{0,8},{8,16},{16,24},{24,28},{28,20},{20,12},{12,4},{4,0},{1,9},{9... | collective-permute-start | bytes 1572872 | tf_op jit(solution)/shard_map/ppermute | solution.py:194
  183.0 11.8 %collective-permute-start.16 = (bf16[1024,256]{1,0:T(8,128)(2,1)S(1)}, bf16[1024,256]{1,0:T(8,128)(2,1)S(1)}, u32[]{:S(2)}, u32[]{:S(2)}) collective-permute-start(bf16[1024,256]{1,0:T(8,128)(2,1)S(1)} %get-tuple-element.89), channel_id=1, source_target_pairs={{8,0},{16,8},{24,16},{28,24},{20,28},{12,20},{4,12},{0,4},{9,1},{1... | collective-permute-start | bytes 1572872 | tf_op jit(solution)/shard_map/ppermute | solution.py:195
  196.6 9.8 %collective-permute-start.14 = (bf16[1024,256]{1,0:T(8,128)(2,1)S(1)}, bf16[1024,256]{1,0:T(8,128)(2,1)S(1)}, u32[]{:S(2)}, u32[]{:S(2)}) collective-permute-start(bf16[1024,256]{1,0:T(8,128)(2,1)S(1)} %get-tuple-element.86), channel_id=1, source_target_pairs={{0,8},{8,16},{16,24},{24,28},{28,20},{20,12},{12,4},{4,0},{1,9},{9... | collective-permute-start | bytes 1572872 | tf_op jit(solution)/shard_map/ppermute | solution.py:194
  199.1 9.2 %collective-permute-start.17 = (bf16[1024,256]{1,0:T(8,128)(2,1)S(1)}, bf16[1024,256]{1,0:T(8,128)(2,1)S(1)}, u32[]{:S(2)}, u32[]{:S(2)}) collective-permute-start(bf16[1024,256]{1,0:T(8,128)(2,1)S(1)} %get-tuple-element.87), channel_id=1, source_target_pairs={{8,0},{16,8},{24,16},{28,24},{20,28},{12,20},{4,12},{0,4},{9,1},{1... | collective-permute-start | bytes 1572872 | tf_op jit(solution)/shard_map/ppermute | solution.py:195
Sparse Core Ops, SparseCore 0:
  9.6 37.1 all-gather.1
  86.2 45.2 reduce-scatter.1

commit v5 on v4

--- a/solution.py
+++ b/solution.py
@@ -50,33 +50,37 @@
 def band_mix(padded_rows, table, lane_tile=128):
     group_count, tap_count, window_rows = table.shape
     row_count = padded_rows.shape[0] - tap_count
+    block_count = row_count // tap_count
     channels = padded_rows.shape[1]
     members = channels // group_count
     per_tile = lane_tile // members
 
-    def body(table_ref, lower_ref, upper_ref, out_ref):
+    def body(table_ref, rows_ref, out_ref):
         lane_group = lax.broadcasted_iota(jnp.int32, (1, lane_tile), 1) // members
-        lower = lower_ref[...]
-        upper = upper_ref[...]
-        mixed = jnp.zeros((tap_count, lane_tile), jnp.float32)
+        rows = rows_ref[...]
+        window = jnp.concatenate(
+            [rows[n * tap_count : n * tap_count + window_rows] for n in range(block_count)], axis=1
+        )
+        mixed = [jnp.zeros((tap_count, lane_tile), jnp.float32) for _ in range(block_count)]
         for member in range(per_tile):
-            part = jnp.dot(table_ref[member, :, :tap_count], lower, preferred_element_type=jnp.float32)
-            part = part + jnp.dot(table_ref[member, :, tap_count:], upper, preferred_element_type=jnp.float32)
-            mixed = jnp.where(lane_group == member, part, mixed)
-        out_ref[...] = mixed
-
-    grid = (channels // lane_tile, row_count // tap_count)
+            part = jnp.dot(table_ref[member], window, preferred_element_type=jnp.float32)
+            for n in range(block_count):
+                mixed[n] = jnp.where(
+                    lane_group == member, part[:, n * lane_tile : (n + 1) * lane_tile], mixed[n]
+                )
+        for n in range(block_count):
+            out_ref[n * tap_count : (n + 1) * tap_count, :] = mixed[n]
+
     return pl.pallas_call(
         body,
-        grid=grid,
+        grid=(channels // lane_tile,),
         in_specs=[
-            pl.BlockSpec((per_tile, tap_count, window_rows), lambda j, n: (j, 0, 0)),
-            pl.BlockSpec((tap_count, lane_tile), lambda j, n: (n, j)),
-            pl.BlockSpec((tap_count, lane_tile), lambda j, n: (n + 1, j)),
+            pl.BlockSpec((per_tile, tap_count, window_rows), lambda j: (j, 0, 0)),
+            pl.BlockSpec((row_count + tap_count, lane_tile), lambda j: (0, j)),
         ],
-        out_specs=pl.BlockSpec((tap_count, lane_tile), lambda j, n: (n, j)),
+        out_specs=pl.BlockSpec((row_count, lane_tile), lambda j: (0, j)),
         out_shape=jax.ShapeDtypeStruct((row_count, channels), jnp.float32),
-    )(table, padded_rows, padded_rows)
+    )(table, padded_rows)
 
 
 def per_device(query_in, key_in, value_in, feature_taps, filter_taps, out_weight, cotangent, ring):

time: 222 us -> 192 us (0.86); the launches traced: 218 us -> 190 us
  Pallas kernels: 42.7 us -> 15.9 us
    pallas_call x2, Pallas kernels: 42.7 us -> 15.9 us  [band_mix(): pl.pallas_call(body, grid=(channels // lane_tile,), in_specs=[pl.BlockSpe...]
  transfers between devices with their start and end apart: 20 -> 20, of which waited for: 7 -> 7; matrix products, arithmetic and copies ran while one was open for 37% -> 42% of each run, Pallas kernels for 20% -> 8%
where the time goes in v5:
time: 192 us; the launch traced here: 190 us
  other arithmetic  44.1 us (23%)
  waiting for transfers between devices  36.2 us (19%)
  matrix products  31.4 us (16%)
  starting transfers between devices  28.7 us (15%)
  local copies, waits for them, and re-layouts  19.3 us (10%)
  Pallas kernels  15.9 us (8%)
  between operations  14.8 us (8%)
    ppermute x7, waiting for transfers between devices, ring_reduce_scatter(): ahead = lax.ppermute(sent_ahead, 'seq', forward)  27 us
    pallas_call x2, Pallas kernels, band_mix(): pl.pallas_call(body, grid=(channels // lane_tile,), in_specs=[pl.BlockSpe...  15.9 us
    unnamed x24, local copies, waits for them, and re-layouts  13.5 us
    ppermute x7, starting transfers between devices, ring_reduce_scatter(): ahead = lax.ppermute(sent_ahead, 'seq', forward)  11.1 us
    ppermute x4, starting transfers between devices, passed_along(): lax.ppermute(value, axis, [(source, source + steps) for source in range(l...  10.9 us
    dot_general x1, matrix products, project(): jnp.dot(gated_rows, out_weight, preferred_element_type=jnp.float32)  9.4 us
    convert_element_type x3, other arithmetic, feature_back(): grads = tuple((spread_back(jnp.concatenate([grad_features[i], features_af...  8.9 us
    convert_element_type x3, other arithmetic, ring_reduce_scatter(): sent_behind = behind.astype(jnp.bfloat16)  8.18 us
  transfers between devices with their start and end apart: 20, of which 7 were waited for; matrix products, arithmetic and copies ran while one was open for 42% of the time, Pallas kernels for 8%

profile of v5, /device:TPU:0, one launch (start us, length us, event | category | flops | bytes accessed | tf_op | source)
XLA Modules:
  0.0 190.5 jit_solution(1232577689787237192)
XLA Ops:
  9.5 4.9 %collective-permute-start = (bf16[3,6,1024]{2,1,0:T(8,128)(2,1)S(1)}, bf16[3,6,1024]{2,1,0:T(8,128)(2,1)S(1)}, u32[]{:S(2)}, u32[]{:S(2)}) collective-permute-start(bf16[3,6,1024]{2,1,0:T(8,128)(2,1)S(1)} %pad_maximum_fusion.9), channel_id=1, source_target_pairs={{0,4},{4,8},{8,12},{12,16},{16,20},{20,24},{24,28},{1,5},{5,9},{9,... | collective-permute-start | bytes 110600 | tf_op jit(solution)/shard_map/ppermute | solution.py:13
  14.6 1.4 fusion.77
  17.4 5.0 %multiply_convert_fusion.1 = (bf16[512,1024]{1,0:T(8,128)(2,1)S(1)}, f32[512,1024]{1,0:T(8,128)}, f32[512,1024]{1,0:T(8,128)}) fusion(bf16[512,1024]{1,0:T(8,128)(2,1)S(1)} %copy-done.7, bf16[6,1024]{1,0:T(8,128)(2,1)S(1)} %get-tuple-element.131, f32[1024]{0:T(1024)S(1)} %bitcast.107, f32[1024]{0:T(1024)S(1)} %bitcast.105, f32[1024]{0:T(1024)S(1)} %bitcast.95, ...), kind=kLoop, calls=%fused_computation.108 | loop fusion | flops 40894464 | bytes 7421952 | tf_op jit(solution)/shard_map/convert_element_type | solution.py:99
  22.4 3.5 %collective-permute-start.1 = (bf16[128,1024]{1,0:T(8,128)(2,1)S(1)}, bf16[128,1024]{1,0:T(8,128)(2,1)S(1)}, u32[]{:S(2)}, u32[]{:S(2)}) collective-permute-start(bf16[128,1024]{1,0:T(8,128)(2,1)S(1)} %slice.389), channel_id=1, source_target_pairs={{0,4},{4,8},{8,12},{12,16},{16,20},{20,24},{24,28},{1,5},{5,9},{9,... | collective-permute-start | bytes 786440 | tf_op jit(solution)/shard_map/ppermute | solution.py:13
  25.9 3.9 %convolution_convert_fusion.1 = bf16[32768,64]{0,1:T(8,128)(2,1)S(1)} fusion(bf16[64,128]{1,0:T(8,128)(2,1)S(1)} %copy-done, s32[32768]{0:T(1024)S(1)} %get-tuple-element.105), kind=kOutput, calls=%fused_computation.1 | convolution fusion | flops 543162368 | bytes 4341760 | tf_op jit(solution)/shard_map/dot_general | solution.py:46
  29.8 3.1 %copy.15 = bf16[8,8,128,256]{3,2,1,0:T(8,128)(2,1)} copy(bf16[8,8,128,256]{3,1,2,0:T(8,128)(2,1)S(1)} %bitcast.76) | data formatting | bytes 8388608
  32.9 1.2 pad_maximum_fusion.3.rows_ref
  34.1 8.0 %shard_map.110 = f32[512,1024]{1,0:T(8,128)} custom-call(bf16[64,128,256]{2,1,0:T(8,128)(2,1)} %bitcast.75, bf16[640,1024]{1,0:T(8,128)(2,1)} %pad_maximum_fusion.3.rows_ref), custom_call_target="tpu_custom_call" | custom-call | tf_op jit(solution)/shard_map/pallas_call | solution.py:74
  42.0 5.8 %multiply_convert_fusion = (bf16[512,1024]{1,0:T(8,128)(2,1)S(1)}, f32[512,1024]{1,0:T(8,128)S(1)}) fusion(f32[512,1024]{1,0:T(8,128)} %shard_map.110, bf16[512,1024]{1,0:T(8,128)(2,1)} %param.7, bf16[6,1024]{1,0:T(8,128)(2,1)S(1)} %get-tuple-element.130, f32[1024]{0:T(1024)S(1)} %bitcast.111, f32[1024]{0:T(1024)S(1)} %bitcast.113, f32[1024]{0:T(1024)S(1)} %bitcast.115, ...), kind=kLoop, calls=%fused_computation.107 | loop fusion | flops 20971520 | bytes 6332416 | tf_op jit(solution)/shard_map/convert_element_type | solution.py:103
  47.9 6.5 %convolution_multiply_fusion = f32[1024,4096]{1,0:T(8,128)S(1)} fusion(bf16[512,1024]{1,0:T(8,128)(2,1)S(1)} %get-tuple-element.42, bf16[512,4096]{1,0:T(8,128)(2,1)} %all-gather.2.cloned.1.call-done), kind=kOutput, calls=%fused_computation.4 | convolution fusion | flops 4299161600 | bytes 22020096 | tf_op jit(solution)/shard_map/dot_general | solution.py:176
  54.3 5.7 %copy-done.1 = f32[1024,4096]{1,0:T(8,128)} copy-done((f32[1024,4096]{1,0:T(8,128)}, f32[1024,4096]{1,0:T(8,128)S(1)}, u32[]{:S(2)}) %copy-start.1) | copy-done | bytes 16777240
  60.1 1.1 dynamic-slice_convert_fusion
  61.2 1.7 collective-permute-start.2
  63.2 9.4 %convolution_convert_fusion.2 = bf16[512,4096]{1,0:T(8,128)(2,1)} fusion(bf16[512,1024]{1,0:T(8,128)(2,1)S(1)} %get-tuple-element.42, bf16[1024,4096]{1,0:T(8,128)(2,1)} %param.12), kind=kOutput, calls=%fused_computation.7 | convolution fusion | flops 4297064448 | bytes 13631488 | tf_op jit(solution)/shard_map/dot_general | solution.py:113
  72.7 2.0 %collective-permute-done.2 = bf16[1024,256]{1,0:T(8,128)(2,1)} collective-permute-done((bf16[1024,256]{1,0:T(8,128)(2,1)}, bf16[1024,256]{1,0:T(8,128)(2,1)}, u32[]{:S(2)}, u32[]{:S(2)}) %collective-permute-start.2) | collective-permute-done | bytes 524320 | tf_op jit(solution)/shard_map/ppermute | solution.py:198
  74.6 1.3 collective-permute-done.3
  75.9 3.0 %add_convert_fusion.12 = (bf16[1024,256]{1,0:T(8,128)(2,1)}, bf16[1024,256]{1,0:T(8,128)(2,1)}) fusion(f32[1024,4096]{1,0:T(8,128)} %copy-done.1, s32[]{:T(128)S(6)} %select_n.533, bf16[1024,256]{1,0:T(8,128)(2,1)} %collective-permute-done.3, s32[]{:T(128)S(6)} %select_n.524, bf16[1024,256]{1,0:T(8,128)(2,1)} %collective-permute-done.2), kind=kLoop, calls=%fused_computation.154 | loop fusion | flops 1572864 | bytes 4194312 | tf_op jit(solution)/shard_map/convert_element_type | solution.py:193
  79.0 1.6 collective-permute-start.4
  81.0 7.8 %fusion.79 = f32[1024,512]{0,1:T(8,128)S(1)} fusion(bf16[1024,4096]{1,0:T(8,128)(2,1)} %param.12, bf16[512,4096]{1,0:T(8,128)(2,1)S(1)} %copy-done.6), kind=kOutput, calls=%fused_computation.182 | convolution fusion | flops 4294967296 | bytes 14680064 | tf_op jit(solution)/shard_map/dot_general | solution.py:124
  88.8 2.0 %bitcast_multiply_fusion = (f32[512,1024]{1,0:T(8,128)}, bf16[512,1024]{1,0:T(8,128)(2,1)S(1)}) fusion(f32[512,1024]{1,0:T(8,128)S(1)} %copy-done.2, f32[1024,512]{0,1:T(8,128)S(1)} %fusion.79, f32[512,1024]{1,0:T(8,128)S(1)} %get-tuple-element.80), kind=kLoop, calls=%fused_computation.104 | loop fusion | flops 1572864 | bytes 9437184 | tf_op jit(solution)/shard_map/mul | solution.py:128
  90.9 1.3 collective-permute-start.6
  92.2 3.9 %convolution_convert_fusion = bf16[32768,64]{0,1:T(8,128)(2,1)S(1)} fusion(bf16[64,128]{1,0:T(8,128)(2,1)S(1)} %copy-done, s32[32768]{0:T(1024)S(1)} %get-tuple-element.104), kind=kOutput, calls=%fused_computation | convolution fusion | flops 543162368 | bytes 4341760 | tf_op jit(solution)/shard_map/dot_general | solution.py:46
  96.1 3.1 %copy.17 = bf16[8,8,128,256]{3,2,1,0:T(8,128)(2,1)} copy(bf16[8,8,128,256]{3,1,2,0:T(8,128)(2,1)S(1)} %bitcast.77) | data formatting | bytes 8388608
  99.2 3.1 %add_convert_fusion.10 = (bf16[1024,256]{1,0:T(8,128)(2,1)}, bf16[1024,256]{1,0:T(8,128)(2,1)}) fusion(f32[1024,4096]{1,0:T(8,128)} %copy-done.1, s32[]{:T(128)S(6)} %select_n.551, bf16[1024,256]{1,0:T(8,128)(2,1)} %collective-permute-done.5, s32[]{:T(128)S(6)} %select_n.542, bf16[1024,256]{1,0:T(8,128)(2,1)} %collective-permute-done.4), kind=kLoop, calls=%fused_computation.152 | loop fusion | flops 1572864 | bytes 4194312 | tf_op jit(solution)/shard_map/convert_element_type | solution.py:193
  102.3 2.3 %collective-permute-start.7 = (bf16[1024,256]{1,0:T(8,128)(2,1)}, bf16[1024,256]{1,0:T(8,128)(2,1)}, u32[]{:S(2)}, u32[]{:S(2)}) collective-permute-start(bf16[1024,256]{1,0:T(8,128)(2,1)} %get-tuple-element.57), channel_id=1, source_target_pairs={{0,8},{8,16},{16,24},{24,28},{28,20},{20,12},{12,4},{4,0},{1,9},{9... | collective-permute-start | bytes 1572872 | tf_op jit(solution)/shard_map/ppermute | solution.py:198
  105.0 1.2 pad_maximum_fusion.4.rows_ref
  106.2 8.0 %shard_map.111 = f32[512,1024]{1,0:T(8,128)} custom-call(bf16[64,128,256]{2,1,0:T(8,128)(2,1)} %bitcast.74, bf16[640,1024]{1,0:T(8,128)(2,1)} %pad_maximum_fusion.4.rows_ref), custom_call_target="tpu_custom_call" | custom-call | tf_op jit(solution)/shard_map/pallas_call | solution.py:74
  114.1 3.5 %fusion.75 = (f32[512,1024]{1,0:T(8,128)S(1)}, f32[512,1024]{1,0:T(8,128)S(1)}) fusion(f32[512,1024]{1,0:T(8,128)} %shard_map.111, f32[512,1024]{1,0:T(8,128)} %get-tuple-element.83, f32[512,1024]{1,0:T(8,128)} %get-tuple-element.82), kind=kLoop, calls=%fused_computation.178 | loop fusion | flops 1048576 | bytes 10485760 | tf_op jit(solution)/shard_map/mul | solution.py:137
  117.7 1.3 copy-done.3
  119.8 1.3 collective-permute-start.9
  121.3 4.5 %collective-permute-done.9 = bf16[3,6,1024]{2,1,0:T(8,128)(2,1)S(1)} collective-permute-done((bf16[3,6,1024]{2,1,0:T(8,128)(2,1)S(1)}, bf16[3,6,1024]{2,1,0:T(8,128)(2,1)S(1)}, u32[]{:S(2)}, u32[]{:S(2)}) %collective-permute-start.9) | collective-permute-done | bytes 36896 | tf_op jit(solution)/shard_map/ppermute | solution.py:13
  125.8 2.1 %add_convert_fusion.8 = (bf16[1024,256]{1,0:T(8,128)(2,1)S(1)}, bf16[1024,256]{1,0:T(8,128)(2,1)S(1)}) fusion(f32[1024,4096]{1,0:T(8,128)} %copy-done.1, s32[]{:T(128)S(6)} %select_n.569, bf16[1024,256]{1,0:T(8,128)(2,1)} %collective-permute-done.8, s32[]{:T(128)S(6)} %select_n.560, bf16[1024,256]{1,0:T(8,128)(2,1)} %collective-permute-done.7), kind=kLoop, calls=%fused_computation.150 | loop fusion | flops 1572864 | bytes 4194312 | tf_op jit(solution)/shard_map/convert_element_type | solution.py:193
  127.9 1.7 collective-permute-start.10
  129.6 1.6 collective-permute-start.11
  131.2 3.0 %fusion.6 = bf16[512,1024]{1,0:T(8,128)(2,1)} fusion(f32[6,1024]{1,0:T(8,128)S(1)} %get-tuple-element.127, f32[512,1024]{1,0:T(8,128)S(1)} %copy-done.4, f32[1024]{0:T(1024)S(1)} %bitcast.108, f32[1024]{0:T(1024)S(1)} %bitcast.106, f32[1024]{0:T(1024)S(1)} %bitcast.96, f32[1024]{0:T(1024)S(1)} %bitcast.98, f32[1024]{0:T(1024)S(1)} %bitcast.100, ...), kind=kLoop, calls=%fused_computation.42 | loop fusion | flops 10485760 | bytes 3198976 | tf_op jit(solution)/shard_map/convert_element_type | solution.py:152
  134.2 3.0 %fusion.23 = bf16[512,1024]{1,0:T(8,128)(2,1)} fusion(f32[6,1024]{1,0:T(8,128)S(1)} %get-tuple-element.128, f32[512,1024]{1,0:T(8,128)S(1)} %get-tuple-element.72, f32[1024]{0:T(1024)S(1)} %bitcast.82, f32[1024]{0:T(1024)S(1)} %bitcast.84, f32[1024]{0:T(1024)S(1)} %bitcast.86, f32[1024]{0:T(1024)S(1)} %bitcast.88, f32[1024]{0:T(1024)S(1)} %bitcast.90, ...), kind=kLoop, calls=%fused_computation.59 | loop fusion | flops 10485760 | bytes 3198976 | tf_op jit(solution)/shard_map/convert_element_type | solution.py:152
  137.1 3.0 %fusion.40 = bf16[512,1024]{1,0:T(8,128)(2,1)} fusion(f32[6,1024]{1,0:T(8,128)S(1)} %get-tuple-element.129, f32[512,1024]{1,0:T(8,128)S(1)} %copy-done.5, f32[1024]{0:T(1024)S(1)} %bitcast.112, f32[1024]{0:T(1024)S(1)} %bitcast.114, f32[1024]{0:T(1024)S(1)} %bitcast.116, f32[1024]{0:T(1024)S(1)} %bitcast.118, f32[1024]{0:T(1024)S(1)} %bitcast.120, ...), kind=kLoop, calls=%fused_computation.76 | loop fusion | flops 10485760 | bytes 3198976 | tf_op jit(solution)/shard_map/convert_element_type | solution.py:152
  140.1 1.8 add_convert_fusion.7
  142.4 1.5 collective-permute-start.15
  144.0 8.6 %collective-permute-done.12 = bf16[1024,256]{1,0:T(8,128)(2,1)S(1)} collective-permute-done((bf16[1024,256]{1,0:T(8,128)(2,1)S(1)}, bf16[1024,256]{1,0:T(8,128)(2,1)S(1)}, u32[]{:S(2)}, u32[]{:S(2)}) %collective-permute-start.12) | collective-permute-done | bytes 524320 | tf_op jit(solution)/shard_map/ppermute | solution.py:198
  152.5 1.8 add_convert_fusion.6
  155.3 1.4 collective-permute-start.16
  156.7 9.4 %collective-permute-done.13 = bf16[1024,256]{1,0:T(8,128)(2,1)S(1)} collective-permute-done((bf16[1024,256]{1,0:T(8,128)(2,1)S(1)}, bf16[1024,256]{1,0:T(8,128)(2,1)S(1)}, u32[]{:S(2)}, u32[]{:S(2)}) %collective-permute-start.13) | collective-permute-done | bytes 524320 | tf_op jit(solution)/shard_map/ppermute | solution.py:198
  166.1 1.8 add_convert_fusion.5
  167.9 2.4 %collective-permute-start.14 = (bf16[1024,256]{1,0:T(8,128)(2,1)S(1)}, bf16[1024,256]{1,0:T(8,128)(2,1)S(1)}, u32[]{:S(2)}, u32[]{:S(2)}) collective-permute-start(bf16[1024,256]{1,0:T(8,128)(2,1)S(1)} %get-tuple-element.86), channel_id=1, source_target_pairs={{0,8},{8,16},{16,24},{24,28},{28,20},{20,12},{12,4},{4,0},{1,9},{9... | collective-permute-start | bytes 1572872 | tf_op jit(solution)/shard_map/ppermute | solution.py:198
  171.1 7.1 %collective-permute-done.14 = bf16[1024,256]{1,0:T(8,128)(2,1)S(1)} collective-permute-done((bf16[1024,256]{1,0:T(8,128)(2,1)S(1)}, bf16[1024,256]{1,0:T(8,128)(2,1)S(1)}, u32[]{:S(2)}, u32[]{:S(2)}) %collective-permute-start.14) | collective-permute-done | bytes 524320 | tf_op jit(solution)/shard_map/ppermute | solution.py:198
  178.2 2.6 %collective-permute-done.17 = bf16[1024,256]{1,0:T(8,128)(2,1)S(1)} collective-permute-done((bf16[1024,256]{1,0:T(8,128)(2,1)S(1)}, bf16[1024,256]{1,0:T(8,128)(2,1)S(1)}, u32[]{:S(2)}, u32[]{:S(2)}) %collective-permute-start.17) | collective-permute-done | bytes 524320 | tf_op jit(solution)/shard_map/ppermute | solution.py:199
  180.8 1.8 add_convert_fusion.4
  (59 shorter events, 9.0 us)
Async XLA Ops:
  7.2 18.8 %copy-start = (bf16[64,128]{1,0:T(8,128)(2,1)S(1)}, bf16[64,128]{1,0:T(8,128)(2,1)}, u32[]{:S(2)}) copy-start(bf16[64,128]{1,0:T(8,128)(2,1)} %param.11) | copy-start | bytes 49156
  7.2 10.2 %copy-start.8 = (bf16[512,1024]{1,0:T(8,128)(2,1)S(1)}, bf16[512,1024]{1,0:T(8,128)(2,1)}, u32[]{:S(2)}) copy-start(bf16[512,1024]{1,0:T(8,128)(2,1)} %param.8) | copy-start | bytes 3145732
  7.2 10.2 %copy-start.7 = (bf16[512,1024]{1,0:T(8,128)(2,1)S(1)}, bf16[512,1024]{1,0:T(8,128)(2,1)}, u32[]{:S(2)}) copy-start(bf16[512,1024]{1,0:T(8,128)(2,1)} %param.9) | copy-start | bytes 3145732
  7.2 40.7 %all-gather.2.cloned.1.call-start = ((), (), s32[]{:S(2)}) async-start(), calls=%async_computation.1 | async-start | bytes 5242880 | tf_op jit(solution)/shard_map/all_gather | solution.py:90
  7.9 175.7 %reduce-scatter.2.cloned.1.call-start = ((), (), s32[]{:S(2)}) async-start(), calls=%async_computation.2 | async-start | bytes 5242880 | tf_op jit(solution)/shard_map/reduce_scatter | solution.py:112
  9.5 7.9 %collective-permute-start = (bf16[3,6,1024]{2,1,0:T(8,128)(2,1)S(1)}, bf16[3,6,1024]{2,1,0:T(8,128)(2,1)S(1)}, u32[]{:S(2)}, u32[]{:S(2)}) collective-permute-start(bf16[3,6,1024]{2,1,0:T(8,128)(2,1)S(1)} %pad_maximum_fusion.9), channel_id=1, source_target_pairs={{0,4},{4,8},{8,12},{12,16},{16,20},{20,24},{24,28},{1,5},{5,9},{9,... | collective-permute-start | bytes 110600 | tf_op jit(solution)/shard_map/ppermute | solution.py:13
  22.4 10.4 %collective-permute-start.1 = (bf16[128,1024]{1,0:T(8,128)(2,1)S(1)}, bf16[128,1024]{1,0:T(8,128)(2,1)S(1)}, u32[]{:S(2)}, u32[]{:S(2)}) collective-permute-start(bf16[128,1024]{1,0:T(8,128)(2,1)S(1)} %slice.389), channel_id=1, source_target_pairs={{0,4},{4,8},{8,12},{12,16},{16,20},{20,24},{24,28},{1,5},{5,9},{9,... | collective-permute-start | bytes 786440 | tf_op jit(solution)/shard_map/ppermute | solution.py:13
  54.3 5.8 %copy-start.1 = (f32[1024,4096]{1,0:T(8,128)}, f32[1024,4096]{1,0:T(8,128)S(1)}, u32[]{:S(2)}) copy-start(f32[1024,4096]{1,0:T(8,128)S(1)} %convolution_multiply_fusion) | copy-start | bytes 50331652
  61.2 13.4 %collective-permute-start.2 = (bf16[1024,256]{1,0:T(8,128)(2,1)}, bf16[1024,256]{1,0:T(8,128)(2,1)}, u32[]{:S(2)}, u32[]{:S(2)}) collective-permute-start(bf16[1024,256]{1,0:T(8,128)(2,1)} %get-tuple-element.44), channel_id=1, source_target_pairs={{0,8},{8,16},{16,24},{24,28},{28,20},{20,12},{12,4},{4,0},{1,9},{9... | collective-permute-start | bytes 1572872 | tf_op jit(solution)/shard_map/ppermute | solution.py:198
  62.9 13.0 %collective-permute-start.3 = (bf16[1024,256]{1,0:T(8,128)(2,1)}, bf16[1024,256]{1,0:T(8,128)(2,1)}, u32[]{:S(2)}, u32[]{:S(2)}) collective-permute-start(bf16[1024,256]{1,0:T(8,128)(2,1)} %get-tuple-element.45), channel_id=1, source_target_pairs={{8,0},{16,8},{24,16},{28,24},{20,28},{12,20},{4,12},{0,4},{9,1},{1... | collective-permute-start | bytes 1572872 | tf_op jit(solution)/shard_map/ppermute | solution.py:199
  72.7 8.3 %copy-start.6 = (bf16[512,4096]{1,0:T(8,128)(2,1)S(1)}, bf16[512,4096]{1,0:T(8,128)(2,1)}, u32[]{:S(2)}) copy-start(bf16[512,4096]{1,0:T(8,128)(2,1)} %all-gather.2.cloned.1.call-done) | copy-start | bytes 12582916
  78.9 9.8 %copy-start.2 = (f32[512,1024]{1,0:T(8,128)S(1)}, f32[512,1024]{1,0:T(8,128)}, u32[]{:S(2)}) copy-start(f32[512,1024]{1,0:T(8,128)} %shard_map.110) | copy-start | bytes 6291460
  79.0 20.2 %collective-permute-start.4 = (bf16[1024,256]{1,0:T(8,128)(2,1)}, bf16[1024,256]{1,0:T(8,128)(2,1)}, u32[]{:S(2)}, u32[]{:S(2)}) collective-permute-start(bf16[1024,256]{1,0:T(8,128)(2,1)} %get-tuple-element.49), channel_id=1, source_target_pairs={{0,8},{8,16},{16,24},{24,28},{28,20},{20,12},{12,4},{4,0},{1,9},{9... | collective-permute-start | bytes 1572872 | tf_op jit(solution)/shard_map/ppermute | solution.py:198
  80.5 18.7 %collective-permute-start.5 = (bf16[1024,256]{1,0:T(8,128)(2,1)}, bf16[1024,256]{1,0:T(8,128)(2,1)}, u32[]{:S(2)}, u32[]{:S(2)}) collective-permute-start(bf16[1024,256]{1,0:T(8,128)(2,1)} %get-tuple-element.50), channel_id=1, source_target_pairs={{8,0},{16,8},{24,16},{28,24},{20,28},{12,20},{4,12},{0,4},{9,1},{1... | collective-permute-start | bytes 1572872 | tf_op jit(solution)/shard_map/ppermute | solution.py:199
  90.9 8.3 %collective-permute-start.6 = (bf16[128,1024]{1,0:T(8,128)(2,1)S(1)}, bf16[128,1024]{1,0:T(8,128)(2,1)S(1)}, u32[]{:S(2)}, u32[]{:S(2)}) collective-permute-start(bf16[128,1024]{1,0:T(8,128)(2,1)S(1)} %slice.390), channel_id=1, source_target_pairs={{4,0},{8,4},{12,8},{16,12},{20,16},{24,20},{28,24},{5,1},{9,5},{13... | collective-permute-start | bytes 786440 | tf_op jit(solution)/shard_map/ppermute | solution.py:13
  102.3 23.6 %collective-permute-start.7 = (bf16[1024,256]{1,0:T(8,128)(2,1)}, bf16[1024,256]{1,0:T(8,128)(2,1)}, u32[]{:S(2)}, u32[]{:S(2)}) collective-permute-start(bf16[1024,256]{1,0:T(8,128)(2,1)} %get-tuple-element.57), channel_id=1, source_target_pairs={{0,8},{8,16},{16,24},{24,28},{28,20},{20,12},{12,4},{4,0},{1,9},{9... | collective-permute-start | bytes 1572872 | tf_op jit(solution)/shard_map/ppermute | solution.py:198
  104.6 21.3 %collective-permute-start.8 = (bf16[1024,256]{1,0:T(8,128)(2,1)}, bf16[1024,256]{1,0:T(8,128)(2,1)}, u32[]{:S(2)}, u32[]{:S(2)}) collective-permute-start(bf16[1024,256]{1,0:T(8,128)(2,1)} %get-tuple-element.58), channel_id=1, source_target_pairs={{8,0},{16,8},{24,16},{28,24},{20,28},{12,20},{4,12},{0,4},{9,1},{1... | collective-permute-start | bytes 1572872 | tf_op jit(solution)/shard_map/ppermute | solution.py:199
  117.7 1.4 copy-start.3
  119.8 6.0 %collective-permute-start.9 = (bf16[3,6,1024]{2,1,0:T(8,128)(2,1)S(1)}, bf16[3,6,1024]{2,1,0:T(8,128)(2,1)S(1)}, u32[]{:S(2)}, u32[]{:S(2)}) collective-permute-start(bf16[3,6,1024]{2,1,0:T(8,128)(2,1)S(1)} %pad_maximum_fusion.10), channel_id=1, source_target_pairs={{4,0},{8,4},{12,8},{16,12},{20,16},{24,20},{28,24},{5,1},{9,5},{13... | collective-permute-start | bytes 110600 | tf_op jit(solution)/shard_map/ppermute | solution.py:13
  121.3 9.9 %copy-start.4 = (f32[512,1024]{1,0:T(8,128)S(1)}, f32[512,1024]{1,0:T(8,128)}, u32[]{:S(2)}) copy-start(f32[512,1024]{1,0:T(8,128)} %copy-done.3) | copy-start | bytes 6291460
  127.9 12.2 %collective-permute-start.10 = (bf16[1024,256]{1,0:T(8,128)(2,1)S(1)}, bf16[1024,256]{1,0:T(8,128)(2,1)S(1)}, u32[]{:S(2)}, u32[]{:S(2)}) collective-permute-start(bf16[1024,256]{1,0:T(8,128)(2,1)S(1)} %get-tuple-element.68), channel_id=1, source_target_pairs={{0,8},{8,16},{16,24},{24,28},{28,20},{20,12},{12,4},{4,0},{1,9},{9... | collective-permute-start | bytes 1572872 | tf_op jit(solution)/shard_map/ppermute | solution.py:198
  129.6 10.5 %collective-permute-start.11 = (bf16[1024,256]{1,0:T(8,128)(2,1)S(1)}, bf16[1024,256]{1,0:T(8,128)(2,1)S(1)}, u32[]{:S(2)}, u32[]{:S(2)}) collective-permute-start(bf16[1024,256]{1,0:T(8,128)(2,1)S(1)} %get-tuple-element.69), channel_id=1, source_target_pairs={{8,0},{16,8},{24,16},{28,24},{20,28},{12,20},{4,12},{0,4},{9,1},{1... | collective-permute-start | bytes 1572872 | tf_op jit(solution)/shard_map/ppermute | solution.py:199
  134.2 3.0 %copy-start.5 = (f32[512,1024]{1,0:T(8,128)S(1)}, f32[512,1024]{1,0:T(8,128)}, u32[]{:S(2)}) copy-start(f32[512,1024]{1,0:T(8,128)} %get-tuple-element.70) | copy-start | bytes 6291460
  141.9 10.6 %collective-permute-start.12 = (bf16[1024,256]{1,0:T(8,128)(2,1)S(1)}, bf16[1024,256]{1,0:T(8,128)(2,1)S(1)}, u32[]{:S(2)}, u32[]{:S(2)}) collective-permute-start(bf16[1024,256]{1,0:T(8,128)(2,1)S(1)} %get-tuple-element.90), channel_id=1, source_target_pairs={{0,8},{8,16},{16,24},{24,28},{28,20},{20,12},{12,4},{4,0},{1,9},{9... | collective-permute-start | bytes 1572872 | tf_op jit(solution)/shard_map/ppermute | solution.py:198
  142.4 10.1 %collective-permute-start.15 = (bf16[1024,256]{1,0:T(8,128)(2,1)S(1)}, bf16[1024,256]{1,0:T(8,128)(2,1)S(1)}, u32[]{:S(2)}, u32[]{:S(2)}) collective-permute-start(bf16[1024,256]{1,0:T(8,128)(2,1)S(1)} %get-tuple-element.91), channel_id=1, source_target_pairs={{8,0},{16,8},{24,16},{28,24},{20,28},{12,20},{4,12},{0,4},{9,1},{1... | collective-permute-start | bytes 1572872 | tf_op jit(solution)/shard_map/ppermute | solution.py:199
  154.3 11.8 %collective-permute-start.13 = (bf16[1024,256]{1,0:T(8,128)(2,1)S(1)}, bf16[1024,256]{1,0:T(8,128)(2,1)S(1)}, u32[]{:S(2)}, u32[]{:S(2)}) collective-permute-start(bf16[1024,256]{1,0:T(8,128)(2,1)S(1)} %get-tuple-element.88), channel_id=1, source_target_pairs={{0,8},{8,16},{16,24},{24,28},{28,20},{20,12},{12,4},{4,0},{1,9},{9... | collective-permute-start | bytes 1572872 | tf_op jit(solution)/shard_map/ppermute | solution.py:198
  155.3 10.8 %collective-permute-start.16 = (bf16[1024,256]{1,0:T(8,128)(2,1)S(1)}, bf16[1024,256]{1,0:T(8,128)(2,1)S(1)}, u32[]{:S(2)}, u32[]{:S(2)}) collective-permute-start(bf16[1024,256]{1,0:T(8,128)(2,1)S(1)} %get-tuple-element.89), channel_id=1, source_target_pairs={{8,0},{16,8},{24,16},{28,24},{20,28},{12,20},{4,12},{0,4},{9,1},{1... | collective-permute-start | bytes 1572872 | tf_op jit(solution)/shard_map/ppermute | solution.py:199
  167.9 10.3 %collective-permute-start.14 = (bf16[1024,256]{1,0:T(8,128)(2,1)S(1)}, bf16[1024,256]{1,0:T(8,128)(2,1)S(1)}, u32[]{:S(2)}, u32[]{:S(2)}) collective-permute-start(bf16[1024,256]{1,0:T(8,128)(2,1)S(1)} %get-tuple-element.86), channel_id=1, source_target_pairs={{0,8},{8,16},{16,24},{24,28},{28,20},{20,12},{12,4},{4,0},{1,9},{9... | collective-permute-start | bytes 1572872 | tf_op jit(solution)/shard_map/ppermute | solution.py:198
  170.3 10.5 %collective-permute-start.17 = (bf16[1024,256]{1,0:T(8,128)(2,1)S(1)}, bf16[1024,256]{1,0:T(8,128)(2,1)S(1)}, u32[]{:S(2)}, u32[]{:S(2)}) collective-permute-start(bf16[1024,256]{1,0:T(8,128)(2,1)S(1)} %get-tuple-element.87), channel_id=1, source_target_pairs={{8,0},{16,8},{24,16},{28,24},{20,28},{12,20},{4,12},{0,4},{9,1},{1... | collective-permute-start | bytes 1572872 | tf_op jit(solution)/shard_map/ppermute | solution.py:199
Sparse Core Ops, SparseCore 0:
  9.6 37.1 all-gather.1
  72.8 45.2 reduce-scatter.1

commit v6 on v5

--- a/solution.py
+++ b/solution.py
@@ -172,36 +172,36 @@
     place = sum(jnp.where(seq_index == member, place_of[member], 0) for member in range(count))
     forward = [(ring[i], ring[(i + 1) % count]) for i in range(count)]
     backward = [(ring[(i + 1) % count], ring[i]) for i in range(count)]
-    local_grad = (
-        lax.dot_general(
-            gated_rows, full_cotangent, (((0,), (0,)), ((), ())), preferred_element_type=jnp.float32
-        )
-        * grad_scale
-    )
-
-    def contribution(step, direction):
+    def contribution(step, direction, gated_rows):
         position = (place - direction * (1 + step)) % count
         owner = sum(jnp.where(position == i, ring[i], 0) for i in range(count))
         first = owner * width + (0 if direction == 1 else half)
-        return lax.dynamic_slice_in_dim(local_grad, first, half, 1)
-
-    ahead = contribution(0, 1)
-    behind = contribution(0, -1)
+        columns = lax.dynamic_slice_in_dim(full_cotangent, first, half, 1)
+        return (
+            lax.dot_general(
+                gated_rows, columns, (((0,), (0,)), ((), ())), preferred_element_type=jnp.float32
+            )
+            * grad_scale
+        )
+
+    ahead = contribution(0, 1, gated_rows)
+    behind = contribution(0, -1, gated_rows)
     stages = list(stages)
     for step in range(1, count):
-        sent_ahead = ahead.astype(jnp.bfloat16)
-        sent_behind = behind.astype(jnp.bfloat16)
-        if stages:
-            sent_ahead, sent_behind, state = lax.optimization_barrier(
-                (sent_ahead, sent_behind, state)
-            )
+        sent_ahead, sent_behind, state, rows = lax.optimization_barrier(
+            (ahead.astype(jnp.bfloat16), behind.astype(jnp.bfloat16), state, gated_rows)
+        )
         ahead = lax.ppermute(sent_ahead, "seq", forward)
         behind = lax.ppermute(sent_behind, "seq", backward)
         if stages:
             state = stages.pop(0)(state)
-            ahead, behind, state = lax.optimization_barrier((ahead, behind, state))
-        ahead = ahead.astype(jnp.float32) + contribution(step, 1)
-        behind = behind.astype(jnp.float32) + contribution(step, -1)
+        more_ahead = contribution(step, 1, rows)
+        more_behind = contribution(step, -1, rows)
+        ahead, behind, state, more_ahead, more_behind = lax.optimization_barrier(
+            (ahead, behind, state, more_ahead, more_behind)
+        )
+        ahead = ahead.astype(jnp.float32) + more_ahead
+        behind = behind.astype(jnp.float32) + more_behind
     while stages:
         state = stages.pop(0)(state)
     return state, jnp.concatenate([ahead, behind], axis=1).astype(jnp.bfloat16)

time: 192 us -> 198 us (1.031)
  waiting for transfers between devices: 36.2 us -> 56.8 us
  other arithmetic: 44.1 us -> 29.3 us
  matrix products: 31.4 us -> 38.4 us
  local copies, waits for them, and re-layouts: 19.3 us -> 13.2 us
    ppermute x7, waiting for transfers between devices: 27 us -> 45.5 us  [ring_reduce_scatter(): ahead = lax.ppermute(sent_ahead, 'seq', forward)]
    convert_element_type x6 -> x12, other arithmetic: 13.5 us -> 2.96 us  [the longest x6 1.48 us: ring_reduce_scatter(): ahead.astype(jnp.bfloat16)]
    dot_general x1 -> x16, matrix products: 6.46 us -> 11.7 us  [contribution(): lax.dot_general(gated_rows, columns, (((0,), (0,)), ((), ())), preferred_...]
    unnamed x24 -> x28, local copies, waits for them, and re-layouts: 13.5 us -> 9.22 us
    dot_general x2, matrix products: 7.78 us -> 9.83 us  [band_table(): table = jnp.dot(filter_taps, select, preferred_element_type=jnp.float32)]
  transfers between devices with their start and end apart: 20 -> 20, of which waited for: 7 -> 12; matrix products, arithmetic and copies ran while one was open for 42% -> 39% of each run, Pallas kernels for 8% -> 8%
where the time goes in v6:
time: 198 us
  waiting for transfers between devices  56.8 us (29%)
  matrix products  38.4 us (19%)
  other arithmetic  29.3 us (15%)
  starting transfers between devices  28.5 us (14%)
  Pallas kernels  16 us (8%)
  between operations  15.2 us (8%)
  local copies, waits for them, and re-layouts  13.2 us (7%)
    ppermute x7, waiting for transfers between devices, ring_reduce_scatter(): ahead = lax.ppermute(sent_ahead, 'seq', forward)  45.5 us
    pallas_call x2, Pallas kernels, band_mix(): pl.pallas_call(body, grid=(channels // lane_tile,), in_specs=[pl.BlockSpe...  16 us
    dot_general x16, matrix products, contribution(): lax.dot_general(gated_rows, columns, (((0,), (0,)), ((), ())), preferred_...  11.7 us
    ppermute x7, starting transfers between devices, ring_reduce_scatter(): ahead = lax.ppermute(sent_ahead, 'seq', forward)  11.6 us
    ppermute x4, starting transfers between devices, passed_along(): lax.ppermute(value, axis, [(source, source + steps) for source in range(l...  11.2 us
    dot_general x2, matrix products, band_table(): table = jnp.dot(filter_taps, select, preferred_element_type=jnp.float32)  9.83 us
    dot_general x1, matrix products, project(): jnp.dot(gated_rows, out_weight, preferred_element_type=jnp.float32)  9.48 us
    unnamed x28, local copies, waits for them, and re-layouts  9.22 us
  transfers between devices with their start and end apart: 20, of which 12 were waited for; matrix products, arithmetic and copies ran while one was open for 39% of the time, Pallas kernels for 8%

profile of v6, /device:TPU:0, one launch (start us, length us, event | category | flops | bytes accessed | tf_op | source)
XLA Modules:
  0.0 197.5 jit_solution(1334755447068983654)
XLA Ops:
  8.7 0.7 slice_bitcast_fusion.3
  9.5 4.9 %collective-permute-start = (bf16[3,6,1024]{2,1,0:T(8,128)(2,1)S(1)}, bf16[3,6,1024]{2,1,0:T(8,128)(2,1)S(1)}, u32[]{:S(2)}, u32[]{:S(2)}) collective-permute-start(bf16[3,6,1024]{2,1,0:T(8,128)(2,1)S(1)} %pad_maximum_fusion.9), channel_id=1, source_target_pairs={{0,4},{4,8},{8,12},{12,16},{16,20},{20,24},{24,28},{1,5},{5,9},{9,... | collective-permute-start | bytes 110600 | tf_op jit(solution)/shard_map/ppermute | solution.py:13
  14.5 1.4 fusion.111
  16.2 6.0 %convolution_convert_fusion.1 = bf16[32768,64]{0,1:T(8,128)(2,1)} fusion(bf16[64,128]{1,0:T(8,128)(2,1)S(1)} %copy-done, s32[32768]{0:T(1024)S(1)} %get-tuple-element.191), kind=kOutput, calls=%fused_computation.1 | convolution fusion | flops 543162368 | bytes 4341760 | tf_op jit(solution)/shard_map/dot_general | solution.py:46
  22.2 0.8 fusion.112
  23.8 5.5 %copy.15 = bf16[8,8,128,256]{3,2,1,0:T(8,128)(2,1)} copy(bf16[8,8,128,256]{3,1,2,0:T(8,128)(2,1)} %bitcast.90) | data formatting | bytes 8388608
  29.3 5.0 %multiply_convert_fusion.1 = (bf16[512,1024]{1,0:T(8,128)(2,1)S(1)}, f32[512,1024]{1,0:T(8,128)}, f32[512,1024]{1,0:T(8,128)}) fusion(bf16[512,1024]{1,0:T(8,128)(2,1)S(1)} %copy-done.6, bf16[6,1024]{1,0:T(8,128)(2,1)S(1)} %get-tuple-element.217, f32[1024]{0:T(1024)S(1)} %bitcast.121, f32[1024]{0:T(1024)S(1)} %bitcast.119, f32[1024]{0:T(1024)S(1)} %bitcast.109, ...), kind=kLoop, calls=%fused_computation.107 | loop fusion | flops 40894464 | bytes 7421952 | tf_op jit(solution)/shard_map/convert_element_type | solution.py:99
  34.2 3.7 %collective-permute-start.1 = (bf16[128,1024]{1,0:T(8,128)(2,1)S(1)}, bf16[128,1024]{1,0:T(8,128)(2,1)S(1)}, u32[]{:S(2)}, u32[]{:S(2)}) collective-permute-start(bf16[128,1024]{1,0:T(8,128)(2,1)S(1)} %slice.389), channel_id=1, source_target_pairs={{0,4},{4,8},{8,12},{12,16},{16,20},{20,24},{24,28},{1,5},{5,9},{9,... | collective-permute-start | bytes 786440 | tf_op jit(solution)/shard_map/ppermute | solution.py:13
  38.0 3.9 %convolution_convert_fusion = bf16[32768,64]{0,1:T(8,128)(2,1)S(1)} fusion(bf16[64,128]{1,0:T(8,128)(2,1)S(1)} %copy-done, s32[32768]{0:T(1024)S(1)} %get-tuple-element.190), kind=kOutput, calls=%fused_computation | convolution fusion | flops 543162368 | bytes 4341760 | tf_op jit(solution)/shard_map/dot_general | solution.py:46
  41.9 3.1 %copy.17 = bf16[8,8,128,256]{3,2,1,0:T(8,128)(2,1)} copy(bf16[8,8,128,256]{3,1,2,0:T(8,128)(2,1)S(1)} %bitcast.91) | data formatting | bytes 8388608
  45.0 1.2 pad_maximum_fusion.3.rows_ref
  46.1 8.0 %shard_map.110 = f32[512,1024]{1,0:T(8,128)} custom-call(bf16[64,128,256]{2,1,0:T(8,128)(2,1)} %bitcast.89, bf16[640,1024]{1,0:T(8,128)(2,1)} %pad_maximum_fusion.3.rows_ref), custom_call_target="tpu_custom_call" | custom-call | tf_op jit(solution)/shard_map/pallas_call | solution.py:74
  54.2 4.2 %multiply_convert_fusion = (bf16[512,1024]{1,0:T(8,128)(2,1)S(1)}, f32[512,1024]{1,0:T(8,128)}) fusion(f32[512,1024]{1,0:T(8,128)} %shard_map.110, bf16[512,1024]{1,0:T(8,128)(2,1)S(1)} %copy-done.8, bf16[6,1024]{1,0:T(8,128)(2,1)S(1)} %get-tuple-element.216, f32[1024]{0:T(1024)S(1)} %bitcast.125, f32[1024]{0:T(1024)S(1)} %bitcast.127, ...), kind=kLoop, calls=%fused_computation.106 | loop fusion | flops 20971520 | bytes 6332416 | tf_op jit(solution)/shard_map/convert_element_type | solution.py:103
  58.4 1.4 fusion.58
  59.9 1.4 fusion.57
  61.3 1.6 collective-permute-start.2
  63.4 9.5 %convolution_convert_fusion.2 = bf16[512,4096]{1,0:T(8,128)(2,1)} fusion(bf16[512,1024]{1,0:T(8,128)(2,1)S(1)} %get-tuple-element.173, bf16[1024,4096]{1,0:T(8,128)(2,1)} %param.12), kind=kOutput, calls=%fused_computation.6 | convolution fusion | flops 4297064448 | bytes 13631488 | tf_op jit(solution)/shard_map/dot_general | solution.py:113
  72.9 1.4 convolution_multiply_fusion.12
  74.3 1.6 convolution_multiply_fusion.13
  76.6 7.4 %fusion.113 = f32[1024,512]{0,1:T(8,128)S(1)} fusion(bf16[1024,4096]{1,0:T(8,128)(2,1)} %param.12, bf16[512,4096]{1,0:T(8,128)(2,1)S(1)} %copy-done.4), kind=kOutput, calls=%fused_computation.229 | convolution fusion | flops 4294967296 | bytes 14680064 | tf_op jit(solution)/shard_map/dot_general | solution.py:124
  84.0 0.8 bitcast_multiply_fusion
  84.8 1.3 collective-permute-start.6
  86.1 3.3 %collective-permute-start.4 = (bf16[1024,256]{1,0:T(8,128)(2,1)S(1)}, bf16[1024,256]{1,0:T(8,128)(2,1)S(1)}, u32[]{:S(2)}, u32[]{:S(2)}) collective-permute-start(bf16[1024,256]{1,0:T(8,128)(2,1)S(1)} %add_convert_fusion.13), channel_id=1, source_target_pairs={{0,8},{8,16},{16,24},{24,28},{28,20},{20,12},{12,4},{4,0},{1,9},{9... | collective-permute-start | bytes 1572872 | tf_op jit(solution)/shard_map/ppermute | solution.py:194
  90.4 5.5 %collective-permute-done.6 = bf16[128,1024]{1,0:T(8,128)(2,1)S(1)} collective-permute-done((bf16[128,1024]{1,0:T(8,128)(2,1)S(1)}, bf16[128,1024]{1,0:T(8,128)(2,1)S(1)}, u32[]{:S(2)}, u32[]{:S(2)}) %collective-permute-start.6) | collective-permute-done | bytes 262176 | tf_op jit(solution)/shard_map/ppermute | solution.py:13
  95.9 8.6 %collective-permute-done.4 = bf16[1024,256]{1,0:T(8,128)(2,1)S(1)} collective-permute-done((bf16[1024,256]{1,0:T(8,128)(2,1)S(1)}, bf16[1024,256]{1,0:T(8,128)(2,1)S(1)}, u32[]{:S(2)}, u32[]{:S(2)}) %collective-permute-start.4) | collective-permute-done | bytes 524320 | tf_op jit(solution)/shard_map/ppermute | solution.py:194
  104.6 1.1 collective-permute-done.5
  105.6 0.9 add_convert_fusion.10
  106.6 0.9 add_convert_fusion.11
  107.5 1.1 pad_maximum_fusion.4.rows_ref
  108.6 8.0 %shard_map.111 = f32[512,1024]{1,0:T(8,128)} custom-call(bf16[64,128,256]{2,1,0:T(8,128)(2,1)} %bitcast.88, bf16[640,1024]{1,0:T(8,128)(2,1)} %pad_maximum_fusion.4.rows_ref), custom_call_target="tpu_custom_call" | custom-call | tf_op jit(solution)/shard_map/pallas_call | solution.py:74
  116.6 3.8 %fusion.109 = (f32[512,1024]{1,0:T(8,128)S(1)}, f32[512,1024]{1,0:T(8,128)S(1)}) fusion(f32[512,1024]{1,0:T(8,128)} %shard_map.111, f32[512,1024]{1,0:T(8,128)} %get-tuple-element.185, f32[512,1024]{1,0:T(8,128)} %get-tuple-element.184), kind=kLoop, calls=%fused_computation.225 | loop fusion | flops 1048576 | bytes 10485760 | tf_op jit(solution)/shard_map/mul | solution.py:137
  120.5 1.3 collective-permute-start.9
  121.8 3.5 %collective-permute-start.7 = (bf16[1024,256]{1,0:T(8,128)(2,1)S(1)}, bf16[1024,256]{1,0:T(8,128)(2,1)S(1)}, u32[]{:S(2)}, u32[]{:S(2)}) collective-permute-start(bf16[1024,256]{1,0:T(8,128)(2,1)S(1)} %copy-done.10), channel_id=1, source_target_pairs={{0,8},{8,16},{16,24},{24,28},{28,20},{20,12},{12,4},{4,0},{1,9},{9... | collective-permute-start | bytes 1572872 | tf_op jit(solution)/shard_map/ppermute | solution.py:194
  127.0 10.1 %collective-permute-done.7 = bf16[1024,256]{1,0:T(8,128)(2,1)S(1)} collective-permute-done((bf16[1024,256]{1,0:T(8,128)(2,1)S(1)}, bf16[1024,256]{1,0:T(8,128)(2,1)S(1)}, u32[]{:S(2)}, u32[]{:S(2)}) %collective-permute-start.7) | collective-permute-done | bytes 524320 | tf_op jit(solution)/shard_map/ppermute | solution.py:194
  137.1 1.7 collective-permute-done.8
  139.4 1.7 collective-permute-start.11
  142.0 3.0 %fusion.6 = bf16[512,1024]{1,0:T(8,128)(2,1)} fusion(f32[6,1024]{1,0:T(8,128)S(1)} %get-tuple-element.213, f32[512,1024]{1,0:T(8,128)S(1)} %get-tuple-element.133, f32[1024]{0:T(1024)S(1)} %bitcast.122, f32[1024]{0:T(1024)S(1)} %bitcast.120, f32[1024]{0:T(1024)S(1)} %bitcast.110, f32[1024]{0:T(1024)S(1)} %bitcast.112, f32[1024]{0:T(1024)S(1)} %bitcast.114, ...), kind=kLoop, calls=%fused_computation.41 | loop fusion | flops 10485760 | bytes 3198976 | tf_op jit(solution)/shard_map/convert_element_type | solution.py:152
  145.0 3.0 %fusion.23 = bf16[512,1024]{1,0:T(8,128)(2,1)} fusion(f32[6,1024]{1,0:T(8,128)S(1)} %get-tuple-element.214, f32[512,1024]{1,0:T(8,128)S(1)} %get-tuple-element.132, f32[1024]{0:T(1024)S(1)} %bitcast.96, f32[1024]{0:T(1024)S(1)} %bitcast.98, f32[1024]{0:T(1024)S(1)} %bitcast.100, f32[1024]{0:T(1024)S(1)} %bitcast.102, f32[1024]{0:T(1024)S(1)} %bitcast.104, ...), kind=kLoop, calls=%fused_computation.58 | loop fusion | flops 10485760 | bytes 3198976 | tf_op jit(solution)/shard_map/convert_element_type | solution.py:152
  148.0 3.0 %fusion.40 = bf16[512,1024]{1,0:T(8,128)(2,1)} fusion(f32[6,1024]{1,0:T(8,128)S(1)} %get-tuple-element.215, f32[512,1024]{1,0:T(8,128)S(1)} %get-tuple-element.130, f32[1024]{0:T(1024)S(1)} %bitcast.126, f32[1024]{0:T(1024)S(1)} %bitcast.128, f32[1024]{0:T(1024)S(1)} %bitcast.130, f32[1024]{0:T(1024)S(1)} %bitcast.132, f32[1024]{0:T(1024)S(1)} %bitcast.134, ...), kind=kLoop, calls=%fused_computation.75 | loop fusion | flops 10485760 | bytes 3198976 | tf_op jit(solution)/shard_map/convert_element_type | solution.py:152
  150.9 0.8 collective-permute-done.10
  152.7 1.5 collective-permute-start.13
  155.2 9.5 %collective-permute-done.12 = bf16[1024,256]{1,0:T(8,128)(2,1)S(1)} collective-permute-done((bf16[1024,256]{1,0:T(8,128)(2,1)S(1)}, bf16[1024,256]{1,0:T(8,128)(2,1)S(1)}, u32[]{:S(2)}, u32[]{:S(2)}) %collective-permute-start.12) | collective-permute-done | bytes 524320 | tf_op jit(solution)/shard_map/ppermute | solution.py:194
  165.2 1.7 collective-permute-start.15
  167.9 8.8 %collective-permute-done.14 = bf16[1024,256]{1,0:T(8,128)(2,1)S(1)} collective-permute-done((bf16[1024,256]{1,0:T(8,128)(2,1)S(1)}, bf16[1024,256]{1,0:T(8,128)(2,1)S(1)}, u32[]{:S(2)}, u32[]{:S(2)}) %collective-permute-start.14) | collective-permute-done | bytes 524320 | tf_op jit(solution)/shard_map/ppermute | solution.py:194
  177.0 1.8 collective-permute-start.16
  180.0 7.8 %collective-permute-done.16 = bf16[1024,256]{1,0:T(8,128)(2,1)S(1)} collective-permute-done((bf16[1024,256]{1,0:T(8,128)(2,1)S(1)}, bf16[1024,256]{1,0:T(8,128)(2,1)S(1)}, u32[]{:S(2)}, u32[]{:S(2)}) %collective-permute-start.16) | collective-permute-done | bytes 524320 | tf_op jit(solution)/shard_map/ppermute | solution.py:194
  187.8 1.6 collective-permute-done.17
  189.6 1.1 pad_maximum_fusion.8
  (84 shorter events, 12.6 us)
Async XLA Ops:
  7.2 9.1 %copy-start = (bf16[64,128]{1,0:T(8,128)(2,1)S(1)}, bf16[64,128]{1,0:T(8,128)(2,1)}, u32[]{:S(2)}) copy-start(bf16[64,128]{1,0:T(8,128)(2,1)} %param.11) | copy-start | bytes 49156
  7.2 51.2 %all-gather.2.cloned.1.call-start = ((), (), s32[]{:S(2)}) async-start(), calls=%async_computation.1 | async-start | bytes 5242880 | tf_op jit(solution)/shard_map/all_gather | solution.py:90
  7.9 182.7 %reduce-scatter.2.cloned.1.call-start = ((), (), s32[]{:S(2)}) async-start(), calls=%async_computation.2 | async-start | bytes 5242880 | tf_op jit(solution)/shard_map/reduce_scatter | solution.py:112
  9.5 19.8 %collective-permute-start = (bf16[3,6,1024]{2,1,0:T(8,128)(2,1)S(1)}, bf16[3,6,1024]{2,1,0:T(8,128)(2,1)S(1)}, u32[]{:S(2)}, u32[]{:S(2)}) collective-permute-start(bf16[3,6,1024]{2,1,0:T(8,128)(2,1)S(1)} %pad_maximum_fusion.9), channel_id=1, source_target_pairs={{0,4},{4,8},{8,12},{12,16},{16,20},{20,24},{24,28},{1,5},{5,9},{9,... | collective-permute-start | bytes 110600 | tf_op jit(solution)/shard_map/ppermute | solution.py:13
  23.7 5.5 %copy-start.6 = (bf16[512,1024]{1,0:T(8,128)(2,1)S(1)}, bf16[512,1024]{1,0:T(8,128)(2,1)}, u32[]{:S(2)}) copy-start(bf16[512,1024]{1,0:T(8,128)(2,1)} %param.9) | copy-start | bytes 3145732
  23.7 5.5 %copy-start.7 = (bf16[512,1024]{1,0:T(8,128)(2,1)S(1)}, bf16[512,1024]{1,0:T(8,128)(2,1)}, u32[]{:S(2)}) copy-start(bf16[512,1024]{1,0:T(8,128)(2,1)} %param.8) | copy-start | bytes 3145732
  34.2 10.8 %collective-permute-start.1 = (bf16[128,1024]{1,0:T(8,128)(2,1)S(1)}, bf16[128,1024]{1,0:T(8,128)(2,1)S(1)}, u32[]{:S(2)}, u32[]{:S(2)}) collective-permute-start(bf16[128,1024]{1,0:T(8,128)(2,1)S(1)} %slice.389), channel_id=1, source_target_pairs={{0,4},{4,8},{8,12},{12,16},{16,20},{20,24},{24,28},{1,5},{5,9},{9,... | collective-permute-start | bytes 786440 | tf_op jit(solution)/shard_map/ppermute | solution.py:13
  46.1 8.0 %copy-start.8 = (bf16[512,1024]{1,0:T(8,128)(2,1)S(1)}, bf16[512,1024]{1,0:T(8,128)(2,1)}, u32[]{:S(2)}) copy-start(bf16[512,1024]{1,0:T(8,128)(2,1)} %param.7) | copy-start | bytes 3145732
  61.3 14.6 %collective-permute-start.2 = (bf16[1024,256]{1,0:T(8,128)(2,1)S(1)}, bf16[1024,256]{1,0:T(8,128)(2,1)S(1)}, u32[]{:S(2)}, u32[]{:S(2)}) collective-permute-start(bf16[1024,256]{1,0:T(8,128)(2,1)S(1)} %fusion.57), channel_id=1, source_target_pairs={{0,8},{8,16},{16,24},{24,28},{28,20},{20,12},{12,4},{4,0},{1,9},{9... | collective-permute-start | bytes 1572872 | tf_op jit(solution)/shard_map/ppermute | solution.py:194
  62.9 13.0 %collective-permute-start.3 = (bf16[1024,256]{1,0:T(8,128)(2,1)S(1)}, bf16[1024,256]{1,0:T(8,128)(2,1)S(1)}, u32[]{:S(2)}, u32[]{:S(2)}) collective-permute-start(bf16[1024,256]{1,0:T(8,128)(2,1)S(1)} %fusion.58), channel_id=1, source_target_pairs={{8,0},{16,8},{24,16},{28,24},{20,28},{12,20},{4,12},{0,4},{9,1},{1... | collective-permute-start | bytes 1572872 | tf_op jit(solution)/shard_map/ppermute | solution.py:195
  74.3 2.3 %copy-start.4 = (bf16[512,4096]{1,0:T(8,128)(2,1)S(1)}, bf16[512,4096]{1,0:T(8,128)(2,1)}, u32[]{:S(2)}) copy-start(bf16[512,4096]{1,0:T(8,128)(2,1)} %all-gather.2.cloned.1.call-done) | copy-start | bytes 12582916
  76.6 7.4 %copy-start.2 = (f32[512,1024]{1,0:T(8,128)S(1)}, f32[512,1024]{1,0:T(8,128)}, u32[]{:S(2)}) copy-start(f32[512,1024]{1,0:T(8,128)} %shard_map.110) | copy-start | bytes 6291460
  76.6 7.4 %copy-start.3 = (f32[512,1024]{1,0:T(8,128)S(1)}, f32[512,1024]{1,0:T(8,128)}, u32[]{:S(2)}) copy-start(f32[512,1024]{1,0:T(8,128)} %get-tuple-element.182) | copy-start | bytes 6291460
  84.8 11.1 %collective-permute-start.6 = (bf16[128,1024]{1,0:T(8,128)(2,1)S(1)}, bf16[128,1024]{1,0:T(8,128)(2,1)S(1)}, u32[]{:S(2)}, u32[]{:S(2)}) collective-permute-start(bf16[128,1024]{1,0:T(8,128)(2,1)S(1)} %slice.390), channel_id=1, source_target_pairs={{4,0},{8,4},{12,8},{16,12},{20,16},{24,20},{28,24},{5,1},{9,5},{13... | collective-permute-start | bytes 786440 | tf_op jit(solution)/shard_map/ppermute | solution.py:13
  86.1 18.4 %collective-permute-start.4 = (bf16[1024,256]{1,0:T(8,128)(2,1)S(1)}, bf16[1024,256]{1,0:T(8,128)(2,1)S(1)}, u32[]{:S(2)}, u32[]{:S(2)}) collective-permute-start(bf16[1024,256]{1,0:T(8,128)(2,1)S(1)} %add_convert_fusion.13), channel_id=1, source_target_pairs={{0,8},{8,16},{16,24},{24,28},{28,20},{20,12},{12,4},{4,0},{1,9},{9... | collective-permute-start | bytes 1572872 | tf_op jit(solution)/shard_map/ppermute | solution.py:194
  89.5 16.2 %collective-permute-start.5 = (bf16[1024,256]{1,0:T(8,128)(2,1)S(1)}, bf16[1024,256]{1,0:T(8,128)(2,1)S(1)}, u32[]{:S(2)}, u32[]{:S(2)}) collective-permute-start(bf16[1024,256]{1,0:T(8,128)(2,1)S(1)} %add_convert_fusion.12), channel_id=1, source_target_pairs={{8,0},{16,8},{24,16},{28,24},{20,28},{12,20},{4,12},{0,4},{9,1},{1... | collective-permute-start | bytes 1572872 | tf_op jit(solution)/shard_map/ppermute | solution.py:195
  116.6 5.2 %copy-start.10 = (bf16[1024,256]{1,0:T(8,128)(2,1)S(1)}, bf16[1024,256]{1,0:T(8,128)(2,1)}, u32[]{:S(2)}) copy-start(bf16[1024,256]{1,0:T(8,128)(2,1)} %add_convert_fusion.11) | copy-start | bytes 1572868
  116.6 8.8 %copy-start.9 = (bf16[1024,256]{1,0:T(8,128)(2,1)S(1)}, bf16[1024,256]{1,0:T(8,128)(2,1)}, u32[]{:S(2)}) copy-start(bf16[1024,256]{1,0:T(8,128)(2,1)} %add_convert_fusion.10) | copy-start | bytes 1572868
  116.6 8.8 %copy-start.5 = (bf16[512,4096]{1,0:T(8,128)(2,1)S(1)}, bf16[512,4096]{1,0:T(8,128)(2,1)}, u32[]{:S(2)}) copy-start(bf16[512,4096]{1,0:T(8,128)(2,1)} %all-gather.2.cloned.1.call-done) | copy-start | bytes 12582916
  120.5 6.5 %collective-permute-start.9 = (bf16[3,6,1024]{2,1,0:T(8,128)(2,1)S(1)}, bf16[3,6,1024]{2,1,0:T(8,128)(2,1)S(1)}, u32[]{:S(2)}, u32[]{:S(2)}) collective-permute-start(bf16[3,6,1024]{2,1,0:T(8,128)(2,1)S(1)} %pad_maximum_fusion.10), channel_id=1, source_target_pairs={{4,0},{8,4},{12,8},{16,12},{20,16},{24,20},{28,24},{5,1},{9,5},{13... | collective-permute-start | bytes 110600 | tf_op jit(solution)/shard_map/ppermute | solution.py:13
  121.8 15.3 %collective-permute-start.7 = (bf16[1024,256]{1,0:T(8,128)(2,1)S(1)}, bf16[1024,256]{1,0:T(8,128)(2,1)S(1)}, u32[]{:S(2)}, u32[]{:S(2)}) collective-permute-start(bf16[1024,256]{1,0:T(8,128)(2,1)S(1)} %copy-done.10), channel_id=1, source_target_pairs={{0,8},{8,16},{16,24},{24,28},{28,20},{20,12},{12,4},{4,0},{1,9},{9... | collective-permute-start | bytes 1572872 | tf_op jit(solution)/shard_map/ppermute | solution.py:194
  125.3 13.4 %collective-permute-start.8 = (bf16[1024,256]{1,0:T(8,128)(2,1)S(1)}, bf16[1024,256]{1,0:T(8,128)(2,1)S(1)}, u32[]{:S(2)}, u32[]{:S(2)}) collective-permute-start(bf16[1024,256]{1,0:T(8,128)(2,1)S(1)} %copy-done.9), channel_id=1, source_target_pairs={{8,0},{16,8},{24,16},{28,24},{20,28},{12,20},{4,12},{0,4},{9,1},{1... | collective-permute-start | bytes 1572872 | tf_op jit(solution)/shard_map/ppermute | solution.py:195
  139.0 12.8 %collective-permute-start.10 = (bf16[1024,256]{1,0:T(8,128)(2,1)S(1)}, bf16[1024,256]{1,0:T(8,128)(2,1)S(1)}, u32[]{:S(2)}, u32[]{:S(2)}) collective-permute-start(bf16[1024,256]{1,0:T(8,128)(2,1)S(1)} %add_convert_fusion.9), channel_id=1, source_target_pairs={{0,8},{8,16},{16,24},{24,28},{28,20},{20,12},{12,4},{4,0},{1,9},{9... | collective-permute-start | bytes 1572872 | tf_op jit(solution)/shard_map/ppermute | solution.py:194
  139.4 12.5 %collective-permute-start.11 = (bf16[1024,256]{1,0:T(8,128)(2,1)S(1)}, bf16[1024,256]{1,0:T(8,128)(2,1)S(1)}, u32[]{:S(2)}, u32[]{:S(2)}) collective-permute-start(bf16[1024,256]{1,0:T(8,128)(2,1)S(1)} %add_convert_fusion.8), channel_id=1, source_target_pairs={{8,0},{16,8},{24,16},{28,24},{20,28},{12,20},{4,12},{0,4},{9,1},{1... | collective-permute-start | bytes 1572872 | tf_op jit(solution)/shard_map/ppermute | solution.py:195
  152.1 12.5 %collective-permute-start.12 = (bf16[1024,256]{1,0:T(8,128)(2,1)S(1)}, bf16[1024,256]{1,0:T(8,128)(2,1)S(1)}, u32[]{:S(2)}, u32[]{:S(2)}) collective-permute-start(bf16[1024,256]{1,0:T(8,128)(2,1)S(1)} %add_convert_fusion.7), channel_id=1, source_target_pairs={{0,8},{8,16},{16,24},{24,28},{28,20},{20,12},{12,4},{4,0},{1,9},{9... | collective-permute-start | bytes 1572872 | tf_op jit(solution)/shard_map/ppermute | solution.py:194
  152.7 11.9 %collective-permute-start.13 = (bf16[1024,256]{1,0:T(8,128)(2,1)S(1)}, bf16[1024,256]{1,0:T(8,128)(2,1)S(1)}, u32[]{:S(2)}, u32[]{:S(2)}) collective-permute-start(bf16[1024,256]{1,0:T(8,128)(2,1)S(1)} %add_convert_fusion.6), channel_id=1, source_target_pairs={{8,0},{16,8},{24,16},{28,24},{20,28},{12,20},{4,12},{0,4},{9,1},{1... | collective-permute-start | bytes 1572872 | tf_op jit(solution)/shard_map/ppermute | solution.py:195
  164.9 11.8 %collective-permute-start.14 = (bf16[1024,256]{1,0:T(8,128)(2,1)S(1)}, bf16[1024,256]{1,0:T(8,128)(2,1)S(1)}, u32[]{:S(2)}, u32[]{:S(2)}) collective-permute-start(bf16[1024,256]{1,0:T(8,128)(2,1)S(1)} %add_convert_fusion.5), channel_id=1, source_target_pairs={{0,8},{8,16},{16,24},{24,28},{28,20},{20,12},{12,4},{4,0},{1,9},{9... | collective-permute-start | bytes 1572872 | tf_op jit(solution)/shard_map/ppermute | solution.py:194
  165.2 11.5 %collective-permute-start.15 = (bf16[1024,256]{1,0:T(8,128)(2,1)S(1)}, bf16[1024,256]{1,0:T(8,128)(2,1)S(1)}, u32[]{:S(2)}, u32[]{:S(2)}) collective-permute-start(bf16[1024,256]{1,0:T(8,128)(2,1)S(1)} %add_convert_fusion.4), channel_id=1, source_target_pairs={{8,0},{16,8},{24,16},{28,24},{20,28},{12,20},{4,12},{0,4},{9,1},{1... | collective-permute-start | bytes 1572872 | tf_op jit(solution)/shard_map/ppermute | solution.py:195
  177.0 10.8 %collective-permute-start.16 = (bf16[1024,256]{1,0:T(8,128)(2,1)S(1)}, bf16[1024,256]{1,0:T(8,128)(2,1)S(1)}, u32[]{:S(2)}, u32[]{:S(2)}) collective-permute-start(bf16[1024,256]{1,0:T(8,128)(2,1)S(1)} %add_convert_fusion.3), channel_id=1, source_target_pairs={{0,8},{8,16},{16,24},{24,28},{28,20},{20,12},{12,4},{4,0},{1,9},{9... | collective-permute-start | bytes 1572872 | tf_op jit(solution)/shard_map/ppermute | solution.py:194
  178.7 10.6 %collective-permute-start.17 = (bf16[1024,256]{1,0:T(8,128)(2,1)S(1)}, bf16[1024,256]{1,0:T(8,128)(2,1)S(1)}, u32[]{:S(2)}, u32[]{:S(2)}) collective-permute-start(bf16[1024,256]{1,0:T(8,128)(2,1)S(1)} %add_convert_fusion.2), channel_id=1, source_target_pairs={{8,0},{16,8},{24,16},{28,24},{20,28},{12,20},{4,12},{0,4},{9,1},{1... | collective-permute-start | bytes 1572872 | tf_op jit(solution)/shard_map/ppermute | solution.py:195
  189.4 1.3 copy-start.1
Sparse Core Ops, SparseCore 0:
  9.5 37.1 all-gather.1
  73.0 44.8 reduce-scatter.1

commit v7 on v5

--- a/solution.py
+++ b/solution.py
@@ -129,11 +129,12 @@
         conv_after = passed_along(grad_conv[:tap_count], "seq", -1)
         return (grad_conv, conv_after, grad_query)
 
+    def table_back(state):
+        return state + (band_table(filter_taps, reverse=True),)
+
     def filter_back(state):
-        grad_conv, conv_after, grad_query = state
-        grad_mix = band_mix(
-            jnp.concatenate([grad_conv, conv_after], axis=0), band_table(filter_taps, reverse=True)
-        )
+        grad_conv, conv_after, grad_query, table = state
+        grad_mix = band_mix(jnp.concatenate([grad_conv, conv_after], axis=0), table)
         grad_features = (grad_query, grad_mix * value_feat, grad_mix * key_feat)
         features_after = passed_along(
             jnp.stack([rows[: tap_span - 1] for rows in grad_features], axis=0).astype(jnp.bfloat16),
@@ -142,19 +143,39 @@
         )
         return (grad_features, features_after)
 
-    def feature_back(state):
+    def feature_back(first, last):
+        def stage(state):
+            grad_features, features_after, done = state
+            grads = tuple(
+                spread_back(
+                    jnp.concatenate(
+                        [grad_features[i], features_after[i].astype(jnp.float32)], axis=0
+                    ),
+                    feature_taps[:, i],
+                    row_count,
+                ).astype(jnp.bfloat16)
+                for i in range(first, last)
+            )
+            return (grad_features, features_after, done + grads)
+
+        return stage
+
+    def finish(state):
+        return state[2]
+
+    def unpack(state):
         grad_features, features_after = state
-        grads = tuple(
-            spread_back(
-                jnp.concatenate([grad_features[i], features_after[i].astype(jnp.float32)], axis=0),
-                feature_taps[:, i],
-                row_count,
-            ).astype(jnp.bfloat16)
-            for i in range(3)
-        )
-        return grads
-
-    stages = [project, gate_back, filter_back, feature_back]
+        return (grad_features, features_after, ())
+
+    stages = [
+        project,
+        gate_back,
+        table_back,
+        filter_back,
+        lambda state: feature_back(0, 1)(unpack(state)),
+        feature_back(1, 3),
+        finish,
+    ]
     state, summed_grad = ring_reduce_scatter(
         gated_rows, full_cotangent, grad_scale, ring, stages, (gated_rows, out_weight)
     )
@@ -177,7 +198,7 @@
             gated_rows, full_cotangent, (((0,), (0,)), ((), ())), preferred_element_type=jnp.float32
         )
         * grad_scale
-    )
+    ).astype(jnp.bfloat16)
 
     def contribution(step, direction):
         position = (place - direction * (1 + step)) % count
@@ -200,8 +221,8 @@
         if stages:
             state = stages.pop(0)(state)
             ahead, behind, state = lax.optimization_barrier((ahead, behind, state))
-        ahead = ahead.astype(jnp.float32) + contribution(step, 1)
-        behind = behind.astype(jnp.float32) + contribution(step, -1)
+        ahead = ahead.astype(jnp.float32) + contribution(step, 1).astype(jnp.float32)
+        behind = behind.astype(jnp.float32) + contribution(step, -1).astype(jnp.float32)
     while stages:
         state = stages.pop(0)(state)
     return state, jnp.concatenate([ahead, behind], axis=1).astype(jnp.bfloat16)

time: 192 us -> 191 us (level)
  other arithmetic: 44.1 us -> 41 us
  waiting for transfers between devices: 36.2 us -> 38.7 us
  matrix products: 31.4 us -> 33.8 us
    ppermute x7, waiting for transfers between devices: 27 us -> 18.8 us  [ring_reduce_scatter(): ahead = lax.ppermute(sent_ahead, 'seq', forward)]
    ppermute x4, waiting for transfers between devices: 4.52 us -> 11.8 us  [passed_along(): lax.ppermute(value, axis, [(source, source + steps) for source in range(l...]
    convert_element_type x7 -> x5, other arithmetic: 14.3 us -> 8.96 us  [the longest x3 8.95 us: stage(): grads = tuple((spread_back(jnp.concatenate([grad_features[i], features_af...]
    convert_element_type x3 -> x6, other arithmetic: 8.18 us -> 11.6 us  [ring_reduce_scatter(): sent_behind = behind.astype(jnp.bfloat16)]
    ppermute x7, waiting for transfers between devices: 3.92 us -> 7.38 us  [ring_reduce_scatter(): behind = lax.ppermute(sent_behind, 'seq', backward)]
    ppermute x7, starting transfers between devices: 6.6 us -> 3.53 us  [ring_reduce_scatter(): behind = lax.ppermute(sent_behind, 'seq', backward)]
    unnamed x24 -> x98, local copies, waits for them, and re-layouts: 13.5 us -> 11.1 us
  transfers between devices with their start and end apart: 20 -> 20, of which waited for: 7 -> 12; matrix products, arithmetic and copies ran while one was open for 42% -> 42% of each run, Pallas kernels for 8% -> 8%
where the time goes in v7:
time: 191 us; the launch traced here: 189 us
  other arithmetic  41 us (21%)
  waiting for transfers between devices  38.7 us (20%)
  matrix products  33.8 us (18%)
  starting transfers between devices  27 us (14%)
  local copies, waits for them, and re-layouts  17.8 us (9%)
  Pallas kernels  16 us (8%)
  between operations  15.2 us (8%)
    ppermute x7, waiting for transfers between devices, ring_reduce_scatter(): ahead = lax.ppermute(sent_ahead, 'seq', forward)  18.8 us
    pallas_call x2, Pallas kernels, band_mix(): pl.pallas_call(body, grid=(channels // lane_tile,), in_specs=[pl.BlockSpe...  16 us
    ppermute x7, starting transfers between devices, ring_reduce_scatter(): ahead = lax.ppermute(sent_ahead, 'seq', forward)  12 us
    ppermute x4, waiting for transfers between devices, passed_along(): lax.ppermute(value, axis, [(source, source + steps) for source in range(l...  11.8 us
    convert_element_type x6, other arithmetic, ring_reduce_scatter(): sent_behind = behind.astype(jnp.bfloat16)  11.6 us
    ppermute x4, starting transfers between devices, passed_along(): lax.ppermute(value, axis, [(source, source + steps) for source in range(l...  11.4 us
    unnamed x98, local copies, waits for them, and re-layouts  11.1 us
    dot_general x1, matrix products, project(): jnp.dot(gated_rows, out_weight, preferred_element_type=jnp.float32)  9.53 us
  transfers between devices with their start and end apart: 20, of which 12 were waited for; matrix products, arithmetic and copies ran while one was open for 42% of the time, Pallas kernels for 8%

profile of v7, /device:TPU:0, one launch (start us, length us, event | category | flops | bytes accessed | tf_op | source)
XLA Modules:
  0.0 189.4 jit_solution(4191995402141046725)
XLA Ops:
  9.5 4.9 %collective-permute-start = (bf16[3,6,1024]{2,1,0:T(8,128)(2,1)S(1)}, bf16[3,6,1024]{2,1,0:T(8,128)(2,1)S(1)}, u32[]{:S(2)}, u32[]{:S(2)}) collective-permute-start(bf16[3,6,1024]{2,1,0:T(8,128)(2,1)S(1)} %pad_maximum_fusion.9), channel_id=1, source_target_pairs={{0,4},{4,8},{8,12},{12,16},{16,20},{20,24},{24,28},{1,5},{5,9},{9,... | collective-permute-start | bytes 110600 | tf_op jit(solution)/shard_map/ppermute | solution.py:13
  14.6 1.9 fusion.77
  16.7 1.4 fusion.78
  18.2 5.8 %multiply_convert_fusion.2 = (bf16[512,1024]{1,0:T(8,128)(2,1)S(1)}, f32[512,1024]{1,0:T(8,128)}, f32[512,1024]{1,0:T(8,128)}) fusion(bf16[512,1024]{1,0:T(8,128)(2,1)S(1)} %copy-done.6, bf16[6,1024]{1,0:T(8,128)(2,1)S(1)} %get-tuple-element.198, f32[1024]{0:T(1024)} %bitcast.107, f32[1024]{0:T(1024)} %bitcast.105, f32[1024]{0:T(1024)S(1)} %bitcast.95, ...), kind=kLoop, calls=%fused_computation.108 | loop fusion | flops 40894464 | bytes 7421952 | tf_op jit(solution)/shard_map/convert_element_type | solution.py:99
  24.1 3.7 %collective-permute-start.1 = (bf16[128,1024]{1,0:T(8,128)(2,1)S(1)}, bf16[128,1024]{1,0:T(8,128)(2,1)S(1)}, u32[]{:S(2)}, u32[]{:S(2)}) collective-permute-start(bf16[128,1024]{1,0:T(8,128)(2,1)S(1)} %slice.389), channel_id=1, source_target_pairs={{0,4},{4,8},{8,12},{12,16},{16,20},{20,24},{24,28},{1,5},{5,9},{9,... | collective-permute-start | bytes 786440 | tf_op jit(solution)/shard_map/ppermute | solution.py:13
  27.8 3.9 %convolution_convert_fusion.1 = bf16[32768,64]{0,1:T(8,128)(2,1)S(1)} fusion(bf16[64,128]{1,0:T(8,128)(2,1)S(1)} %copy-done, s32[32768]{0:T(1024)S(1)} %get-tuple-element.173), kind=kOutput, calls=%fused_computation.1 | convolution fusion | flops 543162368 | bytes 4341760 | tf_op jit(solution)/shard_map/dot_general | solution.py:46
  31.7 3.1 %copy.15 = bf16[8,8,128,256]{3,2,1,0:T(8,128)(2,1)} copy(bf16[8,8,128,256]{3,1,2,0:T(8,128)(2,1)S(1)} %bitcast.76) | data formatting | bytes 8388608
  34.8 1.2 pad_maximum_fusion.3.rows_ref
  36.0 8.0 %shard_map.110 = f32[512,1024]{1,0:T(8,128)} custom-call(bf16[64,128,256]{2,1,0:T(8,128)(2,1)} %bitcast.75, bf16[640,1024]{1,0:T(8,128)(2,1)} %pad_maximum_fusion.3.rows_ref), custom_call_target="tpu_custom_call" | custom-call | tf_op jit(solution)/shard_map/pallas_call | solution.py:74
  44.1 4.0 %multiply_convert_fusion.1 = (bf16[512,1024]{1,0:T(8,128)(2,1)}, f32[512,1024]{1,0:T(8,128)S(1)}) fusion(f32[512,1024]{1,0:T(8,128)} %shard_map.110, bf16[512,1024]{1,0:T(8,128)(2,1)S(1)} %copy-done.8, bf16[6,1024]{1,0:T(8,128)(2,1)S(1)} %get-tuple-element.197, f32[1024]{0:T(1024)S(1)} %bitcast.111, f32[1024]{0:T(1024)S(1)} %bitcast.113, ...), kind=kLoop, calls=%fused_computation.107 | loop fusion | flops 20971520 | bytes 6332416 | tf_op jit(solution)/shard_map/convert_element_type | solution.py:103
  48.1 7.1 %multiply_convert_fusion = bf16[1024,4096]{1,0:T(8,128)(2,1)S(1)} fusion(bf16[512,1024]{1,0:T(8,128)(2,1)} %get-tuple-element.76, bf16[512,4096]{1,0:T(8,128)(2,1)} %all-gather.2.cloned.1.call-done), kind=kOutput, calls=%fused_computation.3 | convolution fusion | flops 4303355904 | bytes 13631488 | tf_op jit(solution)/shard_map/dot_general | solution.py:197
  55.2 3.4 %copy-done.5 = bf16[1024,4096]{1,0:T(8,128)(2,1)} copy-done((bf16[1024,4096]{1,0:T(8,128)(2,1)}, bf16[1024,4096]{1,0:T(8,128)(2,1)S(1)}, u32[]{:S(2)}) %copy-start.5) | copy-done | bytes 8388632
  59.5 1.6 collective-permute-start.2
  61.6 9.5 %convolution_convert_fusion.2 = bf16[512,4096]{1,0:T(8,128)(2,1)} fusion(bf16[512,1024]{1,0:T(8,128)(2,1)S(1)} %copy-done.9, bf16[1024,4096]{1,0:T(8,128)(2,1)} %param.12), kind=kOutput, calls=%fused_computation.7 | convolution fusion | flops 4297064448 | bytes 13631488 | tf_op jit(solution)/shard_map/dot_general | solution.py:113
  71.1 1.7 collective-permute-done.2
  74.0 2.6 %add_convert_fusion.12 = (bf16[1024,256]{1,0:T(8,128)(2,1)}, bf16[1024,256]{1,0:T(8,128)(2,1)}) fusion(bf16[1024,256]{1,0:T(8,128)(2,1)} %collective-permute-done.3, bf16[1024,4096]{1,0:T(8,128)(2,1)} %copy-done.5, s32[]{:T(128)S(6)} %select_n.533, s32[]{:T(128)S(6)} %select_n.524, bf16[1024,256]{1,0:T(8,128)(2,1)S(1)} %collective-permute-done.2), kind=kLoop, calls=%fused_computation.154 | loop fusion | flops 2097152 | bytes 3145736 | tf_op jit(solution)/shard_map/convert_element_type | solution.py:214
  76.6 1.6 collective-permute-start.4
  78.7 9.4 %fusion.79 = f32[1024,512]{0,1:T(8,128)S(1)} fusion(bf16[1024,4096]{1,0:T(8,128)(2,1)} %param.12, bf16[512,4096]{1,0:T(8,128)(2,1)} %all-gather.2.cloned.1.call-done), kind=kOutput, calls=%fused_computation.182 | convolution fusion | flops 4294967296 | bytes 14680064 | tf_op jit(solution)/shard_map/dot_general | solution.py:124
  88.1 2.1 %bitcast_multiply_fusion = (f32[512,1024]{1,0:T(8,128)}, bf16[512,1024]{1,0:T(8,128)(2,1)S(1)}) fusion(f32[512,1024]{1,0:T(8,128)S(1)} %copy-done.1, f32[1024,512]{0,1:T(8,128)S(1)} %fusion.79, f32[512,1024]{1,0:T(8,128)S(1)} %get-tuple-element.148), kind=kLoop, calls=%fused_computation.104 | loop fusion | flops 1572864 | bytes 9437184 | tf_op jit(solution)/shard_map/mul | solution.py:128
  90.2 1.3 collective-permute-start.6
  91.6 6.9 %collective-permute-done.6 = bf16[128,1024]{1,0:T(8,128)(2,1)S(1)} collective-permute-done((bf16[128,1024]{1,0:T(8,128)(2,1)S(1)}, bf16[128,1024]{1,0:T(8,128)(2,1)S(1)}, u32[]{:S(2)}, u32[]{:S(2)}) %collective-permute-start.6) | collective-permute-done | bytes 262176 | tf_op jit(solution)/shard_map/ppermute | solution.py:13
  98.5 1.9 add_convert_fusion.10
  100.4 1.7 collective-permute-start.7
  102.4 3.9 %convolution_convert_fusion = bf16[32768,64]{0,1:T(8,128)(2,1)S(1)} fusion(bf16[64,128]{1,0:T(8,128)(2,1)S(1)} %copy-done, s32[32768]{0:T(1024)S(1)} %get-tuple-element.172), kind=kOutput, calls=%fused_computation | convolution fusion | flops 543162368 | bytes 4341760 | tf_op jit(solution)/shard_map/dot_general | solution.py:46
  106.3 3.0 %copy.17 = bf16[8,8,128,256]{3,2,1,0:T(8,128)(2,1)} copy(bf16[8,8,128,256]{3,1,2,0:T(8,128)(2,1)S(1)} %bitcast.77) | data formatting | bytes 8388608
  109.4 1.6 collective-permute-done.7
  111.0 1.3 collective-permute-done.8
  112.3 2.4 %add_convert_fusion.8 = (bf16[1024,256]{1,0:T(8,128)(2,1)}, bf16[1024,256]{1,0:T(8,128)(2,1)}) fusion(bf16[1024,256]{1,0:T(8,128)(2,1)S(1)} %collective-permute-done.8, bf16[1024,4096]{1,0:T(8,128)(2,1)} %copy-done.5, s32[]{:T(128)S(6)} %select_n.569, s32[]{:T(128)S(6)} %select_n.560, bf16[1024,256]{1,0:T(8,128)(2,1)S(1)} %collective-permute-done.7), kind=kLoop, calls=%fused_computation.150 | loop fusion | flops 2097152 | bytes 3145736 | tf_op jit(solution)/shard_map/convert_element_type | solution.py:214
  115.1 1.6 collective-permute-start.9
  117.9 7.9 %shard_map.111 = f32[512,1024]{1,0:T(8,128)} custom-call(bf16[64,128,256]{2,1,0:T(8,128)(2,1)} %bitcast.74, bf16[640,1024]{1,0:T(8,128)(2,1)} %pad_maximum_fusion.4.rows_ref), custom_call_target="tpu_custom_call" | custom-call | tf_op jit(solution)/shard_map/pallas_call | solution.py:74
  125.8 3.5 %fusion.75 = (f32[512,1024]{1,0:T(8,128)S(1)}, f32[512,1024]{1,0:T(8,128)S(1)}) fusion(f32[512,1024]{1,0:T(8,128)} %shard_map.111, f32[512,1024]{1,0:T(8,128)} %get-tuple-element.151, f32[512,1024]{1,0:T(8,128)} %get-tuple-element.150), kind=kLoop, calls=%fused_computation.178 | loop fusion | flops 1048576 | bytes 10485760 | tf_op jit(solution)/shard_map/mul | solution.py:138
  129.5 1.2 copy-done.2
  131.5 1.6 collective-permute-start.11
  133.3 4.9 %collective-permute-done.11 = bf16[3,6,1024]{2,1,0:T(8,128)(2,1)S(1)} collective-permute-done((bf16[3,6,1024]{2,1,0:T(8,128)(2,1)S(1)}, bf16[3,6,1024]{2,1,0:T(8,128)(2,1)S(1)}, u32[]{:S(2)}, u32[]{:S(2)}) %collective-permute-start.11) | collective-permute-done | bytes 36896 | tf_op jit(solution)/shard_map/ppermute | solution.py:13
  138.2 1.8 add_convert_fusion.6
  140.0 1.4 collective-permute-start.12
  142.2 3.0 %fusion.40 = bf16[512,1024]{1,0:T(8,128)(2,1)} fusion(f32[6,1024]{1,0:T(8,128)S(1)} %bitcast_convert_fusion.2, f32[512,1024]{1,0:T(8,128)S(1)} %copy-done.4, f32[1024]{0:T(1024)S(1)} %bitcast.112, f32[1024]{0:T(1024)S(1)} %bitcast.114, f32[1024]{0:T(1024)S(1)} %bitcast.116, f32[1024]{0:T(1024)S(1)} %bitcast.118, f32[1024]{0:T(1024)S(1)} %bitcast.120, ...), kind=kLoop, calls=%fused_computation.76 | loop fusion | flops 10485760 | bytes 3198976 | tf_op jit(solution)/shard_map/convert_element_type | solution.py:156
  145.2 4.6 %collective-permute-done.12 = bf16[1024,256]{1,0:T(8,128)(2,1)S(1)} collective-permute-done((bf16[1024,256]{1,0:T(8,128)(2,1)S(1)}, bf16[1024,256]{1,0:T(8,128)(2,1)S(1)}, u32[]{:S(2)}, u32[]{:S(2)}) %collective-permute-start.12) | collective-permute-done | bytes 524320 | tf_op jit(solution)/shard_map/ppermute | solution.py:219
  149.8 1.3 collective-permute-done.13
  151.1 1.5 add_convert_fusion.4
  152.7 3.2 %collective-permute-start.14 = (bf16[1024,256]{1,0:T(8,128)(2,1)S(1)}, bf16[1024,256]{1,0:T(8,128)(2,1)S(1)}, u32[]{:S(2)}, u32[]{:S(2)}) collective-permute-start(bf16[1024,256]{1,0:T(8,128)(2,1)S(1)} %get-tuple-element.126), channel_id=1, source_target_pairs={{0,8},{8,16},{16,24},{24,28},{28,20},{20,12},{12,4},{4,0},{1,9},{9... | collective-permute-start | bytes 1572872 | tf_op jit(solution)/shard_map/ppermute | solution.py:219
  156.0 3.0 %fusion.6 = bf16[512,1024]{1,0:T(8,128)(2,1)} fusion(f32[6,1024]{1,0:T(8,128)S(1)} %get-tuple-element.195, f32[512,1024]{1,0:T(8,128)S(1)} %copy-done.3, f32[1024]{0:T(1024)S(1)} %bitcast.108, f32[1024]{0:T(1024)S(1)} %bitcast.106, f32[1024]{0:T(1024)S(1)} %bitcast.96, f32[1024]{0:T(1024)S(1)} %bitcast.98, f32[1024]{0:T(1024)S(1)} %bitcast.100, ...), kind=kLoop, calls=%fused_computation.42 | loop fusion | flops 10485760 | bytes 3198976 | tf_op jit(solution)/shard_map/convert_element_type | solution.py:156
  159.0 3.0 %fusion.23 = bf16[512,1024]{1,0:T(8,128)(2,1)} fusion(f32[6,1024]{1,0:T(8,128)S(1)} %get-tuple-element.196, f32[512,1024]{1,0:T(8,128)S(1)} %get-tuple-element.128, f32[1024]{0:T(1024)S(1)} %bitcast.82, f32[1024]{0:T(1024)S(1)} %bitcast.84, f32[1024]{0:T(1024)S(1)} %bitcast.86, f32[1024]{0:T(1024)S(1)} %bitcast.88, f32[1024]{0:T(1024)S(1)} %bitcast.90, ...), kind=kLoop, calls=%fused_computation.59 | loop fusion | flops 10485760 | bytes 3198976 | tf_op jit(solution)/shard_map/convert_element_type | solution.py:156
  162.0 3.7 %collective-permute-done.14 = bf16[1024,256]{1,0:T(8,128)(2,1)S(1)} collective-permute-done((bf16[1024,256]{1,0:T(8,128)(2,1)S(1)}, bf16[1024,256]{1,0:T(8,128)(2,1)S(1)}, u32[]{:S(2)}, u32[]{:S(2)}) %collective-permute-start.14) | collective-permute-done | bytes 524320 | tf_op jit(solution)/shard_map/ppermute | solution.py:219
  165.7 2.8 %collective-permute-done.15 = bf16[1024,256]{1,0:T(8,128)(2,1)S(1)} collective-permute-done((bf16[1024,256]{1,0:T(8,128)(2,1)S(1)}, bf16[1024,256]{1,0:T(8,128)(2,1)S(1)}, u32[]{:S(2)}, u32[]{:S(2)}) %collective-permute-start.15) | collective-permute-done | bytes 524320 | tf_op jit(solution)/shard_map/ppermute | solution.py:220
  168.5 1.5 add_convert_fusion.2
  172.0 7.2 %collective-permute-done.16 = bf16[1024,256]{1,0:T(8,128)(2,1)S(1)} collective-permute-done((bf16[1024,256]{1,0:T(8,128)(2,1)S(1)}, bf16[1024,256]{1,0:T(8,128)(2,1)S(1)}, u32[]{:S(2)}, u32[]{:S(2)}) %collective-permute-start.16) | collective-permute-done | bytes 524320 | tf_op jit(solution)/shard_map/ppermute | solution.py:219
  180.0 1.5 add_convert_fusion.1
  (134 shorter events, 13.3 us)
Async XLA Ops:
  7.2 20.6 %copy-start = (bf16[64,128]{1,0:T(8,128)(2,1)S(1)}, bf16[64,128]{1,0:T(8,128)(2,1)}, u32[]{:S(2)}) copy-start(bf16[64,128]{1,0:T(8,128)(2,1)} %param.11) | copy-start | bytes 49156
  7.2 11.0 %copy-start.7 = (bf16[512,1024]{1,0:T(8,128)(2,1)S(1)}, bf16[512,1024]{1,0:T(8,128)(2,1)}, u32[]{:S(2)}) copy-start(bf16[512,1024]{1,0:T(8,128)(2,1)} %param.8) | copy-start | bytes 3145732
  7.2 11.0 %copy-start.6 = (bf16[512,1024]{1,0:T(8,128)(2,1)S(1)}, bf16[512,1024]{1,0:T(8,128)(2,1)}, u32[]{:S(2)}) copy-start(bf16[512,1024]{1,0:T(8,128)(2,1)} %param.9) | copy-start | bytes 3145732
  7.2 40.9 %all-gather.2.cloned.1.call-start = ((), (), s32[]{:S(2)}) async-start(), calls=%async_computation.1 | async-start | bytes 5242880 | tf_op jit(solution)/shard_map/all_gather | solution.py:90
  7.9 174.6 %reduce-scatter.2.cloned.1.call-start = ((), (), s32[]{:S(2)}) async-start(), calls=%async_computation.2 | async-start | bytes 5242880 | tf_op jit(solution)/shard_map/reduce_scatter | solution.py:112
  9.5 8.7 %collective-permute-start = (bf16[3,6,1024]{2,1,0:T(8,128)(2,1)S(1)}, bf16[3,6,1024]{2,1,0:T(8,128)(2,1)S(1)}, u32[]{:S(2)}, u32[]{:S(2)}) collective-permute-start(bf16[3,6,1024]{2,1,0:T(8,128)(2,1)S(1)} %pad_maximum_fusion.9), channel_id=1, source_target_pairs={{0,4},{4,8},{8,12},{12,16},{16,20},{20,24},{24,28},{1,5},{5,9},{9,... | collective-permute-start | bytes 110600 | tf_op jit(solution)/shard_map/ppermute | solution.py:13
  24.1 10.7 %collective-permute-start.1 = (bf16[128,1024]{1,0:T(8,128)(2,1)S(1)}, bf16[128,1024]{1,0:T(8,128)(2,1)S(1)}, u32[]{:S(2)}, u32[]{:S(2)}) collective-permute-start(bf16[128,1024]{1,0:T(8,128)(2,1)S(1)} %slice.389), channel_id=1, source_target_pairs={{0,4},{4,8},{8,12},{12,16},{16,20},{20,24},{24,28},{1,5},{5,9},{9,... | collective-permute-start | bytes 786440 | tf_op jit(solution)/shard_map/ppermute | solution.py:13
  36.0 8.1 %copy-start.8 = (bf16[512,1024]{1,0:T(8,128)(2,1)S(1)}, bf16[512,1024]{1,0:T(8,128)(2,1)}, u32[]{:S(2)}) copy-start(bf16[512,1024]{1,0:T(8,128)(2,1)} %param.7) | copy-start | bytes 3145732
  36.0 8.1 %copy-start.32 = (f32[1,1,1024]{2,0,1:T(1,128)S(1)}, f32[1,1,1024]{2,0,1:T(1,128)}, u32[]{:S(2)}) copy-start(f32[1,1,1024]{2,0,1:T(1,128)} %get-tuple-element.174) | copy-start | bytes 12292
  36.0 8.1 %copy-start.34 = (f32[1,1,1024]{2,0,1:T(1,128)S(1)}, f32[1,1,1024]{2,0,1:T(1,128)}, u32[]{:S(2)}) copy-start(f32[1,1,1024]{2,0,1:T(1,128)} %get-tuple-element.187) | copy-start | bytes 12292
  36.0 8.1 %copy-start.36 = (f32[1,1,1024]{2,0,1:T(1,128)S(1)}, f32[1,1,1024]{2,0,1:T(1,128)}, u32[]{:S(2)}) copy-start(f32[1,1,1024]{2,0,1:T(1,128)} %get-tuple-element.188) | copy-start | bytes 12292
  36.0 8.1 %copy-start.38 = (f32[1,1,1024]{2,0,1:T(1,128)S(1)}, f32[1,1,1024]{2,0,1:T(1,128)}, u32[]{:S(2)}) copy-start(f32[1,1,1024]{2,0,1:T(1,128)} %get-tuple-element.189) | copy-start | bytes 12292
  36.0 8.1 %copy-start.40 = (f32[1,1,1024]{2,0,1:T(1,128)S(1)}, f32[1,1,1024]{2,0,1:T(1,128)}, u32[]{:S(2)}) copy-start(f32[1,1,1024]{2,0,1:T(1,128)} %get-tuple-element.190) | copy-start | bytes 12292
  36.0 8.1 %copy-start.42 = (f32[1,1,1024]{2,0,1:T(1,128)S(1)}, f32[1,1,1024]{2,0,1:T(1,128)}, u32[]{:S(2)}) copy-start(f32[1,1,1024]{2,0,1:T(1,128)} %get-tuple-element.191) | copy-start | bytes 12292
  36.0 8.1 %copy-start.44 = (f32[1,1,1024]{2,0,1:T(1,128)S(1)}, f32[1,1,1024]{2,0,1:T(1,128)}, u32[]{:S(2)}) copy-start(f32[1,1,1024]{2,0,1:T(1,128)} %get-tuple-element.192) | copy-start | bytes 12292
  59.5 13.3 %collective-permute-start.2 = (bf16[1024,256]{1,0:T(8,128)(2,1)}, bf16[1024,256]{1,0:T(8,128)(2,1)S(1)}, u32[]{:S(2)}, u32[]{:S(2)}) collective-permute-start(bf16[1024,256]{1,0:T(8,128)(2,1)} %get-tuple-element.78), channel_id=1, source_target_pairs={{0,8},{8,16},{16,24},{24,28},{28,20},{20,12},{12,4},{4,0},{1,9},{9... | collective-permute-start | bytes 1572872 | tf_op jit(solution)/shard_map/ppermute | solution.py:219
  61.1 12.9 %collective-permute-start.3 = (bf16[1024,256]{1,0:T(8,128)(2,1)S(1)}, bf16[1024,256]{1,0:T(8,128)(2,1)}, u32[]{:S(2)}, u32[]{:S(2)}) collective-permute-start(bf16[1024,256]{1,0:T(8,128)(2,1)S(1)} %get-tuple-element.79), channel_id=1, source_target_pairs={{8,0},{16,8},{24,16},{28,24},{20,28},{12,20},{4,12},{0,4},{9,1},{1... | collective-permute-start | bytes 1572872 | tf_op jit(solution)/shard_map/ppermute | solution.py:220
  76.6 11.5 %copy-start.1 = (f32[512,1024]{1,0:T(8,128)S(1)}, f32[512,1024]{1,0:T(8,128)}, u32[]{:S(2)}) copy-start(f32[512,1024]{1,0:T(8,128)} %shard_map.110) | copy-start | bytes 6291460
  76.6 21.9 %collective-permute-start.4 = (bf16[1024,256]{1,0:T(8,128)(2,1)}, bf16[1024,256]{1,0:T(8,128)(2,1)}, u32[]{:S(2)}, u32[]{:S(2)}) collective-permute-start(bf16[1024,256]{1,0:T(8,128)(2,1)} %get-tuple-element.83), channel_id=1, source_target_pairs={{0,8},{8,16},{16,24},{24,28},{28,20},{20,12},{12,4},{4,0},{1,9},{9... | collective-permute-start | bytes 1572872 | tf_op jit(solution)/shard_map/ppermute | solution.py:219
  78.2 20.3 %collective-permute-start.5 = (bf16[1024,256]{1,0:T(8,128)(2,1)}, bf16[1024,256]{1,0:T(8,128)(2,1)}, u32[]{:S(2)}, u32[]{:S(2)}) collective-permute-start(bf16[1024,256]{1,0:T(8,128)(2,1)} %get-tuple-element.84), channel_id=1, source_target_pairs={{8,0},{16,8},{24,16},{28,24},{20,28},{12,20},{4,12},{0,4},{9,1},{1... | collective-permute-start | bytes 1572872 | tf_op jit(solution)/shard_map/ppermute | solution.py:220
  90.2 8.3 %collective-permute-start.6 = (bf16[128,1024]{1,0:T(8,128)(2,1)S(1)}, bf16[128,1024]{1,0:T(8,128)(2,1)S(1)}, u32[]{:S(2)}, u32[]{:S(2)}) collective-permute-start(bf16[128,1024]{1,0:T(8,128)(2,1)S(1)} %slice.390), channel_id=1, source_target_pairs={{4,0},{8,4},{12,8},{16,12},{20,16},{24,20},{28,24},{5,1},{9,5},{13... | collective-permute-start | bytes 786440 | tf_op jit(solution)/shard_map/ppermute | solution.py:13
  100.4 10.6 %collective-permute-start.7 = (bf16[1024,256]{1,0:T(8,128)(2,1)S(1)}, bf16[1024,256]{1,0:T(8,128)(2,1)S(1)}, u32[]{:S(2)}, u32[]{:S(2)}) collective-permute-start(bf16[1024,256]{1,0:T(8,128)(2,1)S(1)} %get-tuple-element.91), channel_id=1, source_target_pairs={{0,8},{8,16},{16,24},{24,28},{28,20},{20,12},{12,4},{4,0},{1,9},{9... | collective-permute-start | bytes 1572872 | tf_op jit(solution)/shard_map/ppermute | solution.py:219
  102.1 10.2 %collective-permute-start.8 = (bf16[1024,256]{1,0:T(8,128)(2,1)S(1)}, bf16[1024,256]{1,0:T(8,128)(2,1)S(1)}, u32[]{:S(2)}, u32[]{:S(2)}) collective-permute-start(bf16[1024,256]{1,0:T(8,128)(2,1)S(1)} %get-tuple-element.92), channel_id=1, source_target_pairs={{8,0},{16,8},{24,16},{28,24},{20,28},{12,20},{4,12},{0,4},{9,1},{1... | collective-permute-start | bytes 1572872 | tf_op jit(solution)/shard_map/ppermute | solution.py:220
  114.7 23.5 %collective-permute-start.10 = (bf16[1024,256]{1,0:T(8,128)(2,1)}, bf16[1024,256]{1,0:T(8,128)(2,1)}, u32[]{:S(2)}, u32[]{:S(2)}) collective-permute-start(bf16[1024,256]{1,0:T(8,128)(2,1)} %get-tuple-element.103), channel_id=1, source_target_pairs={{8,0},{16,8},{24,16},{28,24},{20,28},{12,20},{4,12},{0,4},{9,1},{1... | collective-permute-start | bytes 1572872 | tf_op jit(solution)/shard_map/ppermute | solution.py:220
  115.1 23.1 %collective-permute-start.9 = (bf16[1024,256]{1,0:T(8,128)(2,1)}, bf16[1024,256]{1,0:T(8,128)(2,1)}, u32[]{:S(2)}, u32[]{:S(2)}) collective-permute-start(bf16[1024,256]{1,0:T(8,128)(2,1)} %get-tuple-element.102), channel_id=1, source_target_pairs={{0,8},{8,16},{16,24},{24,28},{28,20},{20,12},{12,4},{4,0},{1,9},{9... | collective-permute-start | bytes 1572872 | tf_op jit(solution)/shard_map/ppermute | solution.py:219
  129.4 12.7 %copy-start.33 = (f32[1,1,1024]{2,0,1:T(1,128)S(1)}, f32[1,1,1024]{2,0,1:T(1,128)}, u32[]{:S(2)}) copy-start(f32[1,1,1024]{2,0,1:T(1,128)} %get-tuple-element.174) | copy-start | bytes 12292
  129.4 12.7 %copy-start.35 = (f32[1,1,1024]{2,0,1:T(1,128)S(1)}, f32[1,1,1024]{2,0,1:T(1,128)}, u32[]{:S(2)}) copy-start(f32[1,1,1024]{2,0,1:T(1,128)} %get-tuple-element.187) | copy-start | bytes 12292
  129.4 12.7 %copy-start.37 = (f32[1,1,1024]{2,0,1:T(1,128)S(1)}, f32[1,1,1024]{2,0,1:T(1,128)}, u32[]{:S(2)}) copy-start(f32[1,1,1024]{2,0,1:T(1,128)} %get-tuple-element.188) | copy-start | bytes 12292
  129.4 12.7 %copy-start.39 = (f32[1,1,1024]{2,0,1:T(1,128)S(1)}, f32[1,1,1024]{2,0,1:T(1,128)}, u32[]{:S(2)}) copy-start(f32[1,1,1024]{2,0,1:T(1,128)} %get-tuple-element.189) | copy-start | bytes 12292
  129.4 12.7 %copy-start.41 = (f32[1,1,1024]{2,0,1:T(1,128)S(1)}, f32[1,1,1024]{2,0,1:T(1,128)}, u32[]{:S(2)}) copy-start(f32[1,1,1024]{2,0,1:T(1,128)} %get-tuple-element.190) | copy-start | bytes 12292
  129.5 12.7 %copy-start.43 = (f32[1,1,1024]{2,0,1:T(1,128)S(1)}, f32[1,1,1024]{2,0,1:T(1,128)}, u32[]{:S(2)}) copy-start(f32[1,1,1024]{2,0,1:T(1,128)} %get-tuple-element.191) | copy-start | bytes 12292
  129.5 12.7 %copy-start.45 = (f32[1,1,1024]{2,0,1:T(1,128)S(1)}, f32[1,1,1024]{2,0,1:T(1,128)}, u32[]{:S(2)}) copy-start(f32[1,1,1024]{2,0,1:T(1,128)} %get-tuple-element.192) | copy-start | bytes 12292
  131.5 6.7 %collective-permute-start.11 = (bf16[3,6,1024]{2,1,0:T(8,128)(2,1)S(1)}, bf16[3,6,1024]{2,1,0:T(8,128)(2,1)S(1)}, u32[]{:S(2)}, u32[]{:S(2)}) collective-permute-start(bf16[3,6,1024]{2,1,0:T(8,128)(2,1)S(1)} %pad_maximum_fusion.10), channel_id=1, source_target_pairs={{4,0},{8,4},{12,8},{16,12},{20,16},{24,20},{28,24},{5,1},{9,5},{13... | collective-permute-start | bytes 110600 | tf_op jit(solution)/shard_map/ppermute | solution.py:13
  133.3 8.8 %copy-start.4 = (f32[512,1024]{1,0:T(8,128)S(1)}, f32[512,1024]{1,0:T(8,128)}, u32[]{:S(2)}) copy-start(f32[512,1024]{1,0:T(8,128)} %get-tuple-element.116) | copy-start | bytes 6291460
  140.0 9.8 %collective-permute-start.12 = (bf16[1024,256]{1,0:T(8,128)(2,1)S(1)}, bf16[1024,256]{1,0:T(8,128)(2,1)S(1)}, u32[]{:S(2)}, u32[]{:S(2)}) collective-permute-start(bf16[1024,256]{1,0:T(8,128)(2,1)S(1)} %get-tuple-element.114), channel_id=1, source_target_pairs={{0,8},{8,16},{16,24},{24,28},{28,20},{20,12},{12,4},{4,0},{1,9},{9... | collective-permute-start | bytes 1572872 | tf_op jit(solution)/shard_map/ppermute | solution.py:219
  141.4 9.7 %collective-permute-start.13 = (bf16[1024,256]{1,0:T(8,128)(2,1)S(1)}, bf16[1024,256]{1,0:T(8,128)(2,1)S(1)}, u32[]{:S(2)}, u32[]{:S(2)}) collective-permute-start(bf16[1024,256]{1,0:T(8,128)(2,1)S(1)} %get-tuple-element.115), channel_id=1, source_target_pairs={{8,0},{16,8},{24,16},{28,24},{20,28},{12,20},{4,12},{0,4},{9,1},{1... | collective-permute-start | bytes 1572872 | tf_op jit(solution)/shard_map/ppermute | solution.py:220
  145.1 10.7 %copy-start.3 = (f32[512,1024]{1,0:T(8,128)S(1)}, f32[512,1024]{1,0:T(8,128)}, u32[]{:S(2)}) copy-start(f32[512,1024]{1,0:T(8,128)} %copy-done.2) | copy-start | bytes 6291460
  145.2 10.7 %copy-start.25 = (f32[1,1,1024]{2,0,1:T(1,128)S(1)}, f32[1,1,1024]{2,0,1:T(1,128)}, u32[]{:S(2)}) copy-start(f32[1,1,1024]{2,0,1:T(1,128)} %copy-done.24) | copy-start | bytes 12292
  145.2 10.7 %copy-start.26 = (f32[1,1,1024]{2,0,1:T(1,128)S(1)}, f32[1,1,1024]{2,0,1:T(1,128)}, u32[]{:S(2)}) copy-start(f32[1,1,1024]{2,0,1:T(1,128)} %get-tuple-element.176) | copy-start | bytes 12292
  145.2 10.7 %copy-start.27 = (f32[1,1,1024]{2,0,1:T(1,128)S(1)}, f32[1,1,1024]{2,0,1:T(1,128)}, u32[]{:S(2)}) copy-start(f32[1,1,1024]{2,0,1:T(1,128)} %get-tuple-element.177) | copy-start | bytes 12292
  145.2 10.8 %copy-start.28 = (f32[1,1,1024]{2,0,1:T(1,128)S(1)}, f32[1,1,1024]{2,0,1:T(1,128)}, u32[]{:S(2)}) copy-start(f32[1,1,1024]{2,0,1:T(1,128)} %get-tuple-element.178) | copy-start | bytes 12292
  145.2 10.8 %copy-start.29 = (f32[1,1,1024]{2,0,1:T(1,128)S(1)}, f32[1,1,1024]{2,0,1:T(1,128)}, u32[]{:S(2)}) copy-start(f32[1,1,1024]{2,0,1:T(1,128)} %get-tuple-element.179) | copy-start | bytes 12292
  145.2 10.8 %copy-start.30 = (f32[1,1,1024]{2,0,1:T(1,128)S(1)}, f32[1,1,1024]{2,0,1:T(1,128)}, u32[]{:S(2)}) copy-start(f32[1,1,1024]{2,0,1:T(1,128)} %get-tuple-element.193) | copy-start | bytes 12292
  145.2 10.8 %copy-start.31 = (f32[1,1,1024]{2,0,1:T(1,128)S(1)}, f32[1,1,1024]{2,0,1:T(1,128)}, u32[]{:S(2)}) copy-start(f32[1,1,1024]{2,0,1:T(1,128)} %get-tuple-element.194) | copy-start | bytes 12292
  152.7 13.0 %collective-permute-start.14 = (bf16[1024,256]{1,0:T(8,128)(2,1)S(1)}, bf16[1024,256]{1,0:T(8,128)(2,1)S(1)}, u32[]{:S(2)}, u32[]{:S(2)}) collective-permute-start(bf16[1024,256]{1,0:T(8,128)(2,1)S(1)} %get-tuple-element.126), channel_id=1, source_target_pairs={{0,8},{8,16},{16,24},{24,28},{28,20},{20,12},{12,4},{4,0},{1,9},{9... | collective-permute-start | bytes 1572872 | tf_op jit(solution)/shard_map/ppermute | solution.py:219
  155.9 12.6 %collective-permute-start.15 = (bf16[1024,256]{1,0:T(8,128)(2,1)S(1)}, bf16[1024,256]{1,0:T(8,128)(2,1)S(1)}, u32[]{:S(2)}, u32[]{:S(2)}) collective-permute-start(bf16[1024,256]{1,0:T(8,128)(2,1)S(1)} %get-tuple-element.127), channel_id=1, source_target_pairs={{8,0},{16,8},{24,16},{28,24},{20,28},{12,20},{4,12},{0,4},{9,1},{1... | collective-permute-start | bytes 1572872 | tf_op jit(solution)/shard_map/ppermute | solution.py:220
  169.9 9.2 %collective-permute-start.16 = (bf16[1024,256]{1,0:T(8,128)(2,1)S(1)}, bf16[1024,256]{1,0:T(8,128)(2,1)S(1)}, u32[]{:S(2)}, u32[]{:S(2)}) collective-permute-start(bf16[1024,256]{1,0:T(8,128)(2,1)S(1)} %get-tuple-element.137), channel_id=1, source_target_pairs={{0,8},{8,16},{16,24},{24,28},{28,20},{20,12},{12,4},{4,0},{1,9},{9... | collective-permute-start | bytes 1572872 | tf_op jit(solution)/shard_map/ppermute | solution.py:219
  170.8 9.2 %collective-permute-start.17 = (bf16[1024,256]{1,0:T(8,128)(2,1)S(1)}, bf16[1024,256]{1,0:T(8,128)(2,1)S(1)}, u32[]{:S(2)}, u32[]{:S(2)}) collective-permute-start(bf16[1024,256]{1,0:T(8,128)(2,1)S(1)} %get-tuple-element.138), channel_id=1, source_target_pairs={{8,0},{16,8},{24,16},{28,24},{20,28},{12,20},{4,12},{0,4},{9,1},{1... | collective-permute-start | bytes 1572872 | tf_op jit(solution)/shard_map/ppermute | solution.py:220
  (18 other events, 112.8 us)
Sparse Core Ops, SparseCore 0:
  9.6 37.1 all-gather.1
  71.2 44.8 reduce-scatter.1

commit v8 on v7

--- a/solution.py
+++ b/solution.py
@@ -88,17 +88,25 @@
     tap_count = filter_taps.shape[1]
     tap_span = feature_taps.shape[0]
     full_cotangent = lax.all_gather(cotangent, "tp", axis=0, tiled=True)
-    inputs = (query_in, key_in, value_in)
-    before = passed_along(
-        jnp.stack([rows[row_count - tap_span + 1 :] for rows in inputs], axis=0), "seq", 1
-    )
-    query_feat, key_feat, value_feat = (
-        featurize(jnp.concatenate([before[i], inputs[i]], axis=0), feature_taps[:, i], row_count)
-        for i in range(3)
-    )
-    mix_rows = (key_feat * value_feat).astype(jnp.bfloat16)
-    mix_before = passed_along(mix_rows[row_count - tap_count :], "seq", 1)
-    padded_mix = jnp.concatenate([mix_before, mix_rows], axis=0)
+    reach = tap_count + tap_span - 1
+    query_before = passed_along(query_in[row_count - tap_span + 1 :], "seq", 1)
+    pair_before = passed_along(
+        jnp.stack([key_in[row_count - reach :], value_in[row_count - reach :]], axis=0), "seq", 1
+    )
+    query_feat = featurize(
+        jnp.concatenate([query_before, query_in], axis=0), feature_taps[:, 0], row_count
+    )
+    key_wide, value_wide = (
+        featurize(
+            jnp.concatenate([pair_before[i], rows], axis=0),
+            feature_taps[:, i + 1],
+            row_count + tap_count,
+        )
+        for i, rows in enumerate((key_in, value_in))
+    )
+    padded_mix = (key_wide * value_wide).astype(jnp.bfloat16)
+    key_feat = key_wide[tap_count:]
+    value_feat = value_wide[tap_count:]
     long_conv = band_mix(padded_mix, band_table(filter_taps))
     gated_rows = (query_feat * long_conv).astype(jnp.bfloat16)
     seq_count = lax.axis_size("seq")
@@ -127,13 +135,13 @@
         grad_conv = (grad_gated * query_feat).astype(jnp.bfloat16)
         grad_query = grad_gated * long_conv
         conv_after = passed_along(grad_conv[:tap_count], "seq", -1)
-        return (grad_conv, conv_after, grad_query)
+        return (grad_conv, conv_after, grad_query, out_weight)
 
     def table_back(state):
         return state + (band_table(filter_taps, reverse=True),)
 
     def filter_back(state):
-        grad_conv, conv_after, grad_query, table = state
+        grad_conv, conv_after, grad_query, out_weight, table = state
         grad_mix = band_mix(jnp.concatenate([grad_conv, conv_after], axis=0), table)
         grad_features = (grad_query, grad_mix * value_feat, grad_mix * key_feat)
         features_after = passed_along(
@@ -141,7 +149,7 @@
             "seq",
             -1,
         )
-        return (grad_features, features_after)
+        return (grad_features, features_after, out_weight)
 
     def feature_back(first, last):
         def stage(state):
@@ -167,17 +175,20 @@
         grad_features, features_after = state
         return (grad_features, features_after, ())
 
+    def start_back(out_weight):
+        return out_weight
+
     stages = [
-        project,
+        start_back,
         gate_back,
         table_back,
         filter_back,
-        lambda state: feature_back(0, 1)(unpack(state)),
-        feature_back(1, 3),
-        finish,
+        lambda state: (project((gated_rows, state[2])), state[:2])[1],
+        lambda state: feature_back(0, 2)(unpack(state)),
+        lambda state: finish(feature_back(2, 3)(state)),
     ]
     state, summed_grad = ring_reduce_scatter(
-        gated_rows, full_cotangent, grad_scale, ring, stages, (gated_rows, out_weight)
+        gated_rows, full_cotangent, grad_scale, ring, stages, out_weight
     )
     return (projected[0],) + state + (summed_grad,)
 
@@ -193,36 +204,48 @@
     place = sum(jnp.where(seq_index == member, place_of[member], 0) for member in range(count))
     forward = [(ring[i], ring[(i + 1) % count]) for i in range(count)]
     backward = [(ring[(i + 1) % count], ring[i]) for i in range(count)]
-    local_grad = (
-        lax.dot_general(
-            gated_rows, full_cotangent, (((0,), (0,)), ((), ())), preferred_element_type=jnp.float32
-        )
-        * grad_scale
-    ).astype(jnp.bfloat16)
-
-    def contribution(step, direction):
+    def product(rows, columns):
+        return (
+            lax.dot_general(
+                rows, columns, (((0,), (0,)), ((), ())), preferred_element_type=jnp.float32
+            )
+            * grad_scale
+        ).astype(jnp.bfloat16)
+
+    def column_of(step, direction):
         position = (place - direction * (1 + step)) % count
         owner = sum(jnp.where(position == i, ring[i], 0) for i in range(count))
-        first = owner * width + (0 if direction == 1 else half)
-        return lax.dynamic_slice_in_dim(local_grad, first, half, 1)
-
-    ahead = contribution(0, 1)
-    behind = contribution(0, -1)
+        return owner * width + (0 if direction == 1 else half)
+
+    def first_slice(direction):
+        columns = lax.dynamic_slice_in_dim(full_cotangent, column_of(0, direction), half, 1)
+        return product(gated_rows, columns).astype(jnp.float32)
+
+    ahead = first_slice(1)
+    behind = first_slice(-1)
     stages = list(stages)
+    local_grad = None
     for step in range(1, count):
         sent_ahead = ahead.astype(jnp.bfloat16)
         sent_behind = behind.astype(jnp.bfloat16)
-        if stages:
-            sent_ahead, sent_behind, state = lax.optimization_barrier(
-                (sent_ahead, sent_behind, state)
-            )
+        sent_ahead, sent_behind, state, rows = lax.optimization_barrier(
+            (sent_ahead, sent_behind, state, gated_rows)
+        )
         ahead = lax.ppermute(sent_ahead, "seq", forward)
         behind = lax.ppermute(sent_behind, "seq", backward)
+        if local_grad is None:
+            local_grad = product(rows, full_cotangent)
         if stages:
             state = stages.pop(0)(state)
-            ahead, behind, state = lax.optimization_barrier((ahead, behind, state))
-        ahead = ahead.astype(jnp.float32) + contribution(step, 1).astype(jnp.float32)
-        behind = behind.astype(jnp.float32) + contribution(step, -1).astype(jnp.float32)
+        ahead, behind, state, local_grad = lax.optimization_barrier(
+            (ahead, behind, state, local_grad)
+        )
+        ahead = ahead.astype(jnp.float32) + lax.dynamic_slice_in_dim(
+            local_grad, column_of(step, 1), half, 1
+        ).astype(jnp.float32)
+        behind = behind.astype(jnp.float32) + lax.dynamic_slice_in_dim(
+            local_grad, column_of(step, -1), half, 1
+        ).astype(jnp.float32)
     while stages:
         state = stages.pop(0)(state)
     return state, jnp.concatenate([ahead, behind], axis=1).astype(jnp.bfloat16)

time: 191 us -> 201 us (1.052)
  other arithmetic: 41 us -> 48.1 us
  waiting for transfers between devices: 38.7 us -> 43.9 us
  local copies, waits for them, and re-layouts: 17.8 us -> 15.1 us
  matrix products: 33.8 us -> 36.1 us
    convert_element_type x1, other arithmetic: 5.82 us -> 12.3 us  [per_device(): padded_mix = (key_wide * value_wide).astype(jnp.bfloat16)]
    dot_general x1 -> x3, matrix products: 7.08 us -> 10.4 us  [product(): lax.dot_general(rows, columns, (((0,), (0,)), ((), ())), preferred_elemen...]
    slice x2, local copies, waits for them, and re-layouts: 3.3 us -> 0.07 us  [featurize(): feature_taps[offset]]
    ppermute x7, waiting for transfers between devices: 18.8 us -> 22 us  [ring_reduce_scatter(): ahead = lax.ppermute(sent_ahead, 'seq', forward)]
    dot_general x1, matrix products: 9.44 us -> 6.35 us  [gate_back(): lax.dot_general(full_cotangent, out_weight, (((1,), (1,)), ((), ())), pre...]
    convert_element_type x1, other arithmetic: 4.02 us -> 6.83 us  [per_device(): gated_rows = (query_feat * long_conv).astype(jnp.bfloat16)]
    ppermute x7, starting transfers between devices: 12 us -> 9.85 us  [ring_reduce_scatter(): ahead = lax.ppermute(sent_ahead, 'seq', forward)]
    reduce_scatter x1, waiting for transfers between devices: 0.01 us -> 2.11 us  [project(): lax.psum_scatter(jnp.dot(gated_rows, out_weight, preferred_element_type=j...]
  transfers between devices with their start and end apart: 20 -> 20, of which waited for: 12 -> 12; matrix products, arithmetic and copies ran while one was open for 42% -> 37% of each run, Pallas kernels for 8% -> 4%
where the time goes in v8:
time: 201 us; the launch traced here: 200 us
  other arithmetic  48.1 us (24%)
  waiting for transfers between devices  43.9 us (22%)
  matrix products  36.1 us (18%)
  starting transfers between devices  26.2 us (13%)
  Pallas kernels  15.8 us (8%)
  between operations  15.2 us (8%)
  local copies, waits for them, and re-layouts  15.1 us (8%)
    ppermute x7, waiting for transfers between devices, ring_reduce_scatter(): ahead = lax.ppermute(sent_ahead, 'seq', forward)  22 us
    pallas_call x2, Pallas kernels, band_mix(): pl.pallas_call(body, grid=(channels // lane_tile,), in_specs=[pl.BlockSpe...  15.8 us
    ppermute x4, waiting for transfers between devices, passed_along(): lax.ppermute(value, axis, [(source, source + steps) for source in range(l...  13.3 us
    convert_element_type x1, other arithmetic, per_device(): padded_mix = (key_wide * value_wide).astype(jnp.bfloat16)  12.3 us
    convert_element_type x6, other arithmetic, ring_reduce_scatter(): sent_behind = behind.astype(jnp.bfloat16)  11.1 us
    ppermute x4, starting transfers between devices, passed_along(): lax.ppermute(value, axis, [(source, source + steps) for source in range(l...  10.9 us
    dot_general x3, matrix products, product(): lax.dot_general(rows, columns, (((0,), (0,)), ((), ())), preferred_elemen...  10.4 us
    unnamed x124, local copies, waits for them, and re-layouts  10.1 us
  transfers between devices with their start and end apart: 20, of which 12 were waited for; matrix products, arithmetic and copies ran while one was open for 37% of the time, Pallas kernels for 4%

profile of v8, /device:TPU:0, one launch (start us, length us, event | category | flops | bytes accessed | tf_op | source)
XLA Modules:
  0.0 200.4 jit_solution(9747966762090185378)
XLA Ops:
  8.0 1.2 slice_bitcast_fusion
  9.8 4.9 %collective-permute-start.1 = (bf16[2,134,1024]{2,0,1:T(2,128)(2,1)S(1)}, bf16[2,134,1024]{2,0,1:T(2,128)(2,1)S(1)}, u32[]{:S(2)}, u32[]{:S(2)}) collective-permute-start(bf16[2,134,1024]{2,0,1:T(2,128)(2,1)S(1)} %copy.16), channel_id=1, source_target_pairs={{0,4},{4,8},{8,12},{12,16},{16,20},{20,24},{24,28},{1,5},{5,9},{9,... | collective-permute-start | bytes 1646600 | tf_op jit(solution)/shard_map/ppermute | solution.py:13
  15.4 3.4 %collective-permute-start = (bf16[6,1024]{1,0:T(8,128)(2,1)S(1)}, bf16[6,1024]{1,0:T(8,128)(2,1)S(1)}, u32[]{:S(2)}, u32[]{:S(2)}) collective-permute-start(bf16[6,1024]{1,0:T(8,128)(2,1)S(1)} %slice.293), channel_id=1, source_target_pairs={{0,4},{4,8},{8,12},{12,16},{16,20},{20,24},{24,28},{1,5},{5,9},{9,... | collective-permute-start | bytes 36872 | tf_op jit(solution)/shard_map/ppermute | solution.py:13
  19.3 5.9 %convolution_convert_fusion.1 = bf16[32768,64]{0,1:T(8,128)(2,1)} fusion(bf16[64,128]{1,0:T(8,128)(2,1)S(1)} %copy-done, s32[32768]{0:T(1024)S(1)} %get-tuple-element.203), kind=kOutput, calls=%fused_computation.1 | convolution fusion | flops 543162368 | bytes 4341760 | tf_op jit(solution)/shard_map/dot_general | solution.py:46
  25.2 5.4 %copy.24 = bf16[8,8,128,256]{3,2,1,0:T(8,128)(2,1)} copy(bf16[8,8,128,256]{3,1,2,0:T(8,128)(2,1)} %bitcast.76) | data formatting | bytes 8388608
  31.9 12.3 %multiply_convert_fusion.1 = (bf16[640,1024]{1,0:T(8,128)(2,1)}, f32[640,1024]{1,0:T(8,128)S(1)}, f32[640,1024]{1,0:T(8,128)}) fusion(bf16[512,1024]{1,0:T(8,128)(2,1)} %param.9, bf16[134,1024]{1,0:T(8,128)(2,1)S(1)} %bitcast.78, f32[1024]{0:T(1024)S(1)} %bitcast.109, f32[1024]{0:T(1024)S(1)} %bitcast.107, f32[1024]{0:T(1024)S(1)} %bitcast.83, ...), kind=kLoop, calls=%fused_computation.40 | loop fusion | flops 55050240 | bytes 9256960 | tf_op jit(solution)/shard_map/convert_element_type | solution.py:107
  44.3 7.9 %shard_map.110 = f32[512,1024]{1,0:T(8,128)} custom-call(bf16[64,128,256]{2,1,0:T(8,128)(2,1)} %bitcast.74, bf16[640,1024]{1,0:T(8,128)(2,1)} %get-tuple-element.179.rows_ref), custom_call_target="tpu_custom_call" | custom-call | tf_op jit(solution)/shard_map/pallas_call | solution.py:74
  52.3 6.8 %multiply_convert_fusion.2 = (bf16[512,1024]{1,0:T(8,128)(2,1)}, f32[512,1024]{1,0:T(8,128)}) fusion(f32[512,1024]{1,0:T(8,128)} %shard_map.110, bf16[512,1024]{1,0:T(8,128)(2,1)} %param.7, bf16[6,1024]{1,0:T(8,128)(2,1)S(1)} %collective-permute-done, f32[1024]{0:T(1024)S(1)} %bitcast.113, f32[1024]{0:T(1024)S(1)} %bitcast.115, f32[1024]{0:T(1024)S(1)} %bitcast.117, ...), kind=kLoop, calls=%fused_computation.114 | loop fusion | flops 20971520 | bytes 6332416 | tf_op jit(solution)/shard_map/convert_element_type | solution.py:111
  59.2 1.8 fusion.70
  61.1 1.6 fusion.69
  62.7 1.8 collective-permute-start.2
  64.9 7.0 %multiply_convert_fusion = bf16[1024,4096]{1,0:T(8,128)(2,1)S(1)} fusion(bf16[512,1024]{1,0:T(8,128)(2,1)S(1)} %copy-done.11, bf16[512,4096]{1,0:T(8,128)(2,1)} %all-gather.2.cloned.1.call-done), kind=kOutput, calls=%fused_computation.3 | convolution fusion | flops 4303355904 | bytes 13631488 | tf_op jit(solution)/shard_map/dot_general | solution.py:209
  71.9 4.1 %collective-permute-done.2 = bf16[1024,256]{1,0:T(8,128)(2,1)S(1)} collective-permute-done((bf16[1024,256]{1,0:T(8,128)(2,1)S(1)}, bf16[1024,256]{1,0:T(8,128)(2,1)S(1)}, u32[]{:S(2)}, u32[]{:S(2)}) %collective-permute-start.2) | collective-permute-done | bytes 524320 | tf_op jit(solution)/shard_map/ppermute | solution.py:234
  76.0 1.3 collective-permute-done.3
  77.3 1.2 add_convert_fusion.12
  78.5 1.6 collective-permute-start.4
  80.5 6.3 %fusion.87 = f32[1024,512]{0,1:T(8,128)S(1)} fusion(bf16[1024,4096]{1,0:T(8,128)(2,1)S(1)} %bitcast.126, bf16[512,4096]{1,0:T(8,128)(2,1)} %all-gather.2.cloned.1.call-done), kind=kOutput, calls=%fused_computation.193 | convolution fusion | flops 4294967296 | bytes 14680064 | tf_op jit(solution)/shard_map/dot_general | solution.py:132
  86.9 2.2 %bitcast_multiply_fusion = (f32[512,1024]{1,0:T(8,128)}, bf16[512,1024]{1,0:T(8,128)(2,1)S(1)}) fusion(f32[512,1024]{1,0:T(8,128)S(1)} %copy-done.1, f32[1024,512]{0,1:T(8,128)S(1)} %fusion.87, f32[512,1024]{1,0:T(8,128)S(1)} %copy-done.7), kind=kLoop, calls=%fused_computation.111 | loop fusion | flops 1572864 | bytes 9437184 | tf_op jit(solution)/shard_map/mul | solution.py:136
  90.8 1.3 collective-permute-start.6
  92.2 7.1 %collective-permute-done.6 = bf16[128,1024]{1,0:T(8,128)(2,1)S(1)} collective-permute-done((bf16[128,1024]{1,0:T(8,128)(2,1)}, bf16[128,1024]{1,0:T(8,128)(2,1)S(1)}, u32[]{:S(2)}, u32[]{:S(2)}) %collective-permute-start.6) | collective-permute-done | bytes 262176 | tf_op jit(solution)/shard_map/ppermute | solution.py:13
  99.3 2.6 %add_convert_fusion.10 = (bf16[1024,256]{1,0:T(8,128)(2,1)S(1)}, bf16[1024,256]{1,0:T(8,128)(2,1)}) fusion(bf16[1024,256]{1,0:T(8,128)(2,1)} %collective-permute-done.5, bf16[1024,4096]{1,0:T(8,128)(2,1)} %copy-done.8, s32[]{:T(128)S(6)} %select_n.551, s32[]{:T(128)S(6)} %select_n.542, bf16[1024,256]{1,0:T(8,128)(2,1)} %collective-permute-done.4), kind=kLoop, calls=%fused_computation.163 | loop fusion | flops 2097152 | bytes 3145736 | tf_op jit(solution)/shard_map/convert_element_type | solution.py:230
  101.9 1.6 collective-permute-start.7
  103.9 3.9 %convolution_convert_fusion = bf16[32768,64]{0,1:T(8,128)(2,1)S(1)} fusion(bf16[64,128]{1,0:T(8,128)(2,1)S(1)} %copy-done, s32[32768]{0:T(1024)S(1)} %get-tuple-element.202), kind=kOutput, calls=%fused_computation | convolution fusion | flops 543162368 | bytes 4341760 | tf_op jit(solution)/shard_map/dot_general | solution.py:46
  107.8 3.2 %copy.26 = bf16[8,8,128,256]{3,2,1,0:T(8,128)(2,1)} copy(bf16[8,8,128,256]{3,1,2,0:T(8,128)(2,1)S(1)} %bitcast.77) | data formatting | bytes 8388608
  111.0 1.5 collective-permute-done.7
  113.5 2.6 %add_convert_fusion.8 = (bf16[1024,256]{1,0:T(8,128)(2,1)}, bf16[1024,256]{1,0:T(8,128)(2,1)S(1)}) fusion(bf16[1024,256]{1,0:T(8,128)(2,1)} %collective-permute-done.8, bf16[1024,4096]{1,0:T(8,128)(2,1)} %copy-done.8, s32[]{:T(128)S(6)} %select_n.569, s32[]{:T(128)S(6)} %select_n.560, bf16[1024,256]{1,0:T(8,128)(2,1)} %collective-permute-done.7), kind=kLoop, calls=%fused_computation.161 | loop fusion | flops 2097152 | bytes 3145736 | tf_op jit(solution)/shard_map/convert_element_type | solution.py:230
  116.1 1.2 pad_maximum_fusion.5.rows_ref
  117.3 7.9 %shard_map.111 = f32[512,1024]{1,0:T(8,128)} custom-call(bf16[64,128,256]{2,1,0:T(8,128)(2,1)} %bitcast.75, bf16[640,1024]{1,0:T(8,128)(2,1)} %pad_maximum_fusion.5.rows_ref), custom_call_target="tpu_custom_call" | custom-call | tf_op jit(solution)/shard_map/pallas_call | solution.py:74
  125.2 2.9 %slice_multiply_fusion = (f32[512,1024]{1,0:T(8,128)S(1)}, f32[512,1024]{1,0:T(8,128)S(1)}) fusion(f32[512,1024]{1,0:T(8,128)} %shard_map.111, f32[640,1024]{1,0:T(8,128)} %get-tuple-element.181, f32[640,1024]{1,0:T(8,128)S(1)} %get-tuple-element.180), kind=kLoop, calls=%fused_computation.109 | loop fusion | flops 1048576 | bytes 10485760 | tf_op jit(solution)/shard_map/mul | solution.py:146
  128.6 1.6 collective-permute-start.9
  131.0 1.3 collective-permute-start.11
  132.4 6.2 %collective-permute-done.11 = bf16[3,6,1024]{2,1,0:T(8,128)(2,1)S(1)} collective-permute-done((bf16[3,6,1024]{2,1,0:T(8,128)(2,1)S(1)}, bf16[3,6,1024]{2,1,0:T(8,128)(2,1)S(1)}, u32[]{:S(2)}, u32[]{:S(2)}) %collective-permute-start.11) | collective-permute-done | bytes 36896 | tf_op jit(solution)/shard_map/ppermute | solution.py:13
  138.7 1.5 add_convert_fusion.6
  140.2 9.5 %convolution_convert_fusion.2 = bf16[512,4096]{1,0:T(8,128)(2,1)} fusion(bf16[512,1024]{1,0:T(8,128)(2,1)S(1)} %copy-done.12, bf16[1024,4096]{1,0:T(8,128)(2,1)} %param.12), kind=kOutput, calls=%fused_computation.7 | convolution fusion | flops 4297064448 | bytes 13631488 | tf_op jit(solution)/shard_map/dot_general | solution.py:121
  150.6 1.3 collective-permute-start.13
  151.8 9.1 %collective-permute-done.12 = bf16[1024,256]{1,0:T(8,128)(2,1)} collective-permute-done((bf16[1024,256]{1,0:T(8,128)(2,1)S(1)}, bf16[1024,256]{1,0:T(8,128)(2,1)}, u32[]{:S(2)}, u32[]{:S(2)}) %collective-permute-start.12) | collective-permute-done | bytes 524320 | tf_op jit(solution)/shard_map/ppermute | solution.py:234
  161.0 1.8 add_convert_fusion.4
  162.9 2.3 %collective-permute-start.15 = (bf16[1024,256]{1,0:T(8,128)(2,1)S(1)}, bf16[1024,256]{1,0:T(8,128)(2,1)S(1)}, u32[]{:S(2)}, u32[]{:S(2)}) collective-permute-start(bf16[1024,256]{1,0:T(8,128)(2,1)S(1)} %get-tuple-element.153), channel_id=1, source_target_pairs={{8,0},{16,8},{24,16},{28,24},{20,28},{12,20},{4,12},{0,4},{9,1},{1... | collective-permute-start | bytes 1572872 | tf_op jit(solution)/shard_map/ppermute | solution.py:235
  165.4 3.0 %fusion.23 = bf16[512,1024]{1,0:T(8,128)(2,1)} fusion(f32[6,1024]{1,0:T(8,128)S(1)} %get-tuple-element.225, f32[512,1024]{1,0:T(8,128)S(1)} %copy-done.5, f32[1024]{0:T(1024)S(1)} %bitcast.94, f32[1024]{0:T(1024)S(1)} %bitcast.96, f32[1024]{0:T(1024)S(1)} %bitcast.98, f32[1024]{0:T(1024)S(1)} %bitcast.100, f32[1024]{0:T(1024)S(1)} %bitcast.102, ...), kind=kLoop, calls=%fused_computation.64 | loop fusion | flops 10485760 | bytes 3198976 | tf_op jit(solution)/shard_map/convert_element_type | solution.py:164
  168.4 3.0 %fusion.40 = bf16[512,1024]{1,0:T(8,128)(2,1)} fusion(f32[6,1024]{1,0:T(8,128)S(1)} %get-tuple-element.226, f32[512,1024]{1,0:T(8,128)S(1)} %copy-done.6, f32[1024]{0:T(1024)S(1)} %bitcast.114, f32[1024]{0:T(1024)S(1)} %bitcast.116, f32[1024]{0:T(1024)S(1)} %bitcast.118, f32[1024]{0:T(1024)S(1)} %bitcast.120, f32[1024]{0:T(1024)S(1)} %bitcast.122, ...), kind=kLoop, calls=%fused_computation.81 | loop fusion | flops 10485760 | bytes 3198976 | tf_op jit(solution)/shard_map/convert_element_type | solution.py:164
  171.4 3.5 %collective-permute-done.14 = bf16[1024,256]{1,0:T(8,128)(2,1)S(1)} collective-permute-done((bf16[1024,256]{1,0:T(8,128)(2,1)S(1)}, bf16[1024,256]{1,0:T(8,128)(2,1)S(1)}, u32[]{:S(2)}, u32[]{:S(2)}) %collective-permute-start.14) | collective-permute-done | bytes 524320 | tf_op jit(solution)/shard_map/ppermute | solution.py:234
  175.9 1.5 add_convert_fusion.2
  177.4 2.4 %collective-permute-start.16 = (bf16[1024,256]{1,0:T(8,128)(2,1)S(1)}, bf16[1024,256]{1,0:T(8,128)(2,1)S(1)}, u32[]{:S(2)}, u32[]{:S(2)}) collective-permute-start(bf16[1024,256]{1,0:T(8,128)(2,1)S(1)} %get-tuple-element.165), channel_id=1, source_target_pairs={{0,8},{8,16},{16,24},{24,28},{28,20},{20,12},{12,4},{4,0},{1,9},{9... | collective-permute-start | bytes 1572872 | tf_op jit(solution)/shard_map/ppermute | solution.py:234
  179.9 3.0 %fusion.6 = bf16[512,1024]{1,0:T(8,128)(2,1)} fusion(f32[6,1024]{1,0:T(8,128)S(1)} %bitcast_convert_fusion, f32[512,1024]{1,0:T(8,128)S(1)} %copy-done.3, f32[1024]{0:T(1024)S(1)} %bitcast.110, f32[1024]{0:T(1024)S(1)} %bitcast.108, f32[1024]{0:T(1024)S(1)} %bitcast.84, f32[1024]{0:T(1024)S(1)} %bitcast.86, f32[1024]{0:T(1024)S(1)} %bitcast.88, ...), kind=kLoop, calls=%fused_computation.47 | loop fusion | flops 10485760 | bytes 3198976 | tf_op jit(solution)/shard_map/convert_element_type | solution.py:164
  182.9 3.8 %collective-permute-done.16 = bf16[1024,256]{1,0:T(8,128)(2,1)S(1)} collective-permute-done((bf16[1024,256]{1,0:T(8,128)(2,1)S(1)}, bf16[1024,256]{1,0:T(8,128)(2,1)S(1)}, u32[]{:S(2)}, u32[]{:S(2)}) %collective-permute-start.16) | collective-permute-done | bytes 524320 | tf_op jit(solution)/shard_map/ppermute | solution.py:234
  186.7 2.3 %collective-permute-done.17 = bf16[1024,256]{1,0:T(8,128)(2,1)S(1)} collective-permute-done((bf16[1024,256]{1,0:T(8,128)(2,1)S(1)}, bf16[1024,256]{1,0:T(8,128)(2,1)S(1)}, u32[]{:S(2)}, u32[]{:S(2)}) %collective-permute-start.17) | collective-permute-done | bytes 524320 | tf_op jit(solution)/shard_map/ppermute | solution.py:235
  189.0 1.5 add_convert_fusion.1
  191.5 2.1 %reduce-scatter.2.cloned.1.call-done = bf16[128,4096]{1,0:T(8,128)(2,1)} async-done(((bf16[512,4096]{1,0:T(8,128)(2,1)}), bf16[128,4096]{1,0:T(8,128)(2,1)}) %reduce-scatter.2.cloned.1.call-update) | async-done | bytes 1048592 | tf_op jit(solution)/shard_map/reduce_scatter | solution.py:120
  (161 shorter events, 12.2 us)
Async XLA Ops:
  7.2 52.0 %all-gather.2.cloned.1.call-start = ((), (), s32[]{:S(2)}) async-start(), calls=%async_computation.1 | async-start | bytes 5242880 | tf_op jit(solution)/shard_map/all_gather | solution.py:90
  7.9 185.7 %reduce-scatter.2.cloned.1.call-start = ((), (), s32[]{:S(2)}) async-start(), calls=%async_computation.2 | async-start | bytes 5242880 | tf_op jit(solution)/shard_map/reduce_scatter | solution.py:120
  9.8 21.2 %collective-permute-start.1 = (bf16[2,134,1024]{2,0,1:T(2,128)(2,1)S(1)}, bf16[2,134,1024]{2,0,1:T(2,128)(2,1)S(1)}, u32[]{:S(2)}, u32[]{:S(2)}) collective-permute-start(bf16[2,134,1024]{2,0,1:T(2,128)(2,1)S(1)} %copy.16), channel_id=1, source_target_pairs={{0,4},{4,8},{8,12},{12,16},{16,20},{20,24},{24,28},{1,5},{5,9},{9,... | collective-permute-start | bytes 1646600 | tf_op jit(solution)/shard_map/ppermute | solution.py:13
  15.4 36.8 %collective-permute-start = (bf16[6,1024]{1,0:T(8,128)(2,1)S(1)}, bf16[6,1024]{1,0:T(8,128)(2,1)S(1)}, u32[]{:S(2)}, u32[]{:S(2)}) collective-permute-start(bf16[6,1024]{1,0:T(8,128)(2,1)S(1)} %slice.293), channel_id=1, source_target_pairs={{0,4},{4,8},{8,12},{12,16},{16,20},{20,24},{24,28},{1,5},{5,9},{9,... | collective-permute-start | bytes 36872 | tf_op jit(solution)/shard_map/ppermute | solution.py:13
  30.7 13.5 %copy-start.38 = (f32[1,1,1024]{2,0,1:T(1,128)}, f32[1,1,1024]{2,0,1:T(1,128)S(1)}, u32[]{:S(2)}) copy-start(f32[1,1,1024]{2,0,1:T(1,128)S(1)} %get-tuple-element.223) | copy-start | bytes 12292
  30.7 13.5 %copy-start.40 = (f32[1,1,1024]{2,0,1:T(1,128)}, f32[1,1,1024]{2,0,1:T(1,128)S(1)}, u32[]{:S(2)}) copy-start(f32[1,1,1024]{2,0,1:T(1,128)S(1)} %get-tuple-element.224) | copy-start | bytes 12292
  30.7 13.5 %copy-start.14 = (f32[1,1,1024]{2,0,1:T(1,128)}, f32[1,1,1024]{2,0,1:T(1,128)S(1)}, u32[]{:S(2)}) copy-start(f32[1,1,1024]{2,0,1:T(1,128)S(1)} %get-tuple-element.205) | copy-start | bytes 12292
  30.7 13.5 %copy-start.16 = (f32[1,1,1024]{2,0,1:T(1,128)}, f32[1,1,1024]{2,0,1:T(1,128)S(1)}, u32[]{:S(2)}) copy-start(f32[1,1,1024]{2,0,1:T(1,128)S(1)} %get-tuple-element.206) | copy-start | bytes 12292
  30.8 13.5 %copy-start.18 = (f32[1,1,1024]{2,0,1:T(1,128)}, f32[1,1,1024]{2,0,1:T(1,128)S(1)}, u32[]{:S(2)}) copy-start(f32[1,1,1024]{2,0,1:T(1,128)S(1)} %get-tuple-element.207) | copy-start | bytes 12292
  30.8 13.5 %copy-start.20 = (f32[1,1,1024]{2,0,1:T(1,128)}, f32[1,1,1024]{2,0,1:T(1,128)S(1)}, u32[]{:S(2)}) copy-start(f32[1,1,1024]{2,0,1:T(1,128)S(1)} %get-tuple-element.208) | copy-start | bytes 12292
  30.8 13.5 %copy-start.22 = (f32[1,1,1024]{2,0,1:T(1,128)}, f32[1,1,1024]{2,0,1:T(1,128)S(1)}, u32[]{:S(2)}) copy-start(f32[1,1,1024]{2,0,1:T(1,128)S(1)} %get-tuple-element.209) | copy-start | bytes 12292
  30.8 13.5 %copy-start.24 = (f32[1,1,1024]{2,0,1:T(1,128)}, f32[1,1,1024]{2,0,1:T(1,128)S(1)}, u32[]{:S(2)}) copy-start(f32[1,1,1024]{2,0,1:T(1,128)S(1)} %get-tuple-element.210) | copy-start | bytes 12292
  30.8 13.5 %copy-start.26 = (f32[1,1,1024]{2,0,1:T(1,128)}, f32[1,1,1024]{2,0,1:T(1,128)S(1)}, u32[]{:S(2)}) copy-start(f32[1,1,1024]{2,0,1:T(1,128)S(1)} %get-tuple-element.211) | copy-start | bytes 12292
  30.8 13.5 %copy-start.28 = (f32[1,1,1024]{2,0,1:T(1,128)}, f32[1,1,1024]{2,0,1:T(1,128)S(1)}, u32[]{:S(2)}) copy-start(f32[1,1,1024]{2,0,1:T(1,128)S(1)} %get-tuple-element.212) | copy-start | bytes 12292
  30.9 21.4 %copy-start.42 = (f32[1,1,1024]{2,0,1:T(1,128)}, f32[1,1,1024]{2,0,1:T(1,128)S(1)}, u32[]{:S(2)}) copy-start(f32[1,1,1024]{2,0,1:T(1,128)S(1)} %get-tuple-element.204) | copy-start | bytes 12292
  30.9 21.4 %copy-start.44 = (f32[1,1,1024]{2,0,1:T(1,128)}, f32[1,1,1024]{2,0,1:T(1,128)S(1)}, u32[]{:S(2)}) copy-start(f32[1,1,1024]{2,0,1:T(1,128)S(1)} %get-tuple-element.217) | copy-start | bytes 12292
  30.9 21.4 %copy-start.46 = (f32[1,1,1024]{2,0,1:T(1,128)}, f32[1,1,1024]{2,0,1:T(1,128)S(1)}, u32[]{:S(2)}) copy-start(f32[1,1,1024]{2,0,1:T(1,128)S(1)} %get-tuple-element.218) | copy-start | bytes 12292
  30.9 21.4 %copy-start.48 = (f32[1,1,1024]{2,0,1:T(1,128)}, f32[1,1,1024]{2,0,1:T(1,128)S(1)}, u32[]{:S(2)}) copy-start(f32[1,1,1024]{2,0,1:T(1,128)S(1)} %get-tuple-element.219) | copy-start | bytes 12292
  30.9 21.4 %copy-start.50 = (f32[1,1,1024]{2,0,1:T(1,128)}, f32[1,1,1024]{2,0,1:T(1,128)S(1)}, u32[]{:S(2)}) copy-start(f32[1,1,1024]{2,0,1:T(1,128)S(1)} %get-tuple-element.220) | copy-start | bytes 12292
  30.9 21.4 %copy-start.52 = (f32[1,1,1024]{2,0,1:T(1,128)}, f32[1,1,1024]{2,0,1:T(1,128)S(1)}, u32[]{:S(2)}) copy-start(f32[1,1,1024]{2,0,1:T(1,128)S(1)} %get-tuple-element.221) | copy-start | bytes 12292
  30.9 21.4 %copy-start.54 = (f32[1,1,1024]{2,0,1:T(1,128)}, f32[1,1,1024]{2,0,1:T(1,128)S(1)}, u32[]{:S(2)}) copy-start(f32[1,1,1024]{2,0,1:T(1,128)S(1)} %get-tuple-element.222) | copy-start | bytes 12292
  61.1 19.5 %slice-start = ((s8[8388608]{0:T(1024)(128)(4,1)}), s8[4194304]{0:T(1024)(128)(4,1)S(1)}, s32[]{:S(2)}) async-start(s8[8388608]{0:T(1024)(128)(4,1)} %bitcast.125), calls=%async_computation.3 | async-start | bytes 8388608
  62.7 17.9 %slice-start.1 = ((s8[8388608]{0:T(1024)(128)(4,1)}), s8[4194304]{0:T(1024)(128)(4,1)S(1)}, s32[]{:S(2)}) async-start(s8[8388608]{0:T(1024)(128)(4,1)} %bitcast.125), calls=%async_computation.4 | async-start | bytes 8388608
  62.7 13.3 %collective-permute-start.2 = (bf16[1024,256]{1,0:T(8,128)(2,1)S(1)}, bf16[1024,256]{1,0:T(8,128)(2,1)S(1)}, u32[]{:S(2)}, u32[]{:S(2)}) collective-permute-start(bf16[1024,256]{1,0:T(8,128)(2,1)S(1)} %fusion.69), channel_id=1, source_target_pairs={{0,8},{8,16},{16,24},{24,28},{28,20},{20,12},{12,4},{4,0},{1,9},{9... | collective-permute-start | bytes 1572872 | tf_op jit(solution)/shard_map/ppermute | solution.py:234
  64.5 12.8 %collective-permute-start.3 = (bf16[1024,256]{1,0:T(8,128)(2,1)S(1)}, bf16[1024,256]{1,0:T(8,128)(2,1)S(1)}, u32[]{:S(2)}, u32[]{:S(2)}) collective-permute-start(bf16[1024,256]{1,0:T(8,128)(2,1)S(1)} %fusion.70), channel_id=1, source_target_pairs={{8,0},{16,8},{24,16},{28,24},{20,28},{12,20},{4,12},{0,4},{9,1},{1... | collective-permute-start | bytes 1572872 | tf_op jit(solution)/shard_map/ppermute | solution.py:235
  71.9 15.0 %copy-start.8 = (bf16[1024,4096]{1,0:T(8,128)(2,1)}, bf16[1024,4096]{1,0:T(8,128)(2,1)S(1)}, u32[]{:S(2)}) copy-start(bf16[1024,4096]{1,0:T(8,128)(2,1)S(1)} %multiply_convert_fusion) | copy-start | bytes 25165828
  78.5 20.8 %collective-permute-start.4 = (bf16[1024,256]{1,0:T(8,128)(2,1)}, bf16[1024,256]{1,0:T(8,128)(2,1)}, u32[]{:S(2)}, u32[]{:S(2)}) collective-permute-start(bf16[1024,256]{1,0:T(8,128)(2,1)} %get-tuple-element.99), channel_id=1, source_target_pairs={{0,8},{8,16},{16,24},{24,28},{28,20},{20,12},{12,4},{4,0},{1,9},{9... | collective-permute-start | bytes 1572872 | tf_op jit(solution)/shard_map/ppermute | solution.py:234
  80.1 19.2 %collective-permute-start.5 = (bf16[1024,256]{1,0:T(8,128)(2,1)S(1)}, bf16[1024,256]{1,0:T(8,128)(2,1)}, u32[]{:S(2)}, u32[]{:S(2)}) collective-permute-start(bf16[1024,256]{1,0:T(8,128)(2,1)S(1)} %get-tuple-element.100), channel_id=1, source_target_pairs={{8,0},{16,8},{24,16},{28,24},{20,28},{12,20},{4,12},{0,4},{9,1},{1... | collective-permute-start | bytes 1572872 | tf_op jit(solution)/shard_map/ppermute | solution.py:235
  90.8 8.5 %collective-permute-start.6 = (bf16[128,1024]{1,0:T(8,128)(2,1)}, bf16[128,1024]{1,0:T(8,128)(2,1)S(1)}, u32[]{:S(2)}, u32[]{:S(2)}) collective-permute-start(bf16[128,1024]{1,0:T(8,128)(2,1)} %slice.400), channel_id=1, source_target_pairs={{4,0},{8,4},{12,8},{16,12},{20,16},{24,20},{28,24},{5,1},{9,5},{13... | collective-permute-start | bytes 786440 | tf_op jit(solution)/shard_map/ppermute | solution.py:13
  101.9 10.6 %collective-permute-start.7 = (bf16[1024,256]{1,0:T(8,128)(2,1)}, bf16[1024,256]{1,0:T(8,128)(2,1)}, u32[]{:S(2)}, u32[]{:S(2)}) collective-permute-start(bf16[1024,256]{1,0:T(8,128)(2,1)} %get-tuple-element.109), channel_id=1, source_target_pairs={{0,8},{8,16},{16,24},{24,28},{28,20},{20,12},{12,4},{4,0},{1,9},{9... | collective-permute-start | bytes 1572872 | tf_op jit(solution)/shard_map/ppermute | solution.py:234
  103.5 10.1 %collective-permute-start.8 = (bf16[1024,256]{1,0:T(8,128)(2,1)S(1)}, bf16[1024,256]{1,0:T(8,128)(2,1)}, u32[]{:S(2)}, u32[]{:S(2)}) collective-permute-start(bf16[1024,256]{1,0:T(8,128)(2,1)S(1)} %get-tuple-element.110), channel_id=1, source_target_pairs={{8,0},{16,8},{24,16},{28,24},{20,28},{12,20},{4,12},{0,4},{9,1},{1... | collective-permute-start | bytes 1572872 | tf_op jit(solution)/shard_map/ppermute | solution.py:235
  128.2 10.5 %collective-permute-start.10 = (bf16[1024,256]{1,0:T(8,128)(2,1)}, bf16[1024,256]{1,0:T(8,128)(2,1)S(1)}, u32[]{:S(2)}, u32[]{:S(2)}) collective-permute-start(bf16[1024,256]{1,0:T(8,128)(2,1)} %get-tuple-element.124), channel_id=1, source_target_pairs={{8,0},{16,8},{24,16},{28,24},{20,28},{12,20},{4,12},{0,4},{9,1},{1... | collective-permute-start | bytes 1572872 | tf_op jit(solution)/shard_map/ppermute | solution.py:235
  128.6 10.0 %collective-permute-start.9 = (bf16[1024,256]{1,0:T(8,128)(2,1)S(1)}, bf16[1024,256]{1,0:T(8,128)(2,1)S(1)}, u32[]{:S(2)}, u32[]{:S(2)}) collective-permute-start(bf16[1024,256]{1,0:T(8,128)(2,1)S(1)} %get-tuple-element.123), channel_id=1, source_target_pairs={{0,8},{8,16},{16,24},{24,28},{28,20},{20,12},{12,4},{4,0},{1,9},{9... | collective-permute-start | bytes 1572872 | tf_op jit(solution)/shard_map/ppermute | solution.py:234
  131.0 7.6 %collective-permute-start.11 = (bf16[3,6,1024]{2,1,0:T(8,128)(2,1)S(1)}, bf16[3,6,1024]{2,1,0:T(8,128)(2,1)S(1)}, u32[]{:S(2)}, u32[]{:S(2)}) collective-permute-start(bf16[3,6,1024]{2,1,0:T(8,128)(2,1)S(1)} %pad_maximum_fusion.9), channel_id=1, source_target_pairs={{4,0},{8,4},{12,8},{16,12},{20,16},{24,20},{28,24},{5,1},{9,5},{13... | collective-permute-start | bytes 110600 | tf_op jit(solution)/shard_map/ppermute | solution.py:13
  149.7 15.6 %copy-start.5 = (f32[512,1024]{1,0:T(8,128)S(1)}, f32[512,1024]{1,0:T(8,128)}, u32[]{:S(2)}) copy-start(f32[512,1024]{1,0:T(8,128)} %copy-done.4) | copy-start | bytes 6291460
  149.7 15.6 %copy-start.25 = (f32[1,1,1024]{2,0,1:T(1,128)S(1)}, f32[1,1,1024]{2,0,1:T(1,128)}, u32[]{:S(2)}) copy-start(f32[1,1,1024]{2,0,1:T(1,128)} %copy-done.24) | copy-start | bytes 12292
  149.7 15.6 %copy-start.27 = (f32[1,1,1024]{2,0,1:T(1,128)S(1)}, f32[1,1,1024]{2,0,1:T(1,128)}, u32[]{:S(2)}) copy-start(f32[1,1,1024]{2,0,1:T(1,128)} %copy-done.26) | copy-start | bytes 12292
  149.7 15.6 %copy-start.29 = (f32[1,1,1024]{2,0,1:T(1,128)S(1)}, f32[1,1,1024]{2,0,1:T(1,128)}, u32[]{:S(2)}) copy-start(f32[1,1,1024]{2,0,1:T(1,128)} %copy-done.28) | copy-start | bytes 12292
  149.7 15.6 %copy-start.31 = (f32[1,1,1024]{2,0,1:T(1,128)S(1)}, f32[1,1,1024]{2,0,1:T(1,128)}, u32[]{:S(2)}) copy-start(f32[1,1,1024]{2,0,1:T(1,128)} %copy-done.30) | copy-start | bytes 12292
  149.7 15.6 %copy-start.33 = (f32[1,1,1024]{2,0,1:T(1,128)S(1)}, f32[1,1,1024]{2,0,1:T(1,128)}, u32[]{:S(2)}) copy-start(f32[1,1,1024]{2,0,1:T(1,128)} %copy-done.32) | copy-start | bytes 12292
  149.7 15.6 %copy-start.35 = (f32[1,1,1024]{2,0,1:T(1,128)S(1)}, f32[1,1,1024]{2,0,1:T(1,128)}, u32[]{:S(2)}) copy-start(f32[1,1,1024]{2,0,1:T(1,128)} %copy-done.34) | copy-start | bytes 12292
  149.7 15.6 %copy-start.37 = (f32[1,1,1024]{2,0,1:T(1,128)S(1)}, f32[1,1,1024]{2,0,1:T(1,128)}, u32[]{:S(2)}) copy-start(f32[1,1,1024]{2,0,1:T(1,128)} %copy-done.36) | copy-start | bytes 12292
  149.7 11.2 %collective-permute-start.12 = (bf16[1024,256]{1,0:T(8,128)(2,1)S(1)}, bf16[1024,256]{1,0:T(8,128)(2,1)}, u32[]{:S(2)}, u32[]{:S(2)}) collective-permute-start(bf16[1024,256]{1,0:T(8,128)(2,1)S(1)} %get-tuple-element.139), channel_id=1, source_target_pairs={{0,8},{8,16},{16,24},{24,28},{28,20},{20,12},{12,4},{4,0},{1,9},{9... | collective-permute-start | bytes 1572872 | tf_op jit(solution)/shard_map/ppermute | solution.py:234
  150.6 10.4 %collective-permute-start.13 = (bf16[1024,256]{1,0:T(8,128)(2,1)S(1)}, bf16[1024,256]{1,0:T(8,128)(2,1)}, u32[]{:S(2)}, u32[]{:S(2)}) collective-permute-start(bf16[1024,256]{1,0:T(8,128)(2,1)S(1)} %get-tuple-element.140), channel_id=1, source_target_pairs={{8,0},{16,8},{24,16},{28,24},{20,28},{12,20},{4,12},{0,4},{9,1},{1... | collective-permute-start | bytes 1572872 | tf_op jit(solution)/shard_map/ppermute | solution.py:235
  162.9 12.1 %collective-permute-start.14 = (bf16[1024,256]{1,0:T(8,128)(2,1)S(1)}, bf16[1024,256]{1,0:T(8,128)(2,1)S(1)}, u32[]{:S(2)}, u32[]{:S(2)}) collective-permute-start(bf16[1024,256]{1,0:T(8,128)(2,1)S(1)} %get-tuple-element.152), channel_id=1, source_target_pairs={{0,8},{8,16},{16,24},{24,28},{28,20},{20,12},{12,4},{4,0},{1,9},{9... | collective-permute-start | bytes 1572872 | tf_op jit(solution)/shard_map/ppermute | solution.py:234
  162.9 13.0 %collective-permute-start.15 = (bf16[1024,256]{1,0:T(8,128)(2,1)S(1)}, bf16[1024,256]{1,0:T(8,128)(2,1)S(1)}, u32[]{:S(2)}, u32[]{:S(2)}) collective-permute-start(bf16[1024,256]{1,0:T(8,128)(2,1)S(1)} %get-tuple-element.153), channel_id=1, source_target_pairs={{8,0},{16,8},{24,16},{28,24},{20,28},{12,20},{4,12},{0,4},{9,1},{1... | collective-permute-start | bytes 1572872 | tf_op jit(solution)/shard_map/ppermute | solution.py:235
  177.4 9.2 %collective-permute-start.16 = (bf16[1024,256]{1,0:T(8,128)(2,1)S(1)}, bf16[1024,256]{1,0:T(8,128)(2,1)S(1)}, u32[]{:S(2)}, u32[]{:S(2)}) collective-permute-start(bf16[1024,256]{1,0:T(8,128)(2,1)S(1)} %get-tuple-element.165), channel_id=1, source_target_pairs={{0,8},{8,16},{16,24},{24,28},{28,20},{20,12},{12,4},{4,0},{1,9},{9... | collective-permute-start | bytes 1572872 | tf_op jit(solution)/shard_map/ppermute | solution.py:234
  179.8 9.2 %collective-permute-start.17 = (bf16[1024,256]{1,0:T(8,128)(2,1)S(1)}, bf16[1024,256]{1,0:T(8,128)(2,1)S(1)}, u32[]{:S(2)}, u32[]{:S(2)}) collective-permute-start(bf16[1024,256]{1,0:T(8,128)(2,1)S(1)} %get-tuple-element.166), channel_id=1, source_target_pairs={{8,0},{16,8},{24,16},{28,24},{20,28},{12,20},{4,12},{0,4},{9,1},{1... | collective-permute-start | bytes 1572872 | tf_op jit(solution)/shard_map/ppermute | solution.py:235
  (30 other events, 224.3 us)
Sparse Core Ops, SparseCore 0:
  9.5 37.1 all-gather.1
  149.8 43.7 reduce-scatter.1

commit v9 on v8

--- a/solution.py
+++ b/solution.py
@@ -88,25 +88,17 @@
     tap_count = filter_taps.shape[1]
     tap_span = feature_taps.shape[0]
     full_cotangent = lax.all_gather(cotangent, "tp", axis=0, tiled=True)
-    reach = tap_count + tap_span - 1
-    query_before = passed_along(query_in[row_count - tap_span + 1 :], "seq", 1)
-    pair_before = passed_along(
-        jnp.stack([key_in[row_count - reach :], value_in[row_count - reach :]], axis=0), "seq", 1
-    )
-    query_feat = featurize(
-        jnp.concatenate([query_before, query_in], axis=0), feature_taps[:, 0], row_count
-    )
-    key_wide, value_wide = (
-        featurize(
-            jnp.concatenate([pair_before[i], rows], axis=0),
-            feature_taps[:, i + 1],
-            row_count + tap_count,
-        )
-        for i, rows in enumerate((key_in, value_in))
-    )
-    padded_mix = (key_wide * value_wide).astype(jnp.bfloat16)
-    key_feat = key_wide[tap_count:]
-    value_feat = value_wide[tap_count:]
+    inputs = (query_in, key_in, value_in)
+    before = passed_along(
+        jnp.stack([rows[row_count - tap_span + 1 :] for rows in inputs], axis=0), "seq", 1
+    )
+    query_feat, key_feat, value_feat = (
+        featurize(jnp.concatenate([before[i], inputs[i]], axis=0), feature_taps[:, i], row_count)
+        for i in range(3)
+    )
+    mix_rows = (key_feat * value_feat).astype(jnp.bfloat16)
+    mix_before = passed_along(mix_rows[row_count - tap_count :], "seq", 1)
+    padded_mix = jnp.concatenate([mix_before, mix_rows], axis=0)
     long_conv = band_mix(padded_mix, band_table(filter_taps))
     gated_rows = (query_feat * long_conv).astype(jnp.bfloat16)
     seq_count = lax.axis_size("seq")

time: 201 us -> 195 us (0.970)
  other arithmetic: 48.1 us -> 41 us
  waiting for transfers between devices: 43.9 us -> 46.2 us
  matrix products: 36.1 us -> 33.9 us
    convert_element_type x1, other arithmetic: 12.3 us -> 5.81 us  [per_device(): mix_rows = (key_feat * value_feat).astype(jnp.bfloat16)]
    slice x2, local copies, waits for them, and re-layouts: 0.07 us -> 3.48 us  [featurize(): feature_taps[offset]]
    convert_element_type x1, other arithmetic: 6.83 us -> 4.02 us  [per_device(): gated_rows = (query_feat * long_conv).astype(jnp.bfloat16)]
    ppermute x4, waiting for transfers between devices: 13.3 us -> 16 us  [passed_along(): lax.ppermute(value, axis, [(source, source + steps) for source in range(l...]
    dot_general x2, matrix products: 9.82 us -> 7.77 us  [band_table(): table = jnp.dot(filter_taps, select, preferred_element_type=jnp.float32)]
    unnamed x124 -> x112, local copies, waits for them, and re-layouts: 10.1 us -> 8.99 us
  transfers between devices with their start and end apart: 20 -> 20, of which waited for: 12 -> 13; matrix products, arithmetic and copies ran while one was open for 37% -> 31% of each run, Pallas kernels for 4% -> 4%
where the time goes in v9:
time: 195 us; the launch traced here: 194 us
  waiting for transfers between devices  46.2 us (24%)
  other arithmetic  41 us (21%)
  matrix products  33.9 us (17%)
  starting transfers between devices  27.1 us (14%)
  Pallas kernels  16 us (8%)
  between operations  15 us (8%)
  local copies, waits for them, and re-layouts  14.9 us (8%)
    ppermute x7, waiting for transfers between devices, ring_reduce_scatter(): ahead = lax.ppermute(sent_ahead, 'seq', forward)  20.2 us
    pallas_call x2, Pallas kernels, band_mix(): pl.pallas_call(body, grid=(channels // lane_tile,), in_specs=[pl.BlockSpe...  16 us
    ppermute x4, waiting for transfers between devices, passed_along(): lax.ppermute(value, axis, [(source, source + steps) for source in range(l...  16 us
    dot_general x3, matrix products, product(): lax.dot_general(rows, columns, (((0,), (0,)), ((), ())), preferred_elemen...  12.2 us
    convert_element_type x6, other arithmetic, ring_reduce_scatter(): sent_behind = behind.astype(jnp.bfloat16)  11.6 us
    ppermute x4, starting transfers between devices, passed_along(): lax.ppermute(value, axis, [(source, source + steps) for source in range(l...  10.9 us
    ppermute x7, starting transfers between devices, ring_reduce_scatter(): ahead = lax.ppermute(sent_ahead, 'seq', forward)  10.1 us
    dot_general x1, matrix products, project(): jnp.dot(gated_rows, out_weight, preferred_element_type=jnp.float32)  9.48 us
  transfers between devices with their start and end apart: 20, of which 13 were waited for; matrix products, arithmetic and copies ran while one was open for 31% of the time, Pallas kernels for 4%

profile of v9, /device:TPU:0, one launch (start us, length us, event | category | flops | bytes accessed | tf_op | source)
XLA Modules:
  0.0 194.2 jit_solution(13491624144176291943)
XLA Ops:
  9.5 4.9 %collective-permute-start = (bf16[3,6,1024]{2,1,0:T(8,128)(2,1)S(1)}, bf16[3,6,1024]{2,1,0:T(8,128)(2,1)S(1)}, u32[]{:S(2)}, u32[]{:S(2)}) collective-permute-start(bf16[3,6,1024]{2,1,0:T(8,128)(2,1)S(1)} %pad_maximum_fusion.9), channel_id=1, source_target_pairs={{0,4},{4,8},{8,12},{12,16},{16,20},{20,24},{24,28},{1,5},{5,9},{9,... | collective-permute-start | bytes 110600 | tf_op jit(solution)/shard_map/ppermute | solution.py:13
  14.6 2.0 %fusion.83 = (f32[1,1,1024]{2,0,1:T(1,128)}, f32[1,1,1024]{2,0,1:T(1,128)S(1)}, f32[1,1,1024]{2,0,1:T(1,128)S(1)}, f32[1,1,1024]{2,0,1:T(1,128)S(1)}, f32[1,1,10...) fusion(f32[7,3,1024]{2,0,1:T(8,128)} %param.10), kind=kLoop, calls=%fused_computation.186 | loop fusion | bytes 155648 | tf_op jit(solution)/shard_map/slice | solution.py:21
  16.9 1.4 fusion.84
  18.4 5.8 %multiply_convert_fusion.2 = (bf16[512,1024]{1,0:T(8,128)(2,1)S(1)}, f32[512,1024]{1,0:T(8,128)}, f32[512,1024]{1,0:T(8,128)}) fusion(bf16[512,1024]{1,0:T(8,128)(2,1)S(1)} %copy-done.7, bf16[6,1024]{1,0:T(8,128)(2,1)S(1)} %get-tuple-element.226, f32[1024]{0:T(1024)} %bitcast.109, f32[1024]{0:T(1024)} %bitcast.107, f32[1024]{0:T(1024)S(1)} %bitcast.83, ...), kind=kLoop, calls=%fused_computation.108 | loop fusion | flops 40894464 | bytes 7421952 | tf_op jit(solution)/shard_map/convert_element_type | solution.py:99
  24.3 3.5 %collective-permute-start.1 = (bf16[128,1024]{1,0:T(8,128)(2,1)S(1)}, bf16[128,1024]{1,0:T(8,128)(2,1)S(1)}, u32[]{:S(2)}, u32[]{:S(2)}) collective-permute-start(bf16[128,1024]{1,0:T(8,128)(2,1)S(1)} %slice.389), channel_id=1, source_target_pairs={{0,4},{4,8},{8,12},{12,16},{16,20},{20,24},{24,28},{1,5},{5,9},{9,... | collective-permute-start | bytes 786440 | tf_op jit(solution)/shard_map/ppermute | solution.py:13
  27.8 3.9 %convolution_convert_fusion.1 = bf16[32768,64]{0,1:T(8,128)(2,1)S(1)} fusion(bf16[64,128]{1,0:T(8,128)(2,1)S(1)} %copy-done, s32[32768]{0:T(1024)S(1)} %get-tuple-element.201), kind=kOutput, calls=%fused_computation.1 | convolution fusion | flops 543162368 | bytes 4341760 | tf_op jit(solution)/shard_map/dot_general | solution.py:46
  31.7 3.1 %copy.15 = bf16[8,8,128,256]{3,2,1,0:T(8,128)(2,1)} copy(bf16[8,8,128,256]{3,1,2,0:T(8,128)(2,1)S(1)} %bitcast.78) | data formatting | bytes 8388608
  36.0 8.0 %shard_map.110 = f32[512,1024]{1,0:T(8,128)} custom-call(bf16[64,128,256]{2,1,0:T(8,128)(2,1)} %bitcast.77, bf16[640,1024]{1,0:T(8,128)(2,1)} %pad_maximum_fusion.3.rows_ref), custom_call_target="tpu_custom_call" | custom-call | tf_op jit(solution)/shard_map/pallas_call | solution.py:74
  44.1 4.0 %multiply_convert_fusion.1 = (bf16[512,1024]{1,0:T(8,128)(2,1)}, f32[512,1024]{1,0:T(8,128)S(1)}) fusion(f32[512,1024]{1,0:T(8,128)} %shard_map.110, bf16[512,1024]{1,0:T(8,128)(2,1)S(1)} %copy-done.9, bf16[6,1024]{1,0:T(8,128)(2,1)S(1)} %get-tuple-element.225, f32[1024]{0:T(1024)S(1)} %bitcast.113, f32[1024]{0:T(1024)S(1)} %bitcast.115, ...), kind=kLoop, calls=%fused_computation.107 | loop fusion | flops 20971520 | bytes 6332416 | tf_op jit(solution)/shard_map/convert_element_type | solution.py:103
  48.2 2.6 %fusion.58 = bf16[1024,256]{1,0:T(8,128)(2,1)} fusion(bf16[512,1024]{1,0:T(8,128)(2,1)} %get-tuple-element.94, bf16[512,4096]{1,0:T(8,128)(2,1)} %all-gather.2.cloned.1.call-done, s32[]{:T(128)S(6)} %select_n.515), kind=kOutput, calls=%fused_computation.117 | convolution fusion | flops 268959744 | bytes 1835012 | tf_op jit(solution)/shard_map/dot_general | solution.py:201
  50.8 2.4 %fusion.57 = bf16[1024,256]{1,0:T(8,128)(2,1)} fusion(bf16[512,1024]{1,0:T(8,128)(2,1)S(1)} %copy-done.10, bf16[512,4096]{1,0:T(8,128)(2,1)} %all-gather.2.cloned.1.call-done, s32[]{:T(128)S(6)} %select_n.506), kind=kOutput, calls=%fused_computation.116 | convolution fusion | flops 268959744 | bytes 1835012 | tf_op jit(solution)/shard_map/dot_general | solution.py:201
  53.2 1.7 collective-permute-start.2
  55.2 7.1 %multiply_convert_fusion = bf16[1024,4096]{1,0:T(8,128)(2,1)S(1)} fusion(bf16[512,1024]{1,0:T(8,128)(2,1)S(1)} %copy-done.10, bf16[512,4096]{1,0:T(8,128)(2,1)} %all-gather.2.cloned.1.call-done), kind=kOutput, calls=%fused_computation.3 | convolution fusion | flops 4303355904 | bytes 13631488 | tf_op jit(solution)/shard_map/dot_general | solution.py:201
  62.4 4.1 %collective-permute-done.2 = bf16[1024,256]{1,0:T(8,128)(2,1)S(1)} collective-permute-done((bf16[1024,256]{1,0:T(8,128)(2,1)}, bf16[1024,256]{1,0:T(8,128)(2,1)S(1)}, u32[]{:S(2)}, u32[]{:S(2)}) %collective-permute-start.2) | collective-permute-done | bytes 524320 | tf_op jit(solution)/shard_map/ppermute | solution.py:226
  66.5 1.3 collective-permute-done.3
  67.8 1.4 add_convert_fusion.12
  69.2 1.6 collective-permute-start.4
  71.2 4.5 %fusion.85 = f32[1024,512]{0,1:T(8,128)S(1)} fusion(bf16[1024,4096]{1,0:T(8,128)(2,1)S(1)} %bitcast.126, bf16[512,4096]{1,0:T(8,128)(2,1)S(1)} %copy-done.50), kind=kOutput, calls=%fused_computation.188 | convolution fusion | flops 4294967296 | bytes 14680064 | tf_op jit(solution)/shard_map/dot_general | solution.py:124
  75.8 2.1 %bitcast_multiply_fusion = (f32[512,1024]{1,0:T(8,128)}, bf16[512,1024]{1,0:T(8,128)(2,1)S(1)}) fusion(f32[512,1024]{1,0:T(8,128)S(1)} %copy-done.2, f32[1024,512]{0,1:T(8,128)S(1)} %fusion.85, f32[512,1024]{1,0:T(8,128)S(1)} %get-tuple-element.178), kind=kLoop, calls=%fused_computation.104 | loop fusion | flops 1572864 | bytes 9437184 | tf_op jit(solution)/shard_map/mul | solution.py:128
  79.2 7.6 %collective-permute-done.6 = bf16[128,1024]{1,0:T(8,128)(2,1)S(1)} collective-permute-done((bf16[128,1024]{1,0:T(8,128)(2,1)S(1)}, bf16[128,1024]{1,0:T(8,128)(2,1)S(1)}, u32[]{:S(2)}, u32[]{:S(2)}) %collective-permute-start.6) | collective-permute-done | bytes 262176 | tf_op jit(solution)/shard_map/ppermute | solution.py:13
  86.9 1.8 add_convert_fusion.10
  89.6 2.2 %collective-permute-start.8 = (bf16[1024,256]{1,0:T(8,128)(2,1)S(1)}, bf16[1024,256]{1,0:T(8,128)(2,1)S(1)}, u32[]{:S(2)}, u32[]{:S(2)}) collective-permute-start(bf16[1024,256]{1,0:T(8,128)(2,1)S(1)} %get-tuple-element.110), channel_id=1, source_target_pairs={{8,0},{16,8},{24,16},{28,24},{20,28},{12,20},{4,12},{0,4},{9,1},{1... | collective-permute-start | bytes 1572872 | tf_op jit(solution)/shard_map/ppermute | solution.py:227
  91.8 3.9 %convolution_convert_fusion = bf16[32768,64]{0,1:T(8,128)(2,1)S(1)} fusion(bf16[64,128]{1,0:T(8,128)(2,1)S(1)} %copy-done, s32[32768]{0:T(1024)S(1)} %get-tuple-element.200), kind=kOutput, calls=%fused_computation | convolution fusion | flops 543162368 | bytes 4341760 | tf_op jit(solution)/shard_map/dot_general | solution.py:46
  95.7 3.2 %copy.17 = bf16[8,8,128,256]{3,2,1,0:T(8,128)(2,1)} copy(bf16[8,8,128,256]{3,1,2,0:T(8,128)(2,1)S(1)} %bitcast.79) | data formatting | bytes 8388608
  98.9 2.1 %collective-permute-done.7 = bf16[1024,256]{1,0:T(8,128)(2,1)S(1)} collective-permute-done((bf16[1024,256]{1,0:T(8,128)(2,1)S(1)}, bf16[1024,256]{1,0:T(8,128)(2,1)S(1)}, u32[]{:S(2)}, u32[]{:S(2)}) %collective-permute-start.7) | collective-permute-done | bytes 524320 | tf_op jit(solution)/shard_map/ppermute | solution.py:226
  101.0 2.4 %add_convert_fusion.8 = (bf16[1024,256]{1,0:T(8,128)(2,1)}, bf16[1024,256]{1,0:T(8,128)(2,1)}) fusion(bf16[1024,256]{1,0:T(8,128)(2,1)S(1)} %collective-permute-done.8, bf16[1024,4096]{1,0:T(8,128)(2,1)} %copy-done.6, s32[]{:T(128)S(6)} %select_n.569, s32[]{:T(128)S(6)} %select_n.560, bf16[1024,256]{1,0:T(8,128)(2,1)S(1)} %collective-permute-done.7), kind=kLoop, calls=%fused_computation.154 | loop fusion | flops 2097152 | bytes 3145736 | tf_op jit(solution)/shard_map/convert_element_type | solution.py:222
  104.6 8.0 %shard_map.111 = f32[512,1024]{1,0:T(8,128)} custom-call(bf16[64,128,256]{2,1,0:T(8,128)(2,1)} %bitcast.76, bf16[640,1024]{1,0:T(8,128)(2,1)} %pad_maximum_fusion.4.rows_ref), custom_call_target="tpu_custom_call" | custom-call | tf_op jit(solution)/shard_map/pallas_call | solution.py:74
  112.6 3.5 %fusion.81 = (f32[512,1024]{1,0:T(8,128)S(1)}, f32[512,1024]{1,0:T(8,128)S(1)}) fusion(f32[512,1024]{1,0:T(8,128)} %shard_map.111, f32[512,1024]{1,0:T(8,128)} %get-tuple-element.181, f32[512,1024]{1,0:T(8,128)} %get-tuple-element.180), kind=kLoop, calls=%fused_computation.184 | loop fusion | flops 1048576 | bytes 10485760 | tf_op jit(solution)/shard_map/mul | solution.py:138
  116.2 1.3 copy-done.3
  117.5 2.0 %collective-permute-start.10 = (bf16[1024,256]{1,0:T(8,128)(2,1)}, bf16[1024,256]{1,0:T(8,128)(2,1)}, u32[]{:S(2)}, u32[]{:S(2)}) collective-permute-start(bf16[1024,256]{1,0:T(8,128)(2,1)} %get-tuple-element.124), channel_id=1, source_target_pairs={{8,0},{16,8},{24,16},{28,24},{20,28},{12,20},{4,12},{0,4},{9,1},{1... | collective-permute-start | bytes 1572872 | tf_op jit(solution)/shard_map/ppermute | solution.py:227
  122.4 8.4 %collective-permute-done.11 = bf16[3,6,1024]{2,1,0:T(8,128)(2,1)S(1)} collective-permute-done((bf16[3,6,1024]{2,1,0:T(8,128)(2,1)S(1)}, bf16[3,6,1024]{2,1,0:T(8,128)(2,1)S(1)}, u32[]{:S(2)}, u32[]{:S(2)}) %collective-permute-start.11) | collective-permute-done | bytes 36896 | tf_op jit(solution)/shard_map/ppermute | solution.py:13
  130.8 2.8 %add_convert_fusion.6 = (bf16[1024,256]{1,0:T(8,128)(2,1)}, bf16[1024,256]{1,0:T(8,128)(2,1)}) fusion(bf16[1024,256]{1,0:T(8,128)(2,1)} %collective-permute-done.10, bf16[1024,4096]{1,0:T(8,128)(2,1)} %copy-done.6, s32[]{:T(128)S(6)} %select_n.587, s32[]{:T(128)S(6)} %select_n.578, bf16[1024,256]{1,0:T(8,128)(2,1)} %collective-permute-done.9), kind=kLoop, calls=%fused_computation.152 | loop fusion | flops 2097152 | bytes 3145736 | tf_op jit(solution)/shard_map/convert_element_type | solution.py:222
  133.5 9.5 %convolution_convert_fusion.2 = bf16[512,4096]{1,0:T(8,128)(2,1)} fusion(bf16[512,1024]{1,0:T(8,128)(2,1)S(1)} %copy-done.11, bf16[1024,4096]{1,0:T(8,128)(2,1)} %param.12), kind=kOutput, calls=%fused_computation.7 | convolution fusion | flops 4297064448 | bytes 13631488 | tf_op jit(solution)/shard_map/dot_general | solution.py:113
  144.1 1.6 collective-permute-start.12
  146.2 8.5 %collective-permute-done.12 = bf16[1024,256]{1,0:T(8,128)(2,1)} collective-permute-done((bf16[1024,256]{1,0:T(8,128)(2,1)S(1)}, bf16[1024,256]{1,0:T(8,128)(2,1)}, u32[]{:S(2)}, u32[]{:S(2)}) %collective-permute-start.12) | collective-permute-done | bytes 524320 | tf_op jit(solution)/shard_map/ppermute | solution.py:226
  155.5 1.8 add_convert_fusion.4
  157.4 1.5 collective-permute-start.14
  159.5 3.0 %fusion.23 = bf16[512,1024]{1,0:T(8,128)(2,1)} fusion(f32[6,1024]{1,0:T(8,128)S(1)} %get-tuple-element.223, f32[512,1024]{1,0:T(8,128)S(1)} %copy-done.4, f32[1024]{0:T(1024)S(1)} %bitcast.94, f32[1024]{0:T(1024)S(1)} %bitcast.96, f32[1024]{0:T(1024)S(1)} %bitcast.98, f32[1024]{0:T(1024)S(1)} %bitcast.100, f32[1024]{0:T(1024)S(1)} %bitcast.102, ...), kind=kLoop, calls=%fused_computation.59 | loop fusion | flops 10485760 | bytes 3198976 | tf_op jit(solution)/shard_map/convert_element_type | solution.py:156
  162.6 3.0 %fusion.40 = bf16[512,1024]{1,0:T(8,128)(2,1)} fusion(f32[6,1024]{1,0:T(8,128)S(1)} %get-tuple-element.224, f32[512,1024]{1,0:T(8,128)S(1)} %copy-done.5, f32[1024]{0:T(1024)S(1)} %bitcast.114, f32[1024]{0:T(1024)S(1)} %bitcast.116, f32[1024]{0:T(1024)S(1)} %bitcast.118, f32[1024]{0:T(1024)S(1)} %bitcast.120, f32[1024]{0:T(1024)S(1)} %bitcast.122, ...), kind=kLoop, calls=%fused_computation.76 | loop fusion | flops 10485760 | bytes 3198976 | tf_op jit(solution)/shard_map/convert_element_type | solution.py:156
  165.6 1.3 collective-permute-done.14
  166.9 1.3 collective-permute-done.15
  168.3 1.5 add_convert_fusion.2
  169.7 2.0 %collective-permute-start.16 = (bf16[1024,256]{1,0:T(8,128)(2,1)S(1)}, bf16[1024,256]{1,0:T(8,128)(2,1)S(1)}, u32[]{:S(2)}, u32[]{:S(2)}) collective-permute-start(bf16[1024,256]{1,0:T(8,128)(2,1)S(1)} %get-tuple-element.165), channel_id=1, source_target_pairs={{0,8},{8,16},{16,24},{24,28},{28,20},{20,12},{12,4},{4,0},{1,9},{9... | collective-permute-start | bytes 1572872 | tf_op jit(solution)/shard_map/ppermute | solution.py:226
  171.9 3.0 %fusion.6 = bf16[512,1024]{1,0:T(8,128)(2,1)} fusion(f32[6,1024]{1,0:T(8,128)S(1)} %bitcast_convert_fusion, f32[512,1024]{1,0:T(8,128)S(1)} %get-tuple-element.169, f32[1024]{0:T(1024)S(1)} %bitcast.110, f32[1024]{0:T(1024)S(1)} %bitcast.108, f32[1024]{0:T(1024)S(1)} %bitcast.84, f32[1024]{0:T(1024)S(1)} %bitcast.86, f32[1024]{0:T(1024)S(1)} %bitcast.88, ...), kind=kLoop, calls=%fused_computation.42 | loop fusion | flops 10485760 | bytes 3198976 | tf_op jit(solution)/shard_map/convert_element_type | solution.py:156
  174.9 4.1 %collective-permute-done.16 = bf16[1024,256]{1,0:T(8,128)(2,1)S(1)} collective-permute-done((bf16[1024,256]{1,0:T(8,128)(2,1)S(1)}, bf16[1024,256]{1,0:T(8,128)(2,1)S(1)}, u32[]{:S(2)}, u32[]{:S(2)}) %collective-permute-start.16) | collective-permute-done | bytes 524320 | tf_op jit(solution)/shard_map/ppermute | solution.py:226
  179.0 2.0 %collective-permute-done.17 = bf16[1024,256]{1,0:T(8,128)(2,1)S(1)} collective-permute-done((bf16[1024,256]{1,0:T(8,128)(2,1)S(1)}, bf16[1024,256]{1,0:T(8,128)(2,1)S(1)}, u32[]{:S(2)}, u32[]{:S(2)}) %collective-permute-start.17) | collective-permute-done | bytes 524320 | tf_op jit(solution)/shard_map/ppermute | solution.py:227
  180.9 1.5 add_convert_fusion.1
  183.5 3.9 %reduce-scatter.2.cloned.1.call-done = bf16[128,4096]{1,0:T(8,128)(2,1)} async-done(((bf16[512,4096]{1,0:T(8,128)(2,1)}), bf16[128,4096]{1,0:T(8,128)(2,1)}) %reduce-scatter.2.cloned.1.call-update) | async-done | bytes 1048592 | tf_op jit(solution)/shard_map/reduce_scatter | solution.py:112
  (150 shorter events, 15.1 us)
Async XLA Ops:
  7.2 20.6 %copy-start = (bf16[64,128]{1,0:T(8,128)(2,1)S(1)}, bf16[64,128]{1,0:T(8,128)(2,1)}, u32[]{:S(2)}) copy-start(bf16[64,128]{1,0:T(8,128)(2,1)} %param.11) | copy-start | bytes 49156
  7.2 11.2 %copy-start.8 = (bf16[512,1024]{1,0:T(8,128)(2,1)S(1)}, bf16[512,1024]{1,0:T(8,128)(2,1)}, u32[]{:S(2)}) copy-start(bf16[512,1024]{1,0:T(8,128)(2,1)} %param.8) | copy-start | bytes 3145732
  7.2 11.2 %copy-start.7 = (bf16[512,1024]{1,0:T(8,128)(2,1)S(1)}, bf16[512,1024]{1,0:T(8,128)(2,1)}, u32[]{:S(2)}) copy-start(bf16[512,1024]{1,0:T(8,128)(2,1)} %param.9) | copy-start | bytes 3145732
  7.2 41.0 %all-gather.2.cloned.1.call-start = ((), (), s32[]{:S(2)}) async-start(), calls=%async_computation.1 | async-start | bytes 5242880 | tf_op jit(solution)/shard_map/all_gather | solution.py:90
  7.9 179.4 %reduce-scatter.2.cloned.1.call-start = ((), (), s32[]{:S(2)}) async-start(), calls=%async_computation.2 | async-start | bytes 5242880 | tf_op jit(solution)/shard_map/reduce_scatter | solution.py:112
  9.5 8.9 %collective-permute-start = (bf16[3,6,1024]{2,1,0:T(8,128)(2,1)S(1)}, bf16[3,6,1024]{2,1,0:T(8,128)(2,1)S(1)}, u32[]{:S(2)}, u32[]{:S(2)}) collective-permute-start(bf16[3,6,1024]{2,1,0:T(8,128)(2,1)S(1)} %pad_maximum_fusion.9), channel_id=1, source_target_pairs={{0,4},{4,8},{8,12},{12,16},{16,20},{20,24},{24,28},{1,5},{5,9},{9,... | collective-permute-start | bytes 110600 | tf_op jit(solution)/shard_map/ppermute | solution.py:13
  16.6 7.6 %copy-start.14 = (f32[1,1,1024]{2,0,1:T(1,128)}, f32[1,1,1024]{2,0,1:T(1,128)S(1)}, u32[]{:S(2)}) copy-start(f32[1,1,1024]{2,0,1:T(1,128)S(1)} %get-tuple-element.203) | copy-start | bytes 12292
  16.6 7.6 %copy-start.16 = (f32[1,1,1024]{2,0,1:T(1,128)}, f32[1,1,1024]{2,0,1:T(1,128)S(1)}, u32[]{:S(2)}) copy-start(f32[1,1,1024]{2,0,1:T(1,128)S(1)} %get-tuple-element.204) | copy-start | bytes 12292
  16.6 7.6 %copy-start.18 = (f32[1,1,1024]{2,0,1:T(1,128)}, f32[1,1,1024]{2,0,1:T(1,128)S(1)}, u32[]{:S(2)}) copy-start(f32[1,1,1024]{2,0,1:T(1,128)S(1)} %get-tuple-element.205) | copy-start | bytes 12292
  24.3 10.5 %collective-permute-start.1 = (bf16[128,1024]{1,0:T(8,128)(2,1)S(1)}, bf16[128,1024]{1,0:T(8,128)(2,1)S(1)}, u32[]{:S(2)}, u32[]{:S(2)}) collective-permute-start(bf16[128,1024]{1,0:T(8,128)(2,1)S(1)} %slice.389), channel_id=1, source_target_pairs={{0,4},{4,8},{8,12},{12,16},{16,20},{20,24},{24,28},{1,5},{5,9},{9,... | collective-permute-start | bytes 786440 | tf_op jit(solution)/shard_map/ppermute | solution.py:13
  36.0 8.1 %copy-start.9 = (bf16[512,1024]{1,0:T(8,128)(2,1)S(1)}, bf16[512,1024]{1,0:T(8,128)(2,1)}, u32[]{:S(2)}) copy-start(bf16[512,1024]{1,0:T(8,128)(2,1)} %param.7) | copy-start | bytes 3145732
  36.0 8.1 %copy-start.36 = (f32[1,1,1024]{2,0,1:T(1,128)S(1)}, f32[1,1,1024]{2,0,1:T(1,128)}, u32[]{:S(2)}) copy-start(f32[1,1,1024]{2,0,1:T(1,128)} %get-tuple-element.202) | copy-start | bytes 12292
  36.0 8.1 %copy-start.38 = (f32[1,1,1024]{2,0,1:T(1,128)S(1)}, f32[1,1,1024]{2,0,1:T(1,128)}, u32[]{:S(2)}) copy-start(f32[1,1,1024]{2,0,1:T(1,128)} %get-tuple-element.215) | copy-start | bytes 12292
  36.0 8.1 %copy-start.40 = (f32[1,1,1024]{2,0,1:T(1,128)S(1)}, f32[1,1,1024]{2,0,1:T(1,128)}, u32[]{:S(2)}) copy-start(f32[1,1,1024]{2,0,1:T(1,128)} %get-tuple-element.216) | copy-start | bytes 12292
  36.0 8.1 %copy-start.42 = (f32[1,1,1024]{2,0,1:T(1,128)S(1)}, f32[1,1,1024]{2,0,1:T(1,128)}, u32[]{:S(2)}) copy-start(f32[1,1,1024]{2,0,1:T(1,128)} %get-tuple-element.217) | copy-start | bytes 12292
  36.0 8.1 %copy-start.44 = (f32[1,1,1024]{2,0,1:T(1,128)S(1)}, f32[1,1,1024]{2,0,1:T(1,128)}, u32[]{:S(2)}) copy-start(f32[1,1,1024]{2,0,1:T(1,128)} %get-tuple-element.218) | copy-start | bytes 12292
  36.0 8.1 %copy-start.46 = (f32[1,1,1024]{2,0,1:T(1,128)S(1)}, f32[1,1,1024]{2,0,1:T(1,128)}, u32[]{:S(2)}) copy-start(f32[1,1,1024]{2,0,1:T(1,128)} %get-tuple-element.219) | copy-start | bytes 12292
  36.0 8.1 %copy-start.48 = (f32[1,1,1024]{2,0,1:T(1,128)S(1)}, f32[1,1,1024]{2,0,1:T(1,128)}, u32[]{:S(2)}) copy-start(f32[1,1,1024]{2,0,1:T(1,128)} %get-tuple-element.220) | copy-start | bytes 12292
  50.8 20.4 %slice-start = ((s8[8388608]{0:T(1024)(128)(4,1)}), s8[4194304]{0:T(1024)(128)(4,1)S(1)}, s32[]{:S(2)}) async-start(s8[8388608]{0:T(1024)(128)(4,1)} %bitcast.125), calls=%async_computation.3 | async-start | bytes 8388608
  53.2 18.0 %slice-start.1 = ((s8[8388608]{0:T(1024)(128)(4,1)}), s8[4194304]{0:T(1024)(128)(4,1)S(1)}, s32[]{:S(2)}) async-start(s8[8388608]{0:T(1024)(128)(4,1)} %bitcast.125), calls=%async_computation.4 | async-start | bytes 8388608
  53.2 13.3 %collective-permute-start.2 = (bf16[1024,256]{1,0:T(8,128)(2,1)}, bf16[1024,256]{1,0:T(8,128)(2,1)S(1)}, u32[]{:S(2)}, u32[]{:S(2)}) collective-permute-start(bf16[1024,256]{1,0:T(8,128)(2,1)} %fusion.57), channel_id=1, source_target_pairs={{0,8},{8,16},{16,24},{24,28},{28,20},{20,12},{12,4},{4,0},{1,9},{9... | collective-permute-start | bytes 1572872 | tf_op jit(solution)/shard_map/ppermute | solution.py:226
  54.9 12.9 %collective-permute-start.3 = (bf16[1024,256]{1,0:T(8,128)(2,1)}, bf16[1024,256]{1,0:T(8,128)(2,1)S(1)}, u32[]{:S(2)}, u32[]{:S(2)}) collective-permute-start(bf16[1024,256]{1,0:T(8,128)(2,1)} %fusion.58), channel_id=1, source_target_pairs={{8,0},{16,8},{24,16},{28,24},{20,28},{12,20},{4,12},{0,4},{9,1},{1... | collective-permute-start | bytes 1572872 | tf_op jit(solution)/shard_map/ppermute | solution.py:227
  55.2 16.0 %copy-start.50 = (bf16[512,4096]{1,0:T(8,128)(2,1)S(1)}, bf16[512,4096]{1,0:T(8,128)(2,1)}, u32[]{:S(2)}) copy-start(bf16[512,4096]{1,0:T(8,128)(2,1)} %all-gather.2.cloned.1.call-done) | copy-start | bytes 12582916
  62.4 13.4 %copy-start.6 = (bf16[1024,4096]{1,0:T(8,128)(2,1)}, bf16[1024,4096]{1,0:T(8,128)(2,1)S(1)}, u32[]{:S(2)}) copy-start(bf16[1024,4096]{1,0:T(8,128)(2,1)S(1)} %multiply_convert_fusion) | copy-start | bytes 25165828
  69.2 17.7 %collective-permute-start.4 = (bf16[1024,256]{1,0:T(8,128)(2,1)}, bf16[1024,256]{1,0:T(8,128)(2,1)}, u32[]{:S(2)}, u32[]{:S(2)}) collective-permute-start(bf16[1024,256]{1,0:T(8,128)(2,1)} %get-tuple-element.99), channel_id=1, source_target_pairs={{0,8},{8,16},{16,24},{24,28},{28,20},{20,12},{12,4},{4,0},{1,9},{9... | collective-permute-start | bytes 1572872 | tf_op jit(solution)/shard_map/ppermute | solution.py:226
  70.8 16.1 %collective-permute-start.5 = (bf16[1024,256]{1,0:T(8,128)(2,1)}, bf16[1024,256]{1,0:T(8,128)(2,1)}, u32[]{:S(2)}, u32[]{:S(2)}) collective-permute-start(bf16[1024,256]{1,0:T(8,128)(2,1)} %get-tuple-element.100), channel_id=1, source_target_pairs={{8,0},{16,8},{24,16},{28,24},{20,28},{12,20},{4,12},{0,4},{9,1},{1... | collective-permute-start | bytes 1572872 | tf_op jit(solution)/shard_map/ppermute | solution.py:227
  77.8 9.0 %collective-permute-start.6 = (bf16[128,1024]{1,0:T(8,128)(2,1)S(1)}, bf16[128,1024]{1,0:T(8,128)(2,1)S(1)}, u32[]{:S(2)}, u32[]{:S(2)}) collective-permute-start(bf16[128,1024]{1,0:T(8,128)(2,1)S(1)} %slice.390), channel_id=1, source_target_pairs={{4,0},{8,4},{12,8},{16,12},{20,16},{24,20},{28,24},{5,1},{9,5},{13... | collective-permute-start | bytes 786440 | tf_op jit(solution)/shard_map/ppermute | solution.py:13
  88.7 12.3 %collective-permute-start.7 = (bf16[1024,256]{1,0:T(8,128)(2,1)S(1)}, bf16[1024,256]{1,0:T(8,128)(2,1)S(1)}, u32[]{:S(2)}, u32[]{:S(2)}) collective-permute-start(bf16[1024,256]{1,0:T(8,128)(2,1)S(1)} %get-tuple-element.109), channel_id=1, source_target_pairs={{0,8},{8,16},{16,24},{24,28},{28,20},{20,12},{12,4},{4,0},{1,9},{9... | collective-permute-start | bytes 1572872 | tf_op jit(solution)/shard_map/ppermute | solution.py:226
  89.6 11.4 %collective-permute-start.8 = (bf16[1024,256]{1,0:T(8,128)(2,1)S(1)}, bf16[1024,256]{1,0:T(8,128)(2,1)S(1)}, u32[]{:S(2)}, u32[]{:S(2)}) collective-permute-start(bf16[1024,256]{1,0:T(8,128)(2,1)S(1)} %get-tuple-element.110), channel_id=1, source_target_pairs={{8,0},{16,8},{24,16},{28,24},{20,28},{12,20},{4,12},{0,4},{9,1},{1... | collective-permute-start | bytes 1572872 | tf_op jit(solution)/shard_map/ppermute | solution.py:227
  116.2 17.4 %copy-start.11 = (bf16[512,1024]{1,0:T(8,128)(2,1)S(1)}, bf16[512,1024]{1,0:T(8,128)(2,1)}, u32[]{:S(2)}) copy-start(bf16[512,1024]{1,0:T(8,128)(2,1)} %get-tuple-element.94) | copy-start | bytes 3145732
  117.5 13.3 %collective-permute-start.10 = (bf16[1024,256]{1,0:T(8,128)(2,1)}, bf16[1024,256]{1,0:T(8,128)(2,1)}, u32[]{:S(2)}, u32[]{:S(2)}) collective-permute-start(bf16[1024,256]{1,0:T(8,128)(2,1)} %get-tuple-element.124), channel_id=1, source_target_pairs={{8,0},{16,8},{24,16},{28,24},{20,28},{12,20},{4,12},{0,4},{9,1},{1... | collective-permute-start | bytes 1572872 | tf_op jit(solution)/shard_map/ppermute | solution.py:227
  119.4 11.3 %collective-permute-start.9 = (bf16[1024,256]{1,0:T(8,128)(2,1)}, bf16[1024,256]{1,0:T(8,128)(2,1)}, u32[]{:S(2)}, u32[]{:S(2)}) collective-permute-start(bf16[1024,256]{1,0:T(8,128)(2,1)} %get-tuple-element.123), channel_id=1, source_target_pairs={{0,8},{8,16},{16,24},{24,28},{28,20},{20,12},{12,4},{4,0},{1,9},{9... | collective-permute-start | bytes 1572872 | tf_op jit(solution)/shard_map/ppermute | solution.py:226
  121.0 9.8 %collective-permute-start.11 = (bf16[3,6,1024]{2,1,0:T(8,128)(2,1)S(1)}, bf16[3,6,1024]{2,1,0:T(8,128)(2,1)S(1)}, u32[]{:S(2)}, u32[]{:S(2)}) collective-permute-start(bf16[3,6,1024]{2,1,0:T(8,128)(2,1)S(1)} %pad_maximum_fusion.10), channel_id=1, source_target_pairs={{4,0},{8,4},{12,8},{16,12},{20,16},{24,20},{28,24},{5,1},{9,5},{13... | collective-permute-start | bytes 110600 | tf_op jit(solution)/shard_map/ppermute | solution.py:13
  144.0 15.4 %copy-start.25 = (f32[1,1,1024]{2,0,1:T(1,128)S(1)}, f32[1,1,1024]{2,0,1:T(1,128)}, u32[]{:S(2)}) copy-start(f32[1,1,1024]{2,0,1:T(1,128)} %copy-done.24) | copy-start | bytes 12292
  144.0 15.4 %copy-start.27 = (f32[1,1,1024]{2,0,1:T(1,128)S(1)}, f32[1,1,1024]{2,0,1:T(1,128)}, u32[]{:S(2)}) copy-start(f32[1,1,1024]{2,0,1:T(1,128)} %copy-done.26) | copy-start | bytes 12292
  144.1 15.4 %copy-start.29 = (f32[1,1,1024]{2,0,1:T(1,128)S(1)}, f32[1,1,1024]{2,0,1:T(1,128)}, u32[]{:S(2)}) copy-start(f32[1,1,1024]{2,0,1:T(1,128)} %copy-done.28) | copy-start | bytes 12292
  144.1 15.4 %copy-start.30 = (f32[1,1,1024]{2,0,1:T(1,128)S(1)}, f32[1,1,1024]{2,0,1:T(1,128)}, u32[]{:S(2)}) copy-start(f32[1,1,1024]{2,0,1:T(1,128)} %get-tuple-element.211) | copy-start | bytes 12292
  144.1 15.4 %copy-start.31 = (f32[1,1,1024]{2,0,1:T(1,128)S(1)}, f32[1,1,1024]{2,0,1:T(1,128)}, u32[]{:S(2)}) copy-start(f32[1,1,1024]{2,0,1:T(1,128)} %get-tuple-element.212) | copy-start | bytes 12292
  144.1 15.4 %copy-start.32 = (f32[1,1,1024]{2,0,1:T(1,128)S(1)}, f32[1,1,1024]{2,0,1:T(1,128)}, u32[]{:S(2)}) copy-start(f32[1,1,1024]{2,0,1:T(1,128)} %get-tuple-element.213) | copy-start | bytes 12292
  144.1 15.4 %copy-start.33 = (f32[1,1,1024]{2,0,1:T(1,128)S(1)}, f32[1,1,1024]{2,0,1:T(1,128)}, u32[]{:S(2)}) copy-start(f32[1,1,1024]{2,0,1:T(1,128)} %get-tuple-element.214) | copy-start | bytes 12292
  144.1 10.6 %collective-permute-start.12 = (bf16[1024,256]{1,0:T(8,128)(2,1)S(1)}, bf16[1024,256]{1,0:T(8,128)(2,1)}, u32[]{:S(2)}, u32[]{:S(2)}) collective-permute-start(bf16[1024,256]{1,0:T(8,128)(2,1)S(1)} %copy-done.13), channel_id=1, source_target_pairs={{0,8},{8,16},{16,24},{24,28},{28,20},{20,12},{12,4},{4,0},{1,9},{9... | collective-permute-start | bytes 1572872 | tf_op jit(solution)/shard_map/ppermute | solution.py:226
  145.7 9.7 %collective-permute-start.13 = (bf16[1024,256]{1,0:T(8,128)(2,1)S(1)}, bf16[1024,256]{1,0:T(8,128)(2,1)}, u32[]{:S(2)}, u32[]{:S(2)}) collective-permute-start(bf16[1024,256]{1,0:T(8,128)(2,1)S(1)} %copy-done.12), channel_id=1, source_target_pairs={{8,0},{16,8},{24,16},{28,24},{20,28},{12,20},{4,12},{0,4},{9,1},{1... | collective-permute-start | bytes 1572872 | tf_op jit(solution)/shard_map/ppermute | solution.py:227
  146.2 13.3 %copy-start.4 = (f32[512,1024]{1,0:T(8,128)S(1)}, f32[512,1024]{1,0:T(8,128)}, u32[]{:S(2)}) copy-start(f32[512,1024]{1,0:T(8,128)} %copy-done.3) | copy-start | bytes 6291460
  157.4 9.6 %collective-permute-start.14 = (bf16[1024,256]{1,0:T(8,128)(2,1)S(1)}, bf16[1024,256]{1,0:T(8,128)(2,1)S(1)}, u32[]{:S(2)}, u32[]{:S(2)}) collective-permute-start(bf16[1024,256]{1,0:T(8,128)(2,1)S(1)} %get-tuple-element.152), channel_id=1, source_target_pairs={{0,8},{8,16},{16,24},{24,28},{28,20},{20,12},{12,4},{4,0},{1,9},{9... | collective-permute-start | bytes 1572872 | tf_op jit(solution)/shard_map/ppermute | solution.py:226
  158.9 9.4 %collective-permute-start.15 = (bf16[1024,256]{1,0:T(8,128)(2,1)S(1)}, bf16[1024,256]{1,0:T(8,128)(2,1)S(1)}, u32[]{:S(2)}, u32[]{:S(2)}) collective-permute-start(bf16[1024,256]{1,0:T(8,128)(2,1)S(1)} %get-tuple-element.153), channel_id=1, source_target_pairs={{8,0},{16,8},{24,16},{28,24},{20,28},{12,20},{4,12},{0,4},{9,1},{1... | collective-permute-start | bytes 1572872 | tf_op jit(solution)/shard_map/ppermute | solution.py:227
  169.7 9.2 %collective-permute-start.16 = (bf16[1024,256]{1,0:T(8,128)(2,1)S(1)}, bf16[1024,256]{1,0:T(8,128)(2,1)S(1)}, u32[]{:S(2)}, u32[]{:S(2)}) collective-permute-start(bf16[1024,256]{1,0:T(8,128)(2,1)S(1)} %get-tuple-element.165), channel_id=1, source_target_pairs={{0,8},{8,16},{16,24},{24,28},{28,20},{20,12},{12,4},{4,0},{1,9},{9... | collective-permute-start | bytes 1572872 | tf_op jit(solution)/shard_map/ppermute | solution.py:226
  171.8 9.2 %collective-permute-start.17 = (bf16[1024,256]{1,0:T(8,128)(2,1)S(1)}, bf16[1024,256]{1,0:T(8,128)(2,1)S(1)}, u32[]{:S(2)}, u32[]{:S(2)}) collective-permute-start(bf16[1024,256]{1,0:T(8,128)(2,1)S(1)} %get-tuple-element.166), channel_id=1, source_target_pairs={{8,0},{16,8},{24,16},{28,24},{20,28},{12,20},{4,12},{0,4},{9,1},{1... | collective-permute-start | bytes 1572872 | tf_op jit(solution)/shard_map/ppermute | solution.py:227
  171.9 15.5 %copy-start.1 = (bf16[64,128]{1,0:T(8,128)(2,1)S(1)}, bf16[64,128]{1,0:T(8,128)(2,1)}, u32[]{:S(2)}) copy-start(bf16[64,128]{1,0:T(8,128)(2,1)} %param.11) | copy-start | bytes 49156
  (25 other events, 138.1 us)
Sparse Core Ops, SparseCore 0:
  9.6 37.1 all-gather.1
  143.2 44.1 reduce-scatter.1

commit v10 on v7

--- a/solution.py
+++ b/solution.py
@@ -61,12 +61,16 @@
         window = jnp.concatenate(
             [rows[n * tap_count : n * tap_count + window_rows] for n in range(block_count)], axis=1
         )
+        stacked = table_ref[...].reshape(per_tile * tap_count, window_rows)
+        part = jnp.dot(stacked, window, preferred_element_type=jnp.float32)
         mixed = [jnp.zeros((tap_count, lane_tile), jnp.float32) for _ in range(block_count)]
         for member in range(per_tile):
-            part = jnp.dot(table_ref[member], window, preferred_element_type=jnp.float32)
+            rows_of = slice(member * tap_count, (member + 1) * tap_count)
             for n in range(block_count):
                 mixed[n] = jnp.where(
-                    lane_group == member, part[:, n * lane_tile : (n + 1) * lane_tile], mixed[n]
+                    lane_group == member,
+                    part[rows_of, n * lane_tile : (n + 1) * lane_tile],
+                    mixed[n],
                 )
         for n in range(block_count):
             out_ref[n * tap_count : (n + 1) * tap_count, :] = mixed[n]

time: 191 us -> 191 us (level)
  no operation moved by 1% of the time
where the time goes in v10:
time: 191 us; the launch traced here: 189 us
  other arithmetic  41 us (21%)
  waiting for transfers between devices  38.6 us (20%)
  matrix products  33.8 us (18%)
  starting transfers between devices  26.9 us (14%)
  local copies, waits for them, and re-layouts  17.8 us (9%)
  Pallas kernels  15.9 us (8%)
  between operations  15.2 us (8%)
    ppermute x7, waiting for transfers between devices, ring_reduce_scatter(): ahead = lax.ppermute(sent_ahead, 'seq', forward)  19.2 us
    pallas_call x2, Pallas kernels, band_mix(): pl.pallas_call(body, grid=(channels // lane_tile,), in_specs=[pl.BlockSpe...  15.9 us
    ppermute x7, starting transfers between devices, ring_reduce_scatter(): ahead = lax.ppermute(sent_ahead, 'seq', forward)  11.9 us
    convert_element_type x6, other arithmetic, ring_reduce_scatter(): sent_behind = behind.astype(jnp.bfloat16)  11.6 us
    ppermute x4, waiting for transfers between devices, passed_along(): lax.ppermute(value, axis, [(source, source + steps) for source in range(l...  11.6 us
    ppermute x4, starting transfers between devices, passed_along(): lax.ppermute(value, axis, [(source, source + steps) for source in range(l...  11.4 us
    unnamed x98, local copies, waits for them, and re-layouts  11.1 us
    dot_general x1, matrix products, project(): jnp.dot(gated_rows, out_weight, preferred_element_type=jnp.float32)  9.53 us
  transfers between devices with their start and end apart: 20, of which 12 were waited for; matrix products, arithmetic and copies ran while one was open for 42% of the time, Pallas kernels for 8%

profile of v10, /device:TPU:0, one launch (start us, length us, event | category | flops | bytes accessed | tf_op | source)
XLA Modules:
  0.0 189.2 jit_solution(4403183735532640246)
XLA Ops:
  9.5 4.9 %collective-permute-start = (bf16[3,6,1024]{2,1,0:T(8,128)(2,1)S(1)}, bf16[3,6,1024]{2,1,0:T(8,128)(2,1)S(1)}, u32[]{:S(2)}, u32[]{:S(2)}) collective-permute-start(bf16[3,6,1024]{2,1,0:T(8,128)(2,1)S(1)} %pad_maximum_fusion.9), channel_id=1, source_target_pairs={{0,4},{4,8},{8,12},{12,16},{16,20},{20,24},{24,28},{1,5},{5,9},{9,... | collective-permute-start | bytes 110600 | tf_op jit(solution)/shard_map/ppermute | solution.py:13
  14.6 1.9 fusion.77
  16.7 1.4 fusion.78
  18.2 5.8 %multiply_convert_fusion.2 = (bf16[512,1024]{1,0:T(8,128)(2,1)S(1)}, f32[512,1024]{1,0:T(8,128)}, f32[512,1024]{1,0:T(8,128)}) fusion(bf16[512,1024]{1,0:T(8,128)(2,1)S(1)} %copy-done.6, bf16[6,1024]{1,0:T(8,128)(2,1)S(1)} %get-tuple-element.198, f32[1024]{0:T(1024)} %bitcast.107, f32[1024]{0:T(1024)} %bitcast.105, f32[1024]{0:T(1024)S(1)} %bitcast.95, ...), kind=kLoop, calls=%fused_computation.108 | loop fusion | flops 40894464 | bytes 7421952 | tf_op jit(solution)/shard_map/convert_element_type | solution.py:103
  24.1 3.7 %collective-permute-start.1 = (bf16[128,1024]{1,0:T(8,128)(2,1)S(1)}, bf16[128,1024]{1,0:T(8,128)(2,1)S(1)}, u32[]{:S(2)}, u32[]{:S(2)}) collective-permute-start(bf16[128,1024]{1,0:T(8,128)(2,1)S(1)} %slice.389), channel_id=1, source_target_pairs={{0,4},{4,8},{8,12},{12,16},{16,20},{20,24},{24,28},{1,5},{5,9},{9,... | collective-permute-start | bytes 786440 | tf_op jit(solution)/shard_map/ppermute | solution.py:13
  27.8 3.9 %convolution_convert_fusion.1 = bf16[32768,64]{0,1:T(8,128)(2,1)S(1)} fusion(bf16[64,128]{1,0:T(8,128)(2,1)S(1)} %copy-done, s32[32768]{0:T(1024)S(1)} %get-tuple-element.173), kind=kOutput, calls=%fused_computation.1 | convolution fusion | flops 543162368 | bytes 4341760 | tf_op jit(solution)/shard_map/dot_general | solution.py:46
  31.7 3.1 %copy.15 = bf16[8,8,128,256]{3,2,1,0:T(8,128)(2,1)} copy(bf16[8,8,128,256]{3,1,2,0:T(8,128)(2,1)S(1)} %bitcast.76) | data formatting | bytes 8388608
  34.8 1.2 pad_maximum_fusion.3.rows_ref
  36.0 8.0 %shard_map.110 = f32[512,1024]{1,0:T(8,128)} custom-call(bf16[64,128,256]{2,1,0:T(8,128)(2,1)} %bitcast.75, bf16[640,1024]{1,0:T(8,128)(2,1)} %pad_maximum_fusion.3.rows_ref), custom_call_target="tpu_custom_call" | custom-call | tf_op jit(solution)/shard_map/pallas_call | solution.py:78
  44.1 4.0 %multiply_convert_fusion.1 = (bf16[512,1024]{1,0:T(8,128)(2,1)}, f32[512,1024]{1,0:T(8,128)S(1)}) fusion(f32[512,1024]{1,0:T(8,128)} %shard_map.110, bf16[512,1024]{1,0:T(8,128)(2,1)S(1)} %copy-done.8, bf16[6,1024]{1,0:T(8,128)(2,1)S(1)} %get-tuple-element.197, f32[1024]{0:T(1024)S(1)} %bitcast.111, f32[1024]{0:T(1024)S(1)} %bitcast.113, ...), kind=kLoop, calls=%fused_computation.107 | loop fusion | flops 20971520 | bytes 6332416 | tf_op jit(solution)/shard_map/convert_element_type | solution.py:107
  48.1 7.1 %multiply_convert_fusion = bf16[1024,4096]{1,0:T(8,128)(2,1)S(1)} fusion(bf16[512,1024]{1,0:T(8,128)(2,1)} %get-tuple-element.76, bf16[512,4096]{1,0:T(8,128)(2,1)} %all-gather.2.cloned.1.call-done), kind=kOutput, calls=%fused_computation.3 | convolution fusion | flops 4303355904 | bytes 13631488 | tf_op jit(solution)/shard_map/dot_general | solution.py:201
  55.2 3.4 %copy-done.5 = bf16[1024,4096]{1,0:T(8,128)(2,1)} copy-done((bf16[1024,4096]{1,0:T(8,128)(2,1)}, bf16[1024,4096]{1,0:T(8,128)(2,1)S(1)}, u32[]{:S(2)}) %copy-start.5) | copy-done | bytes 8388632
  59.5 1.6 collective-permute-start.2
  61.5 9.5 %convolution_convert_fusion.2 = bf16[512,4096]{1,0:T(8,128)(2,1)} fusion(bf16[512,1024]{1,0:T(8,128)(2,1)S(1)} %copy-done.9, bf16[1024,4096]{1,0:T(8,128)(2,1)} %param.12), kind=kOutput, calls=%fused_computation.7 | convolution fusion | flops 4297064448 | bytes 13631488 | tf_op jit(solution)/shard_map/dot_general | solution.py:117
  71.1 1.7 collective-permute-done.2
  72.8 1.2 collective-permute-done.3
  74.0 2.6 %add_convert_fusion.12 = (bf16[1024,256]{1,0:T(8,128)(2,1)}, bf16[1024,256]{1,0:T(8,128)(2,1)}) fusion(bf16[1024,256]{1,0:T(8,128)(2,1)} %collective-permute-done.3, bf16[1024,4096]{1,0:T(8,128)(2,1)} %copy-done.5, s32[]{:T(128)S(6)} %select_n.533, s32[]{:T(128)S(6)} %select_n.524, bf16[1024,256]{1,0:T(8,128)(2,1)S(1)} %collective-permute-done.2), kind=kLoop, calls=%fused_computation.154 | loop fusion | flops 2097152 | bytes 3145736 | tf_op jit(solution)/shard_map/convert_element_type | solution.py:218
  76.6 1.6 collective-permute-start.4
  78.6 9.4 %fusion.79 = f32[1024,512]{0,1:T(8,128)S(1)} fusion(bf16[1024,4096]{1,0:T(8,128)(2,1)} %param.12, bf16[512,4096]{1,0:T(8,128)(2,1)} %all-gather.2.cloned.1.call-done), kind=kOutput, calls=%fused_computation.182 | convolution fusion | flops 4294967296 | bytes 14680064 | tf_op jit(solution)/shard_map/dot_general | solution.py:128
  88.0 2.1 %bitcast_multiply_fusion = (f32[512,1024]{1,0:T(8,128)}, bf16[512,1024]{1,0:T(8,128)(2,1)S(1)}) fusion(f32[512,1024]{1,0:T(8,128)S(1)} %copy-done.1, f32[1024,512]{0,1:T(8,128)S(1)} %fusion.79, f32[512,1024]{1,0:T(8,128)S(1)} %get-tuple-element.148), kind=kLoop, calls=%fused_computation.104 | loop fusion | flops 1572864 | bytes 9437184 | tf_op jit(solution)/shard_map/mul | solution.py:132
  90.2 1.3 collective-permute-start.6
  91.5 6.9 %collective-permute-done.6 = bf16[128,1024]{1,0:T(8,128)(2,1)S(1)} collective-permute-done((bf16[128,1024]{1,0:T(8,128)(2,1)S(1)}, bf16[128,1024]{1,0:T(8,128)(2,1)S(1)}, u32[]{:S(2)}, u32[]{:S(2)}) %collective-permute-start.6) | collective-permute-done | bytes 262176 | tf_op jit(solution)/shard_map/ppermute | solution.py:13
  98.4 1.9 add_convert_fusion.10
  100.3 1.7 collective-permute-start.7
  102.4 3.9 %convolution_convert_fusion = bf16[32768,64]{0,1:T(8,128)(2,1)S(1)} fusion(bf16[64,128]{1,0:T(8,128)(2,1)S(1)} %copy-done, s32[32768]{0:T(1024)S(1)} %get-tuple-element.172), kind=kOutput, calls=%fused_computation | convolution fusion | flops 543162368 | bytes 4341760 | tf_op jit(solution)/shard_map/dot_general | solution.py:46
  106.3 3.0 %copy.17 = bf16[8,8,128,256]{3,2,1,0:T(8,128)(2,1)} copy(bf16[8,8,128,256]{3,1,2,0:T(8,128)(2,1)S(1)} %bitcast.77) | data formatting | bytes 8388608
  109.3 1.6 collective-permute-done.7
  110.9 1.3 collective-permute-done.8
  112.2 2.4 %add_convert_fusion.8 = (bf16[1024,256]{1,0:T(8,128)(2,1)}, bf16[1024,256]{1,0:T(8,128)(2,1)}) fusion(bf16[1024,256]{1,0:T(8,128)(2,1)S(1)} %collective-permute-done.8, bf16[1024,4096]{1,0:T(8,128)(2,1)} %copy-done.5, s32[]{:T(128)S(6)} %select_n.569, s32[]{:T(128)S(6)} %select_n.560, bf16[1024,256]{1,0:T(8,128)(2,1)S(1)} %collective-permute-done.7), kind=kLoop, calls=%fused_computation.150 | loop fusion | flops 2097152 | bytes 3145736 | tf_op jit(solution)/shard_map/convert_element_type | solution.py:218
  115.1 1.6 collective-permute-start.9
  117.8 7.9 %shard_map.111 = f32[512,1024]{1,0:T(8,128)} custom-call(bf16[64,128,256]{2,1,0:T(8,128)(2,1)} %bitcast.74, bf16[640,1024]{1,0:T(8,128)(2,1)} %pad_maximum_fusion.4.rows_ref), custom_call_target="tpu_custom_call" | custom-call | tf_op jit(solution)/shard_map/pallas_call | solution.py:78
  125.7 3.5 %fusion.75 = (f32[512,1024]{1,0:T(8,128)S(1)}, f32[512,1024]{1,0:T(8,128)S(1)}) fusion(f32[512,1024]{1,0:T(8,128)} %shard_map.111, f32[512,1024]{1,0:T(8,128)} %get-tuple-element.151, f32[512,1024]{1,0:T(8,128)} %get-tuple-element.150), kind=kLoop, calls=%fused_computation.178 | loop fusion | flops 1048576 | bytes 10485760 | tf_op jit(solution)/shard_map/mul | solution.py:142
  129.4 1.2 copy-done.2
  131.4 1.6 collective-permute-start.11
  133.2 4.7 %collective-permute-done.11 = bf16[3,6,1024]{2,1,0:T(8,128)(2,1)S(1)} collective-permute-done((bf16[3,6,1024]{2,1,0:T(8,128)(2,1)S(1)}, bf16[3,6,1024]{2,1,0:T(8,128)(2,1)S(1)}, u32[]{:S(2)}, u32[]{:S(2)}) %collective-permute-start.11) | collective-permute-done | bytes 36896 | tf_op jit(solution)/shard_map/ppermute | solution.py:13
  137.9 1.8 add_convert_fusion.6
  139.7 1.3 collective-permute-start.12
  141.9 3.0 %fusion.40 = bf16[512,1024]{1,0:T(8,128)(2,1)} fusion(f32[6,1024]{1,0:T(8,128)S(1)} %bitcast_convert_fusion.2, f32[512,1024]{1,0:T(8,128)S(1)} %copy-done.4, f32[1024]{0:T(1024)S(1)} %bitcast.112, f32[1024]{0:T(1024)S(1)} %bitcast.114, f32[1024]{0:T(1024)S(1)} %bitcast.116, f32[1024]{0:T(1024)S(1)} %bitcast.118, f32[1024]{0:T(1024)S(1)} %bitcast.120, ...), kind=kLoop, calls=%fused_computation.76 | loop fusion | flops 10485760 | bytes 3198976 | tf_op jit(solution)/shard_map/convert_element_type | solution.py:160
  144.9 4.9 %collective-permute-done.12 = bf16[1024,256]{1,0:T(8,128)(2,1)S(1)} collective-permute-done((bf16[1024,256]{1,0:T(8,128)(2,1)S(1)}, bf16[1024,256]{1,0:T(8,128)(2,1)S(1)}, u32[]{:S(2)}, u32[]{:S(2)}) %collective-permute-start.12) | collective-permute-done | bytes 524320 | tf_op jit(solution)/shard_map/ppermute | solution.py:223
  150.8 1.5 add_convert_fusion.4
  152.3 3.2 %collective-permute-start.14 = (bf16[1024,256]{1,0:T(8,128)(2,1)S(1)}, bf16[1024,256]{1,0:T(8,128)(2,1)S(1)}, u32[]{:S(2)}, u32[]{:S(2)}) collective-permute-start(bf16[1024,256]{1,0:T(8,128)(2,1)S(1)} %get-tuple-element.126), channel_id=1, source_target_pairs={{0,8},{8,16},{16,24},{24,28},{28,20},{20,12},{12,4},{4,0},{1,9},{9... | collective-permute-start | bytes 1572872 | tf_op jit(solution)/shard_map/ppermute | solution.py:223
  155.6 3.0 %fusion.6 = bf16[512,1024]{1,0:T(8,128)(2,1)} fusion(f32[6,1024]{1,0:T(8,128)S(1)} %get-tuple-element.195, f32[512,1024]{1,0:T(8,128)S(1)} %copy-done.3, f32[1024]{0:T(1024)S(1)} %bitcast.108, f32[1024]{0:T(1024)S(1)} %bitcast.106, f32[1024]{0:T(1024)S(1)} %bitcast.96, f32[1024]{0:T(1024)S(1)} %bitcast.98, f32[1024]{0:T(1024)S(1)} %bitcast.100, ...), kind=kLoop, calls=%fused_computation.42 | loop fusion | flops 10485760 | bytes 3198976 | tf_op jit(solution)/shard_map/convert_element_type | solution.py:160
  158.6 3.0 %fusion.23 = bf16[512,1024]{1,0:T(8,128)(2,1)} fusion(f32[6,1024]{1,0:T(8,128)S(1)} %get-tuple-element.196, f32[512,1024]{1,0:T(8,128)S(1)} %get-tuple-element.128, f32[1024]{0:T(1024)S(1)} %bitcast.82, f32[1024]{0:T(1024)S(1)} %bitcast.84, f32[1024]{0:T(1024)S(1)} %bitcast.86, f32[1024]{0:T(1024)S(1)} %bitcast.88, f32[1024]{0:T(1024)S(1)} %bitcast.90, ...), kind=kLoop, calls=%fused_computation.59 | loop fusion | flops 10485760 | bytes 3198976 | tf_op jit(solution)/shard_map/convert_element_type | solution.py:160
  161.6 3.8 %collective-permute-done.14 = bf16[1024,256]{1,0:T(8,128)(2,1)S(1)} collective-permute-done((bf16[1024,256]{1,0:T(8,128)(2,1)S(1)}, bf16[1024,256]{1,0:T(8,128)(2,1)S(1)}, u32[]{:S(2)}, u32[]{:S(2)}) %collective-permute-start.14) | collective-permute-done | bytes 524320 | tf_op jit(solution)/shard_map/ppermute | solution.py:223
  165.4 2.8 %collective-permute-done.15 = bf16[1024,256]{1,0:T(8,128)(2,1)S(1)} collective-permute-done((bf16[1024,256]{1,0:T(8,128)(2,1)S(1)}, bf16[1024,256]{1,0:T(8,128)(2,1)S(1)}, u32[]{:S(2)}, u32[]{:S(2)}) %collective-permute-start.15) | collective-permute-done | bytes 524320 | tf_op jit(solution)/shard_map/ppermute | solution.py:224
  168.2 1.5 add_convert_fusion.2
  171.7 7.2 %collective-permute-done.16 = bf16[1024,256]{1,0:T(8,128)(2,1)S(1)} collective-permute-done((bf16[1024,256]{1,0:T(8,128)(2,1)S(1)}, bf16[1024,256]{1,0:T(8,128)(2,1)S(1)}, u32[]{:S(2)}, u32[]{:S(2)}) %collective-permute-start.16) | collective-permute-done | bytes 524320 | tf_op jit(solution)/shard_map/ppermute | solution.py:223
  179.8 1.5 add_convert_fusion.1
  (134 shorter events, 13.3 us)
Async XLA Ops:
  7.2 20.6 %copy-start = (bf16[64,128]{1,0:T(8,128)(2,1)S(1)}, bf16[64,128]{1,0:T(8,128)(2,1)}, u32[]{:S(2)}) copy-start(bf16[64,128]{1,0:T(8,128)(2,1)} %param.11) | copy-start | bytes 49156
  7.2 11.0 %copy-start.7 = (bf16[512,1024]{1,0:T(8,128)(2,1)S(1)}, bf16[512,1024]{1,0:T(8,128)(2,1)}, u32[]{:S(2)}) copy-start(bf16[512,1024]{1,0:T(8,128)(2,1)} %param.8) | copy-start | bytes 3145732
  7.2 11.0 %copy-start.6 = (bf16[512,1024]{1,0:T(8,128)(2,1)S(1)}, bf16[512,1024]{1,0:T(8,128)(2,1)}, u32[]{:S(2)}) copy-start(bf16[512,1024]{1,0:T(8,128)(2,1)} %param.9) | copy-start | bytes 3145732
  7.2 40.9 %all-gather.2.cloned.1.call-start = ((), (), s32[]{:S(2)}) async-start(), calls=%async_computation.1 | async-start | bytes 5242880 | tf_op jit(solution)/shard_map/all_gather | solution.py:94
  7.9 174.4 %reduce-scatter.2.cloned.1.call-start = ((), (), s32[]{:S(2)}) async-start(), calls=%async_computation.2 | async-start | bytes 5242880 | tf_op jit(solution)/shard_map/reduce_scatter | solution.py:116
  9.5 8.7 %collective-permute-start = (bf16[3,6,1024]{2,1,0:T(8,128)(2,1)S(1)}, bf16[3,6,1024]{2,1,0:T(8,128)(2,1)S(1)}, u32[]{:S(2)}, u32[]{:S(2)}) collective-permute-start(bf16[3,6,1024]{2,1,0:T(8,128)(2,1)S(1)} %pad_maximum_fusion.9), channel_id=1, source_target_pairs={{0,4},{4,8},{8,12},{12,16},{16,20},{20,24},{24,28},{1,5},{5,9},{9,... | collective-permute-start | bytes 110600 | tf_op jit(solution)/shard_map/ppermute | solution.py:13
  24.1 10.7 %collective-permute-start.1 = (bf16[128,1024]{1,0:T(8,128)(2,1)S(1)}, bf16[128,1024]{1,0:T(8,128)(2,1)S(1)}, u32[]{:S(2)}, u32[]{:S(2)}) collective-permute-start(bf16[128,1024]{1,0:T(8,128)(2,1)S(1)} %slice.389), channel_id=1, source_target_pairs={{0,4},{4,8},{8,12},{12,16},{16,20},{20,24},{24,28},{1,5},{5,9},{9,... | collective-permute-start | bytes 786440 | tf_op jit(solution)/shard_map/ppermute | solution.py:13
  36.0 8.0 %copy-start.8 = (bf16[512,1024]{1,0:T(8,128)(2,1)S(1)}, bf16[512,1024]{1,0:T(8,128)(2,1)}, u32[]{:S(2)}) copy-start(bf16[512,1024]{1,0:T(8,128)(2,1)} %param.7) | copy-start | bytes 3145732
  36.0 8.0 %copy-start.32 = (f32[1,1,1024]{2,0,1:T(1,128)S(1)}, f32[1,1,1024]{2,0,1:T(1,128)}, u32[]{:S(2)}) copy-start(f32[1,1,1024]{2,0,1:T(1,128)} %get-tuple-element.174) | copy-start | bytes 12292
  36.0 8.0 %copy-start.34 = (f32[1,1,1024]{2,0,1:T(1,128)S(1)}, f32[1,1,1024]{2,0,1:T(1,128)}, u32[]{:S(2)}) copy-start(f32[1,1,1024]{2,0,1:T(1,128)} %get-tuple-element.187) | copy-start | bytes 12292
  36.0 8.0 %copy-start.36 = (f32[1,1,1024]{2,0,1:T(1,128)S(1)}, f32[1,1,1024]{2,0,1:T(1,128)}, u32[]{:S(2)}) copy-start(f32[1,1,1024]{2,0,1:T(1,128)} %get-tuple-element.188) | copy-start | bytes 12292
  36.0 8.0 %copy-start.38 = (f32[1,1,1024]{2,0,1:T(1,128)S(1)}, f32[1,1,1024]{2,0,1:T(1,128)}, u32[]{:S(2)}) copy-start(f32[1,1,1024]{2,0,1:T(1,128)} %get-tuple-element.189) | copy-start | bytes 12292
  36.0 8.0 %copy-start.40 = (f32[1,1,1024]{2,0,1:T(1,128)S(1)}, f32[1,1,1024]{2,0,1:T(1,128)}, u32[]{:S(2)}) copy-start(f32[1,1,1024]{2,0,1:T(1,128)} %get-tuple-element.190) | copy-start | bytes 12292
  36.0 8.0 %copy-start.42 = (f32[1,1,1024]{2,0,1:T(1,128)S(1)}, f32[1,1,1024]{2,0,1:T(1,128)}, u32[]{:S(2)}) copy-start(f32[1,1,1024]{2,0,1:T(1,128)} %get-tuple-element.191) | copy-start | bytes 12292
  36.0 8.0 %copy-start.44 = (f32[1,1,1024]{2,0,1:T(1,128)S(1)}, f32[1,1,1024]{2,0,1:T(1,128)}, u32[]{:S(2)}) copy-start(f32[1,1,1024]{2,0,1:T(1,128)} %get-tuple-element.192) | copy-start | bytes 12292
  59.5 13.3 %collective-permute-start.2 = (bf16[1024,256]{1,0:T(8,128)(2,1)}, bf16[1024,256]{1,0:T(8,128)(2,1)S(1)}, u32[]{:S(2)}, u32[]{:S(2)}) collective-permute-start(bf16[1024,256]{1,0:T(8,128)(2,1)} %get-tuple-element.78), channel_id=1, source_target_pairs={{0,8},{8,16},{16,24},{24,28},{28,20},{20,12},{12,4},{4,0},{1,9},{9... | collective-permute-start | bytes 1572872 | tf_op jit(solution)/shard_map/ppermute | solution.py:223
  61.1 12.9 %collective-permute-start.3 = (bf16[1024,256]{1,0:T(8,128)(2,1)S(1)}, bf16[1024,256]{1,0:T(8,128)(2,1)}, u32[]{:S(2)}, u32[]{:S(2)}) collective-permute-start(bf16[1024,256]{1,0:T(8,128)(2,1)S(1)} %get-tuple-element.79), channel_id=1, source_target_pairs={{8,0},{16,8},{24,16},{28,24},{20,28},{12,20},{4,12},{0,4},{9,1},{1... | collective-permute-start | bytes 1572872 | tf_op jit(solution)/shard_map/ppermute | solution.py:224
  76.6 11.5 %copy-start.1 = (f32[512,1024]{1,0:T(8,128)S(1)}, f32[512,1024]{1,0:T(8,128)}, u32[]{:S(2)}) copy-start(f32[512,1024]{1,0:T(8,128)} %shard_map.110) | copy-start | bytes 6291460
  76.6 21.9 %collective-permute-start.4 = (bf16[1024,256]{1,0:T(8,128)(2,1)}, bf16[1024,256]{1,0:T(8,128)(2,1)}, u32[]{:S(2)}, u32[]{:S(2)}) collective-permute-start(bf16[1024,256]{1,0:T(8,128)(2,1)} %get-tuple-element.83), channel_id=1, source_target_pairs={{0,8},{8,16},{16,24},{24,28},{28,20},{20,12},{12,4},{4,0},{1,9},{9... | collective-permute-start | bytes 1572872 | tf_op jit(solution)/shard_map/ppermute | solution.py:223
  78.2 20.3 %collective-permute-start.5 = (bf16[1024,256]{1,0:T(8,128)(2,1)}, bf16[1024,256]{1,0:T(8,128)(2,1)}, u32[]{:S(2)}, u32[]{:S(2)}) collective-permute-start(bf16[1024,256]{1,0:T(8,128)(2,1)} %get-tuple-element.84), channel_id=1, source_target_pairs={{8,0},{16,8},{24,16},{28,24},{20,28},{12,20},{4,12},{0,4},{9,1},{1... | collective-permute-start | bytes 1572872 | tf_op jit(solution)/shard_map/ppermute | solution.py:224
  90.2 8.3 %collective-permute-start.6 = (bf16[128,1024]{1,0:T(8,128)(2,1)S(1)}, bf16[128,1024]{1,0:T(8,128)(2,1)S(1)}, u32[]{:S(2)}, u32[]{:S(2)}) collective-permute-start(bf16[128,1024]{1,0:T(8,128)(2,1)S(1)} %slice.390), channel_id=1, source_target_pairs={{4,0},{8,4},{12,8},{16,12},{20,16},{24,20},{28,24},{5,1},{9,5},{13... | collective-permute-start | bytes 786440 | tf_op jit(solution)/shard_map/ppermute | solution.py:13
  100.3 10.6 %collective-permute-start.7 = (bf16[1024,256]{1,0:T(8,128)(2,1)S(1)}, bf16[1024,256]{1,0:T(8,128)(2,1)S(1)}, u32[]{:S(2)}, u32[]{:S(2)}) collective-permute-start(bf16[1024,256]{1,0:T(8,128)(2,1)S(1)} %get-tuple-element.91), channel_id=1, source_target_pairs={{0,8},{8,16},{16,24},{24,28},{28,20},{20,12},{12,4},{4,0},{1,9},{9... | collective-permute-start | bytes 1572872 | tf_op jit(solution)/shard_map/ppermute | solution.py:223
  102.0 10.2 %collective-permute-start.8 = (bf16[1024,256]{1,0:T(8,128)(2,1)S(1)}, bf16[1024,256]{1,0:T(8,128)(2,1)S(1)}, u32[]{:S(2)}, u32[]{:S(2)}) collective-permute-start(bf16[1024,256]{1,0:T(8,128)(2,1)S(1)} %get-tuple-element.92), channel_id=1, source_target_pairs={{8,0},{16,8},{24,16},{28,24},{20,28},{12,20},{4,12},{0,4},{9,1},{1... | collective-permute-start | bytes 1572872 | tf_op jit(solution)/shard_map/ppermute | solution.py:224
  114.6 23.3 %collective-permute-start.10 = (bf16[1024,256]{1,0:T(8,128)(2,1)}, bf16[1024,256]{1,0:T(8,128)(2,1)}, u32[]{:S(2)}, u32[]{:S(2)}) collective-permute-start(bf16[1024,256]{1,0:T(8,128)(2,1)} %get-tuple-element.103), channel_id=1, source_target_pairs={{8,0},{16,8},{24,16},{28,24},{20,28},{12,20},{4,12},{0,4},{9,1},{1... | collective-permute-start | bytes 1572872 | tf_op jit(solution)/shard_map/ppermute | solution.py:224
  115.1 22.9 %collective-permute-start.9 = (bf16[1024,256]{1,0:T(8,128)(2,1)}, bf16[1024,256]{1,0:T(8,128)(2,1)}, u32[]{:S(2)}, u32[]{:S(2)}) collective-permute-start(bf16[1024,256]{1,0:T(8,128)(2,1)} %get-tuple-element.102), channel_id=1, source_target_pairs={{0,8},{8,16},{16,24},{24,28},{28,20},{20,12},{12,4},{4,0},{1,9},{9... | collective-permute-start | bytes 1572872 | tf_op jit(solution)/shard_map/ppermute | solution.py:223
  129.3 12.5 %copy-start.33 = (f32[1,1,1024]{2,0,1:T(1,128)S(1)}, f32[1,1,1024]{2,0,1:T(1,128)}, u32[]{:S(2)}) copy-start(f32[1,1,1024]{2,0,1:T(1,128)} %get-tuple-element.174) | copy-start | bytes 12292
  129.3 12.5 %copy-start.35 = (f32[1,1,1024]{2,0,1:T(1,128)S(1)}, f32[1,1,1024]{2,0,1:T(1,128)}, u32[]{:S(2)}) copy-start(f32[1,1,1024]{2,0,1:T(1,128)} %get-tuple-element.187) | copy-start | bytes 12292
  129.3 12.5 %copy-start.37 = (f32[1,1,1024]{2,0,1:T(1,128)S(1)}, f32[1,1,1024]{2,0,1:T(1,128)}, u32[]{:S(2)}) copy-start(f32[1,1,1024]{2,0,1:T(1,128)} %get-tuple-element.188) | copy-start | bytes 12292
  129.3 12.5 %copy-start.39 = (f32[1,1,1024]{2,0,1:T(1,128)S(1)}, f32[1,1,1024]{2,0,1:T(1,128)}, u32[]{:S(2)}) copy-start(f32[1,1,1024]{2,0,1:T(1,128)} %get-tuple-element.189) | copy-start | bytes 12292
  129.3 12.5 %copy-start.41 = (f32[1,1,1024]{2,0,1:T(1,128)S(1)}, f32[1,1,1024]{2,0,1:T(1,128)}, u32[]{:S(2)}) copy-start(f32[1,1,1024]{2,0,1:T(1,128)} %get-tuple-element.190) | copy-start | bytes 12292
  129.4 12.5 %copy-start.43 = (f32[1,1,1024]{2,0,1:T(1,128)S(1)}, f32[1,1,1024]{2,0,1:T(1,128)}, u32[]{:S(2)}) copy-start(f32[1,1,1024]{2,0,1:T(1,128)} %get-tuple-element.191) | copy-start | bytes 12292
  129.4 12.5 %copy-start.45 = (f32[1,1,1024]{2,0,1:T(1,128)S(1)}, f32[1,1,1024]{2,0,1:T(1,128)}, u32[]{:S(2)}) copy-start(f32[1,1,1024]{2,0,1:T(1,128)} %get-tuple-element.192) | copy-start | bytes 12292
  131.4 6.5 %collective-permute-start.11 = (bf16[3,6,1024]{2,1,0:T(8,128)(2,1)S(1)}, bf16[3,6,1024]{2,1,0:T(8,128)(2,1)S(1)}, u32[]{:S(2)}, u32[]{:S(2)}) collective-permute-start(bf16[3,6,1024]{2,1,0:T(8,128)(2,1)S(1)} %pad_maximum_fusion.10), channel_id=1, source_target_pairs={{4,0},{8,4},{12,8},{16,12},{20,16},{24,20},{28,24},{5,1},{9,5},{13... | collective-permute-start | bytes 110600 | tf_op jit(solution)/shard_map/ppermute | solution.py:13
  133.2 8.6 %copy-start.4 = (f32[512,1024]{1,0:T(8,128)S(1)}, f32[512,1024]{1,0:T(8,128)}, u32[]{:S(2)}) copy-start(f32[512,1024]{1,0:T(8,128)} %get-tuple-element.116) | copy-start | bytes 6291460
  139.7 10.1 %collective-permute-start.12 = (bf16[1024,256]{1,0:T(8,128)(2,1)S(1)}, bf16[1024,256]{1,0:T(8,128)(2,1)S(1)}, u32[]{:S(2)}, u32[]{:S(2)}) collective-permute-start(bf16[1024,256]{1,0:T(8,128)(2,1)S(1)} %get-tuple-element.114), channel_id=1, source_target_pairs={{0,8},{8,16},{16,24},{24,28},{28,20},{20,12},{12,4},{4,0},{1,9},{9... | collective-permute-start | bytes 1572872 | tf_op jit(solution)/shard_map/ppermute | solution.py:223
  141.0 9.8 %collective-permute-start.13 = (bf16[1024,256]{1,0:T(8,128)(2,1)S(1)}, bf16[1024,256]{1,0:T(8,128)(2,1)S(1)}, u32[]{:S(2)}, u32[]{:S(2)}) collective-permute-start(bf16[1024,256]{1,0:T(8,128)(2,1)S(1)} %get-tuple-element.115), channel_id=1, source_target_pairs={{8,0},{16,8},{24,16},{28,24},{20,28},{12,20},{4,12},{0,4},{9,1},{1... | collective-permute-start | bytes 1572872 | tf_op jit(solution)/shard_map/ppermute | solution.py:224
  144.8 10.7 %copy-start.3 = (f32[512,1024]{1,0:T(8,128)S(1)}, f32[512,1024]{1,0:T(8,128)}, u32[]{:S(2)}) copy-start(f32[512,1024]{1,0:T(8,128)} %copy-done.2) | copy-start | bytes 6291460
  144.8 10.7 %copy-start.25 = (f32[1,1,1024]{2,0,1:T(1,128)S(1)}, f32[1,1,1024]{2,0,1:T(1,128)}, u32[]{:S(2)}) copy-start(f32[1,1,1024]{2,0,1:T(1,128)} %copy-done.24) | copy-start | bytes 12292
  144.8 10.7 %copy-start.26 = (f32[1,1,1024]{2,0,1:T(1,128)S(1)}, f32[1,1,1024]{2,0,1:T(1,128)}, u32[]{:S(2)}) copy-start(f32[1,1,1024]{2,0,1:T(1,128)} %get-tuple-element.176) | copy-start | bytes 12292
  144.8 10.7 %copy-start.27 = (f32[1,1,1024]{2,0,1:T(1,128)S(1)}, f32[1,1,1024]{2,0,1:T(1,128)}, u32[]{:S(2)}) copy-start(f32[1,1,1024]{2,0,1:T(1,128)} %get-tuple-element.177) | copy-start | bytes 12292
  144.9 10.7 %copy-start.28 = (f32[1,1,1024]{2,0,1:T(1,128)S(1)}, f32[1,1,1024]{2,0,1:T(1,128)}, u32[]{:S(2)}) copy-start(f32[1,1,1024]{2,0,1:T(1,128)} %get-tuple-element.178) | copy-start | bytes 12292
  144.9 10.7 %copy-start.29 = (f32[1,1,1024]{2,0,1:T(1,128)S(1)}, f32[1,1,1024]{2,0,1:T(1,128)}, u32[]{:S(2)}) copy-start(f32[1,1,1024]{2,0,1:T(1,128)} %get-tuple-element.179) | copy-start | bytes 12292
  144.9 10.7 %copy-start.30 = (f32[1,1,1024]{2,0,1:T(1,128)S(1)}, f32[1,1,1024]{2,0,1:T(1,128)}, u32[]{:S(2)}) copy-start(f32[1,1,1024]{2,0,1:T(1,128)} %get-tuple-element.193) | copy-start | bytes 12292
  144.9 10.7 %copy-start.31 = (f32[1,1,1024]{2,0,1:T(1,128)S(1)}, f32[1,1,1024]{2,0,1:T(1,128)}, u32[]{:S(2)}) copy-start(f32[1,1,1024]{2,0,1:T(1,128)} %get-tuple-element.194) | copy-start | bytes 12292
  152.3 13.1 %collective-permute-start.14 = (bf16[1024,256]{1,0:T(8,128)(2,1)S(1)}, bf16[1024,256]{1,0:T(8,128)(2,1)S(1)}, u32[]{:S(2)}, u32[]{:S(2)}) collective-permute-start(bf16[1024,256]{1,0:T(8,128)(2,1)S(1)} %get-tuple-element.126), channel_id=1, source_target_pairs={{0,8},{8,16},{16,24},{24,28},{28,20},{20,12},{12,4},{4,0},{1,9},{9... | collective-permute-start | bytes 1572872 | tf_op jit(solution)/shard_map/ppermute | solution.py:223
  155.5 12.7 %collective-permute-start.15 = (bf16[1024,256]{1,0:T(8,128)(2,1)S(1)}, bf16[1024,256]{1,0:T(8,128)(2,1)S(1)}, u32[]{:S(2)}, u32[]{:S(2)}) collective-permute-start(bf16[1024,256]{1,0:T(8,128)(2,1)S(1)} %get-tuple-element.127), channel_id=1, source_target_pairs={{8,0},{16,8},{24,16},{28,24},{20,28},{12,20},{4,12},{0,4},{9,1},{1... | collective-permute-start | bytes 1572872 | tf_op jit(solution)/shard_map/ppermute | solution.py:224
  169.6 9.2 %collective-permute-start.16 = (bf16[1024,256]{1,0:T(8,128)(2,1)S(1)}, bf16[1024,256]{1,0:T(8,128)(2,1)S(1)}, u32[]{:S(2)}, u32[]{:S(2)}) collective-permute-start(bf16[1024,256]{1,0:T(8,128)(2,1)S(1)} %get-tuple-element.137), channel_id=1, source_target_pairs={{0,8},{8,16},{16,24},{24,28},{28,20},{20,12},{12,4},{4,0},{1,9},{9... | collective-permute-start | bytes 1572872 | tf_op jit(solution)/shard_map/ppermute | solution.py:223
  170.6 9.2 %collective-permute-start.17 = (bf16[1024,256]{1,0:T(8,128)(2,1)S(1)}, bf16[1024,256]{1,0:T(8,128)(2,1)S(1)}, u32[]{:S(2)}, u32[]{:S(2)}) collective-permute-start(bf16[1024,256]{1,0:T(8,128)(2,1)S(1)} %get-tuple-element.138), channel_id=1, source_target_pairs={{8,0},{16,8},{24,16},{28,24},{20,28},{12,20},{4,12},{0,4},{9,1},{1... | collective-permute-start | bytes 1572872 | tf_op jit(solution)/shard_map/ppermute | solution.py:224
  (18 other events, 112.5 us)
Sparse Core Ops, SparseCore 0:
  9.6 37.1 all-gather.1
  71.2 44.8 reduce-scatter.1

commit v11 on v10

--- a/solution.py
+++ b/solution.py
@@ -47,7 +47,7 @@
     return table.astype(jnp.bfloat16).reshape(filter_taps.shape[0], tap_count, window_rows)
 
 
-def band_mix(padded_rows, table, lane_tile=128):
+def band_mix(padded_rows, table, lane_tile=256):
     group_count, tap_count, window_rows = table.shape
     row_count = padded_rows.shape[0] - tap_count
     block_count = row_count // tap_count

time: 191 us -> 190 us (level)
    ppermute x7, starting transfers between devices: 11.9 us -> 9.84 us  [ring_reduce_scatter(): ahead = lax.ppermute(sent_ahead, 'seq', forward)]
  transfers between devices with their start and end apart: 20 -> 20, of which waited for: 12 -> 12; matrix products, arithmetic and copies ran while one was open for 42% -> 43% of each run, Pallas kernels for 8% -> 8%
where the time goes in v11:
time: 190 us; the launch traced here: 187 us
  other arithmetic  41 us (22%)
  waiting for transfers between devices  39 us (21%)
  matrix products  33.8 us (18%)
  starting transfers between devices  25.6 us (13%)
  local copies, waits for them, and re-layouts  17.8 us (9%)
  between operations  15.2 us (8%)
  Pallas kernels  15 us (8%)
    ppermute x7, waiting for transfers between devices, ring_reduce_scatter(): ahead = lax.ppermute(sent_ahead, 'seq', forward)  19 us
    pallas_call x2, Pallas kernels, band_mix(): pl.pallas_call(body, grid=(channels // lane_tile,), in_specs=[pl.BlockSpe...  15 us
    ppermute x4, waiting for transfers between devices, passed_along(): lax.ppermute(value, axis, [(source, source + steps) for source in range(l...  11.8 us
    convert_element_type x6, other arithmetic, ring_reduce_scatter(): sent_behind = behind.astype(jnp.bfloat16)  11.6 us
    ppermute x4, starting transfers between devices, passed_along(): lax.ppermute(value, axis, [(source, source + steps) for source in range(l...  11.1 us
    unnamed x98, local copies, waits for them, and re-layouts  11.1 us
    ppermute x7, starting transfers between devices, ring_reduce_scatter(): ahead = lax.ppermute(sent_ahead, 'seq', forward)  9.84 us
    dot_general x1, matrix products, project(): jnp.dot(gated_rows, out_weight, preferred_element_type=jnp.float32)  9.53 us
  transfers between devices with their start and end apart: 20, of which 12 were waited for; matrix products, arithmetic and copies ran while one was open for 43% of the time, Pallas kernels for 8%

profile of v11, /device:TPU:0, one launch (start us, length us, event | category | flops | bytes accessed | tf_op | source)
XLA Modules:
  0.0 187.4 jit_solution(8577845889144098021)
XLA Ops:
  9.5 4.9 %collective-permute-start = (bf16[3,6,1024]{2,1,0:T(8,128)(2,1)S(1)}, bf16[3,6,1024]{2,1,0:T(8,128)(2,1)S(1)}, u32[]{:S(2)}, u32[]{:S(2)}) collective-permute-start(bf16[3,6,1024]{2,1,0:T(8,128)(2,1)S(1)} %pad_maximum_fusion.9), channel_id=1, source_target_pairs={{0,4},{4,8},{8,12},{12,16},{16,20},{20,24},{24,28},{1,5},{5,9},{9,... | collective-permute-start | bytes 110600 | tf_op jit(solution)/shard_map/ppermute | solution.py:13
  14.6 1.9 fusion.77
  16.7 1.4 fusion.78
  18.2 5.8 %multiply_convert_fusion.2 = (bf16[512,1024]{1,0:T(8,128)(2,1)S(1)}, f32[512,1024]{1,0:T(8,128)}, f32[512,1024]{1,0:T(8,128)}) fusion(bf16[512,1024]{1,0:T(8,128)(2,1)S(1)} %copy-done.6, bf16[6,1024]{1,0:T(8,128)(2,1)S(1)} %get-tuple-element.198, f32[1024]{0:T(1024)} %bitcast.107, f32[1024]{0:T(1024)} %bitcast.105, f32[1024]{0:T(1024)S(1)} %bitcast.95, ...), kind=kLoop, calls=%fused_computation.108 | loop fusion | flops 40894464 | bytes 7421952 | tf_op jit(solution)/shard_map/convert_element_type | solution.py:103
  24.1 3.7 %collective-permute-start.1 = (bf16[128,1024]{1,0:T(8,128)(2,1)S(1)}, bf16[128,1024]{1,0:T(8,128)(2,1)S(1)}, u32[]{:S(2)}, u32[]{:S(2)}) collective-permute-start(bf16[128,1024]{1,0:T(8,128)(2,1)S(1)} %slice.389), channel_id=1, source_target_pairs={{0,4},{4,8},{8,12},{12,16},{16,20},{20,24},{24,28},{1,5},{5,9},{9,... | collective-permute-start | bytes 786440 | tf_op jit(solution)/shard_map/ppermute | solution.py:13
  27.8 3.9 %convolution_convert_fusion.1 = bf16[32768,64]{0,1:T(8,128)(2,1)S(1)} fusion(bf16[64,128]{1,0:T(8,128)(2,1)S(1)} %copy-done, s32[32768]{0:T(1024)S(1)} %get-tuple-element.173), kind=kOutput, calls=%fused_computation.1 | convolution fusion | flops 543162368 | bytes 4341760 | tf_op jit(solution)/shard_map/dot_general | solution.py:46
  31.7 3.1 %copy.15 = bf16[8,8,128,256]{3,2,1,0:T(8,128)(2,1)} copy(bf16[8,8,128,256]{3,1,2,0:T(8,128)(2,1)S(1)} %bitcast.76) | data formatting | bytes 8388608
  36.0 7.6 %shard_map.110 = f32[512,1024]{1,0:T(8,128)} custom-call(bf16[64,128,256]{2,1,0:T(8,128)(2,1)} %bitcast.75, bf16[640,1024]{1,0:T(8,128)(2,1)} %pad_maximum_fusion.3.rows_ref), custom_call_target="tpu_custom_call" | custom-call | tf_op jit(solution)/shard_map/pallas_call | solution.py:78
  43.7 4.0 %multiply_convert_fusion.1 = (bf16[512,1024]{1,0:T(8,128)(2,1)}, f32[512,1024]{1,0:T(8,128)S(1)}) fusion(f32[512,1024]{1,0:T(8,128)} %shard_map.110, bf16[512,1024]{1,0:T(8,128)(2,1)S(1)} %copy-done.8, bf16[6,1024]{1,0:T(8,128)(2,1)S(1)} %get-tuple-element.197, f32[1024]{0:T(1024)S(1)} %bitcast.111, f32[1024]{0:T(1024)S(1)} %bitcast.113, ...), kind=kLoop, calls=%fused_computation.107 | loop fusion | flops 20971520 | bytes 6332416 | tf_op jit(solution)/shard_map/convert_element_type | solution.py:107
  47.7 7.1 %multiply_convert_fusion = bf16[1024,4096]{1,0:T(8,128)(2,1)S(1)} fusion(bf16[512,1024]{1,0:T(8,128)(2,1)} %get-tuple-element.76, bf16[512,4096]{1,0:T(8,128)(2,1)} %all-gather.2.cloned.1.call-done), kind=kOutput, calls=%fused_computation.3 | convolution fusion | flops 4303355904 | bytes 13631488 | tf_op jit(solution)/shard_map/dot_general | solution.py:201
  54.8 3.4 %copy-done.5 = bf16[1024,4096]{1,0:T(8,128)(2,1)} copy-done((bf16[1024,4096]{1,0:T(8,128)(2,1)}, bf16[1024,4096]{1,0:T(8,128)(2,1)S(1)}, u32[]{:S(2)}) %copy-start.5) | copy-done | bytes 8388632
  59.1 1.6 collective-permute-start.2
  61.1 9.5 %convolution_convert_fusion.2 = bf16[512,4096]{1,0:T(8,128)(2,1)} fusion(bf16[512,1024]{1,0:T(8,128)(2,1)S(1)} %copy-done.9, bf16[1024,4096]{1,0:T(8,128)(2,1)} %param.12), kind=kOutput, calls=%fused_computation.7 | convolution fusion | flops 4297064448 | bytes 13631488 | tf_op jit(solution)/shard_map/dot_general | solution.py:117
  70.7 1.8 collective-permute-done.2
  73.6 2.6 %add_convert_fusion.12 = (bf16[1024,256]{1,0:T(8,128)(2,1)}, bf16[1024,256]{1,0:T(8,128)(2,1)}) fusion(bf16[1024,256]{1,0:T(8,128)(2,1)} %collective-permute-done.3, bf16[1024,4096]{1,0:T(8,128)(2,1)} %copy-done.5, s32[]{:T(128)S(6)} %select_n.533, s32[]{:T(128)S(6)} %select_n.524, bf16[1024,256]{1,0:T(8,128)(2,1)S(1)} %collective-permute-done.2), kind=kLoop, calls=%fused_computation.154 | loop fusion | flops 2097152 | bytes 3145736 | tf_op jit(solution)/shard_map/convert_element_type | solution.py:218
  76.2 1.6 collective-permute-start.4
  78.2 9.4 %fusion.79 = f32[1024,512]{0,1:T(8,128)S(1)} fusion(bf16[1024,4096]{1,0:T(8,128)(2,1)} %param.12, bf16[512,4096]{1,0:T(8,128)(2,1)} %all-gather.2.cloned.1.call-done), kind=kOutput, calls=%fused_computation.182 | convolution fusion | flops 4294967296 | bytes 14680064 | tf_op jit(solution)/shard_map/dot_general | solution.py:128
  87.6 2.1 %bitcast_multiply_fusion = (f32[512,1024]{1,0:T(8,128)}, bf16[512,1024]{1,0:T(8,128)(2,1)S(1)}) fusion(f32[512,1024]{1,0:T(8,128)S(1)} %copy-done.1, f32[1024,512]{0,1:T(8,128)S(1)} %fusion.79, f32[512,1024]{1,0:T(8,128)S(1)} %get-tuple-element.148), kind=kLoop, calls=%fused_computation.104 | loop fusion | flops 1572864 | bytes 9437184 | tf_op jit(solution)/shard_map/mul | solution.py:132
  89.8 1.3 collective-permute-start.6
  91.1 6.9 %collective-permute-done.6 = bf16[128,1024]{1,0:T(8,128)(2,1)S(1)} collective-permute-done((bf16[128,1024]{1,0:T(8,128)(2,1)S(1)}, bf16[128,1024]{1,0:T(8,128)(2,1)S(1)}, u32[]{:S(2)}, u32[]{:S(2)}) %collective-permute-start.6) | collective-permute-done | bytes 262176 | tf_op jit(solution)/shard_map/ppermute | solution.py:13
  98.0 1.9 add_convert_fusion.10
  99.9 1.7 collective-permute-start.7
  102.0 3.9 %convolution_convert_fusion = bf16[32768,64]{0,1:T(8,128)(2,1)S(1)} fusion(bf16[64,128]{1,0:T(8,128)(2,1)S(1)} %copy-done, s32[32768]{0:T(1024)S(1)} %get-tuple-element.172), kind=kOutput, calls=%fused_computation | convolution fusion | flops 543162368 | bytes 4341760 | tf_op jit(solution)/shard_map/dot_general | solution.py:46
  105.9 3.0 %copy.17 = bf16[8,8,128,256]{3,2,1,0:T(8,128)(2,1)} copy(bf16[8,8,128,256]{3,1,2,0:T(8,128)(2,1)S(1)} %bitcast.77) | data formatting | bytes 8388608
  108.9 1.6 collective-permute-done.7
  110.5 1.3 collective-permute-done.8
  111.8 2.4 %add_convert_fusion.8 = (bf16[1024,256]{1,0:T(8,128)(2,1)}, bf16[1024,256]{1,0:T(8,128)(2,1)}) fusion(bf16[1024,256]{1,0:T(8,128)(2,1)S(1)} %collective-permute-done.8, bf16[1024,4096]{1,0:T(8,128)(2,1)} %copy-done.5, s32[]{:T(128)S(6)} %select_n.569, s32[]{:T(128)S(6)} %select_n.560, bf16[1024,256]{1,0:T(8,128)(2,1)S(1)} %collective-permute-done.7), kind=kLoop, calls=%fused_computation.150 | loop fusion | flops 2097152 | bytes 3145736 | tf_op jit(solution)/shard_map/convert_element_type | solution.py:218
  114.7 1.6 collective-permute-start.9
  117.5 7.5 %shard_map.111 = f32[512,1024]{1,0:T(8,128)} custom-call(bf16[64,128,256]{2,1,0:T(8,128)(2,1)} %bitcast.74, bf16[640,1024]{1,0:T(8,128)(2,1)} %pad_maximum_fusion.4.rows_ref), custom_call_target="tpu_custom_call" | custom-call | tf_op jit(solution)/shard_map/pallas_call | solution.py:78
  125.0 3.5 %fusion.75 = (f32[512,1024]{1,0:T(8,128)S(1)}, f32[512,1024]{1,0:T(8,128)S(1)}) fusion(f32[512,1024]{1,0:T(8,128)} %shard_map.111, f32[512,1024]{1,0:T(8,128)} %get-tuple-element.151, f32[512,1024]{1,0:T(8,128)} %get-tuple-element.150), kind=kLoop, calls=%fused_computation.178 | loop fusion | flops 1048576 | bytes 10485760 | tf_op jit(solution)/shard_map/mul | solution.py:142
  128.6 1.2 copy-done.2
  130.6 1.3 collective-permute-start.11
  132.2 4.9 %collective-permute-done.11 = bf16[3,6,1024]{2,1,0:T(8,128)(2,1)S(1)} collective-permute-done((bf16[3,6,1024]{2,1,0:T(8,128)(2,1)S(1)}, bf16[3,6,1024]{2,1,0:T(8,128)(2,1)S(1)}, u32[]{:S(2)}, u32[]{:S(2)}) %collective-permute-start.11) | collective-permute-done | bytes 36896 | tf_op jit(solution)/shard_map/ppermute | solution.py:13
  137.1 1.8 add_convert_fusion.6
  138.9 1.3 collective-permute-start.12
  141.1 3.0 %fusion.40 = bf16[512,1024]{1,0:T(8,128)(2,1)} fusion(f32[6,1024]{1,0:T(8,128)S(1)} %bitcast_convert_fusion.2, f32[512,1024]{1,0:T(8,128)S(1)} %copy-done.4, f32[1024]{0:T(1024)S(1)} %bitcast.112, f32[1024]{0:T(1024)S(1)} %bitcast.114, f32[1024]{0:T(1024)S(1)} %bitcast.116, f32[1024]{0:T(1024)S(1)} %bitcast.118, f32[1024]{0:T(1024)S(1)} %bitcast.120, ...), kind=kLoop, calls=%fused_computation.76 | loop fusion | flops 10485760 | bytes 3198976 | tf_op jit(solution)/shard_map/convert_element_type | solution.py:160
  144.1 5.3 %collective-permute-done.12 = bf16[1024,256]{1,0:T(8,128)(2,1)S(1)} collective-permute-done((bf16[1024,256]{1,0:T(8,128)(2,1)S(1)}, bf16[1024,256]{1,0:T(8,128)(2,1)S(1)}, u32[]{:S(2)}, u32[]{:S(2)}) %collective-permute-start.12) | collective-permute-done | bytes 524320 | tf_op jit(solution)/shard_map/ppermute | solution.py:223
  150.3 1.5 add_convert_fusion.4
  151.9 2.1 %collective-permute-start.14 = (bf16[1024,256]{1,0:T(8,128)(2,1)S(1)}, bf16[1024,256]{1,0:T(8,128)(2,1)S(1)}, u32[]{:S(2)}, u32[]{:S(2)}) collective-permute-start(bf16[1024,256]{1,0:T(8,128)(2,1)S(1)} %get-tuple-element.126), channel_id=1, source_target_pairs={{0,8},{8,16},{16,24},{24,28},{28,20},{20,12},{12,4},{4,0},{1,9},{9... | collective-permute-start | bytes 1572872 | tf_op jit(solution)/shard_map/ppermute | solution.py:223
  154.1 3.0 %fusion.6 = bf16[512,1024]{1,0:T(8,128)(2,1)} fusion(f32[6,1024]{1,0:T(8,128)S(1)} %get-tuple-element.195, f32[512,1024]{1,0:T(8,128)S(1)} %copy-done.3, f32[1024]{0:T(1024)S(1)} %bitcast.108, f32[1024]{0:T(1024)S(1)} %bitcast.106, f32[1024]{0:T(1024)S(1)} %bitcast.96, f32[1024]{0:T(1024)S(1)} %bitcast.98, f32[1024]{0:T(1024)S(1)} %bitcast.100, ...), kind=kLoop, calls=%fused_computation.42 | loop fusion | flops 10485760 | bytes 3198976 | tf_op jit(solution)/shard_map/convert_element_type | solution.py:160
  157.1 3.0 %fusion.23 = bf16[512,1024]{1,0:T(8,128)(2,1)} fusion(f32[6,1024]{1,0:T(8,128)S(1)} %get-tuple-element.196, f32[512,1024]{1,0:T(8,128)S(1)} %get-tuple-element.128, f32[1024]{0:T(1024)S(1)} %bitcast.82, f32[1024]{0:T(1024)S(1)} %bitcast.84, f32[1024]{0:T(1024)S(1)} %bitcast.86, f32[1024]{0:T(1024)S(1)} %bitcast.88, f32[1024]{0:T(1024)S(1)} %bitcast.90, ...), kind=kLoop, calls=%fused_computation.59 | loop fusion | flops 10485760 | bytes 3198976 | tf_op jit(solution)/shard_map/convert_element_type | solution.py:160
  160.1 3.2 %collective-permute-done.14 = bf16[1024,256]{1,0:T(8,128)(2,1)S(1)} collective-permute-done((bf16[1024,256]{1,0:T(8,128)(2,1)S(1)}, bf16[1024,256]{1,0:T(8,128)(2,1)S(1)}, u32[]{:S(2)}, u32[]{:S(2)}) %collective-permute-start.14) | collective-permute-done | bytes 524320 | tf_op jit(solution)/shard_map/ppermute | solution.py:223
  163.3 2.6 %collective-permute-done.15 = bf16[1024,256]{1,0:T(8,128)(2,1)S(1)} collective-permute-done((bf16[1024,256]{1,0:T(8,128)(2,1)S(1)}, bf16[1024,256]{1,0:T(8,128)(2,1)S(1)}, u32[]{:S(2)}, u32[]{:S(2)}) %collective-permute-start.15) | collective-permute-done | bytes 524320 | tf_op jit(solution)/shard_map/ppermute | solution.py:224
  165.9 1.5 add_convert_fusion.2
  167.5 2.0 %collective-permute-start.17 = (bf16[1024,256]{1,0:T(8,128)(2,1)S(1)}, bf16[1024,256]{1,0:T(8,128)(2,1)S(1)}, u32[]{:S(2)}, u32[]{:S(2)}) collective-permute-start(bf16[1024,256]{1,0:T(8,128)(2,1)S(1)} %get-tuple-element.138), channel_id=1, source_target_pairs={{8,0},{16,8},{24,16},{28,24},{20,28},{12,20},{4,12},{0,4},{9,1},{1... | collective-permute-start | bytes 1572872 | tf_op jit(solution)/shard_map/ppermute | solution.py:224
  169.5 7.2 %collective-permute-done.16 = bf16[1024,256]{1,0:T(8,128)(2,1)S(1)} collective-permute-done((bf16[1024,256]{1,0:T(8,128)(2,1)S(1)}, bf16[1024,256]{1,0:T(8,128)(2,1)S(1)}, u32[]{:S(2)}, u32[]{:S(2)}) %collective-permute-start.16) | collective-permute-done | bytes 524320 | tf_op jit(solution)/shard_map/ppermute | solution.py:223
  176.7 1.3 collective-permute-done.17
  178.0 1.5 add_convert_fusion.1
  (134 shorter events, 12.7 us)
Async XLA Ops:
  7.2 20.6 %copy-start = (bf16[64,128]{1,0:T(8,128)(2,1)S(1)}, bf16[64,128]{1,0:T(8,128)(2,1)}, u32[]{:S(2)}) copy-start(bf16[64,128]{1,0:T(8,128)(2,1)} %param.11) | copy-start | bytes 49156
  7.2 11.0 %copy-start.7 = (bf16[512,1024]{1,0:T(8,128)(2,1)S(1)}, bf16[512,1024]{1,0:T(8,128)(2,1)}, u32[]{:S(2)}) copy-start(bf16[512,1024]{1,0:T(8,128)(2,1)} %param.8) | copy-start | bytes 3145732
  7.2 11.0 %copy-start.6 = (bf16[512,1024]{1,0:T(8,128)(2,1)S(1)}, bf16[512,1024]{1,0:T(8,128)(2,1)}, u32[]{:S(2)}) copy-start(bf16[512,1024]{1,0:T(8,128)(2,1)} %param.9) | copy-start | bytes 3145732
  7.2 40.5 %all-gather.2.cloned.1.call-start = ((), (), s32[]{:S(2)}) async-start(), calls=%async_computation.1 | async-start | bytes 5242880 | tf_op jit(solution)/shard_map/all_gather | solution.py:94
  7.9 172.6 %reduce-scatter.2.cloned.1.call-start = ((), (), s32[]{:S(2)}) async-start(), calls=%async_computation.2 | async-start | bytes 5242880 | tf_op jit(solution)/shard_map/reduce_scatter | solution.py:116
  9.5 8.7 %collective-permute-start = (bf16[3,6,1024]{2,1,0:T(8,128)(2,1)S(1)}, bf16[3,6,1024]{2,1,0:T(8,128)(2,1)S(1)}, u32[]{:S(2)}, u32[]{:S(2)}) collective-permute-start(bf16[3,6,1024]{2,1,0:T(8,128)(2,1)S(1)} %pad_maximum_fusion.9), channel_id=1, source_target_pairs={{0,4},{4,8},{8,12},{12,16},{16,20},{20,24},{24,28},{1,5},{5,9},{9,... | collective-permute-start | bytes 110600 | tf_op jit(solution)/shard_map/ppermute | solution.py:13
  24.1 10.7 %collective-permute-start.1 = (bf16[128,1024]{1,0:T(8,128)(2,1)S(1)}, bf16[128,1024]{1,0:T(8,128)(2,1)S(1)}, u32[]{:S(2)}, u32[]{:S(2)}) collective-permute-start(bf16[128,1024]{1,0:T(8,128)(2,1)S(1)} %slice.389), channel_id=1, source_target_pairs={{0,4},{4,8},{8,12},{12,16},{16,20},{20,24},{24,28},{1,5},{5,9},{9,... | collective-permute-start | bytes 786440 | tf_op jit(solution)/shard_map/ppermute | solution.py:13
  36.0 7.6 %copy-start.8 = (bf16[512,1024]{1,0:T(8,128)(2,1)S(1)}, bf16[512,1024]{1,0:T(8,128)(2,1)}, u32[]{:S(2)}) copy-start(bf16[512,1024]{1,0:T(8,128)(2,1)} %param.7) | copy-start | bytes 3145732
  36.0 7.6 %copy-start.32 = (f32[1,1,1024]{2,0,1:T(1,128)S(1)}, f32[1,1,1024]{2,0,1:T(1,128)}, u32[]{:S(2)}) copy-start(f32[1,1,1024]{2,0,1:T(1,128)} %get-tuple-element.174) | copy-start | bytes 12292
  36.0 7.6 %copy-start.34 = (f32[1,1,1024]{2,0,1:T(1,128)S(1)}, f32[1,1,1024]{2,0,1:T(1,128)}, u32[]{:S(2)}) copy-start(f32[1,1,1024]{2,0,1:T(1,128)} %get-tuple-element.187) | copy-start | bytes 12292
  36.0 7.6 %copy-start.36 = (f32[1,1,1024]{2,0,1:T(1,128)S(1)}, f32[1,1,1024]{2,0,1:T(1,128)}, u32[]{:S(2)}) copy-start(f32[1,1,1024]{2,0,1:T(1,128)} %get-tuple-element.188) | copy-start | bytes 12292
  36.0 7.6 %copy-start.38 = (f32[1,1,1024]{2,0,1:T(1,128)S(1)}, f32[1,1,1024]{2,0,1:T(1,128)}, u32[]{:S(2)}) copy-start(f32[1,1,1024]{2,0,1:T(1,128)} %get-tuple-element.189) | copy-start | bytes 12292
  36.0 7.6 %copy-start.40 = (f32[1,1,1024]{2,0,1:T(1,128)S(1)}, f32[1,1,1024]{2,0,1:T(1,128)}, u32[]{:S(2)}) copy-start(f32[1,1,1024]{2,0,1:T(1,128)} %get-tuple-element.190) | copy-start | bytes 12292
  36.0 7.6 %copy-start.42 = (f32[1,1,1024]{2,0,1:T(1,128)S(1)}, f32[1,1,1024]{2,0,1:T(1,128)}, u32[]{:S(2)}) copy-start(f32[1,1,1024]{2,0,1:T(1,128)} %get-tuple-element.191) | copy-start | bytes 12292
  36.0 7.6 %copy-start.44 = (f32[1,1,1024]{2,0,1:T(1,128)S(1)}, f32[1,1,1024]{2,0,1:T(1,128)}, u32[]{:S(2)}) copy-start(f32[1,1,1024]{2,0,1:T(1,128)} %get-tuple-element.192) | copy-start | bytes 12292
  59.1 13.4 %collective-permute-start.2 = (bf16[1024,256]{1,0:T(8,128)(2,1)}, bf16[1024,256]{1,0:T(8,128)(2,1)S(1)}, u32[]{:S(2)}, u32[]{:S(2)}) collective-permute-start(bf16[1024,256]{1,0:T(8,128)(2,1)} %get-tuple-element.78), channel_id=1, source_target_pairs={{0,8},{8,16},{16,24},{24,28},{28,20},{20,12},{12,4},{4,0},{1,9},{9... | collective-permute-start | bytes 1572872 | tf_op jit(solution)/shard_map/ppermute | solution.py:223
  60.6 12.9 %collective-permute-start.3 = (bf16[1024,256]{1,0:T(8,128)(2,1)S(1)}, bf16[1024,256]{1,0:T(8,128)(2,1)}, u32[]{:S(2)}, u32[]{:S(2)}) collective-permute-start(bf16[1024,256]{1,0:T(8,128)(2,1)S(1)} %get-tuple-element.79), channel_id=1, source_target_pairs={{8,0},{16,8},{24,16},{28,24},{20,28},{12,20},{4,12},{0,4},{9,1},{1... | collective-permute-start | bytes 1572872 | tf_op jit(solution)/shard_map/ppermute | solution.py:224
  76.2 11.5 %copy-start.1 = (f32[512,1024]{1,0:T(8,128)S(1)}, f32[512,1024]{1,0:T(8,128)}, u32[]{:S(2)}) copy-start(f32[512,1024]{1,0:T(8,128)} %shard_map.110) | copy-start | bytes 6291460
  76.2 21.9 %collective-permute-start.4 = (bf16[1024,256]{1,0:T(8,128)(2,1)}, bf16[1024,256]{1,0:T(8,128)(2,1)}, u32[]{:S(2)}, u32[]{:S(2)}) collective-permute-start(bf16[1024,256]{1,0:T(8,128)(2,1)} %get-tuple-element.83), channel_id=1, source_target_pairs={{0,8},{8,16},{16,24},{24,28},{28,20},{20,12},{12,4},{4,0},{1,9},{9... | collective-permute-start | bytes 1572872 | tf_op jit(solution)/shard_map/ppermute | solution.py:223
  77.7 20.3 %collective-permute-start.5 = (bf16[1024,256]{1,0:T(8,128)(2,1)}, bf16[1024,256]{1,0:T(8,128)(2,1)}, u32[]{:S(2)}, u32[]{:S(2)}) collective-permute-start(bf16[1024,256]{1,0:T(8,128)(2,1)} %get-tuple-element.84), channel_id=1, source_target_pairs={{8,0},{16,8},{24,16},{28,24},{20,28},{12,20},{4,12},{0,4},{9,1},{1... | collective-permute-start | bytes 1572872 | tf_op jit(solution)/shard_map/ppermute | solution.py:224
  89.8 8.3 %collective-permute-start.6 = (bf16[128,1024]{1,0:T(8,128)(2,1)S(1)}, bf16[128,1024]{1,0:T(8,128)(2,1)S(1)}, u32[]{:S(2)}, u32[]{:S(2)}) collective-permute-start(bf16[128,1024]{1,0:T(8,128)(2,1)S(1)} %slice.390), channel_id=1, source_target_pairs={{4,0},{8,4},{12,8},{16,12},{20,16},{24,20},{28,24},{5,1},{9,5},{13... | collective-permute-start | bytes 786440 | tf_op jit(solution)/shard_map/ppermute | solution.py:13
  99.9 10.6 %collective-permute-start.7 = (bf16[1024,256]{1,0:T(8,128)(2,1)S(1)}, bf16[1024,256]{1,0:T(8,128)(2,1)S(1)}, u32[]{:S(2)}, u32[]{:S(2)}) collective-permute-start(bf16[1024,256]{1,0:T(8,128)(2,1)S(1)} %get-tuple-element.91), channel_id=1, source_target_pairs={{0,8},{8,16},{16,24},{24,28},{28,20},{20,12},{12,4},{4,0},{1,9},{9... | collective-permute-start | bytes 1572872 | tf_op jit(solution)/shard_map/ppermute | solution.py:223
  101.6 10.3 %collective-permute-start.8 = (bf16[1024,256]{1,0:T(8,128)(2,1)S(1)}, bf16[1024,256]{1,0:T(8,128)(2,1)S(1)}, u32[]{:S(2)}, u32[]{:S(2)}) collective-permute-start(bf16[1024,256]{1,0:T(8,128)(2,1)S(1)} %get-tuple-element.92), channel_id=1, source_target_pairs={{8,0},{16,8},{24,16},{28,24},{20,28},{12,20},{4,12},{0,4},{9,1},{1... | collective-permute-start | bytes 1572872 | tf_op jit(solution)/shard_map/ppermute | solution.py:224
  114.3 22.8 %collective-permute-start.10 = (bf16[1024,256]{1,0:T(8,128)(2,1)}, bf16[1024,256]{1,0:T(8,128)(2,1)}, u32[]{:S(2)}, u32[]{:S(2)}) collective-permute-start(bf16[1024,256]{1,0:T(8,128)(2,1)} %get-tuple-element.103), channel_id=1, source_target_pairs={{8,0},{16,8},{24,16},{28,24},{20,28},{12,20},{4,12},{0,4},{9,1},{1... | collective-permute-start | bytes 1572872 | tf_op jit(solution)/shard_map/ppermute | solution.py:224
  114.7 22.4 %collective-permute-start.9 = (bf16[1024,256]{1,0:T(8,128)(2,1)}, bf16[1024,256]{1,0:T(8,128)(2,1)}, u32[]{:S(2)}, u32[]{:S(2)}) collective-permute-start(bf16[1024,256]{1,0:T(8,128)(2,1)} %get-tuple-element.102), channel_id=1, source_target_pairs={{0,8},{8,16},{16,24},{24,28},{28,20},{20,12},{12,4},{4,0},{1,9},{9... | collective-permute-start | bytes 1572872 | tf_op jit(solution)/shard_map/ppermute | solution.py:223
  128.5 12.5 %copy-start.33 = (f32[1,1,1024]{2,0,1:T(1,128)S(1)}, f32[1,1,1024]{2,0,1:T(1,128)}, u32[]{:S(2)}) copy-start(f32[1,1,1024]{2,0,1:T(1,128)} %get-tuple-element.174) | copy-start | bytes 12292
  128.5 12.5 %copy-start.35 = (f32[1,1,1024]{2,0,1:T(1,128)S(1)}, f32[1,1,1024]{2,0,1:T(1,128)}, u32[]{:S(2)}) copy-start(f32[1,1,1024]{2,0,1:T(1,128)} %get-tuple-element.187) | copy-start | bytes 12292
  128.6 12.5 %copy-start.37 = (f32[1,1,1024]{2,0,1:T(1,128)S(1)}, f32[1,1,1024]{2,0,1:T(1,128)}, u32[]{:S(2)}) copy-start(f32[1,1,1024]{2,0,1:T(1,128)} %get-tuple-element.188) | copy-start | bytes 12292
  128.6 12.5 %copy-start.39 = (f32[1,1,1024]{2,0,1:T(1,128)S(1)}, f32[1,1,1024]{2,0,1:T(1,128)}, u32[]{:S(2)}) copy-start(f32[1,1,1024]{2,0,1:T(1,128)} %get-tuple-element.189) | copy-start | bytes 12292
  128.6 12.5 %copy-start.41 = (f32[1,1,1024]{2,0,1:T(1,128)S(1)}, f32[1,1,1024]{2,0,1:T(1,128)}, u32[]{:S(2)}) copy-start(f32[1,1,1024]{2,0,1:T(1,128)} %get-tuple-element.190) | copy-start | bytes 12292
  128.6 12.5 %copy-start.43 = (f32[1,1,1024]{2,0,1:T(1,128)S(1)}, f32[1,1,1024]{2,0,1:T(1,128)}, u32[]{:S(2)}) copy-start(f32[1,1,1024]{2,0,1:T(1,128)} %get-tuple-element.191) | copy-start | bytes 12292
  128.6 12.5 %copy-start.45 = (f32[1,1,1024]{2,0,1:T(1,128)S(1)}, f32[1,1,1024]{2,0,1:T(1,128)}, u32[]{:S(2)}) copy-start(f32[1,1,1024]{2,0,1:T(1,128)} %get-tuple-element.192) | copy-start | bytes 12292
  130.6 6.5 %collective-permute-start.11 = (bf16[3,6,1024]{2,1,0:T(8,128)(2,1)S(1)}, bf16[3,6,1024]{2,1,0:T(8,128)(2,1)S(1)}, u32[]{:S(2)}, u32[]{:S(2)}) collective-permute-start(bf16[3,6,1024]{2,1,0:T(8,128)(2,1)S(1)} %pad_maximum_fusion.10), channel_id=1, source_target_pairs={{4,0},{8,4},{12,8},{16,12},{20,16},{24,20},{28,24},{5,1},{9,5},{13... | collective-permute-start | bytes 110600 | tf_op jit(solution)/shard_map/ppermute | solution.py:13
  132.2 8.9 %copy-start.4 = (f32[512,1024]{1,0:T(8,128)S(1)}, f32[512,1024]{1,0:T(8,128)}, u32[]{:S(2)}) copy-start(f32[512,1024]{1,0:T(8,128)} %get-tuple-element.116) | copy-start | bytes 6291460
  138.9 10.4 %collective-permute-start.12 = (bf16[1024,256]{1,0:T(8,128)(2,1)S(1)}, bf16[1024,256]{1,0:T(8,128)(2,1)S(1)}, u32[]{:S(2)}, u32[]{:S(2)}) collective-permute-start(bf16[1024,256]{1,0:T(8,128)(2,1)S(1)} %get-tuple-element.114), channel_id=1, source_target_pairs={{0,8},{8,16},{16,24},{24,28},{28,20},{20,12},{12,4},{4,0},{1,9},{9... | collective-permute-start | bytes 1572872 | tf_op jit(solution)/shard_map/ppermute | solution.py:223
  140.2 10.1 %collective-permute-start.13 = (bf16[1024,256]{1,0:T(8,128)(2,1)S(1)}, bf16[1024,256]{1,0:T(8,128)(2,1)S(1)}, u32[]{:S(2)}, u32[]{:S(2)}) collective-permute-start(bf16[1024,256]{1,0:T(8,128)(2,1)S(1)} %get-tuple-element.115), channel_id=1, source_target_pairs={{8,0},{16,8},{24,16},{28,24},{20,28},{12,20},{4,12},{0,4},{9,1},{1... | collective-permute-start | bytes 1572872 | tf_op jit(solution)/shard_map/ppermute | solution.py:224
  144.1 9.9 %copy-start.3 = (f32[512,1024]{1,0:T(8,128)S(1)}, f32[512,1024]{1,0:T(8,128)}, u32[]{:S(2)}) copy-start(f32[512,1024]{1,0:T(8,128)} %copy-done.2) | copy-start | bytes 6291460
  144.1 9.9 %copy-start.25 = (f32[1,1,1024]{2,0,1:T(1,128)S(1)}, f32[1,1,1024]{2,0,1:T(1,128)}, u32[]{:S(2)}) copy-start(f32[1,1,1024]{2,0,1:T(1,128)} %copy-done.24) | copy-start | bytes 12292
  144.1 9.9 %copy-start.26 = (f32[1,1,1024]{2,0,1:T(1,128)S(1)}, f32[1,1,1024]{2,0,1:T(1,128)}, u32[]{:S(2)}) copy-start(f32[1,1,1024]{2,0,1:T(1,128)} %get-tuple-element.176) | copy-start | bytes 12292
  144.1 9.9 %copy-start.27 = (f32[1,1,1024]{2,0,1:T(1,128)S(1)}, f32[1,1,1024]{2,0,1:T(1,128)}, u32[]{:S(2)}) copy-start(f32[1,1,1024]{2,0,1:T(1,128)} %get-tuple-element.177) | copy-start | bytes 12292
  144.1 9.9 %copy-start.28 = (f32[1,1,1024]{2,0,1:T(1,128)S(1)}, f32[1,1,1024]{2,0,1:T(1,128)}, u32[]{:S(2)}) copy-start(f32[1,1,1024]{2,0,1:T(1,128)} %get-tuple-element.178) | copy-start | bytes 12292
  144.1 9.9 %copy-start.29 = (f32[1,1,1024]{2,0,1:T(1,128)S(1)}, f32[1,1,1024]{2,0,1:T(1,128)}, u32[]{:S(2)}) copy-start(f32[1,1,1024]{2,0,1:T(1,128)} %get-tuple-element.179) | copy-start | bytes 12292
  144.1 9.9 %copy-start.30 = (f32[1,1,1024]{2,0,1:T(1,128)S(1)}, f32[1,1,1024]{2,0,1:T(1,128)}, u32[]{:S(2)}) copy-start(f32[1,1,1024]{2,0,1:T(1,128)} %get-tuple-element.193) | copy-start | bytes 12292
  144.1 9.9 %copy-start.31 = (f32[1,1,1024]{2,0,1:T(1,128)S(1)}, f32[1,1,1024]{2,0,1:T(1,128)}, u32[]{:S(2)}) copy-start(f32[1,1,1024]{2,0,1:T(1,128)} %get-tuple-element.194) | copy-start | bytes 12292
  151.9 11.4 %collective-permute-start.14 = (bf16[1024,256]{1,0:T(8,128)(2,1)S(1)}, bf16[1024,256]{1,0:T(8,128)(2,1)S(1)}, u32[]{:S(2)}, u32[]{:S(2)}) collective-permute-start(bf16[1024,256]{1,0:T(8,128)(2,1)S(1)} %get-tuple-element.126), channel_id=1, source_target_pairs={{0,8},{8,16},{16,24},{24,28},{28,20},{20,12},{12,4},{4,0},{1,9},{9... | collective-permute-start | bytes 1572872 | tf_op jit(solution)/shard_map/ppermute | solution.py:223
  154.0 12.0 %collective-permute-start.15 = (bf16[1024,256]{1,0:T(8,128)(2,1)S(1)}, bf16[1024,256]{1,0:T(8,128)(2,1)S(1)}, u32[]{:S(2)}, u32[]{:S(2)}) collective-permute-start(bf16[1024,256]{1,0:T(8,128)(2,1)S(1)} %get-tuple-element.127), channel_id=1, source_target_pairs={{8,0},{16,8},{24,16},{28,24},{20,28},{12,20},{4,12},{0,4},{9,1},{1... | collective-permute-start | bytes 1572872 | tf_op jit(solution)/shard_map/ppermute | solution.py:224
  167.4 9.2 %collective-permute-start.16 = (bf16[1024,256]{1,0:T(8,128)(2,1)S(1)}, bf16[1024,256]{1,0:T(8,128)(2,1)S(1)}, u32[]{:S(2)}, u32[]{:S(2)}) collective-permute-start(bf16[1024,256]{1,0:T(8,128)(2,1)S(1)} %get-tuple-element.137), channel_id=1, source_target_pairs={{0,8},{8,16},{16,24},{24,28},{28,20},{20,12},{12,4},{4,0},{1,9},{9... | collective-permute-start | bytes 1572872 | tf_op jit(solution)/shard_map/ppermute | solution.py:223
  167.5 10.5 %collective-permute-start.17 = (bf16[1024,256]{1,0:T(8,128)(2,1)S(1)}, bf16[1024,256]{1,0:T(8,128)(2,1)S(1)}, u32[]{:S(2)}, u32[]{:S(2)}) collective-permute-start(bf16[1024,256]{1,0:T(8,128)(2,1)S(1)} %get-tuple-element.138), channel_id=1, source_target_pairs={{8,0},{16,8},{24,16},{28,24},{20,28},{12,20},{4,12},{0,4},{9,1},{1... | collective-permute-start | bytes 1572872 | tf_op jit(solution)/shard_map/ppermute | solution.py:224
  (18 other events, 104.9 us)
Sparse Core Ops, SparseCore 0:
  9.6 37.1 all-gather.1
  70.8 44.8 reduce-scatter.1
